TPU v7x, 32 devices: a whole 2x2x4 slice. The times are simulated.
32 devices in a mesh: ctx: 8 (over y, x, core), mp: 4 (over z).
Axes of the slice: x: 2, y: 2, z: 4, core: 2. Of those that a mesh axis runs over, the one named last changes fastest.
Arguments:
- cotangent: bfloat16 [1536, 8192], P('ctx', 'mp'), may hold values from -6 to 6
- out_weight: bfloat16 [8192, 8192], P('mp', 'ctx'), may hold values from -0.0625 to 0.0625
- query_act: bfloat16 [1536, 8192], P('ctx', 'mp'), may hold values from -6 to 6
- key_act: bfloat16 [1536, 8192], P('ctx', 'mp'), may hold values from -6 to 6
- value_act: bfloat16 [1536, 8192], P('ctx', 'mp'), may hold values from -6 to 6
- filters: float32 [512, 128], replicated, may hold values from -0.5 to 0.5
Outputs:
- grad_query: bfloat16 [1536, 8192], P('ctx', 'mp')
- grad_key: bfloat16 [1536, 8192], P('ctx', 'mp')
- grad_value: bfloat16 [1536, 8192], P('ctx', 'mp')
- grad_filters: float32 [512, 128], replicated
All inputs are finite; a program needn't handle non-finite values.
Results may differ from a plain program's by a relative error of at most 0.0051.
Values may be sent and summed in bfloat16 or wider, within the bound.
No kernel may reach another device: no remote copies, remote signals or barrier semaphores. Data moves between devices by JAX's collectives and lax.ppermute only.
A program may use at most 128 MiB of HBM per device.

v0:
```python
import jax
import jax.numpy as jnp
from jax import lax
from jax.sharding import PartitionSpec as P


def causal(widened, taps, rows, prev):

    def causal_step(shift, total):
        window = lax.dynamic_slice_in_dim(widened, (prev - shift).astype(jnp.int32), rows, 0)
        weight = lax.dynamic_slice_in_dim(taps, shift.astype(jnp.int32), 1, 0)
        return total + weight * window

    return lax.fori_loop(
        jnp.int32(0),
        jnp.int32(prev + 1),
        causal_step,
        jnp.zeros((rows, widened.shape[1]), widened.dtype),
    )


def anticausal(trailing, taps, rows, prev):

    def anticausal_step(shift, total):
        window = lax.dynamic_slice_in_dim(trailing, shift.astype(jnp.int32), rows, 0)
        weight = lax.dynamic_slice_in_dim(taps, shift.astype(jnp.int32), 1, 0)
        return total + weight * window

    return lax.fori_loop(
        jnp.int32(0),
        jnp.int32(prev + 1),
        anticausal_step,
        jnp.zeros((rows, trailing.shape[1]), trailing.dtype),
    )


def lagged(widened, gradient, prev):
    rows = gradient.shape[0]

    def one_lag(shift):
        window = lax.dynamic_slice_in_dim(widened, prev - shift, rows, 0)
        return jnp.sum(window * gradient, axis=0)

    return lax.map(one_lag, jnp.arange(prev + 1, dtype=jnp.int32))


def contract(left, right):
    return lax.dot_general(
        left, right, (((1,), (1,)), ((), ())), preferred_element_type=jnp.float32
    )


def group_table(first, count, per_group, groups):
    channel = first + jnp.arange(count)
    return (channel[None, :] // per_group == jnp.arange(groups)[:, None]).astype(jnp.float32)


def body(cotangent, out_weight, query_act, key_act, value_act, filters):
    tok_rows, chans = cotangent.shape
    groups, taps_len = filters.shape
    prev = taps_len - 1
    ctx_count = lax.axis_size("ctx")
    per_group = chans * lax.axis_size("mp") // groups
    panel = lax.all_gather(out_weight, "ctx", axis=1, tiled=True)
    grad_mixed = contract(lax.all_gather(cotangent, "mp", axis=1, tiled=True), panel)
    product = (key_act.astype(jnp.float32) * value_act.astype(jnp.float32)).astype(jnp.bfloat16)
    grad_conv = (grad_mixed * query_act.astype(jnp.float32)).astype(jnp.bfloat16)
    narrow = chans // ctx_count
    seq_product, seq_grad = (
        lax.all_to_all(product, "ctx", split_axis=1, concat_axis=0, tiled=True),
        lax.all_to_all(grad_conv, "ctx", split_axis=1, concat_axis=0, tiled=True),
    )
    onehot = group_table(
        lax.axis_index("mp") * chans + lax.axis_index("ctx") * narrow, narrow, per_group, groups
    )
    taps = jnp.dot(filters.T, onehot, precision=lax.Precision.HIGHEST)
    seq_rows = seq_grad.shape[0]
    grad_wide = seq_grad.astype(jnp.float32)
    widened = jnp.concatenate(
        [jnp.zeros((prev, narrow), jnp.float32), seq_product.astype(jnp.float32)], 0
    )
    trailing = jnp.concatenate([grad_wide, jnp.zeros((prev, narrow), jnp.float32)], 0)
    seq_mixed = causal(widened, taps, seq_rows, prev)
    seq_back = anticausal(trailing, taps, seq_rows, prev)
    corr = lagged(widened, grad_wide, prev)
    mixed, grad_product = (
        lax.all_to_all(seq_mixed, "ctx", split_axis=0, concat_axis=1, tiled=True),
        lax.all_to_all(seq_back, "ctx", split_axis=0, concat_axis=1, tiled=True),
    )
    grad_query = (grad_mixed * mixed).astype(jnp.bfloat16)
    grad_key = (grad_product * value_act.astype(jnp.float32)).astype(jnp.bfloat16)
    grad_value = (grad_product * key_act.astype(jnp.float32)).astype(jnp.bfloat16)
    partial_terms = jnp.dot(onehot, corr.T, precision=lax.Precision.HIGHEST)
    scale = (tok_rows * ctx_count * per_group) ** (-0.5)
    grad_filters = lax.psum(partial_terms, ("ctx", "mp")) * scale
    return (grad_query, grad_key, grad_value, grad_filters)


def solution(mesh):
    in_specs = (P("ctx", "mp"), P("mp", "ctx"), P("ctx", "mp"), P("ctx", "mp"), P("ctx", "mp"), P())
    out_specs = (P("ctx", "mp"), P("ctx", "mp"), P("ctx", "mp"), P())
    return jax.shard_map(body, mesh=mesh, in_specs=in_specs, out_specs=out_specs, check_vma=False)
```

profile of v0, /device:TPU:0, one launch (start us, length us, event | category | flops | bytes accessed | tf_op | source)
XLA Modules:
  0.0 1397.0 jit_solution(9679557478164837878)
XLA Ops:
  8.7 67.1 %all-gather.3.cloned.1.call-done = bf16[192,8192]{1,0:T(8,128)(2,1)} async-done(((bf16[192,2048]{1,0:T(8,128)(2,1)}), bf16[192,8192]{1,0:T(8,128)(2,1)}) %all-gather.3.cloned.1.call-update) | async-done | bytes 3145744 | tf_op jit(solution)/shard_map/all_gather | solution.py:65
  75.8 161.4 %all-gather.5.cloned.1.call-done = bf16[2048,8192]{1,0:T(8,128)(2,1)} async-done(((bf16[2048,1024]{1,0:T(8,128)(2,1)}), bf16[2048,8192]{1,0:T(8,128)(2,1)}) %all-gather.5.cloned.1.call-update) | async-done | bytes 33554448 | tf_op jit(solution)/shard_map/all_gather | solution.py:64
  237.2 18.0 %multiply_convert_fusion = (bf16[192,2048]{1,0:T(8,128)(2,1)S(1)}, f32[192,2048]{1,0:T(8,128)}) fusion(bf16[192,2048]{1,0:T(8,128)(2,1)S(1)} %copy-done.7, bf16[192,8192]{1,0:T(8,128)(2,1)} %all-gather.3.cloned.1.call-done, bf16[2048,8192]{1,0:T(8,128)(2,1)} %all-gather.5.cloned.1.call-done), kind=kOutput, calls=%fused_computation.11 | convolution fusion | flops 6443630592 | bytes 39845888 | tf_op jit(solution)/shard_map/dot_general | solution.py:48
  256.1 3.5 all-to-all-start.2
  260.5 11.8 all-to-all-done.2
  274.4 282.6 %while.38 = (s32[]{:T(128)}, f32[1536,256]{1,0:T(8,128)S(1)}, f32[128,256]{1,0:T(8,128)S(1)}, f32[1663,256]{1,0:T(8,128)}, s32[]{:T(128)}, /*index=5*/s32[]{:T(128)}) while((s32[]{:T(128)}, f32[1536,256]{1,0:T(8,128)S(1)}, f32[128,256]{1,0:T(8,128)S(1)}, f32[1663,256]{1,0:T(8,128)}, s32[]{:T(128)}, /*index=5*/s32[]{:T(128)}) %tuple.98), condition=%wide.region_3.4_spmd.clone, body=%wide.region_2.3_spmd.clone.sunk | while | flops 1179651 | bytes 4721759 | solution.py:29
  557.0 23.4 %all_to_all.64 = f32[8,192,256]{2,1,0:T(8,128)S(1)} all-to-all(f32[8,192,256]{2,1,0:T(8,128)S(1)} %bitcast.45), channel_id=1, replica_groups=mesh['ctx'=8,'mp'=4] {'ctx'}, dimensions={0} | all-to-all | bytes 3145728 | tf_op jit(solution)/shard_map/all_to_all | solution.py:88
  584.3 3.5 all-to-all-start
  587.9 12.5 all-to-all-done
  602.6 364.1 %while.37 = (s32[]{:T(128)}, f32[1536,256]{1,0:T(8,128)}, f32[128,256]{1,0:T(8,128)S(1)}, f32[1663,256]{1,0:T(8,128)S(1)}, s32[]{:T(128)}, /*index=5*/s32[]{:T(128)}, s32[]{:T(128)}, s32[]{:T(128)}) while((s32[]{:T(128)}, f32[1536,256]{1,0:T(8,128)}, f32[128,256]{1,0:T(8,128)S(1)}, f32[1663,256]{1,0:T(8,128)S(1)}, s32[]{:T(128)}, ...), condition=%wide.region_1.2_spmd.clone, body=%wide.region_0.1_spmd.clone.sunk | while | flops 1179655 | bytes 4721821 | solution.py:14
  604.1 2.9 select_add_fusion.4
  607.0 2.9 select_add_fusion.4
  615.7 2.9 select_add_fusion.4
  618.6 2.9 select_add_fusion.4
  649.8 2.9 select_add_fusion.4
  652.7 2.9 select_add_fusion.4
  661.4 2.9 select_add_fusion.4
  664.3 2.9 select_add_fusion.4
  695.5 2.9 select_add_fusion.4
  698.4 2.9 select_add_fusion.4
  707.1 2.9 select_add_fusion.4
  966.7 4.3 all-to-all-start.1
  971.0 287.3 %while.36 = (s32[]{:T(128)}, f32[128,256]{1,0:T(8,128)S(1)}, s32[128]{0:T(128)S(1)}, f32[1663,256]{1,0:T(8,128)S(1)}, f32[1536,256]{1,0:T(8,128)S(1)}, /*index=5*/s32[]{:T(128)}, s32[1]{0:T(128)}, s32[]{:T(128)}, s32[1]{0:T(128)}) while((s32[]{:T(128)}, f32[128,256]{1,0:T(8,128)S(1)}, s32[128]{0:T(128)S(1)}, f32[1663,256]{1,0:T(8,128)S(1)}, ...), condition=%wide.region_6.7_spmd, body=%wide.region_4.6_spmd.sunk | while | flops 786182 | bytes 3148967 | solution.py:44
  1259.5 126.4 %all-reduce.4.cloned.1.call-done = f32[512,128]{1,0:T(8,128)} async-done(((f32[512,128]{1,0:T(8,128)}), f32[512,128]{1,0:T(8,128)}) %all-reduce.4.cloned.1.call-update) | async-done | bytes 262160 | tf_op jit(solution)/shard_map/psum | solution.py:95
  (926 shorter events, 746.1 us)
Async XLA Ops:
  7.2 252.6 %copy-start = (f32[512,128]{1,0:T(8,128)S(1)}, f32[512,128]{1,0:T(8,128)}, u32[]{:S(2)}) copy-start(f32[512,128]{1,0:T(8,128)} %param.17) | copy-start | bytes 786436
  7.2 68.6 %all-gather.3.cloned.1.call-start = ((), (), s32[]{:S(2)}) async-start(), calls=%async_computation.4 | async-start | bytes 3932160 | tf_op jit(solution)/shard_map/all_gather | solution.py:65
  7.9 229.3 %copy-start.7 = (bf16[192,2048]{1,0:T(8,128)(2,1)S(1)}, bf16[192,2048]{1,0:T(8,128)(2,1)}, u32[]{:S(2)}) copy-start(bf16[192,2048]{1,0:T(8,128)(2,1)} %param.14) | copy-start | bytes 2359300
  7.9 229.3 %all-gather.5.cloned.1.call-start = ((), (), s32[]{:S(2)}) async-start(), calls=%async_computation.5 | async-start | bytes 37748736 | tf_op jit(solution)/shard_map/all_gather | solution.py:64
  256.1 16.1 %all-to-all-start.2 = ((bf16[192,8,256]{2,0,1:T(8,128)(2,1)}), bf16[192,8,256]{2,0,1:T(8,128)(2,1)S(1)}, u32[]{:S(2)}, u32[]{:S(2)}) async-start(bf16[192,8,256]{2,0,1:T(8,128)(2,1)} %bitcast.31), calls=%async_computation.2 | async-start | bytes 1572864 | tf_op jit(solution)/shard_map/all_to_all | solution.py:71
  272.4 2.0 copy-start.2
  580.4 1.1 copy-start.5
  580.4 1.4 copy-start.6
  584.3 16.1 %all-to-all-start = ((bf16[192,8,256]{2,0,1:T(8,128)(2,1)}), bf16[192,8,256]{2,0,1:T(8,128)(2,1)S(1)}, u32[]{:S(2)}, u32[]{:S(2)}) async-start(bf16[192,8,256]{2,0,1:T(8,128)(2,1)} %bitcast.32), calls=%async_computation | async-start | bytes 1572864 | tf_op jit(solution)/shard_map/all_to_all | solution.py:70
  600.4 0.9 copy-start.3
  966.7 420.9 %all-to-all-start.1 = ((f32[8,192,256]{2,1,0:T(8,128)}), f32[8,192,256]{2,1,0:T(8,128)}, u32[]{:S(2)}, u32[]{:S(2)}) async-start(f32[8,192,256]{2,1,0:T(8,128)} %bitcast.46), calls=%async_computation.1 | async-start | bytes 3145728 | tf_op jit(solution)/shard_map/all_to_all | solution.py:87
  970.9 414.9 %all-reduce.4.cloned.1.call-start = ((), (), s32[]{:S(2)}) async-start(), calls=%async_computation.6 | async-start | bytes 524288 | tf_op jit(solution)/shard_map/psum | solution.py:95
  1387.5 1.9 copy-start.4
  1389.2 1.3 copy-start.1
Sparse Core Ops, SparseCore 0:
  9.6 66.1 all-gather.2
  77.7 159.4 all-gather.4
  1259.6 126.2 all-reduce.3
where the time goes:
time: 1410 us; the launch traced here: 1400 us
  other arithmetic  685 us (49%)
  waiting for transfers between devices  381 us (27%)
  loops' own time  173 us (12%)
  local copies, waits for them, and re-layouts  89.3 us (6%)
  blocking collectives  23.4 us (2%)
  matrix products  19.7 us (1%)
    add x128, other arithmetic, causal_step(): return total + weight * window  363 us
    add x128, other arithmetic, anticausal_step(): return total + weight * window  278 us
    another operation x1, loops' own time, lagged(): return lax.map(one_lag, jnp.arange(prev + 1, dtype=jnp.int32))  169 us
    all_gather x1, waiting for transfers between devices, body(): panel = lax.all_gather(out_weight, 'ctx', axis=1, tiled=True)  161 us
    psum x1, waiting for transfers between devices, body(): grad_filters = lax.psum(partial_terms, ('ctx', 'mp')) * scale  126 us
    dynamic_slice x128, local copies, waits for them, and re-layouts, lagged(): return lax.map(one_lag, jnp.arange(prev + 1, dtype=jnp.int32))  75 us
    all_gather x1, waiting for transfers between devices, body(): lax.all_gather(cotangent, 'mp', axis=1, tiled=True)  67.1 us
    reduce_sum x128, other arithmetic, one_lag(): return jnp.sum(window * gradient, axis=0)  38.9 us
  transfers between devices with their start and end apart: 6, of which 5 were waited for; matrix products, arithmetic and copies ran while one was open for 9% of the time, Pallas kernels for 0%

commit v1 on v0

v1 whole, which is shorter than its diff:
```python
import jax
import jax.numpy as jnp
from jax import lax
from jax.sharding import PartitionSpec as P


def contract(left, right):
    return lax.dot_general(
        left, right, (((1,), (1,)), ((), ())), preferred_element_type=jnp.float32
    )


def toeplitz(seq, block, width):
    groups = seq.shape[0]
    flat = jnp.tile(seq, (1, block))[:, : block * width]
    return flat.reshape(groups, block, width)


def split_bf16(x):
    hi = x.astype(jnp.bfloat16)
    lo = (x - hi.astype(jnp.float32)).astype(jnp.bfloat16)
    return hi, lo


def windows(x, tiles, block, width):
    return jnp.stack([x[k * block : k * block + width] for k in range(tiles)])


def filter_apply(mats, wins, groups, per_group):
    tiles, width, chans = wins.shape
    w4 = wins.reshape(tiles, width, groups, per_group)
    total = None
    for m in mats:
        part = jnp.einsum("gij,kjgc->kigc", m, w4, preferred_element_type=jnp.float32)
        total = part if total is None else total + part
    block = mats[0].shape[1]
    return total.reshape(tiles * block, chans)


def body(cotangent, out_weight, query_act, key_act, value_act, filters):
    rows, chans = cotangent.shape
    groups, flen = filters.shape
    ctx_count = lax.axis_size("ctx")
    mp_count = lax.axis_size("mp")
    per_group = chans * mp_count // groups
    local_groups = chans // per_group
    halo = flen
    block = 64 if rows % 64 == 0 else rows
    tiles = rows // block
    width = block + halo

    panel = lax.all_gather(out_weight, "ctx", axis=1, tiled=True)
    grad_mixed = contract(lax.all_gather(cotangent, "mp", axis=1, tiled=True), panel)
    product = (key_act.astype(jnp.float32) * value_act.astype(jnp.float32)).astype(jnp.bfloat16)
    grad_conv = (grad_mixed * query_act.astype(jnp.float32)).astype(jnp.bfloat16)

    fwd = [(k, k + 1) for k in range(ctx_count - 1)]
    bwd = [(k + 1, k) for k in range(ctx_count - 1)]
    prev_tail = lax.ppermute(product[rows - halo :], "ctx", fwd)
    next_head = lax.ppermute(grad_conv[:halo], "ctx", bwd)

    taps = lax.dynamic_slice_in_dim(filters, lax.axis_index("mp") * local_groups, local_groups, 0)
    pad = jnp.zeros((local_groups, width + 1 - flen - 1), jnp.float32)
    one = jnp.zeros((local_groups, 1), jnp.float32)
    seq_causal = jnp.concatenate([one, taps[:, ::-1], pad], 1)
    seq_anti = jnp.concatenate([taps, pad, one], 1)
    mats_causal = split_bf16(toeplitz(seq_causal, block, width))
    mats_anti = split_bf16(toeplitz(seq_anti, block, width))

    widened = jnp.concatenate([prev_tail, product], 0)
    trailing = jnp.concatenate([grad_conv, next_head], 0)
    win_prod = windows(widened, tiles, block, width)
    win_grad = windows(trailing, tiles, block, width)

    mixed = filter_apply(mats_causal, win_prod, local_groups, per_group)
    grad_product = filter_apply(mats_anti, win_grad, local_groups, per_group)

    gc4 = grad_conv.reshape(tiles, block, local_groups, per_group)
    wp4 = win_prod.reshape(tiles, width, local_groups, per_group)
    cross = jnp.einsum("kigc,kjgc->gij", gc4, wp4, preferred_element_type=jnp.float32)
    cross = jnp.pad(cross.reshape(local_groups, block * width), ((0, 0), (0, block)))
    diag = cross.reshape(local_groups, block, width + 1)[:, :, 1 : halo + 1].sum(axis=1)
    scale = (rows * ctx_count * per_group) ** (-0.5)
    local_filters = lax.psum(diag[:, ::-1], "ctx") * scale
    grad_filters = lax.all_gather(local_filters, "mp", axis=0, tiled=True)

    grad_query = (grad_mixed * mixed).astype(jnp.bfloat16)
    grad_key = (grad_product * value_act.astype(jnp.float32)).astype(jnp.bfloat16)
    grad_value = (grad_product * key_act.astype(jnp.float32)).astype(jnp.bfloat16)
    return (grad_query, grad_key, grad_value, grad_filters)


def solution(mesh):
    in_specs = (P("ctx", "mp"), P("mp", "ctx"), P("ctx", "mp"), P("ctx", "mp"), P("ctx", "mp"), P())
    out_specs = (P("ctx", "mp"), P("ctx", "mp"), P("ctx", "mp"), P())
    return jax.shard_map(body, mesh=mesh, in_specs=in_specs, out_specs=out_specs, check_vma=False)
```

time: 1410 us -> 475 us (0.34)
  other arithmetic: 685 us -> 12.9 us
  loops' own time: 173 us -> 0 us
  waiting for transfers between devices: 381 us -> 283 us
  matrix products: 19.7 us -> 44.1 us
    add x256 -> x0, other arithmetic: 641 us -> none  [the longest x128 363 us: causal_step(): return total + weight * window]
    another operation x3 -> x0, loops' own time: 173 us -> none  [the longest x1 169 us: lagged(): return lax.map(one_lag, jnp.arange(prev + 1, dtype=jnp.int32))]
    dynamic_slice x384 -> x1, local copies, waits for them, and re-layouts: 77 us -> 0.01 us  [body(): lax.dynamic_slice_in_dim(filters, lax.axis_index('mp') * local_groups, lo...]
    psum x1, waiting for transfers between devices: 126 us -> 52.9 us  [body(): local_filters = lax.psum(diag[:, ::-1], 'ctx') * scale]
    reshape x0 -> x7, local copies, waits for them, and re-layouts: none -> 40.8 us  [the longest x2 18.1 us: toeplitz(): return flat.reshape(groups, block, width)]
    reduce_sum x128 -> x1, other arithmetic: 38.9 us -> 2.88 us  [body(): cross.reshape(local_groups, block, width + 1)[:, :, 1:halo + 1].sum(axis=1)]
    dot_general x2 -> x5, matrix products: 1.69 us -> 26 us  [the longest x4 19.9 us: filter_apply(): jnp.einsum('gij,kjgc->kigc', m, w4, preferred_element_type=jnp.float32)]
    all_to_all x3 -> x0, waiting for transfers between devices: 24.3 us -> none  [the longest x1 12.5 us: body(): lax.all_to_all(product, 'ctx', split_axis=1, concat_axis=0, tiled=True)]
  transfers between devices with their start and end apart: 6 -> 5, of which waited for: 5 -> 3; matrix products, arithmetic and copies ran while one was open for 9% -> 12% of each run, Pallas kernels for 0% -> 0%
where the time goes in v1:
time: 475 us; the launch traced here: 474 us
  waiting for transfers between devices  283 us (60%)
  local copies, waits for them, and re-layouts  101 us (21%)
  matrix products  44.1 us (9%)
  between operations  14 us (3%)
  blocking collectives  13.9 us (3%)
  other arithmetic  12.9 us (3%)
  starting transfers between devices  5.24 us (1%)
    all_gather x1, waiting for transfers between devices, body(): panel = lax.all_gather(out_weight, 'ctx', axis=1, tiled=True)  161 us
    all_gather x1, waiting for transfers between devices, body(): lax.all_gather(cotangent, 'mp', axis=1, tiled=True)  67.1 us
    psum x1, waiting for transfers between devices, body(): local_filters = lax.psum(diag[:, ::-1], 'ctx') * scale  52.9 us
    dot_general x4, matrix products, filter_apply(): jnp.einsum('gij,kjgc->kigc', m, w4, preferred_element_type=jnp.float32)  19.9 us
    another operation x4, local copies, waits for them, and re-layouts, toeplitz(): flat = jnp.tile(seq, (1, block))[:, :block * width]  18.3 us
    reshape x2, local copies, waits for them, and re-layouts, toeplitz(): return flat.reshape(groups, block, width)  18.1 us
    dot_general x1, matrix products, contract(): lax.dot_general(left, right, (((1,), (1,)), ((), ())), preferred_element_...  18 us
    reshape x3, local copies, waits for them, and re-layouts, filter_apply(): return total.reshape(tiles * block, chans)  14.5 us
  transfers between devices with their start and end apart: 5, of which 3 were waited for; matrix products, arithmetic and copies ran while one was open for 12% of the time, Pallas kernels for 0%

profile of v1, /device:TPU:0, one launch (start us, length us, event | category | flops | bytes accessed | tf_op | source)
XLA Modules:
  0.0 473.6 jit_solution(11213987400638723255)
XLA Ops:
  8.7 67.1 %all-gather.3.cloned.1.call-done = bf16[192,8192]{1,0:T(8,128)(2,1)} async-done(((bf16[192,2048]{1,0:T(8,128)(2,1)}), bf16[192,8192]{1,0:T(8,128)(2,1)}) %all-gather.3.cloned.1.call-update) | async-done | bytes 3145744 | tf_op jit(solution)/shard_map/all_gather | solution.py:53
  75.8 161.4 %all-gather.5.cloned.1.call-done = bf16[2048,8192]{1,0:T(8,128)(2,1)} async-done(((bf16[2048,1024]{1,0:T(8,128)(2,1)}), bf16[2048,8192]{1,0:T(8,128)(2,1)}) %all-gather.5.cloned.1.call-update) | async-done | bytes 33554448 | tf_op jit(solution)/shard_map/all_gather | solution.py:52
  237.2 18.0 %multiply_convert_fusion = (bf16[192,2048]{1,0:T(8,128)(2,1)S(1)}, f32[192,2048]{1,0:T(8,128)}) fusion(bf16[192,2048]{1,0:T(8,128)(2,1)S(1)} %copy-done.8, bf16[192,8192]{1,0:T(8,128)(2,1)} %all-gather.3.cloned.1.call-done, bf16[2048,8192]{1,0:T(8,128)(2,1)} %all-gather.5.cloned.1.call-done), kind=kOutput, calls=%fused_computation.29 | convolution fusion | flops 6443630592 | bytes 39845888 | tf_op jit(solution)/shard_map/dot_general | solution.py:8
  260.1 6.0 %tile.21 = f32[128,12352]{0,1:T(8,128)} reshape(f32[128,64,193]{0,2,1:T(8,128)} %tile.20) | data formatting | bytes 12648448 | tf_op jit(solution)/shard_map/tile | solution.py:15
  266.1 4.7 slice.43
  270.8 9.1 %copy.54 = f32[128,64,192]{2,1,0:T(8,128)} copy(f32[128,64,192]{0,2,1:T(8,128)} %bitcast.66) | data formatting | bytes 12582912 | tf_op jit(solution)/shard_map/reshape | solution.py:16
  287.3 7.1 %fusion.4 = f32[128,3,16,64]{3,2,1,0:T(8,128)S(1)} fusion(f32[128,64,192]{2,1,0:T(8,128)} %copy.54, bf16[1,192,128,16]{1,3,0,2:T(8,128)(2,1)S(1)} %bitcast.76, bf16[1,192,128,16]{1,3,0,2:T(8,128)(2,1)S(1)} %bitcast.78, bf16[1,192,128,16]{1,3,0,2:T(8,128)(2,1)S(1)} %bitcast.68), kind=kOutput, calls=%fused_computation.5 | convolution fusion | flops 159645696 | bytes 10223616 | tf_op jit(solution)/shard_map/gij,kjgc->kigc/dot_general | solution.py:34
  294.3 4.2 add_bitcast_fusion
  298.6 3.7 copy.56
  302.3 5.9 %reshape.55 = f32[192,2048]{0,1:T(8,128)} reshape(f32[3,64,128,16]{1,0,3,2:T(4,128)} %copy.56) | data formatting | bytes 3145728 | tf_op jit(solution)/shard_map/reshape | solution.py:37
  308.2 3.8 fusion.10
  313.0 3.8 collective-permute-start
  320.0 6.0 %tile.9 = f32[128,12352]{0,1:T(8,128)} reshape(f32[128,64,193]{0,2,1:T(8,128)} %tile.8) | data formatting | bytes 12648448 | tf_op jit(solution)/shard_map/tile | solution.py:15
  326.1 4.7 slice.39
  330.8 9.0 %copy.43 = f32[128,64,192]{2,1,0:T(8,128)} copy(f32[128,64,192]{0,2,1:T(8,128)} %bitcast.67) | data formatting | bytes 12582912 | tf_op jit(solution)/shard_map/reshape | solution.py:16
  347.4 7.1 %fusion.1 = f32[128,3,16,64]{3,2,1,0:T(8,128)S(1)} fusion(f32[128,64,192]{2,1,0:T(8,128)} %copy.43, bf16[1,192,128,16]{1,3,0,2:T(8,128)(2,1)S(1)} %bitcast.62, bf16[1,192,128,16]{1,3,0,2:T(8,128)(2,1)S(1)} %bitcast.73, bf16[1,192,128,16]{1,3,0,2:T(8,128)(2,1)S(1)} %bitcast.70), kind=kOutput, calls=%fused_computation.3 | convolution fusion | flops 159645696 | bytes 10223616 | tf_op jit(solution)/shard_map/gij,kjgc->kigc/dot_general | solution.py:34
  356.0 3.7 copy.45
  359.8 5.8 %reshape.53 = f32[192,2048]{0,1:T(8,128)} reshape(f32[3,64,128,16]{1,0,3,2:T(4,128)} %copy.45) | data formatting | bytes 3145728 | tf_op jit(solution)/shard_map/reshape | solution.py:37
  368.3 6.2 %convolution_bitcast_fusion = f32[128,64,192]{2,1,0:T(8,128)} fusion(bf16[3,64,128,16]{1,0,3,2:T(4,128)(2,1)} %reshape.56, bf16[1,192,128,16]{1,3,0,2:T(8,128)(2,1)S(1)} %bitcast.64, bf16[1,192,128,16]{1,3,0,2:T(8,128)(2,1)S(1)} %bitcast.75, bf16[1,192,128,16]{1,3,0,2:T(8,128)(2,1)S(1)} %bitcast.72), kind=kOutput, calls=%fused_computation.11 | convolution fusion | flops 153354240 | bytes 9437184 | tf_op jit(solution)/shard_map/kigc,kjgc->gij/dot_general | solution.py:80
  374.5 8.6 %copy.59 = f32[128,64,192]{0,2,1:T(8,128)} copy(f32[128,64,192]{2,1,0:T(8,128)} %convolution_bitcast_fusion) | data formatting | bytes 12582912 | tf_op jit(solution)/shard_map/kigc,kjgc->gij/dot_general | solution.py:80
  383.1 4.8 %pad.4 = f32[128,12352]{0,1:T(8,128)} pad(f32[128,12288]{0,1:T(8,128)} %bitcast.65, f32[]{:T(128)} %constant.6.clone.1), padding=0_0x0_64 | pad | bytes 12615684 | tf_op jit(solution)/shard_map/jit(_pad)/pad | solution.py:81
  387.8 6.0 %reshape.58 = f32[128,64,193]{0,2,1:T(8,128)} reshape(f32[128,12352]{0,1:T(8,128)} %pad.4) | data formatting | bytes 12648448 | tf_op jit(solution)/shard_map/reshape | solution.py:82
  398.5 52.9 %all-reduce.3.cloned.1.call-done = f32[128,128]{0,1:T(8,128)} async-done(((f32[128,128]{0,1:T(8,128)}), f32[128,128]{0,1:T(8,128)}) %all-reduce.3.cloned.1.call-update) | async-done | bytes 65552 | tf_op jit(solution)/shard_map/psum | solution.py:84
  452.3 13.9 %all_gather.11 = f32[512,128]{0,1:T(8,128)S(1)} all-gather(f32[128,128]{0,1:T(8,128)S(1)} %broadcast_multiply_fusion), channel_id=1, replica_groups=mesh['ctx'=8,'mp'=4] {'mp'}, dimensions={0}, use_global_device_ids=true | all-gather | bytes 327680 | tf_op jit(solution)/shard_map/all_gather | solution.py:85
  (60 shorter events, 36.1 us)
Async XLA Ops:
  7.2 249.4 %copy-start = (f32[512,128]{1,0:T(8,128)S(1)}, f32[512,128]{1,0:T(8,128)}, u32[]{:S(2)}) copy-start(f32[512,128]{1,0:T(8,128)} %param.11) | copy-start | bytes 786436
  7.2 230.0 %copy-start.8 = (bf16[192,2048]{1,0:T(8,128)(2,1)S(1)}, bf16[192,2048]{1,0:T(8,128)(2,1)}, u32[]{:S(2)}) copy-start(bf16[192,2048]{1,0:T(8,128)(2,1)} %param.8) | copy-start | bytes 2359300
  7.2 68.6 %all-gather.3.cloned.1.call-start = ((), (), s32[]{:S(2)}) async-start(), calls=%async_computation | async-start | bytes 3932160 | tf_op jit(solution)/shard_map/all_gather | solution.py:53
  7.9 229.3 %all-gather.5.cloned.1.call-start = ((), (), s32[]{:S(2)}) async-start(), calls=%async_computation.1 | async-start | bytes 37748736 | tf_op jit(solution)/shard_map/all_gather | solution.py:52
  8.7 442.8 %all-reduce.3.cloned.1.call-start = ((), (), s32[]{:S(2)}) async-start(), calls=%async_computation.2 | async-start | bytes 131072 | tf_op jit(solution)/shard_map/psum | solution.py:84
  255.3 27.8 %collective-permute-start.1 = (bf16[128,2048]{1,0:T(8,128)(2,1)S(1)}, bf16[128,2048]{1,0:T(8,128)(2,1)}, u32[]{:S(2)}, u32[]{:S(2)}) collective-permute-start(bf16[128,2048]{1,0:T(8,128)(2,1)S(1)} %slice.40), channel_id=1, source_target_pairs={{4,0},{8,4},{12,8},{16,12},{20,16},{24,20},{28,24},{5,1},{9,5},{13... | collective-permute-start | bytes 1572872 | tf_op jit(solution)/shard_map/ppermute | solution.py:60
  270.8 9.1 %copy-start.6 = (bf16[192,2048]{1,0:T(8,128)(2,1)S(1)}, bf16[192,2048]{1,0:T(8,128)(2,1)}, u32[]{:S(2)}) copy-start(bf16[192,2048]{1,0:T(8,128)(2,1)} %param.9) | copy-start | bytes 2359300
  270.8 10.5 %copy-start.7 = (bf16[192,2048]{1,0:T(8,128)(2,1)S(1)}, bf16[192,2048]{1,0:T(8,128)(2,1)}, u32[]{:S(2)}) copy-start(bf16[192,2048]{1,0:T(8,128)(2,1)} %param.10) | copy-start | bytes 2359300
  302.3 5.9 %copy-start.3 = (bf16[192,2048]{0,1:T(8,128)(2,1)S(1)}, bf16[192,2048]{0,1:T(8,128)(2,1)}, u32[]{:S(2)}) copy-start(bf16[192,2048]{0,1:T(8,128)(2,1)} %copy.40) | copy-start | bytes 2359300
  313.0 32.4 %collective-permute-start = (bf16[128,2048]{0,1:T(8,128)(2,1)}, bf16[128,2048]{0,1:T(8,128)(2,1)}, u32[]{:S(2)}, u32[]{:S(2)}) collective-permute-start(bf16[128,2048]{0,1:T(8,128)(2,1)} %slice.36), channel_id=1, source_target_pairs={{0,4},{4,8},{8,12},{12,16},{16,20},{20,24},{24,28},{1,5},{5,9},{9,... | collective-permute-start | bytes 1572872 | tf_op jit(solution)/shard_map/ppermute | solution.py:59
  339.8 4.4 copy-start.4
  345.4 9.1 %slice-start = ((s8[8388608]{0:T(1024)(128)(4,1)}), s8[4194304]{0:T(1024)(128)(4,1)S(1)}, s32[]{:S(2)}) async-start(s8[8388608]{0:T(1024)(128)(4,1)} %bitcast.60), calls=%async_computation.3 | async-start | bytes 8388608
  347.4 7.2 %slice-start.1 = ((s8[8388608]{0:T(1024)(128)(4,1)}), s8[4194304]{0:T(1024)(128)(4,1)S(1)}, s32[]{:S(2)}) async-start(s8[8388608]{0:T(1024)(128)(4,1)} %bitcast.60), calls=%async_computation.4 | async-start | bytes 8388608
  393.9 3.6 copy-start.2
  393.9 3.6 copy-start.5
  393.9 73.2 %copy-start.1 = (f32[512,128]{1,0:T(8,128)S(1)}, f32[512,128]{1,0:T(8,128)}, u32[]{:S(2)}) copy-start(f32[512,128]{1,0:T(8,128)} %param.11) | copy-start | bytes 786436
Sparse Core Ops, SparseCore 0:
  9.6 66.1 all-gather.2
  77.7 159.4 all-gather.4
  397.5 53.8 all-reduce.2

commit v2 on v1

--- a/solution.py
+++ b/solution.py
@@ -17,9 +17,9 @@
 
 
 def split_bf16(x):
-    hi = x.astype(jnp.bfloat16)
-    lo = (x - hi.astype(jnp.float32)).astype(jnp.bfloat16)
-    return hi, lo
+    hi = lax.reduce_precision(x, exponent_bits=8, mantissa_bits=7)
+    lo = x - hi
+    return hi.astype(jnp.bfloat16), lo.astype(jnp.bfloat16)
 
 
 def windows(x, tiles, block, width):
@@ -49,8 +49,10 @@
     tiles = rows // block
     width = block + halo
 
-    panel = lax.all_gather(out_weight, "ctx", axis=1, tiled=True)
-    grad_mixed = contract(lax.all_gather(cotangent, "mp", axis=1, tiled=True), panel)
+    cot_rows = lax.all_gather(cotangent, "mp", axis=1, tiled=True)
+    cot_cols = lax.all_to_all(cot_rows, "ctx", split_axis=1, concat_axis=0, tiled=True)
+    partial = contract(cot_cols, out_weight)
+    grad_mixed = lax.psum_scatter(partial, "ctx", scatter_dimension=0, tiled=True)
     product = (key_act.astype(jnp.float32) * value_act.astype(jnp.float32)).astype(jnp.bfloat16)
     grad_conv = (grad_mixed * query_act.astype(jnp.float32)).astype(jnp.bfloat16)
 

time: 475 us -> 415 us (0.87)
  waiting for transfers between devices: 283 us -> 190 us
  blocking collectives: 13.9 us -> 55.5 us
  matrix products: 44.1 us -> 32.4 us
    all_gather x2 -> x1, waiting for transfers between devices: 228 us -> 67.8 us  [body(): cot_rows = lax.all_gather(cotangent, 'mp', axis=1, tiled=True)]
    reduce_scatter x0 -> x1, waiting for transfers between devices: none -> 89.4 us  [body(): lax.psum_scatter(partial, 'ctx', scatter_dimension=0, tiled=True)]
    all_to_all x0 -> x1, blocking collectives: none -> 41.6 us  [body(): lax.all_to_all(cot_rows, 'ctx', split_axis=1, concat_axis=0, tiled=True)]
    psum x1, waiting for transfers between devices: 52.9 us -> 31.7 us  [body(): local_filters = lax.psum(diag[:, ::-1], 'ctx') * scale]
    dot_general x1, matrix products: 18 us -> 9.09 us  [contract(): lax.dot_general(left, right, (((1,), (1,)), ((), ())), preferred_element_...]
  transfers between devices with their start and end apart: 5 -> 5, of which waited for: 3 -> 3; matrix products, arithmetic and copies ran while one was open for 12% -> 19% of each run, Pallas kernels for 0% -> 0%
where the time goes in v2:
time: 415 us; the launch traced here: 414 us
  waiting for transfers between devices  190 us (46%)
  local copies, waits for them, and re-layouts  101 us (24%)
  blocking collectives  55.5 us (13%)
  matrix products  32.4 us (8%)
  other arithmetic  16.1 us (4%)
  between operations  14 us (3%)
  starting transfers between devices  5.25 us (1%)
    reduce_scatter x1, waiting for transfers between devices, body(): lax.psum_scatter(partial, 'ctx', scatter_dimension=0, tiled=True)  89.4 us
    all_gather x1, waiting for transfers between devices, body(): cot_rows = lax.all_gather(cotangent, 'mp', axis=1, tiled=True)  67.8 us
    all_to_all x1, blocking collectives, body(): lax.all_to_all(cot_rows, 'ctx', split_axis=1, concat_axis=0, tiled=True)  41.6 us
    psum x1, waiting for transfers between devices, body(): local_filters = lax.psum(diag[:, ::-1], 'ctx') * scale  31.7 us
    another operation x4, local copies, waits for them, and re-layouts, toeplitz(): flat = jnp.tile(seq, (1, block))[:, :block * width]  18.3 us
    reshape x2, local copies, waits for them, and re-layouts, toeplitz(): return flat.reshape(groups, block, width)  18.1 us
    dot_general x4, matrix products, filter_apply(): jnp.einsum('gij,kjgc->kigc', m, w4, preferred_element_type=jnp.float32)  17.2 us
    all_gather x1, blocking collectives, body(): grad_filters = lax.all_gather(local_filters, 'mp', axis=0, tiled=True)  13.9 us
  transfers between devices with their start and end apart: 5, of which 3 were waited for; matrix products, arithmetic and copies ran while one was open for 19% of the time, Pallas kernels for 0%

profile of v2, /device:TPU:0, one launch (start us, length us, event | category | flops | bytes accessed | tf_op | source)
XLA Modules:
  0.0 413.5 jit_solution(9489356137955590670)
XLA Ops:
  8.0 67.8 %all-gather.2.cloned.1.call-done = bf16[192,8192]{1,0:T(8,128)(2,1)} async-done(((bf16[192,2048]{1,0:T(8,128)(2,1)}), bf16[192,8192]{1,0:T(8,128)(2,1)}) %all-gather.2.cloned.1.call-update) | async-done | bytes 3145744 | tf_op jit(solution)/shard_map/all_gather | solution.py:52
  78.1 41.6 %all_to_all.19 = bf16[192,8,1024]{2,0,1:T(8,128)(2,1)S(1)} all-to-all(bf16[192,8,1024]{2,0,1:T(8,128)(2,1)S(1)} %bitcast.81), channel_id=1, replica_groups=mesh['ctx'=8,'mp'=4] {'ctx'}, dimensions={1} | all-to-all | bytes 6291456 | tf_op jit(solution)/shard_map/all_to_all | solution.py:53
  119.7 9.1 %fusion.26 = f32[1536,2048]{1,0:T(8,128)} fusion(bf16[1536,1024]{1,0:T(8,128)(2,1)S(1)} %bitcast.87, bf16[2048,1024]{1,0:T(8,128)(2,1)S(1)} %copy-done.7), kind=kOutput, calls=%fused_computation.44 | convolution fusion | flops 6442450944 | bytes 19922944 | tf_op jit(solution)/shard_map/dot_general | solution.py:8
  128.8 89.4 %reduce-scatter.2.cloned.1.call-done = f32[192,2048]{1,0:T(8,128)} async-done(((f32[1536,2048]{1,0:T(8,128)}), f32[192,2048]{1,0:T(8,128)}) %reduce-scatter.2.cloned.1.call-update) | async-done | bytes 1572880 | tf_op jit(solution)/shard_map/reduce_scatter | solution.py:55
  224.7 6.0 %tile.21 = f32[128,12352]{0,1:T(8,128)} reshape(f32[128,64,193]{0,2,1:T(8,128)} %tile.20) | data formatting | bytes 12648448 | tf_op jit(solution)/shard_map/tile | solution.py:15
  230.7 4.7 %slice.43 = f32[128,12288]{0,1:T(8,128)} slice(f32[128,12352]{0,1:T(8,128)} %tile.21), slice={[0:128], [0:12288]} | slice | bytes 12582912 | tf_op jit(solution)/shard_map/slice | solution.py:15
  235.4 9.1 %copy.78 = f32[128,64,192]{2,1,0:T(8,128)} copy(f32[128,64,192]{0,2,1:T(8,128)} %bitcast.71) | data formatting | bytes 12582912 | tf_op jit(solution)/shard_map/reshape | solution.py:16
  251.9 4.4 %fusion.3 = f32[128,3,16,64]{3,2,1,0:T(8,128)S(1)} fusion(f32[128,64,192]{2,1,0:T(8,128)} %copy.78, bf16[1,192,128,16]{1,3,0,2:T(8,128)(2,1)S(1)} %bitcast.84, bf16[1,192,128,16]{1,3,0,2:T(8,128)(2,1)S(1)} %bitcast.82, bf16[1,192,128,16]{1,3,0,2:T(8,128)(2,1)S(1)} %bitcast.73), kind=kOutput, calls=%fused_computation.7 | convolution fusion | flops 158072832 | bytes 10223616 | tf_op jit(solution)/shard_map/gij,kjgc->kigc/dot_general | solution.py:34
  256.2 4.2 %add_bitcast_fusion = f32[3,64,128,16]{1,3,0,2:T(8,128)S(1)} fusion(f32[128,3,16,64]{3,2,1,0:T(8,128)S(1)} %fusion.3, f32[128,64,192]{2,1,0:T(8,128)} %copy.78, bf16[1,192,128,16]{1,3,0,2:T(8,128)(2,1)S(1)} %bitcast.85, bf16[1,192,128,16]{1,3,0,2:T(8,128)(2,1)S(1)} %bitcast.83, bf16[1,192,128,16]{1,3,0,2:T(8,128)(2,1)S(1)} %bitcast.74), kind=kOutput, calls=%fused_computation.19 | convolution fusion | flops 156893184 | bytes 11796480 | tf_op jit(solution)/shard_map/gij,kjgc->kigc/dot_general | solution.py:34
  264.2 5.9 %reshape.58 = f32[192,2048]{0,1:T(8,128)} reshape(f32[3,64,128,16]{1,0,3,2:T(4,128)} %copy.80) | data formatting | bytes 3145728 | tf_op jit(solution)/shard_map/reshape | solution.py:37
  270.1 3.8 fusion.14
  274.9 3.8 collective-permute-start
  281.9 6.0 %tile.9 = f32[128,12352]{0,1:T(8,128)} reshape(f32[128,64,193]{0,2,1:T(8,128)} %tile.8) | data formatting | bytes 12648448 | tf_op jit(solution)/shard_map/tile | solution.py:15
  287.9 4.7 %slice.39 = f32[128,12288]{0,1:T(8,128)} slice(f32[128,12352]{0,1:T(8,128)} %tile.9), slice={[0:128], [0:12288]} | slice | bytes 12582912 | tf_op jit(solution)/shard_map/slice | solution.py:15
  292.7 9.0 %copy.67 = f32[128,64,192]{2,1,0:T(8,128)} copy(f32[128,64,192]{0,2,1:T(8,128)} %bitcast.72) | data formatting | bytes 12582912 | tf_op jit(solution)/shard_map/reshape | solution.py:16
  309.1 6.1 %convolution_bitcast_fusion = f32[128,64,192]{2,1,0:T(8,128)} fusion(bf16[3,64,128,16]{1,0,3,2:T(4,128)(2,1)} %reshape.59, bf16[1,192,128,16]{1,3,0,2:T(8,128)(2,1)S(1)} %bitcast.67, bf16[1,192,128,16]{1,3,0,2:T(8,128)(2,1)S(1)} %bitcast.78, bf16[1,192,128,16]{1,3,0,2:T(8,128)(2,1)S(1)} %bitcast.75), kind=kOutput, calls=%fused_computation.15 | convolution fusion | flops 153354240 | bytes 9437184 | tf_op jit(solution)/shard_map/kigc,kjgc->gij/dot_general | solution.py:82
  315.2 8.6 %copy.83 = f32[128,64,192]{0,2,1:T(8,128)} copy(f32[128,64,192]{2,1,0:T(8,128)} %convolution_bitcast_fusion) | data formatting | bytes 12582912 | tf_op jit(solution)/shard_map/kigc,kjgc->gij/dot_general | solution.py:82
  323.8 4.7 %pad.4 = f32[128,12352]{0,1:T(8,128)} pad(f32[128,12288]{0,1:T(8,128)} %bitcast.70, f32[]{:T(128)} %constant.6.clone.1), padding=0_0x0_64 | pad | bytes 12615684 | tf_op jit(solution)/shard_map/jit(_pad)/pad | solution.py:83
  328.5 6.1 %reshape.61 = f32[128,64,193]{0,2,1:T(8,128)} reshape(f32[128,12352]{0,1:T(8,128)} %pad.4) | data formatting | bytes 12648448 | tf_op jit(solution)/shard_map/reshape | solution.py:84
  338.0 4.4 %fusion.6 = f32[128,3,16,64]{3,2,1,0:T(8,128)S(1)} fusion(f32[128,64,192]{2,1,0:T(8,128)} %copy.67, bf16[1,192,128,16]{1,3,0,2:T(8,128)(2,1)S(1)} %bitcast.68, bf16[1,192,128,16]{1,3,0,2:T(8,128)(2,1)S(1)} %bitcast.79, bf16[1,192,128,16]{1,3,0,2:T(8,128)(2,1)S(1)} %bitcast.76), kind=kOutput, calls=%fused_computation.9 | convolution fusion | flops 158072832 | bytes 10223616 | tf_op jit(solution)/shard_map/gij,kjgc->kigc/dot_general | solution.py:34
  342.3 4.3 %add_bitcast_fusion.1 = f32[3,64,128,16]{1,3,0,2:T(8,128)S(1)} fusion(f32[128,3,16,64]{3,2,1,0:T(8,128)S(1)} %fusion.6, f32[128,64,192]{2,1,0:T(8,128)} %copy.67, bf16[1,192,128,16]{1,3,0,2:T(8,128)(2,1)S(1)} %bitcast.69, bf16[1,192,128,16]{1,3,0,2:T(8,128)(2,1)S(1)} %bitcast.80, bf16[1,192,128,16]{1,3,0,2:T(8,128)(2,1)S(1)} %bitcast.77), kind=kOutput, calls=%fused_computation.20 | convolution fusion | flops 156893184 | bytes 11796480 | tf_op jit(solution)/shard_map/gij,kjgc->kigc/dot_general | solution.py:34
  350.3 4.7 %reshape.56 = f32[192,2048]{0,1:T(8,128)S(1)} reshape(f32[3,64,128,16]{1,0,3,2:T(4,128)} %copy.69) | data formatting | bytes 3145728 | tf_op jit(solution)/shard_map/reshape | solution.py:37
  359.7 31.7 %all-reduce.3.cloned.1.call-done = f32[128,128]{0,1:T(8,128)} async-done(((f32[128,128]{0,1:T(8,128)}), f32[128,128]{0,1:T(8,128)}) %all-reduce.3.cloned.1.call-update) | async-done | bytes 65552 | tf_op jit(solution)/shard_map/psum | solution.py:86
  392.2 13.9 %all_gather.7 = f32[512,128]{0,1:T(8,128)S(1)} all-gather(f32[128,128]{0,1:T(8,128)S(1)} %broadcast_multiply_fusion), channel_id=1, replica_groups=mesh['ctx'=8,'mp'=4] {'mp'}, dimensions={0}, use_global_device_ids=true | all-gather | bytes 327680 | tf_op jit(solution)/shard_map/all_gather | solution.py:87
  (56 shorter events, 45.7 us)
Async XLA Ops:
  7.2 214.0 %copy-start = (f32[512,128]{1,0:T(8,128)S(1)}, f32[512,128]{1,0:T(8,128)}, u32[]{:S(2)}) copy-start(f32[512,128]{1,0:T(8,128)} %param.11) | copy-start | bytes 786436
  7.2 68.6 %all-gather.2.cloned.1.call-start = ((), (), s32[]{:S(2)}) async-start(), calls=%async_computation.2 | async-start | bytes 3932160 | tf_op jit(solution)/shard_map/all_gather | solution.py:52
  7.9 210.3 %reduce-scatter.2.cloned.1.call-start = ((), (), s32[]{:S(2)}) async-start(), calls=%async_computation.3 | async-start | bytes 14155776 | tf_op jit(solution)/shard_map/reduce_scatter | solution.py:55
  78.1 41.6 %copy-start.7 = (bf16[2048,1024]{1,0:T(8,128)(2,1)S(1)}, bf16[2048,1024]{1,0:T(8,128)(2,1)}, u32[]{:S(2)}) copy-start(bf16[2048,1024]{1,0:T(8,128)(2,1)} %param.7) | copy-start | bytes 12582916
  128.8 89.4 %copy-start.6 = (bf16[192,2048]{1,0:T(8,128)(2,1)S(1)}, bf16[192,2048]{1,0:T(8,128)(2,1)}, u32[]{:S(2)}) copy-start(bf16[192,2048]{1,0:T(8,128)(2,1)} %param.8) | copy-start | bytes 2359300
  128.8 262.6 %all-reduce.3.cloned.1.call-start = ((), (), s32[]{:S(2)}) async-start(), calls=%async_computation.4 | async-start | bytes 131072 | tf_op jit(solution)/shard_map/psum | solution.py:86
  219.8 27.8 %collective-permute-start.1 = (bf16[128,2048]{1,0:T(8,128)(2,1)S(1)}, bf16[128,2048]{1,0:T(8,128)(2,1)}, u32[]{:S(2)}, u32[]{:S(2)}) collective-permute-start(bf16[128,2048]{1,0:T(8,128)(2,1)S(1)} %slice.40), channel_id=1, source_target_pairs={{4,0},{8,4},{12,8},{16,12},{20,16},{24,20},{28,24},{5,1},{9,5},{13... | collective-permute-start | bytes 1572872 | tf_op jit(solution)/shard_map/ppermute | solution.py:62
  235.4 9.1 %copy-start.4 = (bf16[192,2048]{1,0:T(8,128)(2,1)S(1)}, bf16[192,2048]{1,0:T(8,128)(2,1)}, u32[]{:S(2)}) copy-start(bf16[192,2048]{1,0:T(8,128)(2,1)} %param.9) | copy-start | bytes 2359300
  235.4 10.5 %copy-start.5 = (bf16[192,2048]{1,0:T(8,128)(2,1)S(1)}, bf16[192,2048]{1,0:T(8,128)(2,1)}, u32[]{:S(2)}) copy-start(bf16[192,2048]{1,0:T(8,128)(2,1)} %param.10) | copy-start | bytes 2359300
  264.2 5.9 %copy-start.2 = (bf16[192,2048]{0,1:T(8,128)(2,1)S(1)}, bf16[192,2048]{0,1:T(8,128)(2,1)}, u32[]{:S(2)}) copy-start(bf16[192,2048]{0,1:T(8,128)(2,1)} %copy.64) | copy-start | bytes 2359300
  274.9 32.3 %collective-permute-start = (bf16[128,2048]{0,1:T(8,128)(2,1)}, bf16[128,2048]{0,1:T(8,128)(2,1)}, u32[]{:S(2)}, u32[]{:S(2)}) collective-permute-start(bf16[128,2048]{0,1:T(8,128)(2,1)} %slice.36), channel_id=1, source_target_pairs={{0,4},{4,8},{8,12},{12,16},{16,20},{20,24},{24,28},{1,5},{5,9},{9,... | collective-permute-start | bytes 1572872 | tf_op jit(solution)/shard_map/ppermute | solution.py:61
  301.7 4.3 %copy-start.3 = (bf16[192,2048]{0,1:T(8,128)(2,1)S(1)}, bf16[192,2048]{0,1:T(8,128)(2,1)}, u32[]{:S(2)}) copy-start(bf16[192,2048]{0,1:T(8,128)(2,1)} %get-tuple-element.16) | copy-start | bytes 2359300
  355.0 52.0 %copy-start.1 = (f32[512,128]{1,0:T(8,128)S(1)}, f32[512,128]{1,0:T(8,128)}, u32[]{:S(2)}) copy-start(f32[512,128]{1,0:T(8,128)} %param.11) | copy-start | bytes 786436
Sparse Core Ops, SparseCore 0:
  9.6 66.1 all-gather.1
  128.9 89.2 reduce-scatter.1
  338.1 53.2 all-reduce.2

commit v3 on v2

--- a/solution.py
+++ b/solution.py
@@ -49,18 +49,6 @@
     tiles = rows // block
     width = block + halo
 
-    cot_rows = lax.all_gather(cotangent, "mp", axis=1, tiled=True)
-    cot_cols = lax.all_to_all(cot_rows, "ctx", split_axis=1, concat_axis=0, tiled=True)
-    partial = contract(cot_cols, out_weight)
-    grad_mixed = lax.psum_scatter(partial, "ctx", scatter_dimension=0, tiled=True)
-    product = (key_act.astype(jnp.float32) * value_act.astype(jnp.float32)).astype(jnp.bfloat16)
-    grad_conv = (grad_mixed * query_act.astype(jnp.float32)).astype(jnp.bfloat16)
-
-    fwd = [(k, k + 1) for k in range(ctx_count - 1)]
-    bwd = [(k + 1, k) for k in range(ctx_count - 1)]
-    prev_tail = lax.ppermute(product[rows - halo :], "ctx", fwd)
-    next_head = lax.ppermute(grad_conv[:halo], "ctx", bwd)
-
     taps = lax.dynamic_slice_in_dim(filters, lax.axis_index("mp") * local_groups, local_groups, 0)
     pad = jnp.zeros((local_groups, width + 1 - flen - 1), jnp.float32)
     one = jnp.zeros((local_groups, 1), jnp.float32)
@@ -69,12 +57,25 @@
     mats_causal = split_bf16(toeplitz(seq_causal, block, width))
     mats_anti = split_bf16(toeplitz(seq_anti, block, width))
 
+    cot_rows = lax.all_gather(cotangent, "mp", axis=1, tiled=True)
+    cot_rows, mats_causal, mats_anti = lax.optimization_barrier((cot_rows, mats_causal, mats_anti))
+    cot_cols = lax.all_to_all(cot_rows, "ctx", split_axis=1, concat_axis=0, tiled=True)
+    partial = contract(cot_cols, out_weight)
+    grad_mixed = lax.psum_scatter(partial, "ctx", scatter_dimension=0, tiled=True)
+
+    fwd = [(k, k + 1) for k in range(ctx_count - 1)]
+    bwd = [(k + 1, k) for k in range(ctx_count - 1)]
+    product = (key_act.astype(jnp.float32) * value_act.astype(jnp.float32)).astype(jnp.bfloat16)
+    prev_tail = lax.ppermute(product[rows - halo :], "ctx", fwd)
     widened = jnp.concatenate([prev_tail, product], 0)
+    win_prod = windows(widened, tiles, block, width)
+    mixed = filter_apply(mats_causal, win_prod, local_groups, per_group)
+    grad_mixed, mixed = lax.optimization_barrier((grad_mixed, mixed))
+
+    grad_conv = (grad_mixed * query_act.astype(jnp.float32)).astype(jnp.bfloat16)
+    next_head = lax.ppermute(grad_conv[:halo], "ctx", bwd)
     trailing = jnp.concatenate([grad_conv, next_head], 0)
-    win_prod = windows(widened, tiles, block, width)
     win_grad = windows(trailing, tiles, block, width)
-
-    mixed = filter_apply(mats_causal, win_prod, local_groups, per_group)
     grad_product = filter_apply(mats_anti, win_grad, local_groups, per_group)
 
     gc4 = grad_conv.reshape(tiles, block, local_groups, per_group)

time: 415 us -> 361 us (0.87)
  waiting for transfers between devices: 190 us -> 132 us
  local copies, waits for them, and re-layouts: 101 us -> 109 us
  matrix products: 32.4 us -> 25.8 us
  other arithmetic: 16.1 us -> 20.9 us
    reduce_scatter x1, waiting for transfers between devices: 89.4 us -> 52.6 us  [body(): lax.psum_scatter(partial, 'ctx', scatter_dimension=0, tiled=True)]
    optimization_barrier x0 -> x5, local copies, waits for them, and re-layouts: none -> 30.5 us  [the longest x4 28.8 us: body(): lax.optimization_barrier((cot_rows, mats_causal, mats_anti))]
    all_gather x1, waiting for transfers between devices: 67.8 us -> 38 us  [body(): cot_rows = lax.all_gather(cotangent, 'mp', axis=1, tiled=True)]
    reshape x2 -> x0, local copies, waits for them, and re-layouts: 18.1 us -> none  [toeplitz(): return flat.reshape(groups, block, width)]
    psum x1, waiting for transfers between devices: 31.7 us -> 39.6 us  [body(): local_filters = lax.psum(diag[:, ::-1], 'ctx') * scale]
    dot_general x4, matrix products: 17.2 us -> 9.91 us  [filter_apply(): jnp.einsum('gij,kjgc->kigc', m, w4, preferred_element_type=jnp.float32)]
    slice x2 -> x4, local copies, waits for them, and re-layouts: 9.44 us -> 4.65 us  [toeplitz(): flat = jnp.tile(seq, (1, block))[:, :block * width]]
    reshape x3 -> x2, local copies, waits for them, and re-layouts: 12.4 us -> 10.8 us  [filter_apply(): return total.reshape(tiles * block, chans)]
  transfers between devices with their start and end apart: 5 -> 5, of which waited for: 3 -> 4; matrix products, arithmetic and copies ran while one was open for 19% -> 29% of each run, Pallas kernels for 0% -> 0%
where the time goes in v3:
time: 361 us; the launch traced here: 360 us
  waiting for transfers between devices  132 us (37%)
  local copies, waits for them, and re-layouts  109 us (30%)
  blocking collectives  55.7 us (15%)
  matrix products  25.8 us (7%)
  other arithmetic  20.9 us (6%)
  between operations  14 us (4%)
    reduce_scatter x1, waiting for transfers between devices, body(): lax.psum_scatter(partial, 'ctx', scatter_dimension=0, tiled=True)  52.6 us
    all_to_all x1, blocking collectives, body(): lax.all_to_all(cot_rows, 'ctx', split_axis=1, concat_axis=0, tiled=True)  41.5 us
    psum x1, waiting for transfers between devices, body(): local_filters = lax.psum(diag[:, ::-1], 'ctx') * scale  39.6 us
    all_gather x1, waiting for transfers between devices, body(): cot_rows = lax.all_gather(cotangent, 'mp', axis=1, tiled=True)  38 us
    optimization_barrier x4, local copies, waits for them, and re-layouts, body(): lax.optimization_barrier((cot_rows, mats_causal, mats_anti))  28.8 us
    another operation x4, local copies, waits for them, and re-layouts, toeplitz(): flat = jnp.tile(seq, (1, block))[:, :block * width]  18.5 us
    all_gather x1, blocking collectives, body(): grad_filters = lax.all_gather(local_filters, 'mp', axis=0, tiled=True)  14.1 us
    reshape x2, local copies, waits for them, and re-layouts, filter_apply(): return total.reshape(tiles * block, chans)  10.8 us
  transfers between devices with their start and end apart: 5, of which 4 were waited for; matrix products, arithmetic and copies ran while one was open for 29% of the time, Pallas kernels for 0%

profile of v3, /device:TPU:0, one launch (start us, length us, event | category | flops | bytes accessed | tf_op | source)
XLA Modules:
  0.0 360.1 jit_solution(11277831453095542222)
XLA Ops:
  11.7 6.0 %tile.9 = f32[128,12352]{0,1:T(8,128)} reshape(f32[128,64,193]{0,2,1:T(8,128)} %tile.8) | data formatting | bytes 12648448 | tf_op jit(solution)/shard_map/tile | solution.py:15
  21.0 6.1 %tile.21 = f32[128,12352]{0,1:T(8,128)} reshape(f32[128,64,193]{0,2,1:T(8,128)} %tile.20) | data formatting | bytes 12648448 | tf_op jit(solution)/shard_map/tile | solution.py:15
  31.8 6.0 %fusion = (bf16[128,64,192]{0,2,1:T(8,128)(2,1)}, bf16[128,64,192]{0,2,1:T(8,128)(2,1)}, bf16[128,64,192]{0,2,1:T(8,128)(2,1)}, bf16[128,64,192]{0,2,1:T(8,128)(2,1)}) fusion(f32[128,64,192]{0,2,1:T(8,128)S(1)} %bitcast.51, f32[128,64,192]{0,2,1:T(8,128)S(1)} %bitcast.52), kind=kLoop, calls=%fused_computation.4 | loop fusion | flops 12582912 | bytes 25165824 | tf_op jit(solution)/shard_map/convert_element_type | solution.py:22
  37.7 38.0 %all-gather.2.cloned.1.call-done = bf16[192,8192]{1,0:T(8,128)(2,1)} async-done(((bf16[192,2048]{1,0:T(8,128)(2,1)}), bf16[192,8192]{1,0:T(8,128)(2,1)}) %all-gather.2.cloned.1.call-update) | async-done | bytes 3145744 | tf_op jit(solution)/shard_map/all_gather | solution.py:60
  78.1 41.5 %all_to_all.19 = bf16[192,8,1024]{2,0,1:T(8,128)(2,1)S(1)} all-to-all(bf16[192,8,1024]{2,0,1:T(8,128)(2,1)S(1)} %bitcast.61), channel_id=1, replica_groups=mesh['ctx'=8,'mp'=4] {'ctx'}, dimensions={1} | all-to-all | bytes 6291456 | tf_op jit(solution)/shard_map/all_to_all | solution.py:62
  119.7 9.1 %fusion.12 = f32[1536,2048]{1,0:T(8,128)} fusion(bf16[1536,1024]{1,0:T(8,128)(2,1)S(1)} %bitcast.75, bf16[2048,1024]{1,0:T(8,128)(2,1)S(1)} %copy-done.15), kind=kOutput, calls=%fused_computation.38 | convolution fusion | flops 6442450944 | bytes 19922944 | tf_op jit(solution)/shard_map/dot_general | solution.py:8
  137.6 7.2 %copy.88 = bf16[128,64,192,1]{2,1,3,0:T(8,128)(2,1)} copy(bf16[128,64,192,1]{0,2,1,3:T(8,128)(2,1)} %bitcast.60) | data formatting | bytes 6291456 | tf_op jit(solution)/shard_map/optimization_barrier | solution.py:61
  144.8 7.0 %copy.87 = bf16[128,64,192,1]{2,1,3,0:T(8,128)(2,1)} copy(bf16[128,64,192,1]{0,2,1,3:T(8,128)(2,1)} %bitcast.59) | data formatting | bytes 6291456 | tf_op jit(solution)/shard_map/optimization_barrier | solution.py:61
  151.8 3.5 fusion.11
  157.2 3.7 %copy.70 = f32[3,64,128,16]{1,0,3,2:T(4,128)} copy(f32[3,64,128,16]{1,3,0,2:T(8,128)S(1)} %add_bitcast_fusion.1) | data formatting | bytes 3145728 | tf_op jit(solution)/shard_map/add | solution.py:35
  161.0 4.8 %reshape.57 = f32[192,2048]{0,1:T(8,128)S(1)} reshape(f32[3,64,128,16]{1,0,3,2:T(4,128)} %copy.70) | data formatting | bytes 3145728 | tf_op jit(solution)/shard_map/reshape | solution.py:37
  165.8 52.6 %reduce-scatter.2.cloned.1.call-done = f32[192,2048]{1,0:T(8,128)} async-done(((f32[1536,2048]{1,0:T(8,128)}), f32[192,2048]{1,0:T(8,128)}) %reduce-scatter.2.cloned.1.call-update) | async-done | bytes 1572880 | tf_op jit(solution)/shard_map/reduce_scatter | solution.py:64
  220.1 3.4 multiply_convert_fusion
  228.4 6.8 %convolution_bitcast_fusion = f32[128,64,192]{2,1,0:T(8,128)} fusion(bf16[3,64,128,16]{1,0,3,2:T(4,128)(2,1)} %reshape.59, bf16[1,192,128,16]{1,3,0,2:T(8,128)(2,1)S(1)} %bitcast.56, bf16[1,192,128,16]{1,3,0,2:T(8,128)(2,1)} %bitcast.67, bf16[1,192,128,16]{1,3,0,2:T(8,128)(2,1)} %bitcast.64), kind=kOutput, calls=%fused_computation.7 | convolution fusion | flops 153354240 | bytes 9437184 | tf_op jit(solution)/shard_map/kigc,kjgc->gij/dot_general | solution.py:83
  235.2 8.6 %copy.83 = f32[128,64,192]{0,2,1:T(8,128)} copy(f32[128,64,192]{2,1,0:T(8,128)} %convolution_bitcast_fusion) | data formatting | bytes 12582912 | tf_op jit(solution)/shard_map/kigc,kjgc->gij/dot_general | solution.py:83
  243.8 4.8 %pad.4 = f32[128,12352]{0,1:T(8,128)} pad(f32[128,12288]{0,1:T(8,128)} %bitcast.53, f32[]{:T(128)} %constant.6.clone.1), padding=0_0x0_64 | pad | bytes 12615684 | tf_op jit(solution)/shard_map/jit(_pad)/pad | solution.py:84
  248.6 6.0 %reshape.61 = f32[128,64,193]{0,2,1:T(8,128)} reshape(f32[128,12352]{0,1:T(8,128)} %pad.4) | data formatting | bytes 12648448 | tf_op jit(solution)/shard_map/reshape | solution.py:85
  258.0 6.9 %copy.89 = bf16[128,64,192,1]{2,1,3,0:T(8,128)(2,1)} copy(bf16[128,64,192,1]{0,2,1,3:T(8,128)(2,1)} %bitcast.58) | data formatting | bytes 6291456 | tf_op jit(solution)/shard_map/optimization_barrier | solution.py:61
  265.0 7.6 %copy.90 = bf16[128,64,192,1]{2,1,3,0:T(8,128)(2,1)} copy(bf16[128,64,192,1]{0,2,1,3:T(8,128)(2,1)S(1)} %bitcast.57) | data formatting | bytes 6291456 | tf_op jit(solution)/shard_map/optimization_barrier | solution.py:61
  272.6 39.6 %all-reduce.3.cloned.1.call-done = f32[128,128]{0,1:T(8,128)} async-done(((f32[128,128]{0,1:T(8,128)}), f32[128,128]{0,1:T(8,128)}) %all-reduce.3.cloned.1.call-update) | async-done | bytes 65552 | tf_op jit(solution)/shard_map/psum | solution.py:87
  313.1 14.1 %all_gather.7 = f32[512,128]{0,1:T(8,128)S(1)} all-gather(f32[128,128]{0,1:T(8,128)S(1)} %broadcast_multiply_fusion), channel_id=1, replica_groups=mesh['ctx'=8,'mp'=4] {'mp'}, dimensions={0}, use_global_device_ids=true | all-gather | bytes 327680 | tf_op jit(solution)/shard_map/all_gather | solution.py:88
  332.5 3.5 fusion.6
  337.5 3.7 %copy.80 = f32[3,64,128,16]{1,0,3,2:T(4,128)} copy(f32[3,64,128,16]{1,3,0,2:T(8,128)S(1)} %add_bitcast_fusion) | data formatting | bytes 3145728 | tf_op jit(solution)/shard_map/add | solution.py:35
  341.2 6.0 %reshape.58 = f32[192,2048]{0,1:T(8,128)} reshape(f32[3,64,128,16]{1,0,3,2:T(4,128)} %copy.80) | data formatting | bytes 3145728 | tf_op jit(solution)/shard_map/reshape | solution.py:37
  (77 shorter events, 49.2 us)
Async XLA Ops:
  7.2 1.0 copy-start
  7.2 68.6 %all-gather.2.cloned.1.call-start = ((), (), s32[]{:S(2)}) async-start(), calls=%async_computation.2 | async-start | bytes 3932160 | tf_op jit(solution)/shard_map/all_gather | solution.py:60
  7.9 210.5 %reduce-scatter.2.cloned.1.call-start = ((), (), s32[]{:S(2)}) async-start(), calls=%async_computation.3 | async-start | bytes 14155776 | tf_op jit(solution)/shard_map/reduce_scatter | solution.py:64
  27.1 2.8 slice-start
  27.1 4.6 %slice-start.1 = ((f32[128,12352]{0,1:T(8,128)}), f32[128,12288]{0,1:T(8,128)S(1)}, s32[]{:S(2)}) async-start(f32[128,12352]{0,1:T(8,128)} %tile.21), calls=%async_computation.6 | async-start | bytes 12582912 | tf_op jit(solution)/shard_map/slice | solution.py:15
  78.1 41.6 %copy-start.15 = (bf16[2048,1024]{1,0:T(8,128)(2,1)S(1)}, bf16[2048,1024]{1,0:T(8,128)(2,1)}, u32[]{:S(2)}) copy-start(bf16[2048,1024]{1,0:T(8,128)(2,1)} %param.7) | copy-start | bytes 12582916
  128.8 1.1 copy-start.14
  128.8 183.4 %all-reduce.3.cloned.1.call-start = ((), (), s32[]{:S(2)}) async-start(), calls=%async_computation.4 | async-start | bytes 131072 | tf_op jit(solution)/shard_map/psum | solution.py:87
  130.4 7.2 %copy-start.6 = (bf16[192,2048]{0,1:T(8,128)(2,1)}, bf16[192,2048]{0,1:T(8,128)(2,1)S(1)}, u32[]{:S(2)}) copy-start(bf16[192,2048]{0,1:T(8,128)(2,1)S(1)} %copy.67) | copy-start | bytes 2359300
  132.3 5.3 %copy-start.8 = (bf16[192,2048]{0,1:T(8,128)(2,1)}, bf16[192,2048]{0,1:T(8,128)(2,1)S(1)}, u32[]{:S(2)}) copy-start(bf16[192,2048]{0,1:T(8,128)(2,1)S(1)} %copy.66) | copy-start | bytes 2359300
  132.8 2.8 collective-permute-start
  144.8 7.0 %copy-start.12 = (bf16[192,2048]{0,1:T(8,128)(2,1)S(1)}, bf16[192,2048]{0,1:T(8,128)(2,1)}, u32[]{:S(2)}) copy-start(bf16[192,2048]{0,1:T(8,128)(2,1)} %get-tuple-element.38) | copy-start | bytes 2359300
  144.8 7.0 %copy-start.13 = (bf16[192,2048]{0,1:T(8,128)(2,1)S(1)}, bf16[192,2048]{0,1:T(8,128)(2,1)}, u32[]{:S(2)}) copy-start(bf16[192,2048]{0,1:T(8,128)(2,1)} %get-tuple-element.39) | copy-start | bytes 2359300
  151.8 4.0 %copy-start.3 = (bf16[128,64,192,1]{2,1,3,0:T(8,128)(2,1)S(1)}, bf16[128,64,192,1]{2,1,3,0:T(8,128)(2,1)}, u32[]{:S(2)}) copy-start(bf16[128,64,192,1]{2,1,3,0:T(8,128)(2,1)} %copy.87) | copy-start | bytes 9437188
  223.5 11.7 %copy-start.5 = (bf16[192,2048]{1,0:T(8,128)(2,1)}, bf16[192,2048]{1,0:T(8,128)(2,1)S(1)}, u32[]{:S(2)}) copy-start(bf16[192,2048]{1,0:T(8,128)(2,1)S(1)} %get-tuple-element.36) | copy-start | bytes 2359300
  224.9 10.3 %copy-start.10 = (bf16[192,2048]{0,1:T(8,128)(2,1)}, bf16[192,2048]{0,1:T(8,128)(2,1)S(1)}, u32[]{:S(2)}) copy-start(bf16[192,2048]{0,1:T(8,128)(2,1)S(1)} %copy.72) | copy-start | bytes 2359300
  224.9 103.1 %collective-permute-start.1 = (bf16[128,2048]{1,0:T(8,128)(2,1)}, bf16[128,2048]{1,0:T(8,128)(2,1)}, u32[]{:S(2)}, u32[]{:S(2)}) collective-permute-start(bf16[128,2048]{1,0:T(8,128)(2,1)} %slice.41), channel_id=1, source_target_pairs={{4,0},{8,4},{12,8},{16,12},{20,16},{24,20},{28,24},{5,1},{9,5},{13... | collective-permute-start | bytes 1572872 | tf_op jit(solution)/shard_map/ppermute | solution.py:76
  258.0 7.0 %copy-start.4 = (bf16[128,64,192]{0,2,1:T(8,128)(2,1)S(1)}, bf16[128,64,192]{0,2,1:T(8,128)(2,1)}, u32[]{:S(2)}) copy-start(bf16[128,64,192]{0,2,1:T(8,128)(2,1)} %get-tuple-element.17) | copy-start | bytes 9437188
  328.0 4.4 %copy-start.11 = (bf16[192,2048]{0,1:T(8,128)(2,1)S(1)}, bf16[192,2048]{0,1:T(8,128)(2,1)}, u32[]{:S(2)}) copy-start(bf16[192,2048]{0,1:T(8,128)(2,1)} %copy-done.10) | copy-start | bytes 2359300
  332.5 3.6 copy-start.2
  341.2 6.0 %copy-start.7 = (bf16[192,2048]{0,1:T(8,128)(2,1)S(1)}, bf16[192,2048]{0,1:T(8,128)(2,1)}, u32[]{:S(2)}) copy-start(bf16[192,2048]{0,1:T(8,128)(2,1)} %copy-done.6) | copy-start | bytes 2359300
  341.2 6.0 %copy-start.9 = (bf16[192,2048]{0,1:T(8,128)(2,1)S(1)}, bf16[192,2048]{0,1:T(8,128)(2,1)}, u32[]{:S(2)}) copy-start(bf16[192,2048]{0,1:T(8,128)(2,1)} %copy-done.8) | copy-start | bytes 2359300
  347.1 6.4 %copy-start.1 = (f32[512,128]{1,0:T(8,128)S(1)}, f32[512,128]{1,0:T(8,128)}, u32[]{:S(2)}) copy-start(f32[512,128]{1,0:T(8,128)} %param.11) | copy-start | bytes 786436
Sparse Core Ops, SparseCore 0:
  9.6 66.1 all-gather.1
  128.9 89.4 reduce-scatter.1
  258.2 54.0 all-reduce.2

commit v4 on v3

--- a/solution.py
+++ b/solution.py
@@ -37,6 +37,22 @@
     return total.reshape(tiles * block, chans)
 
 
+def exchange_columns(x, count):
+    rows, cols = x.shape
+    width = cols // count
+    me = lax.axis_index("ctx")
+    out = jnp.zeros((count * rows, width), x.dtype)
+    own = lax.dynamic_slice_in_dim(x, me * width, width, 1)
+    out = lax.dynamic_update_slice_in_dim(out, own, me * rows, 0)
+    for shift in range(1, count):
+        dest = (me + shift) % count
+        chunk = lax.dynamic_slice_in_dim(x, dest * width, width, 1)
+        got = lax.ppermute(chunk, "ctx", [(k, (k + shift) % count) for k in range(count)])
+        src = (me + count - shift) % count
+        out = lax.dynamic_update_slice_in_dim(out, got, src * rows, 0)
+    return out
+
+
 def body(cotangent, out_weight, query_act, key_act, value_act, filters):
     rows, chans = cotangent.shape
     groups, flen = filters.shape
@@ -59,7 +75,7 @@
 
     cot_rows = lax.all_gather(cotangent, "mp", axis=1, tiled=True)
     cot_rows, mats_causal, mats_anti = lax.optimization_barrier((cot_rows, mats_causal, mats_anti))
-    cot_cols = lax.all_to_all(cot_rows, "ctx", split_axis=1, concat_axis=0, tiled=True)
+    cot_cols = exchange_columns(cot_rows, ctx_count)
     partial = contract(cot_cols, out_weight)
     grad_mixed = lax.psum_scatter(partial, "ctx", scatter_dimension=0, tiled=True)
 
@@ -74,17 +90,19 @@
 
     grad_conv = (grad_mixed * query_act.astype(jnp.float32)).astype(jnp.bfloat16)
     next_head = lax.ppermute(grad_conv[:halo], "ctx", bwd)
-    trailing = jnp.concatenate([grad_conv, next_head], 0)
-    win_grad = windows(trailing, tiles, block, width)
-    grad_product = filter_apply(mats_anti, win_grad, local_groups, per_group)
-
     gc4 = grad_conv.reshape(tiles, block, local_groups, per_group)
     wp4 = win_prod.reshape(tiles, width, local_groups, per_group)
     cross = jnp.einsum("kigc,kjgc->gij", gc4, wp4, preferred_element_type=jnp.float32)
     cross = jnp.pad(cross.reshape(local_groups, block * width), ((0, 0), (0, block)))
     diag = cross.reshape(local_groups, block, width + 1)[:, :, 1 : halo + 1].sum(axis=1)
     scale = (rows * ctx_count * per_group) ** (-0.5)
+    diag, next_head = lax.optimization_barrier((diag, next_head))
     local_filters = lax.psum(diag[:, ::-1], "ctx") * scale
+    trailing = jnp.concatenate([grad_conv, next_head], 0)
+    win_grad = windows(trailing, tiles, block, width)
+    grad_product = filter_apply(mats_anti, win_grad, local_groups, per_group)
+    local_filters, grad_product = lax.optimization_barrier((local_filters, grad_product))
+
     grad_filters = lax.all_gather(local_filters, "mp", axis=0, tiled=True)
 
     grad_query = (grad_mixed * mixed).astype(jnp.bfloat16)

time: 361 us -> 347 us (0.961)
  blocking collectives: 55.7 us -> 13.9 us
  local copies, waits for them, and re-layouts: 109 us -> 127 us
  starting transfers between devices: 2.91 us -> 18.7 us
  waiting for transfers between devices: 132 us -> 118 us
  other arithmetic: 20.9 us -> 25.9 us
    all_to_all x1 -> x0, blocking collectives: 41.5 us -> none  [body(): lax.all_to_all(cot_rows, 'ctx', split_axis=1, concat_axis=0, tiled=True)]
    ppermute x0 -> x7, waiting for transfers between devices: none -> 19.9 us  [exchange_columns(): lax.ppermute(chunk, 'ctx', [(k, (k + shift) % count) for k in range(count)])]
    reduce_scatter x1, waiting for transfers between devices: 52.6 us -> 35.5 us  [body(): lax.psum_scatter(partial, 'ctx', scatter_dimension=0, tiled=True)]
    ppermute x0 -> x7, starting transfers between devices: none -> 12.8 us  [exchange_columns(): lax.ppermute(chunk, 'ctx', [(k, (k + shift) % count) for k in range(count)])]
    all_gather x1, waiting for transfers between devices: 38 us -> 29.4 us  [body(): cot_rows = lax.all_gather(cotangent, 'mp', axis=1, tiled=True)]
    psum x1, waiting for transfers between devices: 39.6 us -> 31.2 us  [body(): local_filters = lax.psum(diag[:, ::-1], 'ctx') * scale]
    slice x4 -> x2, local copies, waits for them, and re-layouts: 4.65 us -> 10 us  [toeplitz(): flat = jnp.tile(seq, (1, block))[:, :block * width]]
    dynamic_update_slice x0 -> x7, local copies, waits for them, and re-layouts: none -> 4.2 us  [exchange_columns(): out = lax.dynamic_update_slice_in_dim(out, got, src * rows, 0)]
  transfers between devices with their start and end apart: 5 -> 12, of which waited for: 4 -> 7; matrix products, arithmetic and copies ran while one was open for 29% -> 41% of each run, Pallas kernels for 0% -> 0%
where the time goes in v4:
time: 347 us; the launch traced here: 346 us
  local copies, waits for them, and re-layouts  127 us (37%)
  waiting for transfers between devices  118 us (34%)
  matrix products  28.1 us (8%)
  other arithmetic  25.9 us (7%)
  starting transfers between devices  18.7 us (5%)
  between operations  14.1 us (4%)
  blocking collectives  13.9 us (4%)
    reduce_scatter x1, waiting for transfers between devices, body(): lax.psum_scatter(partial, 'ctx', scatter_dimension=0, tiled=True)  35.5 us
    psum x1, waiting for transfers between devices, body(): local_filters = lax.psum(diag[:, ::-1], 'ctx') * scale  31.2 us
    all_gather x1, waiting for transfers between devices, body(): cot_rows = lax.all_gather(cotangent, 'mp', axis=1, tiled=True)  29.4 us
    optimization_barrier x4, local copies, waits for them, and re-layouts, body(): lax.optimization_barrier((cot_rows, mats_causal, mats_anti))  27.4 us
    ppermute x7, waiting for transfers between devices, exchange_columns(): lax.ppermute(chunk, 'ctx', [(k, (k + shift) % count) for k in range(count)])  19.9 us
    another operation x4, local copies, waits for them, and re-layouts, toeplitz(): flat = jnp.tile(seq, (1, block))[:, :block * width]  18.4 us
    all_gather x1, blocking collectives, body(): grad_filters = lax.all_gather(local_filters, 'mp', axis=0, tiled=True)  13.9 us
    ppermute x7, starting transfers between devices, exchange_columns(): lax.ppermute(chunk, 'ctx', [(k, (k + shift) % count) for k in range(count)])  12.8 us
  transfers between devices with their start and end apart: 12, of which 7 were waited for; matrix products, arithmetic and copies ran while one was open for 41% of the time, Pallas kernels for 0%

profile of v4, /device:TPU:0, one launch (start us, length us, event | category | flops | bytes accessed | tf_op | source)
XLA Modules:
  0.0 345.7 jit_solution(17376737709715469070)
XLA Ops:
  11.7 6.0 %tile.9 = f32[128,12352]{0,1:T(8,128)} reshape(f32[128,64,193]{0,2,1:T(8,128)} %tile.8) | data formatting | bytes 12648448 | tf_op jit(solution)/shard_map/tile | solution.py:15
  17.7 5.3 %slice.36 = f32[128,12288]{0,1:T(8,128)} slice(f32[128,12352]{0,1:T(8,128)} %tile.9), slice={[0:128], [0:12288]} | slice | bytes 12582912 | tf_op jit(solution)/shard_map/slice | solution.py:15
  26.2 6.0 %tile.21 = f32[128,12352]{0,1:T(8,128)} reshape(f32[128,64,193]{0,2,1:T(8,128)} %tile.20) | data formatting | bytes 12648448 | tf_op jit(solution)/shard_map/tile | solution.py:15
  37.0 9.3 %fusion = (bf16[128,64,192]{0,2,1:T(8,128)(2,1)}, bf16[128,64,192]{0,2,1:T(8,128)(2,1)}, bf16[128,64,192]{0,2,1:T(8,128)(2,1)}, bf16[128,64,192]{0,2,1:T(8,128)(2,1)}) fusion(f32[128,64,192]{0,2,1:T(8,128)} %bitcast.45, f32[128,64,192]{0,2,1:T(8,128)} %bitcast.46), kind=kLoop, calls=%fused_computation.4 | loop fusion | flops 12582912 | bytes 25165824 | tf_op jit(solution)/shard_map/convert_element_type | solution.py:22
  46.4 29.4 %all-gather.2.cloned.1.call-done = bf16[192,8192]{1,0:T(8,128)(2,1)} async-done(((bf16[192,2048]{1,0:T(8,128)(2,1)}), bf16[192,8192]{1,0:T(8,128)(2,1)}) %all-gather.2.cloned.1.call-update) | async-done | bytes 3145744 | tf_op jit(solution)/shard_map/all_gather | solution.py:76
  83.7 7.7 %collective-permute-done = bf16[192,1024]{1,0:T(8,128)(2,1)} collective-permute-done((bf16[192,1024]{1,0:T(8,128)(2,1)}, bf16[192,1024]{1,0:T(8,128)(2,1)}, u32[]{:S(2)}, u32[]{:S(2)}) %collective-permute-start) | collective-permute-done | bytes 393248 | tf_op jit(solution)/shard_map/ppermute | solution.py:50
  93.8 7.0 %collective-permute-start.6 = (bf16[192,1024]{1,0:T(8,128)(2,1)}, bf16[192,1024]{1,0:T(8,128)(2,1)S(1)}, u32[]{:S(2)}, u32[]{:S(2)}) collective-permute-start(bf16[192,1024]{1,0:T(8,128)(2,1)} %get-tuple-element.38), channel_id=1, source_target_pairs={{0,28},{4,0},{8,4},{12,8},{16,12},{20,16},{24,20},{28,24},{1,29},{... | collective-permute-start | bytes 1179656 | tf_op jit(solution)/shard_map/ppermute | solution.py:50
  101.9 6.8 %collective-permute-done.2 = bf16[192,1024]{1,0:T(8,128)(2,1)} collective-permute-done((bf16[192,1024]{1,0:T(8,128)(2,1)}, bf16[192,1024]{1,0:T(8,128)(2,1)}, u32[]{:S(2)}, u32[]{:S(2)}) %collective-permute-start.2) | collective-permute-done | bytes 393248 | tf_op jit(solution)/shard_map/ppermute | solution.py:50
  110.7 5.4 %collective-permute-done.4 = bf16[192,1024]{1,0:T(8,128)(2,1)S(1)} collective-permute-done((bf16[192,1024]{1,0:T(8,128)(2,1)}, bf16[192,1024]{1,0:T(8,128)(2,1)S(1)}, u32[]{:S(2)}, u32[]{:S(2)}) %collective-permute-start.4) | collective-permute-done | bytes 393248 | tf_op jit(solution)/shard_map/ppermute | solution.py:50
  116.3 9.2 %fusion.12 = f32[1536,2048]{1,0:T(8,128)} fusion(bf16[1536,1024]{1,0:T(8,128)(2,1)S(1)} %constant_dynamic-update-slice_fusion.6, bf16[2048,1024]{1,0:T(8,128)(2,1)S(1)} %copy-done.13), kind=kOutput, calls=%fused_computation.52 | convolution fusion | flops 6442450944 | bytes 19922944 | tf_op jit(solution)/shard_map/dot_general | solution.py:8
  137.7 7.2 %copy.64 = bf16[128,64,192,1]{2,1,3,0:T(8,128)(2,1)} copy(bf16[128,64,192,1]{0,2,1,3:T(8,128)(2,1)} %bitcast.53) | data formatting | bytes 6291456 | tf_op jit(solution)/shard_map/optimization_barrier | solution.py:77
  144.9 6.8 %copy.63 = bf16[128,64,192,1]{2,1,3,0:T(8,128)(2,1)} copy(bf16[128,64,192,1]{0,2,1,3:T(8,128)(2,1)} %bitcast.52) | data formatting | bytes 6291456 | tf_op jit(solution)/shard_map/optimization_barrier | solution.py:77
  151.7 5.1 %fusion.11 = f32[128,3,16,64]{3,2,1,0:T(8,128)S(1)} fusion(bf16[128,64,192,1]{2,1,3,0:T(8,128)(2,1)} %copy.64, bf16[1,192,128,16]{1,3,0,2:T(8,128)(2,1)S(1)} %bitcast.47, bf16[1,192,128,16]{1,3,0,2:T(8,128)(2,1)} %bitcast.59, bf16[1,192,128,16]{1,3,0,2:T(8,128)(2,1)} %bitcast.56), kind=kOutput, calls=%fused_computation.51 | convolution fusion | flops 153354240 | bytes 7077888 | tf_op jit(solution)/shard_map/gij,kjgc->kigc/dot_general | solution.py:34
  162.5 5.9 %reshape.54 = f32[192,2048]{0,1:T(8,128)} reshape(f32[3,64,128,16]{1,0,3,2:T(4,128)} %copy.46) | data formatting | bytes 3145728 | tf_op jit(solution)/shard_map/reshape | solution.py:37
  168.4 6.8 %copy.66 = bf16[128,64,192,1]{2,1,3,0:T(8,128)(2,1)} copy(bf16[128,64,192,1]{0,2,1,3:T(8,128)(2,1)} %bitcast.51) | data formatting | bytes 6291456 | tf_op jit(solution)/shard_map/optimization_barrier | solution.py:77
  175.2 6.7 %copy.67 = bf16[128,64,192,1]{2,1,3,0:T(8,128)(2,1)} copy(bf16[128,64,192,1]{0,2,1,3:T(8,128)(2,1)} %bitcast.50) | data formatting | bytes 6291456 | tf_op jit(solution)/shard_map/optimization_barrier | solution.py:77
  181.9 35.5 %reduce-scatter.2.cloned.1.call-done = f32[192,2048]{1,0:T(8,128)} async-done(((f32[1536,2048]{1,0:T(8,128)}), f32[192,2048]{1,0:T(8,128)}) %reduce-scatter.2.cloned.1.call-update) | async-done | bytes 1572880 | tf_op jit(solution)/shard_map/reduce_scatter | solution.py:80
  225.7 5.0 %reshape.55 = bf16[3,64,128,16]{1,0,3,2:T(4,128)(2,1)} reshape(bf16[192,2048]{0,1:T(8,128)(2,1)} %copy.48) | data formatting | bytes 1572864 | tf_op jit(solution)/shard_map/reshape | solution.py:93
  232.2 6.8 %convolution_bitcast_fusion = f32[128,64,192]{2,1,0:T(8,128)} fusion(bf16[3,64,128,16]{1,0,3,2:T(4,128)(2,1)} %reshape.55, bf16[1,192,128,16]{1,3,0,2:T(8,128)(2,1)S(1)} %bitcast.49, bf16[1,192,128,16]{1,3,0,2:T(8,128)(2,1)} %bitcast.60, bf16[1,192,128,16]{1,3,0,2:T(8,128)(2,1)} %bitcast.57), kind=kOutput, calls=%fused_computation.7 | convolution fusion | flops 153354240 | bytes 9437184 | tf_op jit(solution)/shard_map/kigc,kjgc->gij/dot_general | solution.py:95
  239.0 8.6 %copy.50 = f32[128,64,192]{0,2,1:T(8,128)} copy(f32[128,64,192]{2,1,0:T(8,128)} %convolution_bitcast_fusion) | data formatting | bytes 12582912 | tf_op jit(solution)/shard_map/kigc,kjgc->gij/dot_general | solution.py:95
  252.4 5.9 %reshape.57 = f32[128,64,193]{0,2,1:T(8,128)} reshape(f32[128,12352]{0,1:T(8,128)} %pad.4) | data formatting | bytes 12648448 | tf_op jit(solution)/shard_map/reshape | solution.py:97
  278.7 5.9 %reshape.58 = f32[192,2048]{0,1:T(8,128)} reshape(f32[3,64,128,16]{1,0,3,2:T(4,128)} %copy.59) | data formatting | bytes 3145728 | tf_op jit(solution)/shard_map/reshape | solution.py:37
  284.6 31.2 %all-reduce.3.cloned.1.call-done = f32[128,128]{0,1:T(8,128)} async-done(((f32[128,128]{0,1:T(8,128)}), f32[128,128]{0,1:T(8,128)}) %all-reduce.3.cloned.1.call-update) | async-done | bytes 65552 | tf_op jit(solution)/shard_map/psum | solution.py:100
  324.4 13.9 %all_gather.7 = f32[512,128]{0,1:T(8,128)S(1)} all-gather(f32[128,128]{0,1:T(8,128)S(1)} %broadcast_multiply_fusion), channel_id=1, replica_groups=mesh['ctx'=8,'mp'=4] {'mp'}, dimensions={0}, use_global_device_ids=true | all-gather | bytes 327680 | tf_op jit(solution)/shard_map/all_gather | solution.py:106
  (92 shorter events, 88.0 us)
Async XLA Ops:
  7.2 68.6 %all-gather.2.cloned.1.call-start = ((), (), s32[]{:S(2)}) async-start(), calls=%async_computation.1 | async-start | bytes 3932160 | tf_op jit(solution)/shard_map/all_gather | solution.py:76
  7.9 209.5 %reduce-scatter.2.cloned.1.call-start = ((), (), s32[]{:S(2)}) async-start(), calls=%async_computation.2 | async-start | bytes 14155776 | tf_op jit(solution)/shard_map/reduce_scatter | solution.py:80
  75.8 1.9 copy-start.10
  79.2 12.2 %collective-permute-start = (bf16[192,1024]{1,0:T(8,128)(2,1)}, bf16[192,1024]{1,0:T(8,128)(2,1)}, u32[]{:S(2)}, u32[]{:S(2)}) collective-permute-start(bf16[192,1024]{1,0:T(8,128)(2,1)} %get-tuple-element.44), channel_id=1, source_target_pairs={{0,4},{4,8},{8,12},{12,16},{16,20},{20,24},{24,28},{28,0},{1,5},{5... | collective-permute-start | bytes 1179656 | tf_op jit(solution)/shard_map/ppermute | solution.py:50
  79.2 14.6 %collective-permute-start.1 = (bf16[192,1024]{1,0:T(8,128)(2,1)}, bf16[192,1024]{1,0:T(8,128)(2,1)}, u32[]{:S(2)}, u32[]{:S(2)}) collective-permute-start(bf16[192,1024]{1,0:T(8,128)(2,1)} %get-tuple-element.43), channel_id=1, source_target_pairs={{0,8},{4,12},{8,16},{12,20},{16,24},{20,28},{24,0},{28,4},{1,9},{5... | collective-permute-start | bytes 1179656 | tf_op jit(solution)/shard_map/ppermute | solution.py:50
  80.7 27.9 %collective-permute-start.2 = (bf16[192,1024]{1,0:T(8,128)(2,1)}, bf16[192,1024]{1,0:T(8,128)(2,1)}, u32[]{:S(2)}, u32[]{:S(2)}) collective-permute-start(bf16[192,1024]{1,0:T(8,128)(2,1)} %get-tuple-element.42), channel_id=1, source_target_pairs={{0,12},{4,16},{8,20},{12,24},{16,28},{20,0},{24,4},{28,8},{1,13},{... | collective-permute-start | bytes 1179656 | tf_op jit(solution)/shard_map/ppermute | solution.py:50
  83.1 26.6 %collective-permute-start.3 = (bf16[192,1024]{1,0:T(8,128)(2,1)}, bf16[192,1024]{1,0:T(8,128)(2,1)}, u32[]{:S(2)}, u32[]{:S(2)}) collective-permute-start(bf16[192,1024]{1,0:T(8,128)(2,1)} %get-tuple-element.41), channel_id=1, source_target_pairs={{0,16},{4,20},{8,24},{12,28},{16,0},{20,4},{24,8},{28,12},{1,17},{... | collective-permute-start | bytes 1179656 | tf_op jit(solution)/shard_map/ppermute | solution.py:50
  83.6 32.7 %copy-start.13 = (bf16[2048,1024]{1,0:T(8,128)(2,1)S(1)}, bf16[2048,1024]{1,0:T(8,128)(2,1)}, u32[]{:S(2)}) copy-start(bf16[2048,1024]{1,0:T(8,128)(2,1)} %param.7) | copy-start | bytes 12582916
  83.6 32.5 %collective-permute-start.4 = (bf16[192,1024]{1,0:T(8,128)(2,1)}, bf16[192,1024]{1,0:T(8,128)(2,1)S(1)}, u32[]{:S(2)}, u32[]{:S(2)}) collective-permute-start(bf16[192,1024]{1,0:T(8,128)(2,1)} %get-tuple-element.40), channel_id=1, source_target_pairs={{0,20},{4,24},{8,28},{12,0},{16,4},{20,8},{24,12},{28,16},{1,21},{... | collective-permute-start | bytes 1179656 | tf_op jit(solution)/shard_map/ppermute | solution.py:50
  91.4 24.8 %collective-permute-start.5 = (bf16[192,1024]{1,0:T(8,128)(2,1)}, bf16[192,1024]{1,0:T(8,128)(2,1)S(1)}, u32[]{:S(2)}, u32[]{:S(2)}) collective-permute-start(bf16[192,1024]{1,0:T(8,128)(2,1)} %get-tuple-element.39), channel_id=1, source_target_pairs={{0,24},{4,28},{8,0},{12,4},{16,8},{20,12},{24,16},{28,20},{1,25},{... | collective-permute-start | bytes 1179656 | tf_op jit(solution)/shard_map/ppermute | solution.py:50
  93.8 22.4 %collective-permute-start.6 = (bf16[192,1024]{1,0:T(8,128)(2,1)}, bf16[192,1024]{1,0:T(8,128)(2,1)S(1)}, u32[]{:S(2)}, u32[]{:S(2)}) collective-permute-start(bf16[192,1024]{1,0:T(8,128)(2,1)} %get-tuple-element.38), channel_id=1, source_target_pairs={{0,28},{4,0},{8,4},{12,8},{16,12},{20,16},{24,20},{28,24},{1,29},{... | collective-permute-start | bytes 1179656 | tf_op jit(solution)/shard_map/ppermute | solution.py:50
  125.5 1.6 copy-start.12
  125.5 190.3 %all-reduce.3.cloned.1.call-start = ((), (), s32[]{:S(2)}) async-start(), calls=%async_computation.3 | async-start | bytes 131072 | tf_op jit(solution)/shard_map/psum | solution.py:100
  130.2 5.5 %collective-permute-start.7 = (bf16[128,2048]{0,1:T(8,128)(2,1)S(1)}, bf16[128,2048]{0,1:T(8,128)(2,1)S(1)}, u32[]{:S(2)}, u32[]{:S(2)}) collective-permute-start(bf16[128,2048]{0,1:T(8,128)(2,1)S(1)} %slice.38), channel_id=1, source_target_pairs={{0,4},{4,8},{8,12},{12,16},{16,20},{20,24},{24,28},{1,5},{5,9},{9,... | collective-permute-start | bytes 1572872 | tf_op jit(solution)/shard_map/ppermute | solution.py:85
  151.7 5.1 %copy-start.3 = (bf16[128,64,192,1]{2,1,3,0:T(8,128)(2,1)S(1)}, bf16[128,64,192,1]{2,1,3,0:T(8,128)(2,1)}, u32[]{:S(2)}) copy-start(bf16[128,64,192,1]{2,1,3,0:T(8,128)(2,1)} %copy.63) | copy-start | bytes 9437188
  151.7 5.4 %copy-start.6 = (bf16[192,2048]{0,1:T(8,128)(2,1)S(1)}, bf16[192,2048]{0,1:T(8,128)(2,1)}, u32[]{:S(2)}) copy-start(bf16[192,2048]{0,1:T(8,128)(2,1)} %get-tuple-element.50) | copy-start | bytes 2359300
  151.7 5.7 %copy-start.7 = (bf16[192,2048]{0,1:T(8,128)(2,1)S(1)}, bf16[192,2048]{0,1:T(8,128)(2,1)}, u32[]{:S(2)}) copy-start(bf16[192,2048]{0,1:T(8,128)(2,1)} %get-tuple-element.51) | copy-start | bytes 2359300
  230.7 30.4 %collective-permute-start.8 = (bf16[128,2048]{1,0:T(8,128)(2,1)}, bf16[128,2048]{1,0:T(8,128)(2,1)}, u32[]{:S(2)}, u32[]{:S(2)}) collective-permute-start(bf16[128,2048]{1,0:T(8,128)(2,1)} %slice.42), channel_id=1, source_target_pairs={{4,0},{8,4},{12,8},{16,12},{20,16},{24,20},{28,24},{5,1},{9,5},{13... | collective-permute-start | bytes 1572872 | tf_op jit(solution)/shard_map/ppermute | solution.py:92
  261.8 7.0 %copy-start.5 = (bf16[192,2048]{0,1:T(8,128)(2,1)S(1)}, bf16[192,2048]{0,1:T(8,128)(2,1)}, u32[]{:S(2)}) copy-start(bf16[192,2048]{0,1:T(8,128)(2,1)} %copy.48) | copy-start | bytes 2359300
  268.8 4.2 %copy-start.2 = (bf16[128,64,192,1]{2,1,3,0:T(8,128)(2,1)S(1)}, bf16[128,64,192,1]{2,1,3,0:T(8,128)(2,1)}, u32[]{:S(2)}) copy-start(bf16[128,64,192,1]{2,1,3,0:T(8,128)(2,1)} %copy.67) | copy-start | bytes 9437188
  268.8 4.3 %copy-start.8 = (bf16[192,2048]{0,1:T(8,128)(2,1)S(1)}, bf16[192,2048]{0,1:T(8,128)(2,1)}, u32[]{:S(2)}) copy-start(bf16[192,2048]{0,1:T(8,128)(2,1)} %copy.53) | copy-start | bytes 2359300
  268.8 4.7 %copy-start.9 = (bf16[192,2048]{0,1:T(8,128)(2,1)S(1)}, bf16[192,2048]{0,1:T(8,128)(2,1)}, u32[]{:S(2)}) copy-start(bf16[192,2048]{0,1:T(8,128)(2,1)} %copy.52) | copy-start | bytes 2359300
  278.7 38.0 %copy-start.4 = (bf16[192,2048]{0,1:T(8,128)(2,1)S(1)}, bf16[192,2048]{0,1:T(8,128)(2,1)}, u32[]{:S(2)}) copy-start(bf16[192,2048]{0,1:T(8,128)(2,1)} %copy.42) | copy-start | bytes 2359300
  316.6 22.5 %copy-start.1 = (f32[512,128]{1,0:T(8,128)S(1)}, f32[512,128]{1,0:T(8,128)}, u32[]{:S(2)}) copy-start(f32[512,128]{1,0:T(8,128)} %param.11) | copy-start | bytes 786436
  (2 other events, 2.1 us)
Sparse Core Ops, SparseCore 0:
  9.6 66.1 all-gather.1
  125.6 91.7 reduce-scatter.1
  261.9 53.8 all-reduce.2

commit v5 on v4

--- a/solution.py
+++ b/solution.py
@@ -53,6 +53,29 @@
     return out
 
 
+def butterfly_sum(x, axis, count):
+    if count & (count - 1):
+        return lax.psum(x, axis)
+    step = 1
+    while step < count:
+        x = x + lax.ppermute(x, axis, [(k, k ^ step) for k in range(count)])
+        step *= 2
+    return x
+
+
+def butterfly_gather(x, axis, count):
+    if count & (count - 1):
+        return lax.all_gather(x, axis, axis=0, tiled=True)
+    me = lax.axis_index(axis)
+    step = 1
+    while step < count:
+        got = lax.ppermute(x, axis, [(k, k ^ step) for k in range(count)])
+        low = (me // step) % 2 == 0
+        x = jnp.where(low, jnp.concatenate([x, got]), jnp.concatenate([got, x]))
+        step *= 2
+    return x
+
+
 def body(cotangent, out_weight, query_act, key_act, value_act, filters):
     rows, chans = cotangent.shape
     groups, flen = filters.shape
@@ -97,13 +120,13 @@
     diag = cross.reshape(local_groups, block, width + 1)[:, :, 1 : halo + 1].sum(axis=1)
     scale = (rows * ctx_count * per_group) ** (-0.5)
     diag, next_head = lax.optimization_barrier((diag, next_head))
-    local_filters = lax.psum(diag[:, ::-1], "ctx") * scale
+    local_filters = butterfly_sum(diag[:, ::-1], "ctx", ctx_count) * scale
+    grad_filters = butterfly_gather(local_filters, "mp", mp_count)
     trailing = jnp.concatenate([grad_conv, next_head], 0)
     win_grad = windows(trailing, tiles, block, width)
     grad_product = filter_apply(mats_anti, win_grad, local_groups, per_group)
-    local_filters, grad_product = lax.optimization_barrier((local_filters, grad_product))
+    grad_filters, grad_product = lax.optimization_barrier((grad_filters, grad_product))
 
-    grad_filters = lax.all_gather(local_filters, "mp", axis=0, tiled=True)
 
     grad_query = (grad_mixed * mixed).astype(jnp.bfloat16)
     grad_key = (grad_product * value_act.astype(jnp.float32)).astype(jnp.bfloat16)

time: 347 us -> 315 us (0.908)
  blocking collectives: 13.9 us -> 0 us
  waiting for transfers between devices: 118 us -> 106 us
  local copies, waits for them, and re-layouts: 127 us -> 118 us
  starting transfers between devices: 18.7 us -> 26.3 us
    psum x1 -> x0, waiting for transfers between devices: 31.2 us -> none  [body(): local_filters = lax.psum(diag[:, ::-1], 'ctx') * scale]
    reduce_scatter x1, waiting for transfers between devices: 35.5 us -> 53.3 us  [body(): lax.psum_scatter(partial, 'ctx', scatter_dimension=0, tiled=True)]
    all_gather x1 -> x0, blocking collectives: 13.9 us -> none  [body(): grad_filters = lax.all_gather(local_filters, 'mp', axis=0, tiled=True)]
    ppermute x0 -> x5, starting transfers between devices: none -> 7.95 us  [the longest x2 4.01 us: butterfly_gather(): got = lax.ppermute(x, axis, [(k, k ^ step) for k in range(count)])]
    unnamed x33 -> x41, local copies, waits for them, and re-layouts: 10.7 us -> 9.39 us
  transfers between devices with their start and end apart: 12 -> 16, of which waited for: 7 -> 7; matrix products, arithmetic and copies ran while one was open for 41% -> 44% of each run, Pallas kernels for 0% -> 0%
where the time goes in v5:
time: 315 us; the launch traced here: 314 us
  local copies, waits for them, and re-layouts  118 us (37%)
  waiting for transfers between devices  106 us (34%)
  starting transfers between devices  26.3 us (8%)
  matrix products  25.8 us (8%)
  other arithmetic  24 us (8%)
  between operations  14.5 us (5%)
    reduce_scatter x1, waiting for transfers between devices, body(): lax.psum_scatter(partial, 'ctx', scatter_dimension=0, tiled=True)  53.3 us
    all_gather x1, waiting for transfers between devices, body(): cot_rows = lax.all_gather(cotangent, 'mp', axis=1, tiled=True)  29.4 us
    optimization_barrier x4, local copies, waits for them, and re-layouts, body(): lax.optimization_barrier((cot_rows, mats_causal, mats_anti))  28.6 us
    ppermute x7, waiting for transfers between devices, exchange_columns(): lax.ppermute(chunk, 'ctx', [(k, (k + shift) % count) for k in range(count)])  19.9 us
    another operation x4, local copies, waits for them, and re-layouts, toeplitz(): flat = jnp.tile(seq, (1, block))[:, :block * width]  18.5 us
    ppermute x7, starting transfers between devices, exchange_columns(): lax.ppermute(chunk, 'ctx', [(k, (k + shift) % count) for k in range(count)])  12.8 us
    reshape x2, local copies, waits for them, and re-layouts, filter_apply(): return total.reshape(tiles * block, chans)  10.8 us
    slice x2, local copies, waits for them, and re-layouts, toeplitz(): flat = jnp.tile(seq, (1, block))[:, :block * width]  10 us
  transfers between devices with their start and end apart: 16, of which 7 were waited for; matrix products, arithmetic and copies ran while one was open for 44% of the time, Pallas kernels for 0%

profile of v5, /device:TPU:0, one launch (start us, length us, event | category | flops | bytes accessed | tf_op | source)
XLA Modules:
  0.0 314.0 jit_solution(10757282230324836938)
XLA Ops:
  11.7 6.1 %tile.9 = f32[128,12352]{0,1:T(8,128)} reshape(f32[128,64,193]{0,2,1:T(8,128)} %tile.8) | data formatting | bytes 12648448 | tf_op jit(solution)/shard_map/tile | solution.py:15
  17.7 5.2 %slice.36 = f32[128,12288]{0,1:T(8,128)} slice(f32[128,12352]{0,1:T(8,128)} %tile.9), slice={[0:128], [0:12288]} | slice | bytes 12582912 | tf_op jit(solution)/shard_map/slice | solution.py:15
  26.2 6.1 %tile.21 = f32[128,12352]{0,1:T(8,128)} reshape(f32[128,64,193]{0,2,1:T(8,128)} %tile.20) | data formatting | bytes 12648448 | tf_op jit(solution)/shard_map/tile | solution.py:15
  32.3 4.8 %slice.37 = f32[128,12288]{0,1:T(8,128)} slice(f32[128,12352]{0,1:T(8,128)} %tile.21), slice={[0:128], [0:12288]} | slice | bytes 12582912 | tf_op jit(solution)/shard_map/slice | solution.py:15
  37.1 9.3 %fusion = (bf16[128,64,192]{0,2,1:T(8,128)(2,1)}, bf16[128,64,192]{0,2,1:T(8,128)(2,1)}, bf16[128,64,192]{0,2,1:T(8,128)(2,1)}, bf16[128,64,192]{0,2,1:T(8,128)(2,1)}) fusion(f32[128,64,192]{0,2,1:T(8,128)} %bitcast.45, f32[128,64,192]{0,2,1:T(8,128)} %bitcast.46), kind=kLoop, calls=%fused_computation.4 | loop fusion | flops 12582912 | bytes 25165824 | tf_op jit(solution)/shard_map/convert_element_type | solution.py:22
  46.4 29.4 %all-gather.2.cloned.1.call-done = bf16[192,8192]{1,0:T(8,128)(2,1)} async-done(((bf16[192,2048]{1,0:T(8,128)(2,1)}), bf16[192,8192]{1,0:T(8,128)(2,1)}) %all-gather.2.cloned.1.call-update) | async-done | bytes 3145744 | tf_op jit(solution)/shard_map/all_gather | solution.py:99
  83.7 7.7 %collective-permute-done = bf16[192,1024]{1,0:T(8,128)(2,1)} collective-permute-done((bf16[192,1024]{1,0:T(8,128)(2,1)}, bf16[192,1024]{1,0:T(8,128)(2,1)}, u32[]{:S(2)}, u32[]{:S(2)}) %collective-permute-start) | collective-permute-done | bytes 393248 | tf_op jit(solution)/shard_map/ppermute | solution.py:50
  93.8 7.0 %collective-permute-start.6 = (bf16[192,1024]{1,0:T(8,128)(2,1)}, bf16[192,1024]{1,0:T(8,128)(2,1)S(1)}, u32[]{:S(2)}, u32[]{:S(2)}) collective-permute-start(bf16[192,1024]{1,0:T(8,128)(2,1)} %get-tuple-element.38), channel_id=1, source_target_pairs={{0,28},{4,0},{8,4},{12,8},{16,12},{20,16},{24,20},{28,24},{1,29},{... | collective-permute-start | bytes 1179656 | tf_op jit(solution)/shard_map/ppermute | solution.py:50
  101.9 6.8 %collective-permute-done.2 = bf16[192,1024]{1,0:T(8,128)(2,1)} collective-permute-done((bf16[192,1024]{1,0:T(8,128)(2,1)}, bf16[192,1024]{1,0:T(8,128)(2,1)}, u32[]{:S(2)}, u32[]{:S(2)}) %collective-permute-start.2) | collective-permute-done | bytes 393248 | tf_op jit(solution)/shard_map/ppermute | solution.py:50
  110.7 5.4 %collective-permute-done.4 = bf16[192,1024]{1,0:T(8,128)(2,1)S(1)} collective-permute-done((bf16[192,1024]{1,0:T(8,128)(2,1)}, bf16[192,1024]{1,0:T(8,128)(2,1)S(1)}, u32[]{:S(2)}, u32[]{:S(2)}) %collective-permute-start.4) | collective-permute-done | bytes 393248 | tf_op jit(solution)/shard_map/ppermute | solution.py:50
  116.3 9.1 %fusion.12 = f32[1536,2048]{1,0:T(8,128)} fusion(bf16[1536,1024]{1,0:T(8,128)(2,1)S(1)} %constant_dynamic-update-slice_fusion, bf16[2048,1024]{1,0:T(8,128)(2,1)S(1)} %copy-done.17), kind=kOutput, calls=%fused_computation.54 | convolution fusion | flops 6442450944 | bytes 19922944 | tf_op jit(solution)/shard_map/dot_general | solution.py:8
  129.3 3.9 %collective-permute-start.7 = (bf16[128,2048]{0,1:T(8,128)(2,1)S(1)}, bf16[128,2048]{0,1:T(8,128)(2,1)S(1)}, u32[]{:S(2)}, u32[]{:S(2)}) collective-permute-start(bf16[128,2048]{0,1:T(8,128)(2,1)S(1)} %slice.38), channel_id=1, source_target_pairs={{0,4},{4,8},{8,12},{12,16},{16,20},{20,24},{24,28},{1,5},{5,9},{9,... | collective-permute-start | bytes 1572872 | tf_op jit(solution)/shard_map/ppermute | solution.py:108
  136.6 7.2 %copy.64 = bf16[128,64,192,1]{2,1,3,0:T(8,128)(2,1)} copy(bf16[128,64,192,1]{0,2,1,3:T(8,128)(2,1)} %bitcast.53) | data formatting | bytes 6291456 | tf_op jit(solution)/shard_map/optimization_barrier | solution.py:100
  143.8 6.9 %copy.63 = bf16[128,64,192,1]{2,1,3,0:T(8,128)(2,1)} copy(bf16[128,64,192,1]{0,2,1,3:T(8,128)(2,1)} %bitcast.52) | data formatting | bytes 6291456 | tf_op jit(solution)/shard_map/optimization_barrier | solution.py:100
  159.6 4.8 %reshape.54 = f32[192,2048]{0,1:T(8,128)S(1)} reshape(f32[3,64,128,16]{1,0,3,2:T(4,128)} %copy.46) | data formatting | bytes 3145728 | tf_op jit(solution)/shard_map/reshape | solution.py:37
  164.4 53.3 %reduce-scatter.2.cloned.1.call-done = f32[192,2048]{1,0:T(8,128)} async-done(((f32[1536,2048]{1,0:T(8,128)}), f32[192,2048]{1,0:T(8,128)}) %reduce-scatter.2.cloned.1.call-update) | async-done | bytes 1572880 | tf_op jit(solution)/shard_map/reduce_scatter | solution.py:103
  227.7 6.8 %convolution_bitcast_fusion = f32[128,64,192]{2,1,0:T(8,128)} fusion(bf16[3,64,128,16]{1,0,3,2:T(4,128)(2,1)} %reshape.55, bf16[1,192,128,16]{1,3,0,2:T(8,128)(2,1)S(1)} %bitcast.49, bf16[1,192,128,16]{1,3,0,2:T(8,128)(2,1)} %bitcast.59, bf16[1,192,128,16]{1,3,0,2:T(8,128)(2,1)} %bitcast.56), kind=kOutput, calls=%fused_computation.7 | convolution fusion | flops 153354240 | bytes 9437184 | tf_op jit(solution)/shard_map/kigc,kjgc->gij/dot_general | solution.py:118
  234.5 8.6 %copy.50 = f32[128,64,192]{0,2,1:T(8,128)} copy(f32[128,64,192]{2,1,0:T(8,128)} %convolution_bitcast_fusion) | data formatting | bytes 12582912 | tf_op jit(solution)/shard_map/kigc,kjgc->gij/dot_general | solution.py:118
  243.1 4.8 %pad.4 = f32[128,12352]{0,1:T(8,128)} pad(f32[128,12288]{0,1:T(8,128)} %bitcast.44, f32[]{:T(128)} %constant.132.clone.1), padding=0_0x0_64 | pad | bytes 12615684 | tf_op jit(solution)/shard_map/jit(_pad)/pad | solution.py:119
  247.9 6.0 %reshape.57 = f32[128,64,193]{0,2,1:T(8,128)} reshape(f32[128,12352]{0,1:T(8,128)} %pad.4) | data formatting | bytes 12648448 | tf_op jit(solution)/shard_map/reshape | solution.py:120
  260.2 6.9 %copy.66 = bf16[128,64,192,1]{2,1,3,0:T(8,128)(2,1)} copy(bf16[128,64,192,1]{0,2,1,3:T(8,128)(2,1)} %bitcast.51) | data formatting | bytes 6291456 | tf_op jit(solution)/shard_map/optimization_barrier | solution.py:100
  267.0 7.6 %copy.67 = bf16[128,64,192,1]{2,1,3,0:T(8,128)(2,1)} copy(bf16[128,64,192,1]{0,2,1,3:T(8,128)(2,1)S(1)} %bitcast.50) | data formatting | bytes 6291456 | tf_op jit(solution)/shard_map/optimization_barrier | solution.py:100
  289.4 3.8 %copy.59 = f32[3,64,128,16]{1,0,3,2:T(4,128)} copy(f32[3,64,128,16]{1,3,0,2:T(8,128)S(1)} %add_bitcast_fusion) | data formatting | bytes 3145728 | tf_op jit(solution)/shard_map/add | solution.py:35
  293.2 6.0 %reshape.58 = f32[192,2048]{0,1:T(8,128)} reshape(f32[3,64,128,16]{1,0,3,2:T(4,128)} %copy.59) | data formatting | bytes 3145728 | tf_op jit(solution)/shard_map/reshape | solution.py:37
  (110 shorter events, 76.1 us)
Async XLA Ops:
  7.2 68.6 %all-gather.2.cloned.1.call-start = ((), (), s32[]{:S(2)}) async-start(), calls=%async_computation.1 | async-start | bytes 3932160 | tf_op jit(solution)/shard_map/all_gather | solution.py:99
  7.9 209.7 %reduce-scatter.2.cloned.1.call-start = ((), (), s32[]{:S(2)}) async-start(), calls=%async_computation.2 | async-start | bytes 14155776 | tf_op jit(solution)/shard_map/reduce_scatter | solution.py:103
  79.2 12.2 %collective-permute-start = (bf16[192,1024]{1,0:T(8,128)(2,1)}, bf16[192,1024]{1,0:T(8,128)(2,1)}, u32[]{:S(2)}, u32[]{:S(2)}) collective-permute-start(bf16[192,1024]{1,0:T(8,128)(2,1)} %get-tuple-element.44), channel_id=1, source_target_pairs={{0,4},{4,8},{8,12},{12,16},{16,20},{20,24},{24,28},{28,0},{1,5},{5... | collective-permute-start | bytes 1179656 | tf_op jit(solution)/shard_map/ppermute | solution.py:50
  79.2 14.6 %collective-permute-start.1 = (bf16[192,1024]{1,0:T(8,128)(2,1)}, bf16[192,1024]{1,0:T(8,128)(2,1)}, u32[]{:S(2)}, u32[]{:S(2)}) collective-permute-start(bf16[192,1024]{1,0:T(8,128)(2,1)} %get-tuple-element.43), channel_id=1, source_target_pairs={{0,8},{4,12},{8,16},{12,20},{16,24},{20,28},{24,0},{28,4},{1,9},{5... | collective-permute-start | bytes 1179656 | tf_op jit(solution)/shard_map/ppermute | solution.py:50
  80.7 27.9 %collective-permute-start.2 = (bf16[192,1024]{1,0:T(8,128)(2,1)}, bf16[192,1024]{1,0:T(8,128)(2,1)}, u32[]{:S(2)}, u32[]{:S(2)}) collective-permute-start(bf16[192,1024]{1,0:T(8,128)(2,1)} %get-tuple-element.42), channel_id=1, source_target_pairs={{0,12},{4,16},{8,20},{12,24},{16,28},{20,0},{24,4},{28,8},{1,13},{... | collective-permute-start | bytes 1179656 | tf_op jit(solution)/shard_map/ppermute | solution.py:50
  83.1 26.6 %collective-permute-start.3 = (bf16[192,1024]{1,0:T(8,128)(2,1)}, bf16[192,1024]{1,0:T(8,128)(2,1)}, u32[]{:S(2)}, u32[]{:S(2)}) collective-permute-start(bf16[192,1024]{1,0:T(8,128)(2,1)} %get-tuple-element.41), channel_id=1, source_target_pairs={{0,16},{4,20},{8,24},{12,28},{16,0},{20,4},{24,8},{28,12},{1,17},{... | collective-permute-start | bytes 1179656 | tf_op jit(solution)/shard_map/ppermute | solution.py:50
  83.6 32.7 %copy-start.17 = (bf16[2048,1024]{1,0:T(8,128)(2,1)S(1)}, bf16[2048,1024]{1,0:T(8,128)(2,1)}, u32[]{:S(2)}) copy-start(bf16[2048,1024]{1,0:T(8,128)(2,1)} %param.7) | copy-start | bytes 12582916
  83.6 32.5 %collective-permute-start.4 = (bf16[192,1024]{1,0:T(8,128)(2,1)}, bf16[192,1024]{1,0:T(8,128)(2,1)S(1)}, u32[]{:S(2)}, u32[]{:S(2)}) collective-permute-start(bf16[192,1024]{1,0:T(8,128)(2,1)} %get-tuple-element.40), channel_id=1, source_target_pairs={{0,20},{4,24},{8,28},{12,0},{16,4},{20,8},{24,12},{28,16},{1,21},{... | collective-permute-start | bytes 1179656 | tf_op jit(solution)/shard_map/ppermute | solution.py:50
  91.4 24.8 %collective-permute-start.5 = (bf16[192,1024]{1,0:T(8,128)(2,1)}, bf16[192,1024]{1,0:T(8,128)(2,1)S(1)}, u32[]{:S(2)}, u32[]{:S(2)}) collective-permute-start(bf16[192,1024]{1,0:T(8,128)(2,1)} %get-tuple-element.39), channel_id=1, source_target_pairs={{0,24},{4,28},{8,0},{12,4},{16,8},{20,12},{24,16},{28,20},{1,25},{... | collective-permute-start | bytes 1179656 | tf_op jit(solution)/shard_map/ppermute | solution.py:50
  93.8 22.4 %collective-permute-start.6 = (bf16[192,1024]{1,0:T(8,128)(2,1)}, bf16[192,1024]{1,0:T(8,128)(2,1)S(1)}, u32[]{:S(2)}, u32[]{:S(2)}) collective-permute-start(bf16[192,1024]{1,0:T(8,128)(2,1)} %get-tuple-element.38), channel_id=1, source_target_pairs={{0,28},{4,0},{8,4},{12,8},{16,12},{20,16},{24,20},{28,24},{1,29},{... | collective-permute-start | bytes 1179656 | tf_op jit(solution)/shard_map/ppermute | solution.py:50
  127.1 9.5 %copy-start.6 = (bf16[192,2048]{0,1:T(8,128)(2,1)}, bf16[192,2048]{0,1:T(8,128)(2,1)S(1)}, u32[]{:S(2)}) copy-start(bf16[192,2048]{0,1:T(8,128)(2,1)S(1)} %copy.43) | copy-start | bytes 2359300
  128.8 7.8 %copy-start.8 = (bf16[192,2048]{0,1:T(8,128)(2,1)}, bf16[192,2048]{0,1:T(8,128)(2,1)S(1)}, u32[]{:S(2)}) copy-start(bf16[192,2048]{0,1:T(8,128)(2,1)S(1)} %copy.42) | copy-start | bytes 2359300
  129.3 5.3 %collective-permute-start.7 = (bf16[128,2048]{0,1:T(8,128)(2,1)S(1)}, bf16[128,2048]{0,1:T(8,128)(2,1)S(1)}, u32[]{:S(2)}, u32[]{:S(2)}) collective-permute-start(bf16[128,2048]{0,1:T(8,128)(2,1)S(1)} %slice.38), channel_id=1, source_target_pairs={{0,4},{4,8},{8,12},{12,16},{16,20},{20,24},{24,28},{1,5},{5,9},{9,... | collective-permute-start | bytes 1572872 | tf_op jit(solution)/shard_map/ppermute | solution.py:108
  143.8 6.9 %copy-start.13 = (bf16[192,2048]{0,1:T(8,128)(2,1)S(1)}, bf16[192,2048]{0,1:T(8,128)(2,1)}, u32[]{:S(2)}) copy-start(bf16[192,2048]{0,1:T(8,128)(2,1)} %get-tuple-element.51) | copy-start | bytes 2359300
  222.7 11.8 %copy-start.5 = (bf16[192,2048]{1,0:T(8,128)(2,1)}, bf16[192,2048]{1,0:T(8,128)(2,1)S(1)}, u32[]{:S(2)}) copy-start(bf16[192,2048]{1,0:T(8,128)(2,1)S(1)} %get-tuple-element.48) | copy-start | bytes 2359300
  223.2 11.3 %copy-start.10 = (bf16[192,2048]{0,1:T(8,128)(2,1)}, bf16[192,2048]{0,1:T(8,128)(2,1)S(1)}, u32[]{:S(2)}) copy-start(bf16[192,2048]{0,1:T(8,128)(2,1)S(1)} %copy.48) | copy-start | bytes 2359300
  226.2 30.4 %collective-permute-start.8 = (bf16[128,2048]{1,0:T(8,128)(2,1)}, bf16[128,2048]{1,0:T(8,128)(2,1)}, u32[]{:S(2)}, u32[]{:S(2)}) collective-permute-start(bf16[128,2048]{1,0:T(8,128)(2,1)} %slice.42), channel_id=1, source_target_pairs={{4,0},{8,4},{12,8},{16,12},{20,16},{24,20},{28,24},{5,1},{9,5},{13... | collective-permute-start | bytes 1572872 | tf_op jit(solution)/shard_map/ppermute | solution.py:115
  256.7 2.1 collective-permute-start.9
  258.8 15.9 %collective-permute-start.10 = (f32[128,128]{0,1:T(8,128)S(1)}, f32[128,128]{0,1:T(8,128)S(1)}, u32[]{:S(2)}, u32[]{:S(2)}) collective-permute-start(f32[128,128]{0,1:T(8,128)S(1)} %add.188), channel_id=1, source_target_pairs={{0,8},{4,12},{8,0},{12,4},{16,24},{20,28},{24,16},{28,20},{1,9},{5... | collective-permute-start | bytes 196616 | tf_op jit(solution)/shard_map/ppermute | solution.py:61
  274.7 7.3 %copy-start.11 = (bf16[192,2048]{0,1:T(8,128)(2,1)S(1)}, bf16[192,2048]{0,1:T(8,128)(2,1)}, u32[]{:S(2)}) copy-start(bf16[192,2048]{0,1:T(8,128)(2,1)} %copy-done.10) | copy-start | bytes 2359300
  274.7 5.7 %collective-permute-start.11 = (f32[128,128]{0,1:T(8,128)S(1)}, f32[128,128]{0,1:T(8,128)S(1)}, u32[]{:S(2)}, u32[]{:S(2)}) collective-permute-start(f32[128,128]{0,1:T(8,128)S(1)} %add.189), channel_id=1, source_target_pairs={{0,16},{4,20},{8,24},{12,28},{16,0},{20,4},{24,8},{28,12},{1,17},{... | collective-permute-start | bytes 196616 | tf_op jit(solution)/shard_map/ppermute | solution.py:61
  280.4 5.1 %collective-permute-start.12 = (f32[128,128]{0,1:T(8,128)S(1)}, f32[128,128]{0,1:T(8,128)S(1)}, u32[]{:S(2)}, u32[]{:S(2)}) collective-permute-start(f32[128,128]{0,1:T(8,128)S(1)} %add_multiply_fusion), channel_id=1, source_target_pairs={{0,1},{1,0},{2,3},{3,2},{4,5},{5,4},{6,7},{7,6},{8,9},{9,8},{10,11... | collective-permute-start | bytes 196616 | tf_op jit(solution)/shard_map/ppermute | solution.py:72
  285.5 13.6 %collective-permute-start.13 = (f32[256,128]{0,1:T(8,128)S(1)}, f32[256,128]{0,1:T(8,128)S(1)}, u32[]{:S(2)}, u32[]{:S(2)}) collective-permute-start(f32[256,128]{0,1:T(8,128)S(1)} %maximum_select_fusion.1), channel_id=1, source_target_pairs={{0,2},{1,3},{2,0},{3,1},{4,6},{5,7},{6,4},{7,5},{8,10},{9,11},{10,... | collective-permute-start | bytes 393224 | tf_op jit(solution)/shard_map/ppermute | solution.py:72
  299.9 7.3 %copy-start.1 = (f32[512,128]{1,0:T(8,128)S(1)}, f32[512,128]{1,0:T(8,128)}, u32[]{:S(2)}) copy-start(f32[512,128]{1,0:T(8,128)} %param.11) | copy-start | bytes 786436
  (10 other events, 44.4 us)
Sparse Core Ops, SparseCore 0:
  9.6 66.1 all-gather.1
  125.6 92.0 reduce-scatter.1

commit v6 on v5

--- a/solution.py
+++ b/solution.py
@@ -92,12 +92,10 @@
     pad = jnp.zeros((local_groups, width + 1 - flen - 1), jnp.float32)
     one = jnp.zeros((local_groups, 1), jnp.float32)
     seq_causal = jnp.concatenate([one, taps[:, ::-1], pad], 1)
-    seq_anti = jnp.concatenate([taps, pad, one], 1)
     mats_causal = split_bf16(toeplitz(seq_causal, block, width))
-    mats_anti = split_bf16(toeplitz(seq_anti, block, width))
 
     cot_rows = lax.all_gather(cotangent, "mp", axis=1, tiled=True)
-    cot_rows, mats_causal, mats_anti = lax.optimization_barrier((cot_rows, mats_causal, mats_anti))
+    cot_rows, mats_causal = lax.optimization_barrier((cot_rows, mats_causal))
     cot_cols = exchange_columns(cot_rows, ctx_count)
     partial = contract(cot_cols, out_weight)
     grad_mixed = lax.psum_scatter(partial, "ctx", scatter_dimension=0, tiled=True)
@@ -122,9 +120,9 @@
     diag, next_head = lax.optimization_barrier((diag, next_head))
     local_filters = butterfly_sum(diag[:, ::-1], "ctx", ctx_count) * scale
     grad_filters = butterfly_gather(local_filters, "mp", mp_count)
-    trailing = jnp.concatenate([grad_conv, next_head], 0)
+    trailing = jnp.concatenate([next_head[::-1], grad_conv[::-1]], 0)
     win_grad = windows(trailing, tiles, block, width)
-    grad_product = filter_apply(mats_anti, win_grad, local_groups, per_group)
+    grad_product = filter_apply(mats_causal, win_grad, local_groups, per_group)[::-1]
     grad_filters, grad_product = lax.optimization_barrier((grad_filters, grad_product))
 
 

time: 315 us -> 340 us (1.079)
  waiting for transfers between devices: 106 us -> 118 us
  local copies, waits for them, and re-layouts: 118 us -> 129 us
    unnamed x41 -> x32, local copies, waits for them, and re-layouts: 9.39 us -> 26.9 us
    all_gather x1, waiting for transfers between devices: 29.4 us -> 45.6 us  [body(): cot_rows = lax.all_gather(cotangent, 'mp', axis=1, tiled=True)]
    optimization_barrier x4 -> x3, local copies, waits for them, and re-layouts: 28.6 us -> 16.3 us  [the longest x2 14 us: body(): cot_rows, mats_causal = lax.optimization_barrier((cot_rows, mats_causal))]
    rev x0 -> x3, local copies, waits for them, and re-layouts: none -> 12 us  [body(): trailing = jnp.concatenate([next_head[::-1], grad_conv[::-1]], 0)]
    another operation x4 -> x2, local copies, waits for them, and re-layouts: 18.5 us -> 9.25 us  [toeplitz(): flat = jnp.tile(seq, (1, block))[:, :block * width]]
    slice x2 -> x1, local copies, waits for them, and re-layouts: 10 us -> 5.26 us  [toeplitz(): flat = jnp.tile(seq, (1, block))[:, :block * width]]
    reduce_scatter x1, waiting for transfers between devices: 53.3 us -> 49.1 us  [body(): lax.psum_scatter(partial, 'ctx', scatter_dimension=0, tiled=True)]
  transfers between devices with their start and end apart: 16 -> 16, of which waited for: 7 -> 7; matrix products, arithmetic and copies ran while one was open for 44% -> 43% of each run, Pallas kernels for 0% -> 0%
where the time goes in v6:
time: 340 us; the launch traced here: 336 us
  local copies, waits for them, and re-layouts  129 us (38%)
  waiting for transfers between devices  118 us (35%)
  matrix products  27.9 us (8%)
  starting transfers between devices  26.6 us (8%)
  other arithmetic  20.8 us (6%)
  between operations  14.5 us (4%)
    reduce_scatter x1, waiting for transfers between devices, body(): lax.psum_scatter(partial, 'ctx', scatter_dimension=0, tiled=True)  49.1 us
    all_gather x1, waiting for transfers between devices, body(): cot_rows = lax.all_gather(cotangent, 'mp', axis=1, tiled=True)  45.6 us
    unnamed x32, local copies, waits for them, and re-layouts  26.9 us
    ppermute x7, waiting for transfers between devices, exchange_columns(): lax.ppermute(chunk, 'ctx', [(k, (k + shift) % count) for k in range(count)])  19.9 us
    optimization_barrier x2, local copies, waits for them, and re-layouts, body(): cot_rows, mats_causal = lax.optimization_barrier((cot_rows, mats_causal))  14 us
    ppermute x7, starting transfers between devices, exchange_columns(): lax.ppermute(chunk, 'ctx', [(k, (k + shift) % count) for k in range(count)])  12.8 us
    dot_general x4, matrix products, filter_apply(): jnp.einsum('gij,kjgc->kigc', m, w4, preferred_element_type=jnp.float32)  12 us
    rev x3, local copies, waits for them, and re-layouts, body(): trailing = jnp.concatenate([next_head[::-1], grad_conv[::-1]], 0)  12 us
  transfers between devices with their start and end apart: 16, of which 7 were waited for; matrix products, arithmetic and copies ran while one was open for 43% of the time, Pallas kernels for 0%

profile of v6, /device:TPU:0, one launch (start us, length us, event | category | flops | bytes accessed | tf_op | source)
XLA Modules:
  0.0 336.4 jit_solution(10666750596929456258)
XLA Ops:
  11.7 6.1 %tile.10 = f32[128,12352]{0,1:T(8,128)} reshape(f32[128,64,193]{0,2,1:T(8,128)} %tile.4) | data formatting | bytes 12648448 | tf_op jit(solution)/shard_map/tile | solution.py:15
  17.8 5.3 %slice.32 = f32[128,12288]{0,1:T(8,128)} slice(f32[128,12352]{0,1:T(8,128)} %tile.10), slice={[0:128], [0:12288]} | slice | bytes 12582912 | tf_op jit(solution)/shard_map/slice | solution.py:15
  23.0 7.1 %fusion = (bf16[128,64,192]{0,2,1:T(8,128)(2,1)}, bf16[128,64,192]{0,2,1:T(8,128)(2,1)}) fusion(f32[128,64,192]{0,2,1:T(8,128)} %bitcast.43), kind=kLoop, calls=%fused_computation.2 | loop fusion | flops 6291456 | bytes 12582912 | tf_op jit(solution)/shard_map/convert_element_type | solution.py:22
  30.2 45.6 %all-gather.2.cloned.1.call-done = bf16[192,8192]{1,0:T(8,128)(2,1)} async-done(((bf16[192,2048]{1,0:T(8,128)(2,1)}), bf16[192,8192]{1,0:T(8,128)(2,1)}) %all-gather.2.cloned.1.call-update) | async-done | bytes 3145744 | tf_op jit(solution)/shard_map/all_gather | solution.py:97
  83.7 7.7 %collective-permute-done = bf16[192,1024]{1,0:T(8,128)(2,1)} collective-permute-done((bf16[192,1024]{1,0:T(8,128)(2,1)}, bf16[192,1024]{1,0:T(8,128)(2,1)}, u32[]{:S(2)}, u32[]{:S(2)}) %collective-permute-start) | collective-permute-done | bytes 393248 | tf_op jit(solution)/shard_map/ppermute | solution.py:50
  93.8 7.0 %collective-permute-start.6 = (bf16[192,1024]{1,0:T(8,128)(2,1)}, bf16[192,1024]{1,0:T(8,128)(2,1)S(1)}, u32[]{:S(2)}, u32[]{:S(2)}) collective-permute-start(bf16[192,1024]{1,0:T(8,128)(2,1)} %get-tuple-element.32), channel_id=1, source_target_pairs={{0,28},{4,0},{8,4},{12,8},{16,12},{20,16},{24,20},{28,24},{1,29},{... | collective-permute-start | bytes 1179656 | tf_op jit(solution)/shard_map/ppermute | solution.py:50
  101.9 6.8 %collective-permute-done.2 = bf16[192,1024]{1,0:T(8,128)(2,1)} collective-permute-done((bf16[192,1024]{1,0:T(8,128)(2,1)}, bf16[192,1024]{1,0:T(8,128)(2,1)}, u32[]{:S(2)}, u32[]{:S(2)}) %collective-permute-start.2) | collective-permute-done | bytes 393248 | tf_op jit(solution)/shard_map/ppermute | solution.py:50
  110.7 5.4 %collective-permute-done.4 = bf16[192,1024]{1,0:T(8,128)(2,1)S(1)} collective-permute-done((bf16[192,1024]{1,0:T(8,128)(2,1)}, bf16[192,1024]{1,0:T(8,128)(2,1)S(1)}, u32[]{:S(2)}, u32[]{:S(2)}) %collective-permute-start.4) | collective-permute-done | bytes 393248 | tf_op jit(solution)/shard_map/ppermute | solution.py:50
  116.3 9.1 %fusion.11 = f32[1536,2048]{1,0:T(8,128)} fusion(bf16[1536,1024]{1,0:T(8,128)(2,1)S(1)} %constant_dynamic-update-slice_fusion, bf16[2048,1024]{1,0:T(8,128)(2,1)S(1)} %copy-done.12), kind=kOutput, calls=%fused_computation.50 | convolution fusion | flops 6442450944 | bytes 19922944 | tf_op jit(solution)/shard_map/dot_general | solution.py:8
  130.1 4.2 %collective-permute-start.7 = (bf16[128,2048]{0,1:T(8,128)(2,1)S(1)}, bf16[128,2048]{0,1:T(8,128)(2,1)S(1)}, u32[]{:S(2)}, u32[]{:S(2)}) collective-permute-start(bf16[128,2048]{0,1:T(8,128)(2,1)S(1)} %slice.33), channel_id=1, source_target_pairs={{0,4},{4,8},{8,12},{12,16},{16,20},{20,24},{24,28},{1,5},{5,9},{9,... | collective-permute-start | bytes 1572872 | tf_op jit(solution)/shard_map/ppermute | solution.py:106
  137.6 7.2 %copy.62 = bf16[128,64,192,1]{2,1,3,0:T(8,128)(2,1)} copy(bf16[128,64,192,1]{0,2,1,3:T(8,128)(2,1)} %bitcast.49) | data formatting | bytes 6291456 | tf_op jit(solution)/shard_map/optimization_barrier | solution.py:98
  144.8 6.8 %copy.61 = bf16[128,64,192,1]{2,1,3,0:T(8,128)(2,1)} copy(bf16[128,64,192,1]{0,2,1,3:T(8,128)(2,1)} %bitcast.48) | data formatting | bytes 6291456 | tf_op jit(solution)/shard_map/optimization_barrier | solution.py:98
  151.6 5.1 %fusion.10 = f32[128,3,16,64]{3,2,1,0:T(8,128)S(1)} fusion(bf16[128,64,192,1]{2,1,3,0:T(8,128)(2,1)} %copy.62, bf16[1,192,128,16]{1,3,0,2:T(8,128)(2,1)S(1)} %bitcast.45, bf16[1,192,128,16]{1,3,0,2:T(8,128)(2,1)} %bitcast.53, bf16[1,192,128,16]{1,3,0,2:T(8,128)(2,1)} %bitcast.50), kind=kOutput, calls=%fused_computation.49 | convolution fusion | flops 153354240 | bytes 7077888 | tf_op jit(solution)/shard_map/gij,kjgc->kigc/dot_general | solution.py:34
  162.4 5.9 %reshape.46 = f32[192,2048]{0,1:T(8,128)} reshape(f32[3,64,128,16]{1,0,3,2:T(4,128)} %copy.44) | data formatting | bytes 3145728 | tf_op jit(solution)/shard_map/reshape | solution.py:37
  168.3 49.1 %reduce-scatter.2.cloned.1.call-done = f32[192,2048]{1,0:T(8,128)} async-done(((f32[1536,2048]{1,0:T(8,128)}), f32[192,2048]{1,0:T(8,128)}) %reduce-scatter.2.cloned.1.call-update) | async-done | bytes 1572880 | tf_op jit(solution)/shard_map/reduce_scatter | solution.py:101
  225.7 5.0 %reshape.47 = bf16[3,64,128,16]{1,0,3,2:T(4,128)(2,1)} reshape(bf16[192,2048]{0,1:T(8,128)(2,1)} %copy.46) | data formatting | bytes 1572864 | tf_op jit(solution)/shard_map/reshape | solution.py:114
  232.2 6.8 %convolution_bitcast_fusion = f32[128,64,192]{2,1,0:T(8,128)} fusion(bf16[3,64,128,16]{1,0,3,2:T(4,128)(2,1)} %reshape.47, bf16[1,192,128,16]{1,3,0,2:T(8,128)(2,1)S(1)} %bitcast.47, bf16[1,192,128,16]{1,3,0,2:T(8,128)(2,1)} %bitcast.54, bf16[1,192,128,16]{1,3,0,2:T(8,128)(2,1)} %bitcast.51), kind=kOutput, calls=%fused_computation.4 | convolution fusion | flops 153354240 | bytes 9437184 | tf_op jit(solution)/shard_map/kigc,kjgc->gij/dot_general | solution.py:116
  238.9 8.6 %copy.48 = f32[128,64,192]{0,2,1:T(8,128)} copy(f32[128,64,192]{2,1,0:T(8,128)} %convolution_bitcast_fusion) | data formatting | bytes 12582912 | tf_op jit(solution)/shard_map/kigc,kjgc->gij/dot_general | solution.py:116
  247.5 4.8 %pad.4 = f32[128,12352]{0,1:T(8,128)} pad(f32[128,12288]{0,1:T(8,128)} %bitcast.44, f32[]{:T(128)} %constant.132.clone.1), padding=0_0x0_64 | pad | bytes 12615684 | tf_op jit(solution)/shard_map/jit(_pad)/pad | solution.py:117
  252.3 6.0 %reshape.49 = f32[128,64,193]{0,2,1:T(8,128)} reshape(f32[128,12352]{0,1:T(8,128)} %pad.4) | data formatting | bytes 12648448 | tf_op jit(solution)/shard_map/reshape | solution.py:118
  268.2 8.4 %rev.17 = bf16[128,2048]{1,0:T(8,128)(2,1)} reverse(bf16[128,2048]{1,0:T(8,128)(2,1)} %collective-permute-done.8), dimensions={0} | reverse | bytes 1048576 | tf_op jit(solution)/shard_map/rev | solution.py:123
  286.4 4.2 %fusion.5 = f32[128,3,16,64]{3,2,1,0:T(8,128)S(1)} fusion(bf16[128,64,192,1]{2,1,3,0:T(8,128)(2,1)} %copy.61, bf16[1,192,128,16]{1,3,0,2:T(8,128)(2,1)S(1)} %bitcast.57, bf16[1,192,128,16]{1,3,0,2:T(8,128)(2,1)} %bitcast.59, bf16[1,192,128,16]{1,3,0,2:T(8,128)(2,1)} %bitcast.61), kind=kOutput, calls=%fused_computation.22 | convolution fusion | flops 153354240 | bytes 7077888 | tf_op jit(solution)/shard_map/gij,kjgc->kigc/dot_general | solution.py:34
  298.2 5.8 %reshape.50 = f32[192,2048]{0,1:T(8,128)} reshape(f32[3,64,128,16]{1,0,3,2:T(4,128)} %copy.57) | data formatting | bytes 3145728 | tf_op jit(solution)/shard_map/reshape | solution.py:37
  304.0 17.5 %reverse = f32[256,2048]{0,1:T(8,128)} reverse(f32[256,2048]{0,1:T(8,128)} %bitcast.56), dimensions={0} | reverse | bytes 4194304
  (100 shorter events, 76.5 us)
Async XLA Ops:
  7.2 68.6 %all-gather.2.cloned.1.call-start = ((), (), s32[]{:S(2)}) async-start(), calls=%async_computation.1 | async-start | bytes 3932160 | tf_op jit(solution)/shard_map/all_gather | solution.py:97
  7.9 209.5 %reduce-scatter.2.cloned.1.call-start = ((), (), s32[]{:S(2)}) async-start(), calls=%async_computation.2 | async-start | bytes 14155776 | tf_op jit(solution)/shard_map/reduce_scatter | solution.py:101
  79.2 12.2 %collective-permute-start = (bf16[192,1024]{1,0:T(8,128)(2,1)}, bf16[192,1024]{1,0:T(8,128)(2,1)}, u32[]{:S(2)}, u32[]{:S(2)}) collective-permute-start(bf16[192,1024]{1,0:T(8,128)(2,1)} %get-tuple-element.38), channel_id=1, source_target_pairs={{0,4},{4,8},{8,12},{12,16},{16,20},{20,24},{24,28},{28,0},{1,5},{5... | collective-permute-start | bytes 1179656 | tf_op jit(solution)/shard_map/ppermute | solution.py:50
  79.2 14.6 %collective-permute-start.1 = (bf16[192,1024]{1,0:T(8,128)(2,1)}, bf16[192,1024]{1,0:T(8,128)(2,1)}, u32[]{:S(2)}, u32[]{:S(2)}) collective-permute-start(bf16[192,1024]{1,0:T(8,128)(2,1)} %get-tuple-element.37), channel_id=1, source_target_pairs={{0,8},{4,12},{8,16},{12,20},{16,24},{20,28},{24,0},{28,4},{1,9},{5... | collective-permute-start | bytes 1179656 | tf_op jit(solution)/shard_map/ppermute | solution.py:50
  80.7 27.9 %collective-permute-start.2 = (bf16[192,1024]{1,0:T(8,128)(2,1)}, bf16[192,1024]{1,0:T(8,128)(2,1)}, u32[]{:S(2)}, u32[]{:S(2)}) collective-permute-start(bf16[192,1024]{1,0:T(8,128)(2,1)} %get-tuple-element.36), channel_id=1, source_target_pairs={{0,12},{4,16},{8,20},{12,24},{16,28},{20,0},{24,4},{28,8},{1,13},{... | collective-permute-start | bytes 1179656 | tf_op jit(solution)/shard_map/ppermute | solution.py:50
  83.1 26.6 %collective-permute-start.3 = (bf16[192,1024]{1,0:T(8,128)(2,1)}, bf16[192,1024]{1,0:T(8,128)(2,1)}, u32[]{:S(2)}, u32[]{:S(2)}) collective-permute-start(bf16[192,1024]{1,0:T(8,128)(2,1)} %get-tuple-element.35), channel_id=1, source_target_pairs={{0,16},{4,20},{8,24},{12,28},{16,0},{20,4},{24,8},{28,12},{1,17},{... | collective-permute-start | bytes 1179656 | tf_op jit(solution)/shard_map/ppermute | solution.py:50
  83.6 32.7 %copy-start.12 = (bf16[2048,1024]{1,0:T(8,128)(2,1)S(1)}, bf16[2048,1024]{1,0:T(8,128)(2,1)}, u32[]{:S(2)}) copy-start(bf16[2048,1024]{1,0:T(8,128)(2,1)} %param.7) | copy-start | bytes 12582916
  83.6 32.5 %collective-permute-start.4 = (bf16[192,1024]{1,0:T(8,128)(2,1)}, bf16[192,1024]{1,0:T(8,128)(2,1)S(1)}, u32[]{:S(2)}, u32[]{:S(2)}) collective-permute-start(bf16[192,1024]{1,0:T(8,128)(2,1)} %get-tuple-element.34), channel_id=1, source_target_pairs={{0,20},{4,24},{8,28},{12,0},{16,4},{20,8},{24,12},{28,16},{1,21},{... | collective-permute-start | bytes 1179656 | tf_op jit(solution)/shard_map/ppermute | solution.py:50
  91.4 24.8 %collective-permute-start.5 = (bf16[192,1024]{1,0:T(8,128)(2,1)}, bf16[192,1024]{1,0:T(8,128)(2,1)S(1)}, u32[]{:S(2)}, u32[]{:S(2)}) collective-permute-start(bf16[192,1024]{1,0:T(8,128)(2,1)} %get-tuple-element.33), channel_id=1, source_target_pairs={{0,24},{4,28},{8,0},{12,4},{16,8},{20,12},{24,16},{28,20},{1,25},{... | collective-permute-start | bytes 1179656 | tf_op jit(solution)/shard_map/ppermute | solution.py:50
  93.8 22.4 %collective-permute-start.6 = (bf16[192,1024]{1,0:T(8,128)(2,1)}, bf16[192,1024]{1,0:T(8,128)(2,1)S(1)}, u32[]{:S(2)}, u32[]{:S(2)}) collective-permute-start(bf16[192,1024]{1,0:T(8,128)(2,1)} %get-tuple-element.32), channel_id=1, source_target_pairs={{0,28},{4,0},{8,4},{12,8},{16,12},{20,16},{24,20},{28,24},{1,29},{... | collective-permute-start | bytes 1179656 | tf_op jit(solution)/shard_map/ppermute | solution.py:50
  130.1 5.5 %collective-permute-start.7 = (bf16[128,2048]{0,1:T(8,128)(2,1)S(1)}, bf16[128,2048]{0,1:T(8,128)(2,1)S(1)}, u32[]{:S(2)}, u32[]{:S(2)}) collective-permute-start(bf16[128,2048]{0,1:T(8,128)(2,1)S(1)} %slice.33), channel_id=1, source_target_pairs={{0,4},{4,8},{8,12},{12,16},{16,20},{20,24},{24,28},{1,5},{5,9},{9,... | collective-permute-start | bytes 1572872 | tf_op jit(solution)/shard_map/ppermute | solution.py:106
  151.6 5.1 %copy-start.3 = (bf16[128,64,192,1]{2,1,3,0:T(8,128)(2,1)S(1)}, bf16[128,64,192,1]{2,1,3,0:T(8,128)(2,1)}, u32[]{:S(2)}) copy-start(bf16[128,64,192,1]{2,1,3,0:T(8,128)(2,1)} %copy.61) | copy-start | bytes 9437188
  151.6 5.4 %copy-start.5 = (bf16[192,2048]{0,1:T(8,128)(2,1)S(1)}, bf16[192,2048]{0,1:T(8,128)(2,1)}, u32[]{:S(2)}) copy-start(bf16[192,2048]{0,1:T(8,128)(2,1)} %get-tuple-element.44) | copy-start | bytes 2359300
  151.6 5.7 %copy-start.6 = (bf16[192,2048]{0,1:T(8,128)(2,1)S(1)}, bf16[192,2048]{0,1:T(8,128)(2,1)}, u32[]{:S(2)}) copy-start(bf16[192,2048]{0,1:T(8,128)(2,1)} %get-tuple-element.45) | copy-start | bytes 2359300
  230.6 30.4 %collective-permute-start.8 = (bf16[128,2048]{1,0:T(8,128)(2,1)}, bf16[128,2048]{1,0:T(8,128)(2,1)}, u32[]{:S(2)}, u32[]{:S(2)}) collective-permute-start(bf16[128,2048]{1,0:T(8,128)(2,1)} %slice.37), channel_id=1, source_target_pairs={{4,0},{8,4},{12,8},{16,12},{20,16},{24,20},{28,24},{5,1},{9,5},{13... | collective-permute-start | bytes 1572872 | tf_op jit(solution)/shard_map/ppermute | solution.py:113
  261.1 2.1 collective-permute-start.9
  263.2 13.4 %collective-permute-start.10 = (f32[128,128]{0,1:T(8,128)S(1)}, f32[128,128]{0,1:T(8,128)S(1)}, u32[]{:S(2)}, u32[]{:S(2)}) collective-permute-start(f32[128,128]{0,1:T(8,128)S(1)} %add.188), channel_id=1, source_target_pairs={{0,8},{4,12},{8,0},{12,4},{16,24},{20,28},{24,16},{28,20},{1,9},{5... | collective-permute-start | bytes 196616 | tf_op jit(solution)/shard_map/ppermute | solution.py:61
  276.6 8.2 %collective-permute-start.11 = (f32[128,128]{0,1:T(8,128)S(1)}, f32[128,128]{0,1:T(8,128)S(1)}, u32[]{:S(2)}, u32[]{:S(2)}) collective-permute-start(f32[128,128]{0,1:T(8,128)S(1)} %add.189), channel_id=1, source_target_pairs={{0,16},{4,20},{8,24},{12,28},{16,0},{20,4},{24,8},{28,12},{1,17},{... | collective-permute-start | bytes 196616 | tf_op jit(solution)/shard_map/ppermute | solution.py:61
  284.8 5.7 %collective-permute-start.12 = (f32[128,128]{0,1:T(8,128)S(1)}, f32[128,128]{0,1:T(8,128)S(1)}, u32[]{:S(2)}, u32[]{:S(2)}) collective-permute-start(f32[128,128]{0,1:T(8,128)S(1)} %add_multiply_fusion), channel_id=1, source_target_pairs={{0,1},{1,0},{2,3},{3,2},{4,5},{5,4},{6,7},{7,6},{8,9},{9,8},{10,11... | collective-permute-start | bytes 196616 | tf_op jit(solution)/shard_map/ppermute | solution.py:72
  286.4 6.7 %copy-start.2 = (bf16[128,64,192,1]{2,1,3,0:T(8,128)(2,1)S(1)}, bf16[128,64,192,1]{2,1,3,0:T(8,128)(2,1)}, u32[]{:S(2)}) copy-start(bf16[128,64,192,1]{2,1,3,0:T(8,128)(2,1)} %copy.62) | copy-start | bytes 9437188
  286.4 6.7 %copy-start.7 = (bf16[192,2048]{0,1:T(8,128)(2,1)S(1)}, bf16[192,2048]{0,1:T(8,128)(2,1)}, u32[]{:S(2)}) copy-start(bf16[192,2048]{0,1:T(8,128)(2,1)} %copy.50) | copy-start | bytes 2359300
  286.4 6.7 %copy-start.8 = (bf16[192,2048]{0,1:T(8,128)(2,1)S(1)}, bf16[192,2048]{0,1:T(8,128)(2,1)}, u32[]{:S(2)}) copy-start(bf16[192,2048]{0,1:T(8,128)(2,1)} %copy.49) | copy-start | bytes 2359300
  290.6 33.3 %collective-permute-start.13 = (f32[256,128]{0,1:T(8,128)S(1)}, f32[256,128]{0,1:T(8,128)S(1)}, u32[]{:S(2)}, u32[]{:S(2)}) collective-permute-start(f32[256,128]{0,1:T(8,128)S(1)} %maximum_select_fusion.1), channel_id=1, source_target_pairs={{0,2},{1,3},{2,0},{3,1},{4,6},{5,7},{6,4},{7,5},{8,10},{9,11},{10,... | collective-permute-start | bytes 393224 | tf_op jit(solution)/shard_map/ppermute | solution.py:72
  323.9 5.7 %copy-start.1 = (f32[512,128]{1,0:T(8,128)S(1)}, f32[512,128]{1,0:T(8,128)}, u32[]{:S(2)}) copy-start(f32[512,128]{1,0:T(8,128)} %param.11) | copy-start | bytes 786436
  (5 other events, 8.0 us)
Sparse Core Ops, SparseCore 0:
  9.6 66.1 all-gather.1
  125.6 91.7 reduce-scatter.1

commit v7 on v5

--- a/solution.py
+++ b/solution.py
@@ -14,6 +14,20 @@
     groups = seq.shape[0]
     flat = jnp.tile(seq, (1, block))[:, : block * width]
     return flat.reshape(groups, block, width)
+
+
+def toeplitz_mats(taps, block, width, halo, causal, zero):
+    groups, flen = taps.shape
+    hi = lax.reduce_precision(taps, exponent_bits=8, mantissa_bits=7)
+    both = jnp.concatenate([hi, taps - hi], 0).astype(jnp.bfloat16)
+    i = lax.broadcasted_iota(jnp.int32, (block, width, flen), 0)
+    j = lax.broadcasted_iota(jnp.int32, (block, width, flen), 1)
+    s = lax.broadcasted_iota(jnp.int32, (block, width, flen), 2) + zero
+    lag = i + halo - j if causal else j - i
+    pick = (lag == s).astype(jnp.bfloat16)
+    mats = jnp.einsum("gs,ijs->gij", both, pick, preferred_element_type=jnp.float32)
+    mats = mats.astype(jnp.bfloat16)
+    return mats[:groups], mats[groups:]
 
 
 def split_bf16(x):
@@ -93,8 +107,9 @@
     one = jnp.zeros((local_groups, 1), jnp.float32)
     seq_causal = jnp.concatenate([one, taps[:, ::-1], pad], 1)
     seq_anti = jnp.concatenate([taps, pad, one], 1)
-    mats_causal = split_bf16(toeplitz(seq_causal, block, width))
-    mats_anti = split_bf16(toeplitz(seq_anti, block, width))
+    zero = lax.axis_index("ctx") // ctx_count
+    mats_causal = toeplitz_mats(taps, block, width, halo, True, zero)
+    mats_anti = toeplitz_mats(taps, block, width, halo, False, zero)
 
     cot_rows = lax.all_gather(cotangent, "mp", axis=1, tiled=True)
     cot_rows, mats_causal, mats_anti = lax.optimization_barrier((cot_rows, mats_causal, mats_anti))

time: 315 us -> 315 us (level)
  waiting for transfers between devices: 106 us -> 134 us
  local copies, waits for them, and re-layouts: 118 us -> 93.8 us
  other arithmetic: 24 us -> 15.7 us
  matrix products: 25.8 us -> 29.4 us
    all_gather x1, waiting for transfers between devices: 29.4 us -> 57.9 us  [body(): cot_rows = lax.all_gather(cotangent, 'mp', axis=1, tiled=True)]
    another operation x4 -> x0, local copies, waits for them, and re-layouts: 18.5 us -> none  [toeplitz(): flat = jnp.tile(seq, (1, block))[:, :block * width]]
    convert_element_type x1 -> x0, other arithmetic: 9.3 us -> none  [split_bf16(): return (hi.astype(jnp.bfloat16), lo.astype(jnp.bfloat16))]
    slice x2 -> x1, local copies, waits for them, and re-layouts: 10 us -> 5.26 us  [toeplitz_mats(): return (mats[:groups], mats[groups:])]
    dot_general x0 -> x2, matrix products: none -> 3.65 us  [toeplitz_mats(): jnp.einsum('gs,ijs->gij', both, pick, preferred_element_type=jnp.float32)]
    unnamed x41 -> x35, local copies, waits for them, and re-layouts: 9.39 us -> 9.37 us
  transfers between devices with their start and end apart: 16 -> 16, of which waited for: 7 -> 7; matrix products, arithmetic and copies ran while one was open for 44% -> 35% of each run, Pallas kernels for 0% -> 0%
where the time goes in v7:
time: 315 us; the launch traced here: 314 us
  waiting for transfers between devices  134 us (43%)
  local copies, waits for them, and re-layouts  93.8 us (30%)
  matrix products  29.4 us (9%)
  starting transfers between devices  26.3 us (8%)
  other arithmetic  15.7 us (5%)
  between operations  14.5 us (5%)
    all_gather x1, waiting for transfers between devices, body(): cot_rows = lax.all_gather(cotangent, 'mp', axis=1, tiled=True)  57.9 us
    reduce_scatter x1, waiting for transfers between devices, body(): lax.psum_scatter(partial, 'ctx', scatter_dimension=0, tiled=True)  53 us
    optimization_barrier x4, local copies, waits for them, and re-layouts, body(): lax.optimization_barrier((cot_rows, mats_causal, mats_anti))  28.7 us
    ppermute x7, waiting for transfers between devices, exchange_columns(): lax.ppermute(chunk, 'ctx', [(k, (k + shift) % count) for k in range(count)])  19.9 us
    ppermute x7, starting transfers between devices, exchange_columns(): lax.ppermute(chunk, 'ctx', [(k, (k + shift) % count) for k in range(count)])  12.8 us
    reshape x2, local copies, waits for them, and re-layouts, filter_apply(): return total.reshape(tiles * block, chans)  10.8 us
    dot_general x4, matrix products, filter_apply(): jnp.einsum('gij,kjgc->kigc', m, w4, preferred_element_type=jnp.float32)  9.89 us
    unnamed x35, local copies, waits for them, and re-layouts  9.37 us
  transfers between devices with their start and end apart: 16, of which 7 were waited for; matrix products, arithmetic and copies ran while one was open for 35% of the time, Pallas kernels for 0%

profile of v7, /device:TPU:0, one launch (start us, length us, event | category | flops | bytes accessed | tf_op | source)
XLA Modules:
  0.0 313.6 jit_solution(11927156614571287106)
XLA Ops:
  12.6 5.3 %fusion.20 = (bf16[128,64,192]{0,2,1:T(8,128)(2,1)}, bf16[128,64,192]{0,2,1:T(8,128)(2,1)}, bf16[128,64,192]{0,2,1:T(8,128)(2,1)}, bf16[128,64,192]{0,2,1:T(8,128)(2,1)}) fusion(bf16[256,64,192]{0,2,1:T(8,128)(2,1)S(1)} %fusion.2, bf16[256,64,192]{0,2,1:T(8,128)(2,1)S(1)} %fusion.3), kind=kLoop, calls=%fused_computation.62 | loop fusion | bytes 25165824 | tf_op jit(solution)/shard_map/slice | solution.py:30
  17.9 57.9 %all-gather.2.cloned.1.call-done = bf16[192,8192]{1,0:T(8,128)(2,1)} async-done(((bf16[192,2048]{1,0:T(8,128)(2,1)}), bf16[192,8192]{1,0:T(8,128)(2,1)}) %all-gather.2.cloned.1.call-update) | async-done | bytes 3145744 | tf_op jit(solution)/shard_map/all_gather | solution.py:114
  83.5 7.7 %collective-permute-done = bf16[192,1024]{1,0:T(8,128)(2,1)} collective-permute-done((bf16[192,1024]{1,0:T(8,128)(2,1)}, bf16[192,1024]{1,0:T(8,128)(2,1)}, u32[]{:S(2)}, u32[]{:S(2)}) %collective-permute-start) | collective-permute-done | bytes 393248 | tf_op jit(solution)/shard_map/ppermute | solution.py:64
  93.7 7.0 %collective-permute-start.6 = (bf16[192,1024]{1,0:T(8,128)(2,1)S(1)}, bf16[192,1024]{1,0:T(8,128)(2,1)S(1)}, u32[]{:S(2)}, u32[]{:S(2)}) collective-permute-start(bf16[192,1024]{1,0:T(8,128)(2,1)S(1)} %get-tuple-element.38), channel_id=1, source_target_pairs={{0,28},{4,0},{8,4},{12,8},{16,12},{20,16},{24,20},{28,24},{1,29},{... | collective-permute-start | bytes 1179656 | tf_op jit(solution)/shard_map/ppermute | solution.py:64
  101.7 6.8 %collective-permute-done.2 = bf16[192,1024]{1,0:T(8,128)(2,1)} collective-permute-done((bf16[192,1024]{1,0:T(8,128)(2,1)}, bf16[192,1024]{1,0:T(8,128)(2,1)}, u32[]{:S(2)}, u32[]{:S(2)}) %collective-permute-start.2) | collective-permute-done | bytes 393248 | tf_op jit(solution)/shard_map/ppermute | solution.py:64
  110.5 5.4 %collective-permute-done.4 = bf16[192,1024]{1,0:T(8,128)(2,1)S(1)} collective-permute-done((bf16[192,1024]{1,0:T(8,128)(2,1)}, bf16[192,1024]{1,0:T(8,128)(2,1)S(1)}, u32[]{:S(2)}, u32[]{:S(2)}) %collective-permute-start.4) | collective-permute-done | bytes 393248 | tf_op jit(solution)/shard_map/ppermute | solution.py:64
  116.2 9.1 %fusion.22 = f32[1536,2048]{1,0:T(8,128)} fusion(bf16[1536,1024]{1,0:T(8,128)(2,1)S(1)} %constant_dynamic-update-slice_fusion, bf16[2048,1024]{1,0:T(8,128)(2,1)S(1)} %copy-done.14), kind=kOutput, calls=%fused_computation.64 | convolution fusion | flops 6442450944 | bytes 19922944 | tf_op jit(solution)/shard_map/dot_general | solution.py:8
  129.2 3.9 %collective-permute-start.7 = (bf16[128,2048]{0,1:T(8,128)(2,1)S(1)}, bf16[128,2048]{0,1:T(8,128)(2,1)S(1)}, u32[]{:S(2)}, u32[]{:S(2)}) collective-permute-start(bf16[128,2048]{0,1:T(8,128)(2,1)S(1)} %slice.48), channel_id=1, source_target_pairs={{0,4},{4,8},{8,12},{12,16},{16,20},{20,24},{24,28},{1,5},{5,9},{9,... | collective-permute-start | bytes 1572872 | tf_op jit(solution)/shard_map/ppermute | solution.py:123
  136.5 7.2 %copy.64 = bf16[128,64,192,1]{2,1,3,0:T(8,128)(2,1)} copy(bf16[128,64,192,1]{0,2,1,3:T(8,128)(2,1)} %bitcast.49) | data formatting | bytes 6291456 | tf_op jit(solution)/shard_map/optimization_barrier | solution.py:115
  143.7 7.0 %copy.63 = bf16[128,64,192,1]{2,1,3,0:T(8,128)(2,1)} copy(bf16[128,64,192,1]{0,2,1,3:T(8,128)(2,1)} %bitcast.48) | data formatting | bytes 6291456 | tf_op jit(solution)/shard_map/optimization_barrier | solution.py:115
  150.7 3.6 %fusion.19 = f32[128,3,16,64]{3,2,1,0:T(8,128)S(1)} fusion(bf16[128,64,192,1]{2,1,3,0:T(8,128)(2,1)} %copy.64, bf16[1,192,128,16]{1,3,0,2:T(8,128)(2,1)S(1)} %bitcast.43, bf16[1,192,128,16]{1,3,0,2:T(8,128)(2,1)S(1)} %bitcast.56, bf16[1,192,128,16]{1,3,0,2:T(8,128)(2,1)S(1)} %bitcast.53), kind=kOutput, calls=%fused_computation.61 | convolution fusion | flops 153354240 | bytes 7077888 | tf_op jit(solution)/shard_map/gij,kjgc->kigc/dot_general | solution.py:48
  155.9 3.7 %copy.46 = f32[3,64,128,16]{1,0,3,2:T(4,128)} copy(f32[3,64,128,16]{1,3,0,2:T(8,128)S(1)} %add_bitcast_fusion.1) | data formatting | bytes 3145728 | tf_op jit(solution)/shard_map/add | solution.py:49
  159.6 4.8 %reshape.38 = f32[192,2048]{0,1:T(8,128)S(1)} reshape(f32[3,64,128,16]{1,0,3,2:T(4,128)} %copy.46) | data formatting | bytes 3145728 | tf_op jit(solution)/shard_map/reshape | solution.py:51
  164.5 53.0 %reduce-scatter.2.cloned.1.call-done = f32[192,2048]{1,0:T(8,128)} async-done(((f32[1536,2048]{1,0:T(8,128)}), f32[192,2048]{1,0:T(8,128)}) %reduce-scatter.2.cloned.1.call-update) | async-done | bytes 1572880 | tf_op jit(solution)/shard_map/reduce_scatter | solution.py:118
  219.3 3.4 %multiply_convert_fusion = (bf16[192,2048]{1,0:T(8,128)(2,1)S(1)}, bf16[192,2048]{1,0:T(8,128)(2,1)}) fusion(f32[192,2048]{1,0:T(8,128)} %reduce-scatter.2.cloned.1.call-done, bf16[192,2048]{1,0:T(8,128)(2,1)} %param.8, f32[192,2048]{1,0:T(8,128)} %copy.47), kind=kLoop, calls=%fused_computation.24 | loop fusion | flops 1966080 | bytes 5505024 | tf_op jit(solution)/shard_map/convert_element_type | solution.py:129
  227.0 6.8 %convolution_bitcast_fusion = f32[128,64,192]{2,1,0:T(8,128)} fusion(bf16[3,64,128,16]{1,0,3,2:T(4,128)(2,1)} %reshape.39, bf16[1,192,128,16]{1,3,0,2:T(8,128)(2,1)S(1)} %bitcast.45, bf16[1,192,128,16]{1,3,0,2:T(8,128)(2,1)} %bitcast.55, bf16[1,192,128,16]{1,3,0,2:T(8,128)(2,1)} %bitcast.52), kind=kOutput, calls=%fused_computation.7 | convolution fusion | flops 153354240 | bytes 9437184 | tf_op jit(solution)/shard_map/kigc,kjgc->gij/dot_general | solution.py:133
  233.8 8.7 %copy.50 = f32[128,64,192]{0,2,1:T(8,128)} copy(f32[128,64,192]{2,1,0:T(8,128)} %convolution_bitcast_fusion) | data formatting | bytes 12582912 | tf_op jit(solution)/shard_map/kigc,kjgc->gij/dot_general | solution.py:133
  242.5 4.8 %pad.4 = f32[128,12352]{0,1:T(8,128)} pad(f32[128,12288]{0,1:T(8,128)} %bitcast.42, f32[]{:T(128)} %constant.158.clone.1), padding=0_0x0_64 | pad | bytes 12615684 | tf_op jit(solution)/shard_map/jit(_pad)/pad | solution.py:134
  247.3 6.0 %reshape.41 = f32[128,64,193]{0,2,1:T(8,128)} reshape(f32[128,12352]{0,1:T(8,128)} %pad.4) | data formatting | bytes 12648448 | tf_op jit(solution)/shard_map/reshape | solution.py:135
  259.5 6.9 %copy.66 = bf16[128,64,192,1]{2,1,3,0:T(8,128)(2,1)} copy(bf16[128,64,192,1]{0,2,1,3:T(8,128)(2,1)} %bitcast.47) | data formatting | bytes 6291456 | tf_op jit(solution)/shard_map/optimization_barrier | solution.py:115
  266.5 7.6 %copy.67 = bf16[128,64,192,1]{2,1,3,0:T(8,128)(2,1)} copy(bf16[128,64,192,1]{0,2,1,3:T(8,128)(2,1)S(1)} %bitcast.46) | data formatting | bytes 6291456 | tf_op jit(solution)/shard_map/optimization_barrier | solution.py:115
  281.4 3.5 %fusion.11 = f32[128,3,16,64]{3,2,1,0:T(8,128)S(1)} fusion(bf16[128,64,192,1]{2,1,3,0:T(8,128)(2,1)} %copy.66, bf16[1,192,128,16]{1,3,0,2:T(8,128)(2,1)S(1)} %bitcast.58, bf16[1,192,128,16]{1,3,0,2:T(8,128)(2,1)S(1)} %bitcast.60, bf16[1,192,128,16]{1,3,0,2:T(8,128)(2,1)S(1)} %bitcast.50), kind=kOutput, calls=%fused_computation.28 | convolution fusion | flops 153354240 | bytes 7077888 | tf_op jit(solution)/shard_map/gij,kjgc->kigc/dot_general | solution.py:48
  288.8 3.7 %copy.59 = f32[3,64,128,16]{1,0,3,2:T(4,128)} copy(f32[3,64,128,16]{1,3,0,2:T(8,128)S(1)} %add_bitcast_fusion) | data formatting | bytes 3145728 | tf_op jit(solution)/shard_map/add | solution.py:49
  292.6 6.0 %reshape.42 = f32[192,2048]{0,1:T(8,128)} reshape(f32[3,64,128,16]{1,0,3,2:T(4,128)} %copy.59) | data formatting | bytes 3145728 | tf_op jit(solution)/shard_map/reshape | solution.py:51
  (96 shorter events, 59.2 us)
Async XLA Ops:
  7.2 68.6 %all-gather.2.cloned.1.call-start = ((), (), s32[]{:S(2)}) async-start(), calls=%async_computation.1 | async-start | bytes 3932160 | tf_op jit(solution)/shard_map/all_gather | solution.py:114
  7.9 209.6 %reduce-scatter.2.cloned.1.call-start = ((), (), s32[]{:S(2)}) async-start(), calls=%async_computation.2 | async-start | bytes 14155776 | tf_op jit(solution)/shard_map/reduce_scatter | solution.py:118
  79.1 12.2 %collective-permute-start = (bf16[192,1024]{1,0:T(8,128)(2,1)}, bf16[192,1024]{1,0:T(8,128)(2,1)}, u32[]{:S(2)}, u32[]{:S(2)}) collective-permute-start(bf16[192,1024]{1,0:T(8,128)(2,1)} %get-tuple-element.44), channel_id=1, source_target_pairs={{0,4},{4,8},{8,12},{12,16},{16,20},{20,24},{24,28},{28,0},{1,5},{5... | collective-permute-start | bytes 1179656 | tf_op jit(solution)/shard_map/ppermute | solution.py:64
  79.1 14.6 %collective-permute-start.1 = (bf16[192,1024]{1,0:T(8,128)(2,1)}, bf16[192,1024]{1,0:T(8,128)(2,1)}, u32[]{:S(2)}, u32[]{:S(2)}) collective-permute-start(bf16[192,1024]{1,0:T(8,128)(2,1)} %get-tuple-element.43), channel_id=1, source_target_pairs={{0,8},{4,12},{8,16},{12,20},{16,24},{20,28},{24,0},{28,4},{1,9},{5... | collective-permute-start | bytes 1179656 | tf_op jit(solution)/shard_map/ppermute | solution.py:64
  80.6 27.9 %collective-permute-start.2 = (bf16[192,1024]{1,0:T(8,128)(2,1)}, bf16[192,1024]{1,0:T(8,128)(2,1)}, u32[]{:S(2)}, u32[]{:S(2)}) collective-permute-start(bf16[192,1024]{1,0:T(8,128)(2,1)} %get-tuple-element.42), channel_id=1, source_target_pairs={{0,12},{4,16},{8,20},{12,24},{16,28},{20,0},{24,4},{28,8},{1,13},{... | collective-permute-start | bytes 1179656 | tf_op jit(solution)/shard_map/ppermute | solution.py:64
  82.9 26.6 %collective-permute-start.3 = (bf16[192,1024]{1,0:T(8,128)(2,1)}, bf16[192,1024]{1,0:T(8,128)(2,1)}, u32[]{:S(2)}, u32[]{:S(2)}) collective-permute-start(bf16[192,1024]{1,0:T(8,128)(2,1)} %get-tuple-element.41), channel_id=1, source_target_pairs={{0,16},{4,20},{8,24},{12,28},{16,0},{20,4},{24,8},{28,12},{1,17},{... | collective-permute-start | bytes 1179656 | tf_op jit(solution)/shard_map/ppermute | solution.py:64
  83.5 32.7 %copy-start.14 = (bf16[2048,1024]{1,0:T(8,128)(2,1)S(1)}, bf16[2048,1024]{1,0:T(8,128)(2,1)}, u32[]{:S(2)}) copy-start(bf16[2048,1024]{1,0:T(8,128)(2,1)} %param.7) | copy-start | bytes 12582916
  83.5 32.5 %collective-permute-start.4 = (bf16[192,1024]{1,0:T(8,128)(2,1)}, bf16[192,1024]{1,0:T(8,128)(2,1)S(1)}, u32[]{:S(2)}, u32[]{:S(2)}) collective-permute-start(bf16[192,1024]{1,0:T(8,128)(2,1)} %get-tuple-element.40), channel_id=1, source_target_pairs={{0,20},{4,24},{8,28},{12,0},{16,4},{20,8},{24,12},{28,16},{1,21},{... | collective-permute-start | bytes 1179656 | tf_op jit(solution)/shard_map/ppermute | solution.py:64
  91.3 24.8 %collective-permute-start.5 = (bf16[192,1024]{1,0:T(8,128)(2,1)}, bf16[192,1024]{1,0:T(8,128)(2,1)S(1)}, u32[]{:S(2)}, u32[]{:S(2)}) collective-permute-start(bf16[192,1024]{1,0:T(8,128)(2,1)} %get-tuple-element.39), channel_id=1, source_target_pairs={{0,24},{4,28},{8,0},{12,4},{16,8},{20,12},{24,16},{28,20},{1,25},{... | collective-permute-start | bytes 1179656 | tf_op jit(solution)/shard_map/ppermute | solution.py:64
  93.7 22.4 %collective-permute-start.6 = (bf16[192,1024]{1,0:T(8,128)(2,1)S(1)}, bf16[192,1024]{1,0:T(8,128)(2,1)S(1)}, u32[]{:S(2)}, u32[]{:S(2)}) collective-permute-start(bf16[192,1024]{1,0:T(8,128)(2,1)S(1)} %get-tuple-element.38), channel_id=1, source_target_pairs={{0,28},{4,0},{8,4},{12,8},{16,12},{20,16},{24,20},{28,24},{1,29},{... | collective-permute-start | bytes 1179656 | tf_op jit(solution)/shard_map/ppermute | solution.py:64
  126.9 9.6 %copy-start.4 = (bf16[192,2048]{0,1:T(8,128)(2,1)}, bf16[192,2048]{0,1:T(8,128)(2,1)S(1)}, u32[]{:S(2)}) copy-start(bf16[192,2048]{0,1:T(8,128)(2,1)S(1)} %copy.43) | copy-start | bytes 2359300
  128.7 7.9 %copy-start.6 = (bf16[192,2048]{0,1:T(8,128)(2,1)}, bf16[192,2048]{0,1:T(8,128)(2,1)S(1)}, u32[]{:S(2)}) copy-start(bf16[192,2048]{0,1:T(8,128)(2,1)S(1)} %copy.42) | copy-start | bytes 2359300
  129.2 5.3 %collective-permute-start.7 = (bf16[128,2048]{0,1:T(8,128)(2,1)S(1)}, bf16[128,2048]{0,1:T(8,128)(2,1)S(1)}, u32[]{:S(2)}, u32[]{:S(2)}) collective-permute-start(bf16[128,2048]{0,1:T(8,128)(2,1)S(1)} %slice.48), channel_id=1, source_target_pairs={{0,4},{4,8},{8,12},{12,16},{16,20},{20,24},{24,28},{1,5},{5,9},{9,... | collective-permute-start | bytes 1572872 | tf_op jit(solution)/shard_map/ppermute | solution.py:123
  143.7 7.0 %copy-start.11 = (bf16[192,2048]{0,1:T(8,128)(2,1)S(1)}, bf16[192,2048]{0,1:T(8,128)(2,1)}, u32[]{:S(2)}) copy-start(bf16[192,2048]{0,1:T(8,128)(2,1)} %get-tuple-element.51) | copy-start | bytes 2359300
  222.7 11.1 %copy-start.3 = (bf16[192,2048]{1,0:T(8,128)(2,1)}, bf16[192,2048]{1,0:T(8,128)(2,1)S(1)}, u32[]{:S(2)}) copy-start(bf16[192,2048]{1,0:T(8,128)(2,1)S(1)} %get-tuple-element.48) | copy-start | bytes 2359300
  223.2 10.6 %copy-start.8 = (bf16[192,2048]{0,1:T(8,128)(2,1)}, bf16[192,2048]{0,1:T(8,128)(2,1)S(1)}, u32[]{:S(2)}) copy-start(bf16[192,2048]{0,1:T(8,128)(2,1)S(1)} %copy.48) | copy-start | bytes 2359300
  225.5 30.5 %collective-permute-start.8 = (bf16[128,2048]{1,0:T(8,128)(2,1)S(1)}, bf16[128,2048]{1,0:T(8,128)(2,1)}, u32[]{:S(2)}, u32[]{:S(2)}) collective-permute-start(bf16[128,2048]{1,0:T(8,128)(2,1)S(1)} %slice.52), channel_id=1, source_target_pairs={{4,0},{8,4},{12,8},{16,12},{20,16},{24,20},{28,24},{5,1},{9,5},{13... | collective-permute-start | bytes 1572872 | tf_op jit(solution)/shard_map/ppermute | solution.py:130
  256.0 2.1 collective-permute-start.9
  258.1 15.9 %collective-permute-start.10 = (f32[128,128]{0,1:T(8,128)S(1)}, f32[128,128]{0,1:T(8,128)S(1)}, u32[]{:S(2)}, u32[]{:S(2)}) collective-permute-start(f32[128,128]{0,1:T(8,128)S(1)} %add.209), channel_id=1, source_target_pairs={{0,8},{4,12},{8,0},{12,4},{16,24},{20,28},{24,16},{28,20},{1,9},{5... | collective-permute-start | bytes 196616 | tf_op jit(solution)/shard_map/ppermute | solution.py:75
  274.1 7.3 %copy-start.9 = (bf16[192,2048]{0,1:T(8,128)(2,1)S(1)}, bf16[192,2048]{0,1:T(8,128)(2,1)}, u32[]{:S(2)}) copy-start(bf16[192,2048]{0,1:T(8,128)(2,1)} %copy-done.8) | copy-start | bytes 2359300
  274.1 5.7 %collective-permute-start.11 = (f32[128,128]{0,1:T(8,128)S(1)}, f32[128,128]{0,1:T(8,128)S(1)}, u32[]{:S(2)}, u32[]{:S(2)}) collective-permute-start(f32[128,128]{0,1:T(8,128)S(1)} %add.210), channel_id=1, source_target_pairs={{0,16},{4,20},{8,24},{12,28},{16,0},{20,4},{24,8},{28,12},{1,17},{... | collective-permute-start | bytes 196616 | tf_op jit(solution)/shard_map/ppermute | solution.py:75
  279.8 5.1 %collective-permute-start.12 = (f32[128,128]{0,1:T(8,128)S(1)}, f32[128,128]{0,1:T(8,128)S(1)}, u32[]{:S(2)}, u32[]{:S(2)}) collective-permute-start(f32[128,128]{0,1:T(8,128)S(1)} %add_multiply_fusion), channel_id=1, source_target_pairs={{0,1},{1,0},{2,3},{3,2},{4,5},{5,4},{6,7},{7,6},{8,9},{9,8},{10,11... | collective-permute-start | bytes 196616 | tf_op jit(solution)/shard_map/ppermute | solution.py:86
  285.0 13.6 %collective-permute-start.13 = (f32[256,128]{0,1:T(8,128)S(1)}, f32[256,128]{0,1:T(8,128)}, u32[]{:S(2)}, u32[]{:S(2)}) collective-permute-start(f32[256,128]{0,1:T(8,128)S(1)} %maximum_select_fusion.1), channel_id=1, source_target_pairs={{0,2},{1,3},{2,0},{3,1},{4,6},{5,7},{6,4},{7,5},{8,10},{9,11},{10,... | collective-permute-start | bytes 393224 | tf_op jit(solution)/shard_map/ppermute | solution.py:86
  292.6 7.0 %copy-start.7 = (bf16[192,2048]{0,1:T(8,128)(2,1)S(1)}, bf16[192,2048]{0,1:T(8,128)(2,1)}, u32[]{:S(2)}) copy-start(bf16[192,2048]{0,1:T(8,128)(2,1)} %copy-done.6) | copy-start | bytes 2359300
  (7 other events, 33.8 us)
Sparse Core Ops, SparseCore 0:
  9.6 66.1 all-gather.1
  125.4 92.0 reduce-scatter.1

commit v8 on v7

--- a/solution.py
+++ b/solution.py
@@ -90,6 +90,18 @@
     return x
 
 
+def gather_columns(x, axis, count):
+    rows, cols = x.shape
+    me = lax.axis_index(axis)
+    out = jnp.zeros((rows, count * cols), x.dtype)
+    out = lax.dynamic_update_slice_in_dim(out, x, me * cols, 1)
+    for shift in range(1, count):
+        got = lax.ppermute(x, axis, [(k, (k + shift) % count) for k in range(count)])
+        src = (me + count - shift) % count
+        out = lax.dynamic_update_slice_in_dim(out, got, src * cols, 1)
+    return out
+
+
 def body(cotangent, out_weight, query_act, key_act, value_act, filters):
     rows, chans = cotangent.shape
     groups, flen = filters.shape
@@ -111,7 +123,7 @@
     mats_causal = toeplitz_mats(taps, block, width, halo, True, zero)
     mats_anti = toeplitz_mats(taps, block, width, halo, False, zero)
 
-    cot_rows = lax.all_gather(cotangent, "mp", axis=1, tiled=True)
+    cot_rows = gather_columns(cotangent, "mp", mp_count)
     cot_rows, mats_causal, mats_anti = lax.optimization_barrier((cot_rows, mats_causal, mats_anti))
     cot_cols = exchange_columns(cot_rows, ctx_count)
     partial = contract(cot_cols, out_weight)

time: 315 us -> 319 us (1.013)
  starting transfers between devices: 26.3 us -> 33.3 us
  waiting for transfers between devices: 134 us -> 130 us
    all_gather x1 -> x0, waiting for transfers between devices: 57.9 us -> none  [body(): cot_rows = lax.all_gather(cotangent, 'mp', axis=1, tiled=True)]
    ppermute x0 -> x3, waiting for transfers between devices: none -> 38.6 us  [gather_columns(): lax.ppermute(x, axis, [(k, (k + shift) % count) for k in range(count)])]
    reduce_scatter x1, waiting for transfers between devices: 53 us -> 69.2 us  [body(): lax.psum_scatter(partial, 'ctx', scatter_dimension=0, tiled=True)]
    ppermute x0 -> x3, starting transfers between devices: none -> 7.01 us  [gather_columns(): lax.ppermute(x, axis, [(k, (k + shift) % count) for k in range(count)])]
  transfers between devices with their start and end apart: 16 -> 18, of which waited for: 7 -> 8; matrix products, arithmetic and copies ran while one was open for 35% -> 35% of each run, Pallas kernels for 0% -> 0%
where the time goes in v8:
time: 319 us; the launch traced here: 318 us
  waiting for transfers between devices  130 us (41%)
  local copies, waits for them, and re-layouts  93.9 us (29%)
  starting transfers between devices  33.3 us (10%)
  matrix products  30.6 us (10%)
  other arithmetic  15.7 us (5%)
  between operations  14.4 us (5%)
    reduce_scatter x1, waiting for transfers between devices, body(): lax.psum_scatter(partial, 'ctx', scatter_dimension=0, tiled=True)  69.2 us
    ppermute x3, waiting for transfers between devices, gather_columns(): lax.ppermute(x, axis, [(k, (k + shift) % count) for k in range(count)])  38.6 us
    optimization_barrier x4, local copies, waits for them, and re-layouts, body(): lax.optimization_barrier((cot_rows, mats_causal, mats_anti))  28.3 us
    ppermute x7, waiting for transfers between devices, exchange_columns(): lax.ppermute(chunk, 'ctx', [(k, (k + shift) % count) for k in range(count)])  19.9 us
    ppermute x7, starting transfers between devices, exchange_columns(): lax.ppermute(chunk, 'ctx', [(k, (k + shift) % count) for k in range(count)])  13 us
    dot_general x4, matrix products, filter_apply(): jnp.einsum('gij,kjgc->kigc', m, w4, preferred_element_type=jnp.float32)  11 us
    reshape x2, local copies, waits for them, and re-layouts, filter_apply(): return total.reshape(tiles * block, chans)  10.7 us
    unnamed x35, local copies, waits for them, and re-layouts  9.24 us
  transfers between devices with their start and end apart: 18, of which 8 were waited for; matrix products, arithmetic and copies ran while one was open for 35% of the time, Pallas kernels for 0%

profile of v8, /device:TPU:0, one launch (start us, length us, event | category | flops | bytes accessed | tf_op | source)
XLA Modules:
  0.0 317.8 jit_solution(11218994256611920900)
XLA Ops:
  18.7 5.3 %fusion.20 = (bf16[128,64,192]{0,2,1:T(8,128)(2,1)}, bf16[128,64,192]{0,2,1:T(8,128)(2,1)}, bf16[128,64,192]{0,2,1:T(8,128)(2,1)}, bf16[128,64,192]{0,2,1:T(8,128)(2,1)}) fusion(bf16[256,64,192]{0,2,1:T(8,128)(2,1)S(1)} %fusion.2, bf16[256,64,192]{0,2,1:T(8,128)(2,1)S(1)} %fusion.3), kind=kLoop, calls=%fused_computation.66 | loop fusion | bytes 25165824 | tf_op jit(solution)/shard_map/slice | solution.py:30
  25.2 5.8 %collective-permute-done = bf16[192,2048]{1,0:T(8,128)(2,1)S(1)} collective-permute-done((bf16[192,2048]{1,0:T(8,128)(2,1)}, bf16[192,2048]{1,0:T(8,128)(2,1)S(1)}, u32[]{:S(2)}, u32[]{:S(2)}) %collective-permute-start) | collective-permute-done | bytes 786464 | tf_op jit(solution)/shard_map/ppermute | solution.py:99
  31.1 32.8 %collective-permute-done.1 = bf16[192,2048]{1,0:T(8,128)(2,1)S(1)} collective-permute-done((bf16[192,2048]{1,0:T(8,128)(2,1)}, bf16[192,2048]{1,0:T(8,128)(2,1)S(1)}, u32[]{:S(2)}, u32[]{:S(2)}) %collective-permute-start.1) | collective-permute-done | bytes 786464 | tf_op jit(solution)/shard_map/ppermute | solution.py:99
  70.5 7.7 %collective-permute-done.3 = bf16[192,1024]{1,0:T(8,128)(2,1)} collective-permute-done((bf16[192,1024]{1,0:T(8,128)(2,1)}, bf16[192,1024]{1,0:T(8,128)(2,1)}, u32[]{:S(2)}, u32[]{:S(2)}) %collective-permute-start.3) | collective-permute-done | bytes 393248 | tf_op jit(solution)/shard_map/ppermute | solution.py:64
  80.6 7.0 %collective-permute-start.9 = (bf16[192,1024]{1,0:T(8,128)(2,1)S(1)}, bf16[192,1024]{1,0:T(8,128)(2,1)S(1)}, u32[]{:S(2)}, u32[]{:S(2)}) collective-permute-start(bf16[192,1024]{1,0:T(8,128)(2,1)S(1)} %get-tuple-element.38), channel_id=1, source_target_pairs={{0,28},{4,0},{8,4},{12,8},{16,12},{20,16},{24,20},{28,24},{1,29},{... | collective-permute-start | bytes 1179656 | tf_op jit(solution)/shard_map/ppermute | solution.py:64
  88.7 6.7 %collective-permute-done.5 = bf16[192,1024]{1,0:T(8,128)(2,1)} collective-permute-done((bf16[192,1024]{1,0:T(8,128)(2,1)}, bf16[192,1024]{1,0:T(8,128)(2,1)}, u32[]{:S(2)}, u32[]{:S(2)}) %collective-permute-start.5) | collective-permute-done | bytes 393248 | tf_op jit(solution)/shard_map/ppermute | solution.py:64
  97.4 5.5 %collective-permute-done.7 = bf16[192,1024]{1,0:T(8,128)(2,1)S(1)} collective-permute-done((bf16[192,1024]{1,0:T(8,128)(2,1)}, bf16[192,1024]{1,0:T(8,128)(2,1)S(1)}, u32[]{:S(2)}, u32[]{:S(2)}) %collective-permute-start.7) | collective-permute-done | bytes 393248 | tf_op jit(solution)/shard_map/ppermute | solution.py:64
  103.1 9.1 %fusion.22 = f32[1536,2048]{1,0:T(8,128)} fusion(bf16[1536,1024]{1,0:T(8,128)(2,1)S(1)} %constant_dynamic-update-slice_fusion, bf16[2048,1024]{1,0:T(8,128)(2,1)S(1)} %copy-done.14), kind=kOutput, calls=%fused_computation.68 | convolution fusion | flops 6442450944 | bytes 19922944 | tf_op jit(solution)/shard_map/dot_general | solution.py:8
  116.1 3.8 %collective-permute-start.10 = (bf16[128,2048]{0,1:T(8,128)(2,1)S(1)}, bf16[128,2048]{0,1:T(8,128)(2,1)S(1)}, u32[]{:S(2)}, u32[]{:S(2)}) collective-permute-start(bf16[128,2048]{0,1:T(8,128)(2,1)S(1)} %slice.48), channel_id=1, source_target_pairs={{0,4},{4,8},{8,12},{12,16},{16,20},{20,24},{24,28},{1,5},{5,9},{9,... | collective-permute-start | bytes 1572872 | tf_op jit(solution)/shard_map/ppermute | solution.py:135
  123.3 6.7 %copy.64 = bf16[128,64,192,1]{2,1,3,0:T(8,128)(2,1)} copy(bf16[128,64,192,1]{0,2,1,3:T(8,128)(2,1)} %bitcast.49) | data formatting | bytes 6291456 | tf_op jit(solution)/shard_map/optimization_barrier | solution.py:127
  130.0 7.0 %copy.63 = bf16[128,64,192,1]{2,1,3,0:T(8,128)(2,1)} copy(bf16[128,64,192,1]{0,2,1,3:T(8,128)(2,1)} %bitcast.48) | data formatting | bytes 6291456 | tf_op jit(solution)/shard_map/optimization_barrier | solution.py:127
  137.0 4.7 %fusion.19 = f32[128,3,16,64]{3,2,1,0:T(8,128)S(1)} fusion(bf16[128,64,192,1]{2,1,3,0:T(8,128)(2,1)} %copy.64, bf16[1,192,128,16]{1,3,0,2:T(8,128)(2,1)S(1)} %bitcast.43, bf16[1,192,128,16]{1,3,0,2:T(8,128)(2,1)S(1)} %bitcast.56, bf16[1,192,128,16]{1,3,0,2:T(8,128)(2,1)S(1)} %bitcast.53), kind=kOutput, calls=%fused_computation.65 | convolution fusion | flops 153354240 | bytes 7077888 | tf_op jit(solution)/shard_map/gij,kjgc->kigc/dot_general | solution.py:48
  144.0 3.7 %copy.46 = f32[3,64,128,16]{1,0,3,2:T(4,128)} copy(f32[3,64,128,16]{1,3,0,2:T(8,128)S(1)} %add_bitcast_fusion.1) | data formatting | bytes 3145728 | tf_op jit(solution)/shard_map/add | solution.py:49
  147.7 4.8 %reshape.38 = f32[192,2048]{0,1:T(8,128)S(1)} reshape(f32[3,64,128,16]{1,0,3,2:T(4,128)} %copy.46) | data formatting | bytes 3145728 | tf_op jit(solution)/shard_map/reshape | solution.py:51
  152.5 69.2 %reduce-scatter.2.cloned.1.call-done = f32[192,2048]{1,0:T(8,128)} async-done(((f32[1536,2048]{1,0:T(8,128)}), f32[192,2048]{1,0:T(8,128)}) %reduce-scatter.2.cloned.1.call-update) | async-done | bytes 1572880 | tf_op jit(solution)/shard_map/reduce_scatter | solution.py:130
  231.2 6.8 %convolution_bitcast_fusion = f32[128,64,192]{2,1,0:T(8,128)} fusion(bf16[3,64,128,16]{1,0,3,2:T(4,128)(2,1)} %reshape.39, bf16[1,192,128,16]{1,3,0,2:T(8,128)(2,1)S(1)} %bitcast.45, bf16[1,192,128,16]{1,3,0,2:T(8,128)(2,1)} %bitcast.55, bf16[1,192,128,16]{1,3,0,2:T(8,128)(2,1)} %bitcast.52), kind=kOutput, calls=%fused_computation.7 | convolution fusion | flops 153354240 | bytes 9437184 | tf_op jit(solution)/shard_map/kigc,kjgc->gij/dot_general | solution.py:145
  238.0 8.7 %copy.50 = f32[128,64,192]{0,2,1:T(8,128)} copy(f32[128,64,192]{2,1,0:T(8,128)} %convolution_bitcast_fusion) | data formatting | bytes 12582912 | tf_op jit(solution)/shard_map/kigc,kjgc->gij/dot_general | solution.py:145
  246.7 4.8 %pad.4 = f32[128,12352]{0,1:T(8,128)} pad(f32[128,12288]{0,1:T(8,128)} %bitcast.42, f32[]{:T(128)} %constant.182.clone.1), padding=0_0x0_64 | pad | bytes 12615684 | tf_op jit(solution)/shard_map/jit(_pad)/pad | solution.py:146
  251.5 6.0 %reshape.41 = f32[128,64,193]{0,2,1:T(8,128)} reshape(f32[128,12352]{0,1:T(8,128)} %pad.4) | data formatting | bytes 12648448 | tf_op jit(solution)/shard_map/reshape | solution.py:147
  263.7 6.9 %copy.66 = bf16[128,64,192,1]{2,1,3,0:T(8,128)(2,1)} copy(bf16[128,64,192,1]{0,2,1,3:T(8,128)(2,1)} %bitcast.47) | data formatting | bytes 6291456 | tf_op jit(solution)/shard_map/optimization_barrier | solution.py:127
  270.6 7.6 %copy.67 = bf16[128,64,192,1]{2,1,3,0:T(8,128)(2,1)} copy(bf16[128,64,192,1]{0,2,1,3:T(8,128)(2,1)S(1)} %bitcast.46) | data formatting | bytes 6291456 | tf_op jit(solution)/shard_map/optimization_barrier | solution.py:127
  285.6 3.5 %fusion.11 = f32[128,3,16,64]{3,2,1,0:T(8,128)S(1)} fusion(bf16[128,64,192,1]{2,1,3,0:T(8,128)(2,1)} %copy.66, bf16[1,192,128,16]{1,3,0,2:T(8,128)(2,1)S(1)} %bitcast.58, bf16[1,192,128,16]{1,3,0,2:T(8,128)(2,1)S(1)} %bitcast.60, bf16[1,192,128,16]{1,3,0,2:T(8,128)(2,1)S(1)} %bitcast.50), kind=kOutput, calls=%fused_computation.28 | convolution fusion | flops 153354240 | bytes 7077888 | tf_op jit(solution)/shard_map/gij,kjgc->kigc/dot_general | solution.py:48
  293.1 3.7 %copy.59 = f32[3,64,128,16]{1,0,3,2:T(4,128)} copy(f32[3,64,128,16]{1,3,0,2:T(8,128)S(1)} %add_bitcast_fusion) | data formatting | bytes 3145728 | tf_op jit(solution)/shard_map/add | solution.py:49
  296.8 6.0 %reshape.42 = f32[192,2048]{0,1:T(8,128)} reshape(f32[3,64,128,16]{1,0,3,2:T(4,128)} %copy.59) | data formatting | bytes 3145728 | tf_op jit(solution)/shard_map/reshape | solution.py:51
  (104 shorter events, 69.6 us)
Async XLA Ops:
  7.2 214.5 %reduce-scatter.2.cloned.1.call-start = ((), (), s32[]{:S(2)}) async-start(), calls=%async_computation.1 | async-start | bytes 14155776 | tf_op jit(solution)/shard_map/reduce_scatter | solution.py:130
  7.2 23.8 %collective-permute-start = (bf16[192,2048]{1,0:T(8,128)(2,1)}, bf16[192,2048]{1,0:T(8,128)(2,1)S(1)}, u32[]{:S(2)}, u32[]{:S(2)}) collective-permute-start(bf16[192,2048]{1,0:T(8,128)(2,1)} %param.6), channel_id=1, source_target_pairs={{0,1},{1,2},{2,3},{3,0},{4,5},{5,6},{6,7},{7,4},{8,9},{9,10},{10,1... | collective-permute-start | bytes 2359304 | tf_op jit(solution)/shard_map/ppermute | solution.py:99
  10.3 53.6 %collective-permute-start.1 = (bf16[192,2048]{1,0:T(8,128)(2,1)}, bf16[192,2048]{1,0:T(8,128)(2,1)S(1)}, u32[]{:S(2)}, u32[]{:S(2)}) collective-permute-start(bf16[192,2048]{1,0:T(8,128)(2,1)} %param.6), channel_id=1, source_target_pairs={{0,2},{1,3},{2,0},{3,1},{4,6},{5,7},{6,4},{7,5},{8,10},{9,11},{10,... | collective-permute-start | bytes 2359304 | tf_op jit(solution)/shard_map/ppermute | solution.py:99
  12.9 51.1 %collective-permute-start.2 = (bf16[192,2048]{1,0:T(8,128)(2,1)}, bf16[192,2048]{1,0:T(8,128)(2,1)S(1)}, u32[]{:S(2)}, u32[]{:S(2)}) collective-permute-start(bf16[192,2048]{1,0:T(8,128)(2,1)} %param.6), channel_id=1, source_target_pairs={{0,3},{1,0},{2,1},{3,2},{4,7},{5,4},{6,5},{7,6},{8,11},{9,8},{10,9... | collective-permute-start | bytes 2359304 | tf_op jit(solution)/shard_map/ppermute | solution.py:99
  66.0 12.2 %collective-permute-start.3 = (bf16[192,1024]{1,0:T(8,128)(2,1)}, bf16[192,1024]{1,0:T(8,128)(2,1)}, u32[]{:S(2)}, u32[]{:S(2)}) collective-permute-start(bf16[192,1024]{1,0:T(8,128)(2,1)} %get-tuple-element.44), channel_id=1, source_target_pairs={{0,4},{4,8},{8,12},{12,16},{16,20},{20,24},{24,28},{28,0},{1,5},{5... | collective-permute-start | bytes 1179656 | tf_op jit(solution)/shard_map/ppermute | solution.py:64
  66.0 14.6 %collective-permute-start.4 = (bf16[192,1024]{1,0:T(8,128)(2,1)}, bf16[192,1024]{1,0:T(8,128)(2,1)}, u32[]{:S(2)}, u32[]{:S(2)}) collective-permute-start(bf16[192,1024]{1,0:T(8,128)(2,1)} %get-tuple-element.43), channel_id=1, source_target_pairs={{0,8},{4,12},{8,16},{12,20},{16,24},{20,28},{24,0},{28,4},{1,9},{5... | collective-permute-start | bytes 1179656 | tf_op jit(solution)/shard_map/ppermute | solution.py:64
  67.5 27.9 %collective-permute-start.5 = (bf16[192,1024]{1,0:T(8,128)(2,1)}, bf16[192,1024]{1,0:T(8,128)(2,1)}, u32[]{:S(2)}, u32[]{:S(2)}) collective-permute-start(bf16[192,1024]{1,0:T(8,128)(2,1)} %get-tuple-element.42), channel_id=1, source_target_pairs={{0,12},{4,16},{8,20},{12,24},{16,28},{20,0},{24,4},{28,8},{1,13},{... | collective-permute-start | bytes 1179656 | tf_op jit(solution)/shard_map/ppermute | solution.py:64
  69.9 26.5 %collective-permute-start.6 = (bf16[192,1024]{1,0:T(8,128)(2,1)}, bf16[192,1024]{1,0:T(8,128)(2,1)}, u32[]{:S(2)}, u32[]{:S(2)}) collective-permute-start(bf16[192,1024]{1,0:T(8,128)(2,1)} %get-tuple-element.41), channel_id=1, source_target_pairs={{0,16},{4,20},{8,24},{12,28},{16,0},{20,4},{24,8},{28,12},{1,17},{... | collective-permute-start | bytes 1179656 | tf_op jit(solution)/shard_map/ppermute | solution.py:64
  70.4 32.7 %copy-start.14 = (bf16[2048,1024]{1,0:T(8,128)(2,1)S(1)}, bf16[2048,1024]{1,0:T(8,128)(2,1)}, u32[]{:S(2)}) copy-start(bf16[2048,1024]{1,0:T(8,128)(2,1)} %param.7) | copy-start | bytes 12582916
  70.4 32.5 %collective-permute-start.7 = (bf16[192,1024]{1,0:T(8,128)(2,1)}, bf16[192,1024]{1,0:T(8,128)(2,1)S(1)}, u32[]{:S(2)}, u32[]{:S(2)}) collective-permute-start(bf16[192,1024]{1,0:T(8,128)(2,1)} %get-tuple-element.40), channel_id=1, source_target_pairs={{0,20},{4,24},{8,28},{12,0},{16,4},{20,8},{24,12},{28,16},{1,21},{... | collective-permute-start | bytes 1179656 | tf_op jit(solution)/shard_map/ppermute | solution.py:64
  78.1 24.8 %collective-permute-start.8 = (bf16[192,1024]{1,0:T(8,128)(2,1)}, bf16[192,1024]{1,0:T(8,128)(2,1)S(1)}, u32[]{:S(2)}, u32[]{:S(2)}) collective-permute-start(bf16[192,1024]{1,0:T(8,128)(2,1)} %get-tuple-element.39), channel_id=1, source_target_pairs={{0,24},{4,28},{8,0},{12,4},{16,8},{20,12},{24,16},{28,20},{1,25},{... | collective-permute-start | bytes 1179656 | tf_op jit(solution)/shard_map/ppermute | solution.py:64
  80.6 22.4 %collective-permute-start.9 = (bf16[192,1024]{1,0:T(8,128)(2,1)S(1)}, bf16[192,1024]{1,0:T(8,128)(2,1)S(1)}, u32[]{:S(2)}, u32[]{:S(2)}) collective-permute-start(bf16[192,1024]{1,0:T(8,128)(2,1)S(1)} %get-tuple-element.38), channel_id=1, source_target_pairs={{0,28},{4,0},{8,4},{12,8},{16,12},{20,16},{24,20},{28,24},{1,29},{... | collective-permute-start | bytes 1179656 | tf_op jit(solution)/shard_map/ppermute | solution.py:64
  113.9 9.4 %copy-start.4 = (bf16[192,2048]{0,1:T(8,128)(2,1)}, bf16[192,2048]{0,1:T(8,128)(2,1)S(1)}, u32[]{:S(2)}) copy-start(bf16[192,2048]{0,1:T(8,128)(2,1)S(1)} %copy.43) | copy-start | bytes 2359300
  115.6 7.7 %copy-start.6 = (bf16[192,2048]{0,1:T(8,128)(2,1)}, bf16[192,2048]{0,1:T(8,128)(2,1)S(1)}, u32[]{:S(2)}) copy-start(bf16[192,2048]{0,1:T(8,128)(2,1)S(1)} %copy.42) | copy-start | bytes 2359300
  116.1 5.2 %collective-permute-start.10 = (bf16[128,2048]{0,1:T(8,128)(2,1)S(1)}, bf16[128,2048]{0,1:T(8,128)(2,1)S(1)}, u32[]{:S(2)}, u32[]{:S(2)}) collective-permute-start(bf16[128,2048]{0,1:T(8,128)(2,1)S(1)} %slice.48), channel_id=1, source_target_pairs={{0,4},{4,8},{8,12},{12,16},{16,20},{20,24},{24,28},{1,5},{5,9},{9,... | collective-permute-start | bytes 1572872 | tf_op jit(solution)/shard_map/ppermute | solution.py:135
  226.8 11.1 %copy-start.3 = (bf16[192,2048]{1,0:T(8,128)(2,1)}, bf16[192,2048]{1,0:T(8,128)(2,1)S(1)}, u32[]{:S(2)}) copy-start(bf16[192,2048]{1,0:T(8,128)(2,1)S(1)} %get-tuple-element.48) | copy-start | bytes 2359300
  227.3 10.6 %copy-start.8 = (bf16[192,2048]{0,1:T(8,128)(2,1)}, bf16[192,2048]{0,1:T(8,128)(2,1)S(1)}, u32[]{:S(2)}) copy-start(bf16[192,2048]{0,1:T(8,128)(2,1)S(1)} %copy.48) | copy-start | bytes 2359300
  229.7 30.5 %collective-permute-start.11 = (bf16[128,2048]{1,0:T(8,128)(2,1)S(1)}, bf16[128,2048]{1,0:T(8,128)(2,1)}, u32[]{:S(2)}, u32[]{:S(2)}) collective-permute-start(bf16[128,2048]{1,0:T(8,128)(2,1)S(1)} %slice.52), channel_id=1, source_target_pairs={{4,0},{8,4},{12,8},{16,12},{20,16},{24,20},{28,24},{5,1},{9,5},{13... | collective-permute-start | bytes 1572872 | tf_op jit(solution)/shard_map/ppermute | solution.py:142
  260.2 2.1 collective-permute-start.12
  262.3 16.0 %collective-permute-start.13 = (f32[128,128]{0,1:T(8,128)S(1)}, f32[128,128]{0,1:T(8,128)S(1)}, u32[]{:S(2)}, u32[]{:S(2)}) collective-permute-start(f32[128,128]{0,1:T(8,128)S(1)} %add.249), channel_id=1, source_target_pairs={{0,8},{4,12},{8,0},{12,4},{16,24},{20,28},{24,16},{28,20},{1,9},{5... | collective-permute-start | bytes 196616 | tf_op jit(solution)/shard_map/ppermute | solution.py:75
  278.3 7.3 %copy-start.9 = (bf16[192,2048]{0,1:T(8,128)(2,1)S(1)}, bf16[192,2048]{0,1:T(8,128)(2,1)}, u32[]{:S(2)}) copy-start(bf16[192,2048]{0,1:T(8,128)(2,1)} %copy-done.8) | copy-start | bytes 2359300
  278.3 5.7 %collective-permute-start.14 = (f32[128,128]{0,1:T(8,128)S(1)}, f32[128,128]{0,1:T(8,128)S(1)}, u32[]{:S(2)}, u32[]{:S(2)}) collective-permute-start(f32[128,128]{0,1:T(8,128)S(1)} %add.250), channel_id=1, source_target_pairs={{0,16},{4,20},{8,24},{12,28},{16,0},{20,4},{24,8},{28,12},{1,17},{... | collective-permute-start | bytes 196616 | tf_op jit(solution)/shard_map/ppermute | solution.py:75
  284.0 5.1 %collective-permute-start.15 = (f32[128,128]{0,1:T(8,128)S(1)}, f32[128,128]{0,1:T(8,128)S(1)}, u32[]{:S(2)}, u32[]{:S(2)}) collective-permute-start(f32[128,128]{0,1:T(8,128)S(1)} %add_multiply_fusion), channel_id=1, source_target_pairs={{0,1},{1,0},{2,3},{3,2},{4,5},{5,4},{6,7},{7,6},{8,9},{9,8},{10,11... | collective-permute-start | bytes 196616 | tf_op jit(solution)/shard_map/ppermute | solution.py:86
  289.2 13.6 %collective-permute-start.16 = (f32[256,128]{0,1:T(8,128)S(1)}, f32[256,128]{0,1:T(8,128)}, u32[]{:S(2)}, u32[]{:S(2)}) collective-permute-start(f32[256,128]{0,1:T(8,128)S(1)} %maximum_select_fusion.1), channel_id=1, source_target_pairs={{0,2},{1,3},{2,0},{3,1},{4,6},{5,7},{6,4},{7,5},{8,10},{9,11},{10,... | collective-permute-start | bytes 393224 | tf_op jit(solution)/shard_map/ppermute | solution.py:86
  (9 other events, 48.8 us)
Sparse Core Ops, SparseCore 0:
  112.4 109.2 reduce-scatter.1

commit v9 on v7

--- a/solution.py
+++ b/solution.py
@@ -90,6 +90,20 @@
     return x
 
 
+def pair_scatter(partial, count):
+    rows = partial.shape[0] // count
+    if count % 2:
+        return lax.psum_scatter(partial, "ctx", scatter_dimension=0, tiled=True)
+    me = lax.axis_index("ctx")
+    blocks = partial.reshape(count // 2, 2, rows, partial.shape[1])
+    keep = lax.dynamic_index_in_dim(blocks, me % 2, 1, keepdims=False)
+    give = lax.dynamic_index_in_dim(blocks, 1 - me % 2, 1, keepdims=False)
+    got = lax.ppermute(give, "ctx", [(k, k ^ 1) for k in range(count)])
+    summed = (keep + got).reshape(count // 2 * rows, partial.shape[1])
+    groups = [[p + 2 * q for q in range(count // 2)] for p in range(2)]
+    return lax.psum_scatter(summed, "ctx", scatter_dimension=0, tiled=True, axis_index_groups=groups)
+
+
 def body(cotangent, out_weight, query_act, key_act, value_act, filters):
     rows, chans = cotangent.shape
     groups, flen = filters.shape
@@ -115,7 +129,7 @@
     cot_rows, mats_causal, mats_anti = lax.optimization_barrier((cot_rows, mats_causal, mats_anti))
     cot_cols = exchange_columns(cot_rows, ctx_count)
     partial = contract(cot_cols, out_weight)
-    grad_mixed = lax.psum_scatter(partial, "ctx", scatter_dimension=0, tiled=True)
+    grad_mixed = pair_scatter(partial, ctx_count)
 
     fwd = [(k, k + 1) for k in range(ctx_count - 1)]
     bwd = [(k + 1, k) for k in range(ctx_count - 1)]

time: 315 us -> 321 us (1.019)
  other arithmetic: 15.7 us -> 24.8 us
  waiting for transfers between devices: 134 us -> 127 us
  local copies, waits for them, and re-layouts: 93.8 us -> 99.7 us
    reduce_scatter x1, waiting for transfers between devices: 53 us -> 36.5 us  [pair_scatter(): lax.psum_scatter(summed, 'ctx', scatter_dimension=0, tiled=True, axis_ind...]
    ppermute x0 -> x1, waiting for transfers between devices: none -> 10.1 us  [pair_scatter(): got = lax.ppermute(give, 'ctx', [(k, k ^ 1) for k in range(count)])]
    add x0 -> x1, other arithmetic: none -> 9.12 us  [pair_scatter(): summed = (keep + got).reshape(count // 2 * rows, partial.shape[1])]
    squeeze x0 -> x1, local copies, waits for them, and re-layouts: none -> 3.83 us  [pair_scatter(): give = lax.dynamic_index_in_dim(blocks, 1 - me % 2, 1, keepdims=False)]
    unnamed x35 -> x37, local copies, waits for them, and re-layouts: 9.37 us -> 11.9 us
  transfers between devices with their start and end apart: 16 -> 17, of which waited for: 7 -> 8; matrix products, arithmetic and copies ran while one was open for 35% -> 34% of each run, Pallas kernels for 0% -> 0%
where the time goes in v9:
time: 321 us; the launch traced here: 320 us
  waiting for transfers between devices  127 us (40%)
  local copies, waits for them, and re-layouts  99.7 us (31%)
  matrix products  27 us (8%)
  starting transfers between devices  26.7 us (8%)
  other arithmetic  24.8 us (8%)
  between operations  14.5 us (5%)
    all_gather x1, waiting for transfers between devices, body(): cot_rows = lax.all_gather(cotangent, 'mp', axis=1, tiled=True)  57.9 us
    reduce_scatter x1, waiting for transfers between devices, pair_scatter(): lax.psum_scatter(summed, 'ctx', scatter_dimension=0, tiled=True, axis_ind...  36.5 us
    optimization_barrier x4, local copies, waits for them, and re-layouts, body(): lax.optimization_barrier((cot_rows, mats_causal, mats_anti))  28.3 us
    ppermute x7, waiting for transfers between devices, exchange_columns(): lax.ppermute(chunk, 'ctx', [(k, (k + shift) % count) for k in range(count)])  19.9 us
    ppermute x7, starting transfers between devices, exchange_columns(): lax.ppermute(chunk, 'ctx', [(k, (k + shift) % count) for k in range(count)])  12.8 us
    unnamed x37, local copies, waits for them, and re-layouts  11.9 us
    reshape x2, local copies, waits for them, and re-layouts, filter_apply(): return total.reshape(tiles * block, chans)  10.7 us
    ppermute x1, waiting for transfers between devices, pair_scatter(): got = lax.ppermute(give, 'ctx', [(k, k ^ 1) for k in range(count)])  10.1 us
  transfers between devices with their start and end apart: 17, of which 8 were waited for; matrix products, arithmetic and copies ran while one was open for 34% of the time, Pallas kernels for 0%

profile of v9, /device:TPU:0, one launch (start us, length us, event | category | flops | bytes accessed | tf_op | source)
XLA Modules:
  0.0 320.2 jit_solution(18349297579760651938)
XLA Ops:
  12.6 5.3 %fusion.20 = (bf16[128,64,192]{0,2,1:T(8,128)(2,1)}, bf16[128,64,192]{0,2,1:T(8,128)(2,1)}, bf16[128,64,192]{0,2,1:T(8,128)(2,1)}, bf16[128,64,192]{0,2,1:T(8,128)(2,1)}) fusion(bf16[256,64,192]{0,2,1:T(8,128)(2,1)S(1)} %fusion.2, bf16[256,64,192]{0,2,1:T(8,128)(2,1)S(1)} %fusion.3), kind=kLoop, calls=%fused_computation.64 | loop fusion | bytes 25165824 | tf_op jit(solution)/shard_map/slice | solution.py:30
  17.9 57.9 %all-gather.2.cloned.1.call-done = bf16[192,8192]{1,0:T(8,128)(2,1)} async-done(((bf16[192,2048]{1,0:T(8,128)(2,1)}), bf16[192,8192]{1,0:T(8,128)(2,1)}) %all-gather.2.cloned.1.call-update) | async-done | bytes 3145744 | tf_op jit(solution)/shard_map/all_gather | solution.py:128
  83.6 7.7 %collective-permute-done = bf16[192,1024]{1,0:T(8,128)(2,1)} collective-permute-done((bf16[192,1024]{1,0:T(8,128)(2,1)}, bf16[192,1024]{1,0:T(8,128)(2,1)}, u32[]{:S(2)}, u32[]{:S(2)}) %collective-permute-start) | collective-permute-done | bytes 393248 | tf_op jit(solution)/shard_map/ppermute | solution.py:64
  93.7 7.0 %collective-permute-start.6 = (bf16[192,1024]{1,0:T(8,128)(2,1)S(1)}, bf16[192,1024]{1,0:T(8,128)(2,1)S(1)}, u32[]{:S(2)}, u32[]{:S(2)}) collective-permute-start(bf16[192,1024]{1,0:T(8,128)(2,1)S(1)} %get-tuple-element.42), channel_id=1, source_target_pairs={{0,28},{4,0},{8,4},{12,8},{16,12},{20,16},{24,20},{28,24},{1,29},{... | collective-permute-start | bytes 1179656 | tf_op jit(solution)/shard_map/ppermute | solution.py:64
  101.7 6.8 %collective-permute-done.2 = bf16[192,1024]{1,0:T(8,128)(2,1)} collective-permute-done((bf16[192,1024]{1,0:T(8,128)(2,1)}, bf16[192,1024]{1,0:T(8,128)(2,1)}, u32[]{:S(2)}, u32[]{:S(2)}) %collective-permute-start.2) | collective-permute-done | bytes 393248 | tf_op jit(solution)/shard_map/ppermute | solution.py:64
  110.6 5.4 %collective-permute-done.4 = bf16[192,1024]{1,0:T(8,128)(2,1)S(1)} collective-permute-done((bf16[192,1024]{1,0:T(8,128)(2,1)}, bf16[192,1024]{1,0:T(8,128)(2,1)S(1)}, u32[]{:S(2)}, u32[]{:S(2)}) %collective-permute-start.4) | collective-permute-done | bytes 393248 | tf_op jit(solution)/shard_map/ppermute | solution.py:64
  116.2 6.7 %fusion.22 = f32[1536,2048]{1,0:T(8,128)S(1)} fusion(bf16[1536,1024]{1,0:T(8,128)(2,1)S(1)} %constant_dynamic-update-slice_fusion, bf16[2048,1024]{1,0:T(8,128)(2,1)S(1)} %copy-done.15), kind=kOutput, calls=%fused_computation.66 | convolution fusion | flops 6442450944 | bytes 19922944 | tf_op jit(solution)/shard_map/dot_general | solution.py:8
  122.9 3.8 %dynamic-slice_bitcast_fusion = f32[4,192,2048]{2,1,0:T(8,128)} fusion(f32[4,2,192,2048]{3,2,1,0:T(8,128)S(1)} %bitcast.55, s32[]{:T(128)S(6)} %select_n.168), kind=kLoop, calls=%fused_computation.1 | loop fusion | bytes 12582916 | tf_op jit(solution)/shard_map/jit(dynamic_index_in_dim)/squeeze | solution.py:100
  131.1 10.1 %collective-permute-done.7 = f32[4,192,2048]{2,1,0:T(8,128)} collective-permute-done((f32[4,192,2048]{2,1,0:T(8,128)}, f32[4,192,2048]{2,1,0:T(8,128)}, u32[]{:S(2)}, u32[]{:S(2)}) %collective-permute-start.7) | collective-permute-done | bytes 6291488 | tf_op jit(solution)/shard_map/ppermute | solution.py:101
  141.2 9.1 %bitcast_add_fusion = f32[4,192,2048]{2,1,0:T(8,128)} fusion(f32[4,192,2048]{2,1,0:T(8,128)} %collective-permute-done.7, f32[4,2,192,2048]{3,2,1,0:T(8,128)} %bitcast.56, s32[]{:T(128)S(6)} %select_n.167), kind=kLoop, calls=%fused_computation | loop fusion | flops 1572864 | bytes 18874372 | tf_op jit(solution)/shard_map/add | solution.py:102
  160.1 6.8 %copy.75 = bf16[128,64,192,1]{2,1,3,0:T(8,128)(2,1)} copy(bf16[128,64,192,1]{0,2,1,3:T(8,128)(2,1)} %bitcast.54) | data formatting | bytes 6291456 | tf_op jit(solution)/shard_map/optimization_barrier | solution.py:129
  166.9 7.0 %copy.74 = bf16[128,64,192,1]{2,1,3,0:T(8,128)(2,1)} copy(bf16[128,64,192,1]{0,2,1,3:T(8,128)(2,1)} %bitcast.53) | data formatting | bytes 6291456 | tf_op jit(solution)/shard_map/optimization_barrier | solution.py:129
  173.9 3.6 %fusion.19 = f32[128,3,16,64]{3,2,1,0:T(8,128)S(1)} fusion(bf16[128,64,192,1]{2,1,3,0:T(8,128)(2,1)} %copy.75, bf16[1,192,128,16]{1,3,0,2:T(8,128)(2,1)S(1)} %bitcast.48, bf16[1,192,128,16]{1,3,0,2:T(8,128)(2,1)S(1)} %bitcast.63, bf16[1,192,128,16]{1,3,0,2:T(8,128)(2,1)S(1)} %bitcast.60), kind=kOutput, calls=%fused_computation.63 | convolution fusion | flops 153354240 | bytes 7077888 | tf_op jit(solution)/shard_map/gij,kjgc->kigc/dot_general | solution.py:48
  179.1 3.7 %copy.60 = f32[3,64,128,16]{1,0,3,2:T(4,128)} copy(f32[3,64,128,16]{1,3,0,2:T(8,128)S(1)} %add_bitcast_fusion.1) | data formatting | bytes 3145728 | tf_op jit(solution)/shard_map/add | solution.py:49
  182.9 4.7 %reshape.46 = f32[192,2048]{0,1:T(8,128)S(1)} reshape(f32[3,64,128,16]{1,0,3,2:T(4,128)} %copy.60) | data formatting | bytes 3145728 | tf_op jit(solution)/shard_map/reshape | solution.py:51
  187.6 36.5 %reduce-scatter.2.cloned.1.call-done = f32[192,2048]{1,0:T(8,128)} async-done(((f32[768,2048]{1,0:T(8,128)}), f32[192,2048]{1,0:T(8,128)}) %reduce-scatter.2.cloned.1.call-update) | async-done | bytes 1572880 | tf_op jit(solution)/shard_map/reduce_scatter | solution.py:104
  233.6 6.8 %convolution_bitcast_fusion = f32[128,64,192]{2,1,0:T(8,128)} fusion(bf16[3,64,128,16]{1,0,3,2:T(4,128)(2,1)} %reshape.47, bf16[1,192,128,16]{1,3,0,2:T(8,128)(2,1)S(1)} %bitcast.50, bf16[1,192,128,16]{1,3,0,2:T(8,128)(2,1)} %bitcast.62, bf16[1,192,128,16]{1,3,0,2:T(8,128)(2,1)} %bitcast.59), kind=kOutput, calls=%fused_computation.9 | convolution fusion | flops 153354240 | bytes 9437184 | tf_op jit(solution)/shard_map/kigc,kjgc->gij/dot_general | solution.py:147
  240.4 8.6 %copy.64 = f32[128,64,192]{0,2,1:T(8,128)} copy(f32[128,64,192]{2,1,0:T(8,128)} %convolution_bitcast_fusion) | data formatting | bytes 12582912 | tf_op jit(solution)/shard_map/kigc,kjgc->gij/dot_general | solution.py:147
  249.0 4.8 %pad.4 = f32[128,12352]{0,1:T(8,128)} pad(f32[128,12288]{0,1:T(8,128)} %bitcast.46, f32[]{:T(128)} %constant.171.clone.1), padding=0_0x0_64 | pad | bytes 12615684 | tf_op jit(solution)/shard_map/jit(_pad)/pad | solution.py:148
  253.8 6.0 %reshape.49 = f32[128,64,193]{0,2,1:T(8,128)} reshape(f32[128,12352]{0,1:T(8,128)} %pad.4) | data formatting | bytes 12648448 | tf_op jit(solution)/shard_map/reshape | solution.py:149
  266.1 6.9 %copy.77 = bf16[128,64,192,1]{2,1,3,0:T(8,128)(2,1)} copy(bf16[128,64,192,1]{0,2,1,3:T(8,128)(2,1)} %bitcast.52) | data formatting | bytes 6291456 | tf_op jit(solution)/shard_map/optimization_barrier | solution.py:129
  273.0 7.6 %copy.78 = bf16[128,64,192,1]{2,1,3,0:T(8,128)(2,1)} copy(bf16[128,64,192,1]{0,2,1,3:T(8,128)(2,1)S(1)} %bitcast.51) | data formatting | bytes 6291456 | tf_op jit(solution)/shard_map/optimization_barrier | solution.py:129
  295.4 3.7 %copy.70 = f32[3,64,128,16]{1,0,3,2:T(4,128)} copy(f32[3,64,128,16]{1,3,0,2:T(8,128)S(1)} %add_bitcast_fusion) | data formatting | bytes 3145728 | tf_op jit(solution)/shard_map/add | solution.py:49
  299.1 6.0 %reshape.50 = f32[192,2048]{0,1:T(8,128)} reshape(f32[3,64,128,16]{1,0,3,2:T(4,128)} %copy.70) | data formatting | bytes 3145728 | tf_op jit(solution)/shard_map/reshape | solution.py:51
  (102 shorter events, 73.0 us)
Async XLA Ops:
  7.2 68.6 %all-gather.2.cloned.1.call-start = ((), (), s32[]{:S(2)}) async-start(), calls=%async_computation.1 | async-start | bytes 3932160 | tf_op jit(solution)/shard_map/all_gather | solution.py:128
  7.9 216.2 %reduce-scatter.2.cloned.1.call-start = ((), (), s32[]{:S(2)}) async-start(), calls=%async_computation.2 | async-start | bytes 7864320 | tf_op jit(solution)/shard_map/reduce_scatter | solution.py:104
  79.1 12.2 %collective-permute-start = (bf16[192,1024]{1,0:T(8,128)(2,1)}, bf16[192,1024]{1,0:T(8,128)(2,1)}, u32[]{:S(2)}, u32[]{:S(2)}) collective-permute-start(bf16[192,1024]{1,0:T(8,128)(2,1)} %get-tuple-element.48), channel_id=1, source_target_pairs={{0,4},{4,8},{8,12},{12,16},{16,20},{20,24},{24,28},{28,0},{1,5},{5... | collective-permute-start | bytes 1179656 | tf_op jit(solution)/shard_map/ppermute | solution.py:64
  79.1 14.6 %collective-permute-start.1 = (bf16[192,1024]{1,0:T(8,128)(2,1)}, bf16[192,1024]{1,0:T(8,128)(2,1)}, u32[]{:S(2)}, u32[]{:S(2)}) collective-permute-start(bf16[192,1024]{1,0:T(8,128)(2,1)} %get-tuple-element.47), channel_id=1, source_target_pairs={{0,8},{4,12},{8,16},{12,20},{16,24},{20,28},{24,0},{28,4},{1,9},{5... | collective-permute-start | bytes 1179656 | tf_op jit(solution)/shard_map/ppermute | solution.py:64
  80.6 27.9 %collective-permute-start.2 = (bf16[192,1024]{1,0:T(8,128)(2,1)}, bf16[192,1024]{1,0:T(8,128)(2,1)}, u32[]{:S(2)}, u32[]{:S(2)}) collective-permute-start(bf16[192,1024]{1,0:T(8,128)(2,1)} %get-tuple-element.46), channel_id=1, source_target_pairs={{0,12},{4,16},{8,20},{12,24},{16,28},{20,0},{24,4},{28,8},{1,13},{... | collective-permute-start | bytes 1179656 | tf_op jit(solution)/shard_map/ppermute | solution.py:64
  83.0 26.6 %collective-permute-start.3 = (bf16[192,1024]{1,0:T(8,128)(2,1)}, bf16[192,1024]{1,0:T(8,128)(2,1)}, u32[]{:S(2)}, u32[]{:S(2)}) collective-permute-start(bf16[192,1024]{1,0:T(8,128)(2,1)} %get-tuple-element.45), channel_id=1, source_target_pairs={{0,16},{4,20},{8,24},{12,28},{16,0},{20,4},{24,8},{28,12},{1,17},{... | collective-permute-start | bytes 1179656 | tf_op jit(solution)/shard_map/ppermute | solution.py:64
  83.5 32.7 %copy-start.15 = (bf16[2048,1024]{1,0:T(8,128)(2,1)S(1)}, bf16[2048,1024]{1,0:T(8,128)(2,1)}, u32[]{:S(2)}) copy-start(bf16[2048,1024]{1,0:T(8,128)(2,1)} %param.7) | copy-start | bytes 12582916
  83.5 32.5 %collective-permute-start.4 = (bf16[192,1024]{1,0:T(8,128)(2,1)}, bf16[192,1024]{1,0:T(8,128)(2,1)S(1)}, u32[]{:S(2)}, u32[]{:S(2)}) collective-permute-start(bf16[192,1024]{1,0:T(8,128)(2,1)} %get-tuple-element.44), channel_id=1, source_target_pairs={{0,20},{4,24},{8,28},{12,0},{16,4},{20,8},{24,12},{28,16},{1,21},{... | collective-permute-start | bytes 1179656 | tf_op jit(solution)/shard_map/ppermute | solution.py:64
  91.3 24.8 %collective-permute-start.5 = (bf16[192,1024]{1,0:T(8,128)(2,1)}, bf16[192,1024]{1,0:T(8,128)(2,1)S(1)}, u32[]{:S(2)}, u32[]{:S(2)}) collective-permute-start(bf16[192,1024]{1,0:T(8,128)(2,1)} %get-tuple-element.43), channel_id=1, source_target_pairs={{0,24},{4,28},{8,0},{12,4},{16,8},{20,12},{24,16},{28,20},{1,25},{... | collective-permute-start | bytes 1179656 | tf_op jit(solution)/shard_map/ppermute | solution.py:64
  93.7 22.4 %collective-permute-start.6 = (bf16[192,1024]{1,0:T(8,128)(2,1)S(1)}, bf16[192,1024]{1,0:T(8,128)(2,1)S(1)}, u32[]{:S(2)}, u32[]{:S(2)}) collective-permute-start(bf16[192,1024]{1,0:T(8,128)(2,1)S(1)} %get-tuple-element.42), channel_id=1, source_target_pairs={{0,28},{4,0},{8,4},{12,8},{16,12},{20,16},{24,20},{28,24},{1,29},{... | collective-permute-start | bytes 1179656 | tf_op jit(solution)/shard_map/ppermute | solution.py:64
  129.3 11.9 %collective-permute-start.7 = (f32[4,192,2048]{2,1,0:T(8,128)}, f32[4,192,2048]{2,1,0:T(8,128)}, u32[]{:S(2)}, u32[]{:S(2)}) collective-permute-start(f32[4,192,2048]{2,1,0:T(8,128)} %dynamic-slice_bitcast_fusion), channel_id=1, source_target_pairs={{0,4},{4,0},{8,12},{12,8},{16,20},{20,16},{24,28},{28,24},{1,5},{5... | collective-permute-start | bytes 18874376 | tf_op jit(solution)/shard_map/ppermute | solution.py:101
  152.0 8.1 %copy-start.5 = (bf16[192,2048]{0,1:T(8,128)(2,1)}, bf16[192,2048]{0,1:T(8,128)(2,1)S(1)}, u32[]{:S(2)}) copy-start(bf16[192,2048]{0,1:T(8,128)(2,1)S(1)} %copy.57) | copy-start | bytes 2359300
  154.2 3.8 %collective-permute-start.8 = (bf16[128,2048]{0,1:T(8,128)(2,1)S(1)}, bf16[128,2048]{0,1:T(8,128)(2,1)S(1)}, u32[]{:S(2)}, u32[]{:S(2)}) collective-permute-start(bf16[128,2048]{0,1:T(8,128)(2,1)S(1)} %slice.48), channel_id=1, source_target_pairs={{0,4},{4,8},{8,12},{12,16},{16,20},{20,24},{24,28},{1,5},{5,9},{9,... | collective-permute-start | bytes 1572872 | tf_op jit(solution)/shard_map/ppermute | solution.py:137
  229.2 11.2 %copy-start.4 = (bf16[192,2048]{1,0:T(8,128)(2,1)}, bf16[192,2048]{1,0:T(8,128)(2,1)S(1)}, u32[]{:S(2)}) copy-start(bf16[192,2048]{1,0:T(8,128)(2,1)S(1)} %get-tuple-element.52) | copy-start | bytes 2359300
  229.7 10.7 %copy-start.9 = (bf16[192,2048]{0,1:T(8,128)(2,1)}, bf16[192,2048]{0,1:T(8,128)(2,1)S(1)}, u32[]{:S(2)}) copy-start(bf16[192,2048]{0,1:T(8,128)(2,1)S(1)} %copy.62) | copy-start | bytes 2359300
  232.1 30.5 %collective-permute-start.9 = (bf16[128,2048]{1,0:T(8,128)(2,1)S(1)}, bf16[128,2048]{1,0:T(8,128)(2,1)}, u32[]{:S(2)}, u32[]{:S(2)}) collective-permute-start(bf16[128,2048]{1,0:T(8,128)(2,1)S(1)} %slice.52), channel_id=1, source_target_pairs={{4,0},{8,4},{12,8},{16,12},{20,16},{24,20},{28,24},{5,1},{9,5},{13... | collective-permute-start | bytes 1572872 | tf_op jit(solution)/shard_map/ppermute | solution.py:144
  262.6 2.1 collective-permute-start.10
  264.7 15.9 %collective-permute-start.11 = (f32[128,128]{0,1:T(8,128)S(1)}, f32[128,128]{0,1:T(8,128)S(1)}, u32[]{:S(2)}, u32[]{:S(2)}) collective-permute-start(f32[128,128]{0,1:T(8,128)S(1)} %add.228), channel_id=1, source_target_pairs={{0,8},{4,12},{8,0},{12,4},{16,24},{20,28},{24,16},{28,20},{1,9},{5... | collective-permute-start | bytes 196616 | tf_op jit(solution)/shard_map/ppermute | solution.py:75
  280.6 7.3 %copy-start.10 = (bf16[192,2048]{0,1:T(8,128)(2,1)S(1)}, bf16[192,2048]{0,1:T(8,128)(2,1)}, u32[]{:S(2)}) copy-start(bf16[192,2048]{0,1:T(8,128)(2,1)} %copy-done.9) | copy-start | bytes 2359300
  280.6 5.7 %collective-permute-start.12 = (f32[128,128]{0,1:T(8,128)S(1)}, f32[128,128]{0,1:T(8,128)S(1)}, u32[]{:S(2)}, u32[]{:S(2)}) collective-permute-start(f32[128,128]{0,1:T(8,128)S(1)} %add.229), channel_id=1, source_target_pairs={{0,16},{4,20},{8,24},{12,28},{16,0},{20,4},{24,8},{28,12},{1,17},{... | collective-permute-start | bytes 196616 | tf_op jit(solution)/shard_map/ppermute | solution.py:75
  286.4 5.1 %collective-permute-start.13 = (f32[128,128]{0,1:T(8,128)S(1)}, f32[128,128]{0,1:T(8,128)S(1)}, u32[]{:S(2)}, u32[]{:S(2)}) collective-permute-start(f32[128,128]{0,1:T(8,128)S(1)} %add_multiply_fusion), channel_id=1, source_target_pairs={{0,1},{1,0},{2,3},{3,2},{4,5},{5,4},{6,7},{7,6},{8,9},{9,8},{10,11... | collective-permute-start | bytes 196616 | tf_op jit(solution)/shard_map/ppermute | solution.py:86
  291.5 13.6 %collective-permute-start.14 = (f32[256,128]{0,1:T(8,128)S(1)}, f32[256,128]{0,1:T(8,128)}, u32[]{:S(2)}, u32[]{:S(2)}) collective-permute-start(f32[256,128]{0,1:T(8,128)S(1)} %maximum_select_fusion.1), channel_id=1, source_target_pairs={{0,2},{1,3},{2,0},{3,1},{4,6},{5,7},{6,4},{7,5},{8,10},{9,11},{10,... | collective-permute-start | bytes 393224 | tf_op jit(solution)/shard_map/ppermute | solution.py:86
  299.1 7.0 %copy-start.6 = (bf16[192,2048]{0,1:T(8,128)(2,1)S(1)}, bf16[192,2048]{0,1:T(8,128)(2,1)}, u32[]{:S(2)}) copy-start(bf16[192,2048]{0,1:T(8,128)(2,1)} %copy-done.5) | copy-start | bytes 2359300
  299.1 7.0 %copy-start.8 = (bf16[192,2048]{0,1:T(8,128)(2,1)S(1)}, bf16[192,2048]{0,1:T(8,128)(2,1)}, u32[]{:S(2)}) copy-start(bf16[192,2048]{0,1:T(8,128)(2,1)} %copy-done.7) | copy-start | bytes 2359300
  (9 other events, 46.6 us)
Sparse Core Ops, SparseCore 0:
  9.6 66.1 all-gather.1
  150.5 73.5 reduce-scatter.1

commit v10 on v7

--- a/solution.py
+++ b/solution.py
@@ -131,11 +131,18 @@
     gc4 = grad_conv.reshape(tiles, block, local_groups, per_group)
     wp4 = win_prod.reshape(tiles, width, local_groups, per_group)
     cross = jnp.einsum("kigc,kjgc->gij", gc4, wp4, preferred_element_type=jnp.float32)
-    cross = jnp.pad(cross.reshape(local_groups, block * width), ((0, 0), (0, block)))
-    diag = cross.reshape(local_groups, block, width + 1)[:, :, 1 : halo + 1].sum(axis=1)
+    i = lax.broadcasted_iota(jnp.int32, (block, width, flen), 0)
+    j = lax.broadcasted_iota(jnp.int32, (block, width, flen), 1)
+    lag = lax.broadcasted_iota(jnp.int32, (block, width, flen), 2) + zero
+    pick = (i + halo - j == lag).astype(jnp.bfloat16)
+    cross_hi = lax.reduce_precision(cross, exponent_bits=8, mantissa_bits=7)
+    diag = None
+    for piece in (cross_hi, cross - cross_hi):
+        term = jnp.einsum("gij,ijs->gs", piece.astype(jnp.bfloat16), pick, preferred_element_type=jnp.float32)
+        diag = term if diag is None else diag + term
     scale = (rows * ctx_count * per_group) ** (-0.5)
     diag, next_head = lax.optimization_barrier((diag, next_head))
-    local_filters = butterfly_sum(diag[:, ::-1], "ctx", ctx_count) * scale
+    local_filters = butterfly_sum(diag, "ctx", ctx_count) * scale
     grad_filters = butterfly_gather(local_filters, "mp", mp_count)
     trailing = jnp.concatenate([grad_conv, next_head], 0)
     win_grad = windows(trailing, tiles, block, width)

time: 315 us -> 308 us (0.978)
  local copies, waits for them, and re-layouts: 93.8 us -> 82.6 us
  matrix products: 29.4 us -> 36.8 us
    dot_general x0 -> x2, matrix products: none -> 7.33 us  [body(): jnp.einsum('gij,ijs->gs', piece.astype(jnp.bfloat16), pick, preferred_ele...]
    reshape x1 -> x0, local copies, waits for them, and re-layouts: 6 us -> none  [body(): cross.reshape(local_groups, block, width + 1)[:, :, 1:halo + 1].sum(axis=1)]
    pad x1 -> x0, local copies, waits for them, and re-layouts: 4.8 us -> none  [body(): jnp.pad(cross.reshape(local_groups, block * width), ((0, 0), (0, block)))]
    unnamed x35 -> x38, local copies, waits for them, and re-layouts: 9.37 us -> 9.3 us
  transfers between devices with their start and end apart: 16 -> 16, of which waited for: 7 -> 7; matrix products, arithmetic and copies ran while one was open for 35% -> 28% of each run, Pallas kernels for 0% -> 0%
where the time goes in v10:
time: 308 us; the launch traced here: 307 us
  waiting for transfers between devices  134 us (44%)
  local copies, waits for them, and re-layouts  82.6 us (27%)
  matrix products  36.8 us (12%)
  starting transfers between devices  26.4 us (9%)
  between operations  14.5 us (5%)
  other arithmetic  12.7 us (4%)
    all_gather x1, waiting for transfers between devices, body(): cot_rows = lax.all_gather(cotangent, 'mp', axis=1, tiled=True)  57.9 us
    reduce_scatter x1, waiting for transfers between devices, body(): lax.psum_scatter(partial, 'ctx', scatter_dimension=0, tiled=True)  53.1 us
    optimization_barrier x4, local copies, waits for them, and re-layouts, body(): lax.optimization_barrier((cot_rows, mats_causal, mats_anti))  28.5 us
    ppermute x7, waiting for transfers between devices, exchange_columns(): lax.ppermute(chunk, 'ctx', [(k, (k + shift) % count) for k in range(count)])  19.9 us
    ppermute x7, starting transfers between devices, exchange_columns(): lax.ppermute(chunk, 'ctx', [(k, (k + shift) % count) for k in range(count)])  12.8 us
    reshape x2, local copies, waits for them, and re-layouts, filter_apply(): return total.reshape(tiles * block, chans)  10.8 us
    dot_general x4, matrix products, filter_apply(): jnp.einsum('gij,kjgc->kigc', m, w4, preferred_element_type=jnp.float32)  9.89 us
    unnamed x38, local copies, waits for them, and re-layouts  9.3 us
  transfers between devices with their start and end apart: 16, of which 7 were waited for; matrix products, arithmetic and copies ran while one was open for 28% of the time, Pallas kernels for 0%

profile of v10, /device:TPU:0, one launch (start us, length us, event | category | flops | bytes accessed | tf_op | source)
XLA Modules:
  0.0 307.1 jit_solution(1097700082175636630)
XLA Ops:
  12.6 5.3 %fusion.35 = (bf16[128,64,192]{0,2,1:T(8,128)(2,1)}, bf16[128,64,192]{0,2,1:T(8,128)(2,1)}, bf16[128,64,192]{0,2,1:T(8,128)(2,1)}, bf16[128,64,192]{0,2,1:T(8,128)(2,1)}) fusion(bf16[256,64,192]{0,2,1:T(8,128)(2,1)S(1)} %fusion.5, bf16[256,64,192]{0,2,1:T(8,128)(2,1)S(1)} %fusion.6), kind=kLoop, calls=%fused_computation.73 | loop fusion | bytes 25165824 | tf_op jit(solution)/shard_map/slice | solution.py:30
  17.9 57.9 %all-gather.2.cloned.1.call-done = bf16[192,8192]{1,0:T(8,128)(2,1)} async-done(((bf16[192,2048]{1,0:T(8,128)(2,1)}), bf16[192,8192]{1,0:T(8,128)(2,1)}) %all-gather.2.cloned.1.call-update) | async-done | bytes 3145744 | tf_op jit(solution)/shard_map/all_gather | solution.py:114
  83.5 7.7 %collective-permute-done = bf16[192,1024]{1,0:T(8,128)(2,1)} collective-permute-done((bf16[192,1024]{1,0:T(8,128)(2,1)}, bf16[192,1024]{1,0:T(8,128)(2,1)}, u32[]{:S(2)}, u32[]{:S(2)}) %collective-permute-start) | collective-permute-done | bytes 393248 | tf_op jit(solution)/shard_map/ppermute | solution.py:64
  93.7 7.0 %collective-permute-start.6 = (bf16[192,1024]{1,0:T(8,128)(2,1)S(1)}, bf16[192,1024]{1,0:T(8,128)(2,1)S(1)}, u32[]{:S(2)}, u32[]{:S(2)}) collective-permute-start(bf16[192,1024]{1,0:T(8,128)(2,1)S(1)} %get-tuple-element.38), channel_id=1, source_target_pairs={{0,28},{4,0},{8,4},{12,8},{16,12},{20,16},{24,20},{28,24},{1,29},{... | collective-permute-start | bytes 1179656 | tf_op jit(solution)/shard_map/ppermute | solution.py:64
  101.7 6.8 %collective-permute-done.2 = bf16[192,1024]{1,0:T(8,128)(2,1)} collective-permute-done((bf16[192,1024]{1,0:T(8,128)(2,1)}, bf16[192,1024]{1,0:T(8,128)(2,1)}, u32[]{:S(2)}, u32[]{:S(2)}) %collective-permute-start.2) | collective-permute-done | bytes 393248 | tf_op jit(solution)/shard_map/ppermute | solution.py:64
  110.5 5.4 %collective-permute-done.4 = bf16[192,1024]{1,0:T(8,128)(2,1)S(1)} collective-permute-done((bf16[192,1024]{1,0:T(8,128)(2,1)}, bf16[192,1024]{1,0:T(8,128)(2,1)S(1)}, u32[]{:S(2)}, u32[]{:S(2)}) %collective-permute-start.4) | collective-permute-done | bytes 393248 | tf_op jit(solution)/shard_map/ppermute | solution.py:64
  116.2 9.2 %fusion.37 = f32[1536,2048]{1,0:T(8,128)} fusion(bf16[1536,1024]{1,0:T(8,128)(2,1)S(1)} %constant_dynamic-update-slice_fusion, bf16[2048,1024]{1,0:T(8,128)(2,1)S(1)} %copy-done.16), kind=kOutput, calls=%fused_computation.75 | convolution fusion | flops 6442450944 | bytes 19922944 | tf_op jit(solution)/shard_map/dot_general | solution.py:8
  129.2 3.9 %collective-permute-start.7 = (bf16[128,2048]{0,1:T(8,128)(2,1)S(1)}, bf16[128,2048]{0,1:T(8,128)(2,1)S(1)}, u32[]{:S(2)}, u32[]{:S(2)}) collective-permute-start(bf16[128,2048]{0,1:T(8,128)(2,1)S(1)} %slice.44), channel_id=1, source_target_pairs={{0,4},{4,8},{8,12},{12,16},{16,20},{20,24},{24,28},{1,5},{5,9},{9,... | collective-permute-start | bytes 1572872 | tf_op jit(solution)/shard_map/ppermute | solution.py:123
  136.6 7.2 %copy.67 = bf16[128,64,192,1]{2,1,3,0:T(8,128)(2,1)} copy(bf16[128,64,192,1]{0,2,1,3:T(8,128)(2,1)} %bitcast.51) | data formatting | bytes 6291456 | tf_op jit(solution)/shard_map/optimization_barrier | solution.py:115
  143.8 6.9 %copy.66 = bf16[128,64,192,1]{2,1,3,0:T(8,128)(2,1)} copy(bf16[128,64,192,1]{0,2,1,3:T(8,128)(2,1)} %bitcast.50) | data formatting | bytes 6291456 | tf_op jit(solution)/shard_map/optimization_barrier | solution.py:115
  150.7 3.5 %fusion.34 = f32[128,3,16,64]{3,2,1,0:T(8,128)S(1)} fusion(bf16[128,64,192,1]{2,1,3,0:T(8,128)(2,1)} %copy.67, bf16[1,192,128,16]{1,3,0,2:T(8,128)(2,1)S(1)} %bitcast.45, bf16[1,192,128,16]{1,3,0,2:T(8,128)(2,1)S(1)} %bitcast.58, bf16[1,192,128,16]{1,3,0,2:T(8,128)(2,1)S(1)} %bitcast.55), kind=kOutput, calls=%fused_computation.72 | convolution fusion | flops 153354240 | bytes 7077888 | tf_op jit(solution)/shard_map/gij,kjgc->kigc/dot_general | solution.py:48
  155.9 3.7 %copy.49 = f32[3,64,128,16]{1,0,3,2:T(4,128)} copy(f32[3,64,128,16]{1,3,0,2:T(8,128)S(1)} %add_bitcast_fusion.1) | data formatting | bytes 3145728 | tf_op jit(solution)/shard_map/add | solution.py:49
  159.6 4.8 %reshape.32 = f32[192,2048]{0,1:T(8,128)S(1)} reshape(f32[3,64,128,16]{1,0,3,2:T(4,128)} %copy.49) | data formatting | bytes 3145728 | tf_op jit(solution)/shard_map/reshape | solution.py:51
  164.4 53.1 %reduce-scatter.2.cloned.1.call-done = f32[192,2048]{1,0:T(8,128)} async-done(((f32[1536,2048]{1,0:T(8,128)}), f32[192,2048]{1,0:T(8,128)}) %reduce-scatter.2.cloned.1.call-update) | async-done | bytes 1572880 | tf_op jit(solution)/shard_map/reduce_scatter | solution.py:118
  219.2 3.4 %multiply_convert_fusion = (bf16[192,2048]{1,0:T(8,128)(2,1)S(1)}, bf16[192,2048]{1,0:T(8,128)(2,1)}) fusion(f32[192,2048]{1,0:T(8,128)} %reduce-scatter.2.cloned.1.call-done, bf16[192,2048]{1,0:T(8,128)(2,1)} %param.8, f32[192,2048]{1,0:T(8,128)} %copy.50), kind=kLoop, calls=%fused_computation.32 | loop fusion | flops 1966080 | bytes 5505024 | tf_op jit(solution)/shard_map/convert_element_type | solution.py:129
  225.5 6.8 %convolution_bitcast_fusion = f32[128,64,192]{2,1,0:T(8,128)} fusion(bf16[3,64,128,16]{1,0,3,2:T(4,128)(2,1)} %reshape.33, bf16[1,192,128,16]{1,3,0,2:T(8,128)(2,1)S(1)} %bitcast.47, bf16[1,192,128,16]{1,3,0,2:T(8,128)(2,1)} %bitcast.57, bf16[1,192,128,16]{1,3,0,2:T(8,128)(2,1)} %bitcast.54), kind=kOutput, calls=%fused_computation.11 | convolution fusion | flops 153354240 | bytes 9437184 | tf_op jit(solution)/shard_map/kigc,kjgc->gij/dot_general | solution.py:133
  232.2 8.6 %copy.53 = f32[128,64,192]{0,2,1:T(8,128)} copy(f32[128,64,192]{2,1,0:T(8,128)} %convolution_bitcast_fusion) | data formatting | bytes 12582912 | tf_op jit(solution)/shard_map/kigc,kjgc->gij/dot_general | solution.py:133
  242.6 4.9 %fusion.20 = f32[128,128]{1,0:T(8,128)S(1)} fusion(s32[128]{0:T(128)S(1)} %iota_add_fusion, s32[64]{0:T(128)S(1)} %iota_add_fusion.1, f32[128,64,192]{0,2,1:T(8,128)} %copy.53), kind=kOutput, calls=%fused_computation.37 | convolution fusion | flops 408944640 | bytes 6357760 | tf_op jit(solution)/shard_map/gij,ijs->gs/dot_general | solution.py:141
  255.4 6.9 %copy.69 = bf16[128,64,192,1]{2,1,3,0:T(8,128)(2,1)} copy(bf16[128,64,192,1]{0,2,1,3:T(8,128)(2,1)} %bitcast.49) | data formatting | bytes 6291456 | tf_op jit(solution)/shard_map/optimization_barrier | solution.py:115
  262.3 7.6 %copy.70 = bf16[128,64,192,1]{2,1,3,0:T(8,128)(2,1)} copy(bf16[128,64,192,1]{0,2,1,3:T(8,128)(2,1)S(1)} %bitcast.48) | data formatting | bytes 6291456 | tf_op jit(solution)/shard_map/optimization_barrier | solution.py:115
  276.0 3.5 %fusion.19 = f32[128,3,16,64]{3,2,1,0:T(8,128)S(1)} fusion(bf16[128,64,192,1]{2,1,3,0:T(8,128)(2,1)} %copy.69, bf16[1,192,128,16]{1,3,0,2:T(8,128)(2,1)S(1)} %bitcast.60, bf16[1,192,128,16]{1,3,0,2:T(8,128)(2,1)S(1)} %bitcast.62, bf16[1,192,128,16]{1,3,0,2:T(8,128)(2,1)S(1)} %bitcast.52), kind=kOutput, calls=%fused_computation.36 | convolution fusion | flops 153354240 | bytes 7077888 | tf_op jit(solution)/shard_map/gij,kjgc->kigc/dot_general | solution.py:48
  283.4 3.7 %copy.63 = f32[3,64,128,16]{1,0,3,2:T(4,128)} copy(f32[3,64,128,16]{1,3,0,2:T(8,128)S(1)} %add_bitcast_fusion) | data formatting | bytes 3145728 | tf_op jit(solution)/shard_map/add | solution.py:49
  287.2 6.0 %reshape.34 = f32[192,2048]{0,1:T(8,128)} reshape(f32[3,64,128,16]{1,0,3,2:T(4,128)} %copy.63) | data formatting | bytes 3145728 | tf_op jit(solution)/shard_map/reshape | solution.py:51
  293.9 3.0 fusion.15
  (97 shorter events, 55.8 us)
Async XLA Ops:
  7.2 68.6 %all-gather.2.cloned.1.call-start = ((), (), s32[]{:S(2)}) async-start(), calls=%async_computation.1 | async-start | bytes 3932160 | tf_op jit(solution)/shard_map/all_gather | solution.py:114
  7.9 209.6 %reduce-scatter.2.cloned.1.call-start = ((), (), s32[]{:S(2)}) async-start(), calls=%async_computation.2 | async-start | bytes 14155776 | tf_op jit(solution)/shard_map/reduce_scatter | solution.py:118
  79.1 12.2 %collective-permute-start = (bf16[192,1024]{1,0:T(8,128)(2,1)}, bf16[192,1024]{1,0:T(8,128)(2,1)}, u32[]{:S(2)}, u32[]{:S(2)}) collective-permute-start(bf16[192,1024]{1,0:T(8,128)(2,1)} %get-tuple-element.44), channel_id=1, source_target_pairs={{0,4},{4,8},{8,12},{12,16},{16,20},{20,24},{24,28},{28,0},{1,5},{5... | collective-permute-start | bytes 1179656 | tf_op jit(solution)/shard_map/ppermute | solution.py:64
  79.1 14.6 %collective-permute-start.1 = (bf16[192,1024]{1,0:T(8,128)(2,1)}, bf16[192,1024]{1,0:T(8,128)(2,1)}, u32[]{:S(2)}, u32[]{:S(2)}) collective-permute-start(bf16[192,1024]{1,0:T(8,128)(2,1)} %get-tuple-element.43), channel_id=1, source_target_pairs={{0,8},{4,12},{8,16},{12,20},{16,24},{20,28},{24,0},{28,4},{1,9},{5... | collective-permute-start | bytes 1179656 | tf_op jit(solution)/shard_map/ppermute | solution.py:64
  80.6 27.9 %collective-permute-start.2 = (bf16[192,1024]{1,0:T(8,128)(2,1)}, bf16[192,1024]{1,0:T(8,128)(2,1)}, u32[]{:S(2)}, u32[]{:S(2)}) collective-permute-start(bf16[192,1024]{1,0:T(8,128)(2,1)} %get-tuple-element.42), channel_id=1, source_target_pairs={{0,12},{4,16},{8,20},{12,24},{16,28},{20,0},{24,4},{28,8},{1,13},{... | collective-permute-start | bytes 1179656 | tf_op jit(solution)/shard_map/ppermute | solution.py:64
  82.9 26.6 %collective-permute-start.3 = (bf16[192,1024]{1,0:T(8,128)(2,1)}, bf16[192,1024]{1,0:T(8,128)(2,1)}, u32[]{:S(2)}, u32[]{:S(2)}) collective-permute-start(bf16[192,1024]{1,0:T(8,128)(2,1)} %get-tuple-element.41), channel_id=1, source_target_pairs={{0,16},{4,20},{8,24},{12,28},{16,0},{20,4},{24,8},{28,12},{1,17},{... | collective-permute-start | bytes 1179656 | tf_op jit(solution)/shard_map/ppermute | solution.py:64
  83.5 32.7 %copy-start.16 = (bf16[2048,1024]{1,0:T(8,128)(2,1)S(1)}, bf16[2048,1024]{1,0:T(8,128)(2,1)}, u32[]{:S(2)}) copy-start(bf16[2048,1024]{1,0:T(8,128)(2,1)} %param.7) | copy-start | bytes 12582916
  83.5 32.5 %collective-permute-start.4 = (bf16[192,1024]{1,0:T(8,128)(2,1)}, bf16[192,1024]{1,0:T(8,128)(2,1)S(1)}, u32[]{:S(2)}, u32[]{:S(2)}) collective-permute-start(bf16[192,1024]{1,0:T(8,128)(2,1)} %get-tuple-element.40), channel_id=1, source_target_pairs={{0,20},{4,24},{8,28},{12,0},{16,4},{20,8},{24,12},{28,16},{1,21},{... | collective-permute-start | bytes 1179656 | tf_op jit(solution)/shard_map/ppermute | solution.py:64
  91.3 24.8 %collective-permute-start.5 = (bf16[192,1024]{1,0:T(8,128)(2,1)}, bf16[192,1024]{1,0:T(8,128)(2,1)S(1)}, u32[]{:S(2)}, u32[]{:S(2)}) collective-permute-start(bf16[192,1024]{1,0:T(8,128)(2,1)} %get-tuple-element.39), channel_id=1, source_target_pairs={{0,24},{4,28},{8,0},{12,4},{16,8},{20,12},{24,16},{28,20},{1,25},{... | collective-permute-start | bytes 1179656 | tf_op jit(solution)/shard_map/ppermute | solution.py:64
  93.7 22.4 %collective-permute-start.6 = (bf16[192,1024]{1,0:T(8,128)(2,1)S(1)}, bf16[192,1024]{1,0:T(8,128)(2,1)S(1)}, u32[]{:S(2)}, u32[]{:S(2)}) collective-permute-start(bf16[192,1024]{1,0:T(8,128)(2,1)S(1)} %get-tuple-element.38), channel_id=1, source_target_pairs={{0,28},{4,0},{8,4},{12,8},{16,12},{20,16},{24,20},{28,24},{1,29},{... | collective-permute-start | bytes 1179656 | tf_op jit(solution)/shard_map/ppermute | solution.py:64
  127.0 9.6 %copy-start.4 = (bf16[192,2048]{0,1:T(8,128)(2,1)}, bf16[192,2048]{0,1:T(8,128)(2,1)S(1)}, u32[]{:S(2)}) copy-start(bf16[192,2048]{0,1:T(8,128)(2,1)S(1)} %copy.46) | copy-start | bytes 2359300
  128.7 7.9 %copy-start.6 = (bf16[192,2048]{0,1:T(8,128)(2,1)}, bf16[192,2048]{0,1:T(8,128)(2,1)S(1)}, u32[]{:S(2)}) copy-start(bf16[192,2048]{0,1:T(8,128)(2,1)S(1)} %copy.45) | copy-start | bytes 2359300
  129.2 5.3 %collective-permute-start.7 = (bf16[128,2048]{0,1:T(8,128)(2,1)S(1)}, bf16[128,2048]{0,1:T(8,128)(2,1)S(1)}, u32[]{:S(2)}, u32[]{:S(2)}) collective-permute-start(bf16[128,2048]{0,1:T(8,128)(2,1)S(1)} %slice.44), channel_id=1, source_target_pairs={{0,4},{4,8},{8,12},{12,16},{16,20},{20,24},{24,28},{1,5},{5,9},{9,... | collective-permute-start | bytes 1572872 | tf_op jit(solution)/shard_map/ppermute | solution.py:123
  143.8 6.9 %copy-start.10 = (bf16[192,2048]{0,1:T(8,128)(2,1)S(1)}, bf16[192,2048]{0,1:T(8,128)(2,1)}, u32[]{:S(2)}) copy-start(bf16[192,2048]{0,1:T(8,128)(2,1)} %get-tuple-element.50) | copy-start | bytes 2359300
  143.8 6.9 %copy-start.11 = (bf16[192,2048]{0,1:T(8,128)(2,1)S(1)}, bf16[192,2048]{0,1:T(8,128)(2,1)}, u32[]{:S(2)}) copy-start(bf16[192,2048]{0,1:T(8,128)(2,1)} %get-tuple-element.51) | copy-start | bytes 2359300
  222.6 9.6 %copy-start.3 = (bf16[192,2048]{1,0:T(8,128)(2,1)}, bf16[192,2048]{1,0:T(8,128)(2,1)S(1)}, u32[]{:S(2)}) copy-start(bf16[192,2048]{1,0:T(8,128)(2,1)S(1)} %get-tuple-element.48) | copy-start | bytes 2359300
  223.1 9.1 %copy-start.8 = (bf16[192,2048]{0,1:T(8,128)(2,1)}, bf16[192,2048]{0,1:T(8,128)(2,1)S(1)}, u32[]{:S(2)}) copy-start(bf16[192,2048]{0,1:T(8,128)(2,1)S(1)} %copy.51) | copy-start | bytes 2359300
  240.8 9.1 %collective-permute-start.8 = (bf16[128,2048]{1,0:T(8,128)(2,1)S(1)}, bf16[128,2048]{1,0:T(8,128)(2,1)S(1)}, u32[]{:S(2)}, u32[]{:S(2)}) collective-permute-start(bf16[128,2048]{1,0:T(8,128)(2,1)S(1)} %slice.47), channel_id=1, source_target_pairs={{4,0},{8,4},{12,8},{16,12},{20,16},{24,20},{28,24},{5,1},{9,5},{13... | collective-permute-start | bytes 1572872 | tf_op jit(solution)/shard_map/ppermute | solution.py:130
  250.8 2.5 collective-permute-start.9
  253.3 16.6 %collective-permute-start.10 = (f32[128,128]{1,0:T(8,128)S(1)}, f32[128,128]{1,0:T(8,128)S(1)}, u32[]{:S(2)}, u32[]{:S(2)}) collective-permute-start(f32[128,128]{1,0:T(8,128)S(1)} %add.210), channel_id=1, source_target_pairs={{0,8},{4,12},{8,0},{12,4},{16,24},{20,28},{24,16},{28,20},{1,9},{5... | collective-permute-start | bytes 196616 | tf_op jit(solution)/shard_map/ppermute | solution.py:75
  255.4 6.9 %copy-start.2 = (bf16[128,64,192]{0,2,1:T(8,128)(2,1)S(1)}, bf16[128,64,192]{0,2,1:T(8,128)(2,1)}, u32[]{:S(2)}) copy-start(bf16[128,64,192]{0,2,1:T(8,128)(2,1)} %get-tuple-element.23) | copy-start | bytes 9437188
  269.9 4.5 %collective-permute-start.11 = (f32[128,128]{1,0:T(8,128)S(1)}, f32[128,128]{1,0:T(8,128)S(1)}, u32[]{:S(2)}, u32[]{:S(2)}) collective-permute-start(f32[128,128]{1,0:T(8,128)S(1)} %add.211), channel_id=1, source_target_pairs={{0,16},{4,20},{8,24},{12,28},{16,0},{20,4},{24,8},{28,12},{1,17},{... | collective-permute-start | bytes 196616 | tf_op jit(solution)/shard_map/ppermute | solution.py:75
  274.4 5.1 %collective-permute-start.12 = (f32[128,128]{1,0:T(8,128)S(1)}, f32[128,128]{1,0:T(8,128)S(1)}, u32[]{:S(2)}, u32[]{:S(2)}) collective-permute-start(f32[128,128]{1,0:T(8,128)S(1)} %add_multiply_fusion), channel_id=1, source_target_pairs={{0,1},{1,0},{2,3},{3,2},{4,5},{5,4},{6,7},{7,6},{8,9},{9,8},{10,11... | collective-permute-start | bytes 196616 | tf_op jit(solution)/shard_map/ppermute | solution.py:86
  279.5 13.6 %collective-permute-start.13 = (f32[256,128]{1,0:T(8,128)S(1)}, f32[256,128]{1,0:T(8,128)S(1)}, u32[]{:S(2)}, u32[]{:S(2)}) collective-permute-start(f32[256,128]{1,0:T(8,128)S(1)} %maximum_select_fusion.1), channel_id=1, source_target_pairs={{0,2},{1,3},{2,0},{3,1},{4,6},{5,7},{6,4},{7,5},{8,10},{9,11},{10,... | collective-permute-start | bytes 393224 | tf_op jit(solution)/shard_map/ppermute | solution.py:86
  (9 other events, 39.8 us)
Sparse Core Ops, SparseCore 0:
  9.6 66.1 all-gather.1
  125.5 92.0 reduce-scatter.1

commit v11 on v10

--- a/solution.py
+++ b/solution.py
@@ -90,6 +90,17 @@
     return x
 
 
+def scatter_sum(partial, count):
+    rows = partial.shape[0] // count
+    me = lax.axis_index("ctx")
+    acc = lax.dynamic_slice_in_dim(partial, me * rows, rows, 0)
+    for shift in range(1, count):
+        dest = (me + shift) % count
+        chunk = lax.dynamic_slice_in_dim(partial, dest * rows, rows, 0)
+        acc = acc + lax.ppermute(chunk, "ctx", [(k, (k + shift) % count) for k in range(count)])
+    return acc
+
+
 def body(cotangent, out_weight, query_act, key_act, value_act, filters):
     rows, chans = cotangent.shape
     groups, flen = filters.shape
@@ -115,7 +126,14 @@
     cot_rows, mats_causal, mats_anti = lax.optimization_barrier((cot_rows, mats_causal, mats_anti))
     cot_cols = exchange_columns(cot_rows, ctx_count)
     partial = contract(cot_cols, out_weight)
-    grad_mixed = lax.psum_scatter(partial, "ctx", scatter_dimension=0, tiled=True)
+    half = chans // 2
+    grad_mixed = jnp.concatenate(
+        [
+            lax.psum_scatter(partial[:, :half], "ctx", scatter_dimension=0, tiled=True),
+            scatter_sum(partial[:, half:], ctx_count),
+        ],
+        1,
+    )
 
     fwd = [(k, k + 1) for k in range(ctx_count - 1)]
     bwd = [(k + 1, k) for k in range(ctx_count - 1)]

time: 308 us -> 352 us (1.14)
  local copies, waits for them, and re-layouts: 82.6 us -> 100 us
  waiting for transfers between devices: 134 us -> 145 us
  other arithmetic: 12.7 us -> 18.5 us
  matrix products: 36.8 us -> 41.3 us
  starting transfers between devices: 26.4 us -> 30.6 us
    ppermute x0 -> x7, waiting for transfers between devices: none -> 65.3 us  [scatter_sum(): lax.ppermute(chunk, 'ctx', [(k, (k + shift) % count) for k in range(count)])]
    reduce_scatter x1, waiting for transfers between devices: 53.1 us -> 0.01 us  [body(): lax.psum_scatter(partial[:, :half], 'ctx', scatter_dimension=0, tiled=True)]
    slice x0 -> x1, local copies, waits for them, and re-layouts: none -> 11.9 us  [body(): partial[:, :half]]
    ppermute x0 -> x7, starting transfers between devices: none -> 7.38 us  [scatter_sum(): lax.ppermute(chunk, 'ctx', [(k, (k + shift) % count) for k in range(count)])]
    dynamic_slice x0 -> x1, local copies, waits for them, and re-layouts: none -> 6.05 us  [scatter_sum(): chunk = lax.dynamic_slice_in_dim(partial, dest * rows, rows, 0)]
    dot_general x4, matrix products: 9.89 us -> 14.4 us  [filter_apply(): jnp.einsum('gij,kjgc->kigc', m, w4, preferred_element_type=jnp.float32)]
    add x0 -> x1, other arithmetic: none -> 4.47 us  [scatter_sum(): acc + lax.ppermute(chunk, 'ctx', [(k, (k + shift) % count) for k in range...]
    unnamed x38 -> x36, local copies, waits for them, and re-layouts: 9.3 us -> 9.1 us
  transfers between devices with their start and end apart: 16 -> 23, of which waited for: 7 -> 10; matrix products, arithmetic and copies ran while one was open for 28% -> 29% of each run, Pallas kernels for 0% -> 0%
where the time goes in v11:
time: 352 us; the launch traced here: 351 us
  waiting for transfers between devices  145 us (41%)
  local copies, waits for them, and re-layouts  100 us (28%)
  matrix products  41.3 us (12%)
  starting transfers between devices  30.6 us (9%)
  other arithmetic  18.5 us (5%)
  between operations  14.6 us (4%)
    ppermute x7, waiting for transfers between devices, scatter_sum(): lax.ppermute(chunk, 'ctx', [(k, (k + shift) % count) for k in range(count)])  65.3 us
    all_gather x1, waiting for transfers between devices, body(): cot_rows = lax.all_gather(cotangent, 'mp', axis=1, tiled=True)  57.8 us
    optimization_barrier x4, local copies, waits for them, and re-layouts, body(): lax.optimization_barrier((cot_rows, mats_causal, mats_anti))  28.6 us
    ppermute x7, waiting for transfers between devices, exchange_columns(): lax.ppermute(chunk, 'ctx', [(k, (k + shift) % count) for k in range(count)])  19.9 us
    dot_general x4, matrix products, filter_apply(): jnp.einsum('gij,kjgc->kigc', m, w4, preferred_element_type=jnp.float32)  14.4 us
    ppermute x7, starting transfers between devices, exchange_columns(): lax.ppermute(chunk, 'ctx', [(k, (k + shift) % count) for k in range(count)])  12.8 us
    slice x1, local copies, waits for them, and re-layouts, body(): partial[:, :half]  11.9 us
    reshape x2, local copies, waits for them, and re-layouts, filter_apply(): return total.reshape(tiles * block, chans)  10.7 us
  transfers between devices with their start and end apart: 23, of which 10 were waited for; matrix products, arithmetic and copies ran while one was open for 29% of the time, Pallas kernels for 0%

profile of v11, /device:TPU:0, one launch (start us, length us, event | category | flops | bytes accessed | tf_op | source)
XLA Modules:
  0.0 350.6 jit_solution(14900640067345571185)
XLA Ops:
  12.6 5.3 %fusion.36 = (bf16[128,64,192]{0,2,1:T(8,128)(2,1)}, bf16[128,64,192]{0,2,1:T(8,128)(2,1)}, bf16[128,64,192]{0,2,1:T(8,128)(2,1)}, bf16[128,64,192]{0,2,1:T(8,128)(2,1)}) fusion(bf16[256,64,192]{0,2,1:T(8,128)(2,1)S(1)} %fusion.5, bf16[256,64,192]{0,2,1:T(8,128)(2,1)S(1)} %fusion.6), kind=kLoop, calls=%fused_computation.83 | loop fusion | bytes 25165824 | tf_op jit(solution)/shard_map/slice | solution.py:30
  17.9 57.8 %all-gather.2.cloned.1.call-done = bf16[192,8192]{1,0:T(8,128)(2,1)} async-done(((bf16[192,2048]{1,0:T(8,128)(2,1)}), bf16[192,8192]{1,0:T(8,128)(2,1)}) %all-gather.2.cloned.1.call-update) | async-done | bytes 3145744 | tf_op jit(solution)/shard_map/all_gather | solution.py:125
  83.5 7.7 %collective-permute-done = bf16[192,1024]{1,0:T(8,128)(2,1)} collective-permute-done((bf16[192,1024]{1,0:T(8,128)(2,1)}, bf16[192,1024]{1,0:T(8,128)(2,1)}, u32[]{:S(2)}, u32[]{:S(2)}) %collective-permute-start) | collective-permute-done | bytes 393248 | tf_op jit(solution)/shard_map/ppermute | solution.py:64
  93.7 7.0 %collective-permute-start.6 = (bf16[192,1024]{1,0:T(8,128)(2,1)S(1)}, bf16[192,1024]{1,0:T(8,128)(2,1)S(1)}, u32[]{:S(2)}, u32[]{:S(2)}) collective-permute-start(bf16[192,1024]{1,0:T(8,128)(2,1)S(1)} %get-tuple-element.47), channel_id=1, source_target_pairs={{0,28},{4,0},{8,4},{12,8},{16,12},{20,16},{24,20},{28,24},{1,29},{... | collective-permute-start | bytes 1179656 | tf_op jit(solution)/shard_map/ppermute | solution.py:64
  101.7 6.8 %collective-permute-done.2 = bf16[192,1024]{1,0:T(8,128)(2,1)} collective-permute-done((bf16[192,1024]{1,0:T(8,128)(2,1)}, bf16[192,1024]{1,0:T(8,128)(2,1)}, u32[]{:S(2)}, u32[]{:S(2)}) %collective-permute-start.2) | collective-permute-done | bytes 393248 | tf_op jit(solution)/shard_map/ppermute | solution.py:64
  110.5 5.4 %collective-permute-done.4 = bf16[192,1024]{1,0:T(8,128)(2,1)S(1)} collective-permute-done((bf16[192,1024]{1,0:T(8,128)(2,1)}, bf16[192,1024]{1,0:T(8,128)(2,1)S(1)}, u32[]{:S(2)}, u32[]{:S(2)}) %collective-permute-start.4) | collective-permute-done | bytes 393248 | tf_op jit(solution)/shard_map/ppermute | solution.py:64
  116.2 9.2 %fusion.38 = f32[1536,2048]{1,0:T(8,128)} fusion(bf16[1536,1024]{1,0:T(8,128)(2,1)S(1)} %constant_dynamic-update-slice_fusion, bf16[2048,1024]{1,0:T(8,128)(2,1)S(1)} %copy-done.15), kind=kOutput, calls=%fused_computation.85 | convolution fusion | flops 6442450944 | bytes 19922944 | tf_op jit(solution)/shard_map/dot_general | solution.py:8
  125.4 11.9 %fusion.35 = (f32[1536,1024]{1,0:T(8,128)}, f32[1536,1024]{1,0:T(8,128)}) fusion(f32[1536,2048]{1,0:T(8,128)} %fusion.38), kind=kLoop, calls=%fused_computation.82 | loop fusion | bytes 25165824 | tf_op jit(solution)/shard_map/slice | solution.py:132
  144.8 6.0 %constant_dynamic-slice_fusion.6 = (f32[192,1024]{1,0:T(8,128)}, f32[192,1024]{1,0:T(8,128)}, f32[192,1024]{1,0:T(8,128)}, f32[192,1024]{1,0:T(8,128)}, f32[192,...) fusion(f32[1536,1024]{1,0:T(8,128)} %get-tuple-element.35, s32[]{:T(128)S(6)} %select_n.174, ...), kind=kLoop, calls=%fused_computation.60 | loop fusion | bytes 11010076 | tf_op jit(solution)/shard_map/dynamic_slice | solution.py:99
  154.2 7.4 %copy.67 = bf16[128,64,192,1]{2,1,3,0:T(8,128)(2,1)} copy(bf16[128,64,192,1]{0,2,1,3:T(8,128)(2,1)} %bitcast.51) | data formatting | bytes 6291456 | tf_op jit(solution)/shard_map/optimization_barrier | solution.py:126
  163.7 12.4 %collective-permute-done.13 = f32[192,1024]{1,0:T(8,128)} collective-permute-done((f32[192,1024]{1,0:T(8,128)}, f32[192,1024]{1,0:T(8,128)}, u32[]{:S(2)}, u32[]{:S(2)}) %collective-permute-start.13) | collective-permute-done | bytes 786464 | tf_op jit(solution)/shard_map/ppermute | solution.py:100
  178.7 26.4 %collective-permute-done.12 = f32[192,1024]{1,0:T(8,128)} collective-permute-done((f32[192,1024]{1,0:T(8,128)}, f32[192,1024]{1,0:T(8,128)}, u32[]{:S(2)}, u32[]{:S(2)}) %collective-permute-start.12) | collective-permute-done | bytes 786464 | tf_op jit(solution)/shard_map/ppermute | solution.py:100
  205.1 5.0 %fusion.34 = f32[128,3,16,64]{3,2,1,0:T(8,128)} fusion(bf16[128,64,192,1]{2,1,3,0:T(8,128)(2,1)} %copy.67, bf16[1,192,128,16]{1,3,0,2:T(8,128)(2,1)S(1)} %bitcast.45, bf16[1,192,128,16]{1,3,0,2:T(8,128)(2,1)S(1)} %bitcast.57, bf16[1,192,128,16]{1,3,0,2:T(8,128)(2,1)S(1)} %bitcast.54), kind=kOutput, calls=%fused_computation.81 | convolution fusion | flops 153354240 | bytes 7077888 | tf_op jit(solution)/shard_map/gij,kjgc->kigc/dot_general | solution.py:48
  210.2 6.7 %copy.66 = bf16[128,64,192,1]{2,1,3,0:T(8,128)(2,1)} copy(bf16[128,64,192,1]{0,2,1,3:T(8,128)(2,1)} %bitcast.50) | data formatting | bytes 6291456 | tf_op jit(solution)/shard_map/optimization_barrier | solution.py:126
  216.9 4.4 %add_bitcast_fusion.1 = f32[3,64,128,16]{1,3,0,2:T(8,128)S(1)} fusion(f32[128,3,16,64]{3,2,1,0:T(8,128)} %fusion.34, bf16[128,64,192,1]{2,1,3,0:T(8,128)(2,1)} %copy.66, bf16[1,192,128,16]{1,3,0,2:T(8,128)(2,1)S(1)} %bitcast.46, bf16[1,192,128,16]{1,3,0,2:T(8,128)(2,1)S(1)} %bitcast.58, bf16[1,192,128,16]{1,3,0,2:T(8,128)(2,1)S(1)} %bitcast.55), kind=kOutput, calls=%fused_computation.15 | convolution fusion | flops 153747456 | bytes 8650752 | tf_op jit(solution)/shard_map/gij,kjgc->kigc/dot_general | solution.py:48
  225.1 4.7 %reshape.32 = f32[192,2048]{0,1:T(8,128)S(1)} reshape(f32[3,64,128,16]{1,0,3,2:T(4,128)} %copy.49) | data formatting | bytes 3145728 | tf_op jit(solution)/shard_map/reshape | solution.py:51
  229.8 25.1 %collective-permute-done.10 = f32[192,1024]{1,0:T(8,128)} collective-permute-done((f32[192,1024]{1,0:T(8,128)}, f32[192,1024]{1,0:T(8,128)}, u32[]{:S(2)}, u32[]{:S(2)}) %collective-permute-start.10) | collective-permute-done | bytes 786464 | tf_op jit(solution)/shard_map/ppermute | solution.py:100
  256.3 4.5 %add_add_fusion = f32[192,1024]{1,0:T(8,128)} fusion(f32[192,1024]{1,0:T(8,128)} %collective-permute-done.13, f32[192,1024]{1,0:T(8,128)} %collective-permute-done.12, f32[192,1024]{1,0:T(8,128)} %collective-permute-done.11, f32[192,1024]{1,0:T(8,128)} %collective-permute-done.10, f32[192,1024]{1,0:T(8,128)} %collective-permute-done.9, ...), kind=kLoop, calls=%fused_computation.45 | loop fusion | flops 1376256 | bytes 7077892 | tf_op jit(solution)/shard_map/add | solution.py:100
  271.4 6.8 %convolution_bitcast_fusion = f32[128,64,192]{2,1,0:T(8,128)} fusion(bf16[3,64,128,16]{1,0,3,2:T(4,128)(2,1)} %reshape.33, bf16[1,192,128,16]{1,3,0,2:T(8,128)(2,1)S(1)} %bitcast.47, bf16[1,192,128,16]{1,3,0,2:T(8,128)(2,1)} %bitcast.59, bf16[1,192,128,16]{1,3,0,2:T(8,128)(2,1)} %bitcast.56), kind=kOutput, calls=%fused_computation.11 | convolution fusion | flops 153354240 | bytes 9437184 | tf_op jit(solution)/shard_map/kigc,kjgc->gij/dot_general | solution.py:151
  278.2 8.6 %copy.53 = f32[128,64,192]{0,2,1:T(8,128)} copy(f32[128,64,192]{2,1,0:T(8,128)} %convolution_bitcast_fusion) | data formatting | bytes 12582912 | tf_op jit(solution)/shard_map/kigc,kjgc->gij/dot_general | solution.py:151
  288.5 4.9 %fusion.20 = f32[128,128]{1,0:T(8,128)S(1)} fusion(s32[128]{0:T(128)S(1)} %iota_add_fusion, s32[64]{0:T(128)S(1)} %iota_add_fusion.1, f32[128,64,192]{0,2,1:T(8,128)} %copy.53), kind=kOutput, calls=%fused_computation.38 | convolution fusion | flops 408944640 | bytes 6357760 | tf_op jit(solution)/shard_map/gij,ijs->gs/dot_general | solution.py:159
  299.2 6.9 %copy.69 = bf16[128,64,192,1]{2,1,3,0:T(8,128)(2,1)} copy(bf16[128,64,192,1]{0,2,1,3:T(8,128)(2,1)} %bitcast.49) | data formatting | bytes 6291456 | tf_op jit(solution)/shard_map/optimization_barrier | solution.py:126
  306.1 7.6 %copy.70 = bf16[128,64,192,1]{2,1,3,0:T(8,128)(2,1)} copy(bf16[128,64,192,1]{0,2,1,3:T(8,128)(2,1)S(1)} %bitcast.48) | data formatting | bytes 6291456 | tf_op jit(solution)/shard_map/optimization_barrier | solution.py:126
  330.7 6.0 %reshape.34 = f32[192,2048]{0,1:T(8,128)} reshape(f32[3,64,128,16]{1,0,3,2:T(4,128)} %copy.63) | data formatting | bytes 3145728 | tf_op jit(solution)/shard_map/reshape | solution.py:51
  (113 shorter events, 81.6 us)
Async XLA Ops:
  7.2 68.6 %all-gather.2.cloned.1.call-start = ((), (), s32[]{:S(2)}) async-start(), calls=%async_computation.1 | async-start | bytes 3932160 | tf_op jit(solution)/shard_map/all_gather | solution.py:125
  7.9 252.9 %reduce-scatter.2.cloned.1.call-start = ((), (), s32[]{:S(2)}) async-start(), calls=%async_computation.2 | async-start | bytes 7077888 | tf_op jit(solution)/shard_map/reduce_scatter | solution.py:132
  79.1 12.2 %collective-permute-start = (bf16[192,1024]{1,0:T(8,128)(2,1)}, bf16[192,1024]{1,0:T(8,128)(2,1)}, u32[]{:S(2)}, u32[]{:S(2)}) collective-permute-start(bf16[192,1024]{1,0:T(8,128)(2,1)} %get-tuple-element.53), channel_id=1, source_target_pairs={{0,4},{4,8},{8,12},{12,16},{16,20},{20,24},{24,28},{28,0},{1,5},{5... | collective-permute-start | bytes 1179656 | tf_op jit(solution)/shard_map/ppermute | solution.py:64
  79.1 14.6 %collective-permute-start.1 = (bf16[192,1024]{1,0:T(8,128)(2,1)}, bf16[192,1024]{1,0:T(8,128)(2,1)}, u32[]{:S(2)}, u32[]{:S(2)}) collective-permute-start(bf16[192,1024]{1,0:T(8,128)(2,1)} %get-tuple-element.52), channel_id=1, source_target_pairs={{0,8},{4,12},{8,16},{12,20},{16,24},{20,28},{24,0},{28,4},{1,9},{5... | collective-permute-start | bytes 1179656 | tf_op jit(solution)/shard_map/ppermute | solution.py:64
  80.6 27.9 %collective-permute-start.2 = (bf16[192,1024]{1,0:T(8,128)(2,1)}, bf16[192,1024]{1,0:T(8,128)(2,1)}, u32[]{:S(2)}, u32[]{:S(2)}) collective-permute-start(bf16[192,1024]{1,0:T(8,128)(2,1)} %get-tuple-element.51), channel_id=1, source_target_pairs={{0,12},{4,16},{8,20},{12,24},{16,28},{20,0},{24,4},{28,8},{1,13},{... | collective-permute-start | bytes 1179656 | tf_op jit(solution)/shard_map/ppermute | solution.py:64
  82.9 26.6 %collective-permute-start.3 = (bf16[192,1024]{1,0:T(8,128)(2,1)}, bf16[192,1024]{1,0:T(8,128)(2,1)}, u32[]{:S(2)}, u32[]{:S(2)}) collective-permute-start(bf16[192,1024]{1,0:T(8,128)(2,1)} %get-tuple-element.50), channel_id=1, source_target_pairs={{0,16},{4,20},{8,24},{12,28},{16,0},{20,4},{24,8},{28,12},{1,17},{... | collective-permute-start | bytes 1179656 | tf_op jit(solution)/shard_map/ppermute | solution.py:64
  83.5 32.5 %collective-permute-start.4 = (bf16[192,1024]{1,0:T(8,128)(2,1)}, bf16[192,1024]{1,0:T(8,128)(2,1)S(1)}, u32[]{:S(2)}, u32[]{:S(2)}) collective-permute-start(bf16[192,1024]{1,0:T(8,128)(2,1)} %get-tuple-element.49), channel_id=1, source_target_pairs={{0,20},{4,24},{8,28},{12,0},{16,4},{20,8},{24,12},{28,16},{1,21},{... | collective-permute-start | bytes 1179656 | tf_op jit(solution)/shard_map/ppermute | solution.py:64
  91.3 24.8 %collective-permute-start.5 = (bf16[192,1024]{1,0:T(8,128)(2,1)}, bf16[192,1024]{1,0:T(8,128)(2,1)S(1)}, u32[]{:S(2)}, u32[]{:S(2)}) collective-permute-start(bf16[192,1024]{1,0:T(8,128)(2,1)} %get-tuple-element.48), channel_id=1, source_target_pairs={{0,24},{4,28},{8,0},{12,4},{16,8},{20,12},{24,16},{28,20},{1,25},{... | collective-permute-start | bytes 1179656 | tf_op jit(solution)/shard_map/ppermute | solution.py:64
  93.7 22.4 %collective-permute-start.6 = (bf16[192,1024]{1,0:T(8,128)(2,1)S(1)}, bf16[192,1024]{1,0:T(8,128)(2,1)S(1)}, u32[]{:S(2)}, u32[]{:S(2)}) collective-permute-start(bf16[192,1024]{1,0:T(8,128)(2,1)S(1)} %get-tuple-element.47), channel_id=1, source_target_pairs={{0,28},{4,0},{8,4},{12,8},{16,12},{20,16},{24,20},{28,24},{1,29},{... | collective-permute-start | bytes 1179656 | tf_op jit(solution)/shard_map/ppermute | solution.py:64
  141.1 12.4 %collective-permute-start.14 = (bf16[128,2048]{0,1:T(8,128)(2,1)S(1)}, bf16[128,2048]{0,1:T(8,128)(2,1)S(1)}, u32[]{:S(2)}, u32[]{:S(2)}) collective-permute-start(bf16[128,2048]{0,1:T(8,128)(2,1)S(1)} %slice.54), channel_id=1, source_target_pairs={{0,4},{4,8},{8,12},{12,16},{16,20},{20,24},{24,28},{1,5},{5,9},{9,... | collective-permute-start | bytes 1572872 | tf_op jit(solution)/shard_map/ppermute | solution.py:141
  150.9 25.2 %collective-permute-start.13 = (f32[192,1024]{1,0:T(8,128)}, f32[192,1024]{1,0:T(8,128)}, u32[]{:S(2)}, u32[]{:S(2)}) collective-permute-start(f32[192,1024]{1,0:T(8,128)} %get-tuple-element.37), channel_id=1, source_target_pairs={{0,28},{4,0},{8,4},{12,8},{16,12},{20,16},{24,20},{28,24},{1,29},{... | collective-permute-start | bytes 2359304 | tf_op jit(solution)/shard_map/ppermute | solution.py:100
  151.3 53.8 %collective-permute-start.12 = (f32[192,1024]{1,0:T(8,128)}, f32[192,1024]{1,0:T(8,128)}, u32[]{:S(2)}, u32[]{:S(2)}) collective-permute-start(f32[192,1024]{1,0:T(8,128)} %get-tuple-element.38), channel_id=1, source_target_pairs={{0,24},{4,28},{8,0},{12,4},{16,8},{20,12},{24,16},{28,20},{1,25},{... | collective-permute-start | bytes 2359304 | tf_op jit(solution)/shard_map/ppermute | solution.py:100
  154.2 62.7 %copy-start.9 = (bf16[192,2048]{0,1:T(8,128)(2,1)}, bf16[192,2048]{0,1:T(8,128)(2,1)S(1)}, u32[]{:S(2)}) copy-start(bf16[192,2048]{0,1:T(8,128)(2,1)S(1)} %get-tuple-element.59) | copy-start | bytes 2359300
  161.6 68.2 %collective-permute-start.11 = (f32[192,1024]{1,0:T(8,128)}, f32[192,1024]{1,0:T(8,128)}, u32[]{:S(2)}, u32[]{:S(2)}) collective-permute-start(f32[192,1024]{1,0:T(8,128)} %get-tuple-element.39), channel_id=1, source_target_pairs={{0,20},{4,24},{8,28},{12,0},{16,4},{20,8},{24,12},{28,16},{1,21},{... | collective-permute-start | bytes 2359304 | tf_op jit(solution)/shard_map/ppermute | solution.py:100
  161.6 93.3 %collective-permute-start.10 = (f32[192,1024]{1,0:T(8,128)}, f32[192,1024]{1,0:T(8,128)}, u32[]{:S(2)}, u32[]{:S(2)}) collective-permute-start(f32[192,1024]{1,0:T(8,128)} %get-tuple-element.40), channel_id=1, source_target_pairs={{0,16},{4,20},{8,24},{12,28},{16,0},{20,4},{24,8},{28,12},{1,17},{... | collective-permute-start | bytes 2359304 | tf_op jit(solution)/shard_map/ppermute | solution.py:100
  162.4 93.9 %collective-permute-start.9 = (f32[192,1024]{1,0:T(8,128)}, f32[192,1024]{1,0:T(8,128)}, u32[]{:S(2)}, u32[]{:S(2)}) collective-permute-start(f32[192,1024]{1,0:T(8,128)} %get-tuple-element.41), channel_id=1, source_target_pairs={{0,12},{4,16},{8,20},{12,24},{16,28},{20,0},{24,4},{28,8},{1,13},{... | collective-permute-start | bytes 2359304 | tf_op jit(solution)/shard_map/ppermute | solution.py:100
  176.1 80.2 %collective-permute-start.8 = (f32[192,1024]{1,0:T(8,128)}, f32[192,1024]{1,0:T(8,128)}, u32[]{:S(2)}, u32[]{:S(2)}) collective-permute-start(f32[192,1024]{1,0:T(8,128)} %get-tuple-element.42), channel_id=1, source_target_pairs={{0,8},{4,12},{8,16},{12,20},{16,24},{20,28},{24,0},{28,4},{1,9},{5... | collective-permute-start | bytes 2359304 | tf_op jit(solution)/shard_map/ppermute | solution.py:100
  205.1 51.2 %collective-permute-start.7 = (f32[192,1024]{1,0:T(8,128)}, f32[192,1024]{1,0:T(8,128)}, u32[]{:S(2)}, u32[]{:S(2)}) collective-permute-start(f32[192,1024]{1,0:T(8,128)} %get-tuple-element.36), channel_id=1, source_target_pairs={{0,4},{4,8},{8,12},{12,16},{16,20},{20,24},{24,28},{28,0},{1,5},{5... | collective-permute-start | bytes 2359304 | tf_op jit(solution)/shard_map/ppermute | solution.py:100
  286.8 9.1 %collective-permute-start.15 = (bf16[128,2048]{1,0:T(8,128)(2,1)S(1)}, bf16[128,2048]{1,0:T(8,128)(2,1)S(1)}, u32[]{:S(2)}, u32[]{:S(2)}) collective-permute-start(bf16[128,2048]{1,0:T(8,128)(2,1)S(1)} %slice.57), channel_id=1, source_target_pairs={{4,0},{8,4},{12,8},{16,12},{20,16},{24,20},{28,24},{5,1},{9,5},{13... | collective-permute-start | bytes 1572872 | tf_op jit(solution)/shard_map/ppermute | solution.py:148
  296.7 2.0 collective-permute-start.16
  298.7 15.0 %collective-permute-start.17 = (f32[128,128]{1,0:T(8,128)S(1)}, f32[128,128]{1,0:T(8,128)S(1)}, u32[]{:S(2)}, u32[]{:S(2)}) collective-permute-start(f32[128,128]{1,0:T(8,128)S(1)} %add.260), channel_id=1, source_target_pairs={{0,8},{4,12},{8,0},{12,4},{16,24},{20,28},{24,16},{28,20},{1,9},{5... | collective-permute-start | bytes 196616 | tf_op jit(solution)/shard_map/ppermute | solution.py:75
  313.7 5.1 %collective-permute-start.18 = (f32[128,128]{1,0:T(8,128)S(1)}, f32[128,128]{1,0:T(8,128)S(1)}, u32[]{:S(2)}, u32[]{:S(2)}) collective-permute-start(f32[128,128]{1,0:T(8,128)S(1)} %add.261), channel_id=1, source_target_pairs={{0,16},{4,20},{8,24},{12,28},{16,0},{20,4},{24,8},{28,12},{1,17},{... | collective-permute-start | bytes 196616 | tf_op jit(solution)/shard_map/ppermute | solution.py:75
  318.9 4.3 %collective-permute-start.19 = (f32[128,128]{1,0:T(8,128)S(1)}, f32[128,128]{1,0:T(8,128)S(1)}, u32[]{:S(2)}, u32[]{:S(2)}) collective-permute-start(f32[128,128]{1,0:T(8,128)S(1)} %add_multiply_fusion), channel_id=1, source_target_pairs={{0,1},{1,0},{2,3},{3,2},{4,5},{5,4},{6,7},{7,6},{8,9},{9,8},{10,11... | collective-permute-start | bytes 196616 | tf_op jit(solution)/shard_map/ppermute | solution.py:86
  323.2 13.5 %collective-permute-start.20 = (f32[256,128]{1,0:T(8,128)S(1)}, f32[256,128]{1,0:T(8,128)S(1)}, u32[]{:S(2)}, u32[]{:S(2)}) collective-permute-start(f32[256,128]{1,0:T(8,128)S(1)} %maximum_select_fusion.1), channel_id=1, source_target_pairs={{0,2},{1,3},{2,0},{3,1},{4,6},{5,7},{6,4},{7,5},{8,10},{9,11},{10,... | collective-permute-start | bytes 393224 | tf_op jit(solution)/shard_map/ppermute | solution.py:86
  (15 other events, 179.0 us)
Sparse Core Ops, SparseCore 0:
  9.6 66.1 all-gather.1
  137.4 119.9 reduce-scatter.1

commit v12 on v10

--- a/solution.py
+++ b/solution.py
@@ -40,15 +40,11 @@
     return jnp.stack([x[k * block : k * block + width] for k in range(tiles)])
 
 
-def filter_apply(mats, wins, groups, per_group):
+def filter_apply(mat, wins, groups, per_group):
     tiles, width, chans = wins.shape
-    w4 = wins.reshape(tiles, width, groups, per_group)
-    total = None
-    for m in mats:
-        part = jnp.einsum("gij,kjgc->kigc", m, w4, preferred_element_type=jnp.float32)
-        total = part if total is None else total + part
-    block = mats[0].shape[1]
-    return total.reshape(tiles * block, chans)
+    w4 = jnp.concatenate([wins, wins], 1).reshape(tiles, 2 * width, groups, per_group)
+    total = jnp.einsum("gij,kjgc->kigc", mat, w4, preferred_element_type=jnp.float32)
+    return total.reshape(tiles * mat.shape[1], chans)
 
 
 def exchange_columns(x, count):
@@ -112,6 +108,8 @@
     mats_anti = toeplitz_mats(taps, block, width, halo, False, zero)
 
     cot_rows = lax.all_gather(cotangent, "mp", axis=1, tiled=True)
+    mats_causal = jnp.concatenate(mats_causal, 2)
+    mats_anti = jnp.concatenate(mats_anti, 2)
     cot_rows, mats_causal, mats_anti = lax.optimization_barrier((cot_rows, mats_causal, mats_anti))
     cot_cols = exchange_columns(cot_rows, ctx_count)
     partial = contract(cot_cols, out_weight)

time: 308 us -> 319 us (1.036)
  other arithmetic: 12.7 us -> 23.5 us
  matrix products: 36.8 us -> 40 us
    concatenate x1 -> x3, other arithmetic: 2.44 us -> 14.4 us  [the longest x2 9.15 us: filter_apply(): jnp.concatenate([wins, wins], 1)]
    optimization_barrier x4 -> x2, local copies, waits for them, and re-layouts: 28.5 us -> 18.2 us  [body(): lax.optimization_barrier((cot_rows, mats_causal, mats_anti))]
    transpose x0 -> x2, local copies, waits for them, and re-layouts: none -> 7.54 us  [filter_apply(): jnp.einsum('gij,kjgc->kigc', mat, w4, preferred_element_type=jnp.float32)]
    add x2 -> x0, local copies, waits for them, and re-layouts: 7.46 us -> none  [filter_apply(): total = part if total is None else total + part]
    concatenate x0 -> x1, local copies, waits for them, and re-layouts: none -> 6.67 us  [filter_apply(): jnp.concatenate([wins, wins], 1)]
    ppermute x3, waiting for transfers between devices: 0.91 us -> 4.88 us  [butterfly_sum(): x = x + lax.ppermute(x, axis, [(k, k ^ step) for k in range(count)])]
    all_gather x1, waiting for transfers between devices: 57.9 us -> 54.2 us  [body(): cot_rows = lax.all_gather(cotangent, 'mp', axis=1, tiled=True)]
    dot_general x4 -> x2, matrix products: 9.89 us -> 13.5 us  [filter_apply(): jnp.einsum('gij,kjgc->kigc', mat, w4, preferred_element_type=jnp.float32)]
  transfers between devices with their start and end apart: 16 -> 16, of which waited for: 7 -> 8; matrix products, arithmetic and copies ran while one was open for 28% -> 30% of each run, Pallas kernels for 0% -> 0%
where the time goes in v12:
time: 319 us; the launch traced here: 318 us
  waiting for transfers between devices  132 us (41%)
  local copies, waits for them, and re-layouts  81 us (25%)
  matrix products  40 us (13%)
  starting transfers between devices  26.5 us (8%)
  other arithmetic  23.5 us (7%)
  between operations  14.5 us (5%)
    all_gather x1, waiting for transfers between devices, body(): cot_rows = lax.all_gather(cotangent, 'mp', axis=1, tiled=True)  54.2 us
    reduce_scatter x1, waiting for transfers between devices, body(): lax.psum_scatter(partial, 'ctx', scatter_dimension=0, tiled=True)  50.9 us
    ppermute x7, waiting for transfers between devices, exchange_columns(): lax.ppermute(chunk, 'ctx', [(k, (k + shift) % count) for k in range(count)])  19.9 us
    optimization_barrier x2, local copies, waits for them, and re-layouts, body(): lax.optimization_barrier((cot_rows, mats_causal, mats_anti))  18.2 us
    dot_general x2, matrix products, filter_apply(): jnp.einsum('gij,kjgc->kigc', mat, w4, preferred_element_type=jnp.float32)  13.5 us
    ppermute x7, starting transfers between devices, exchange_columns(): lax.ppermute(chunk, 'ctx', [(k, (k + shift) % count) for k in range(count)])  12.8 us
    reshape x2, local copies, waits for them, and re-layouts, filter_apply(): return total.reshape(tiles * mat.shape[1], chans)  11.8 us
    unnamed x22, local copies, waits for them, and re-layouts  9.21 us
  transfers between devices with their start and end apart: 16, of which 8 were waited for; matrix products, arithmetic and copies ran while one was open for 30% of the time, Pallas kernels for 0%

profile of v12, /device:TPU:0, one launch (start us, length us, event | category | flops | bytes accessed | tf_op | source)
XLA Modules:
  0.0 317.5 jit_solution(11037647296584154133)
XLA Ops:
  16.3 5.3 %pad_maximum_fusion = (bf16[128,64,384]{0,2,1:T(8,128)(2,1)}, bf16[128,64,384]{0,2,1:T(8,128)(2,1)}) fusion(bf16[128,64,192]{0,2,1:T(8,128)(2,1)S(1)} %get-tuple-element.33, bf16[128,64,192]{0,2,1:T(8,128)(2,1)S(1)} %get-tuple-element.32, bf16[128,64,192]{0,2,1:T(8,128)(2,1)S(1)} %get-tuple-element.31, bf16[128,64,192]{0,2,1:T(8,128)(2,1)S(1)} %get-tuple-element.30), kind=kLoop, calls=%fused_computation.3 | loop fusion | flops 25165824 | bytes 25165824 | tf_op jit(solution)/shard_map/concatenate | solution.py:111
  21.6 54.2 %all-gather.2.cloned.1.call-done = bf16[192,8192]{1,0:T(8,128)(2,1)} async-done(((bf16[192,2048]{1,0:T(8,128)(2,1)}), bf16[192,8192]{1,0:T(8,128)(2,1)}) %all-gather.2.cloned.1.call-update) | async-done | bytes 3145744 | tf_op jit(solution)/shard_map/all_gather | solution.py:110
  83.6 7.7 %collective-permute-done = bf16[192,1024]{1,0:T(8,128)(2,1)} collective-permute-done((bf16[192,1024]{1,0:T(8,128)(2,1)}, bf16[192,1024]{1,0:T(8,128)(2,1)}, u32[]{:S(2)}, u32[]{:S(2)}) %collective-permute-start) | collective-permute-done | bytes 393248 | tf_op jit(solution)/shard_map/ppermute | solution.py:60
  93.7 7.0 %collective-permute-start.6 = (bf16[192,1024]{1,0:T(8,128)(2,1)S(1)}, bf16[192,1024]{1,0:T(8,128)(2,1)S(1)}, u32[]{:S(2)}, u32[]{:S(2)}) collective-permute-start(bf16[192,1024]{1,0:T(8,128)(2,1)S(1)} %get-tuple-element.34), channel_id=1, source_target_pairs={{0,28},{4,0},{8,4},{12,8},{16,12},{20,16},{24,20},{28,24},{1,29},{... | collective-permute-start | bytes 1179656 | tf_op jit(solution)/shard_map/ppermute | solution.py:60
  101.8 6.8 %collective-permute-done.2 = bf16[192,1024]{1,0:T(8,128)(2,1)} collective-permute-done((bf16[192,1024]{1,0:T(8,128)(2,1)}, bf16[192,1024]{1,0:T(8,128)(2,1)}, u32[]{:S(2)}, u32[]{:S(2)}) %collective-permute-start.2) | collective-permute-done | bytes 393248 | tf_op jit(solution)/shard_map/ppermute | solution.py:60
  110.6 5.4 %collective-permute-done.4 = bf16[192,1024]{1,0:T(8,128)(2,1)S(1)} collective-permute-done((bf16[192,1024]{1,0:T(8,128)(2,1)}, bf16[192,1024]{1,0:T(8,128)(2,1)S(1)}, u32[]{:S(2)}, u32[]{:S(2)}) %collective-permute-start.4) | collective-permute-done | bytes 393248 | tf_op jit(solution)/shard_map/ppermute | solution.py:60
  116.2 9.2 %fusion.51 = f32[1536,2048]{1,0:T(8,128)} fusion(bf16[1536,1024]{1,0:T(8,128)(2,1)S(1)} %constant_dynamic-update-slice_fusion, bf16[2048,1024]{1,0:T(8,128)(2,1)S(1)} %copy-done.8), kind=kOutput, calls=%fused_computation.85 | convolution fusion | flops 6442450944 | bytes 19922944 | tf_op jit(solution)/shard_map/dot_general | solution.py:8
  129.2 3.9 %collective-permute-start.7 = (bf16[128,2048]{0,1:T(8,128)(2,1)S(1)}, bf16[128,2048]{0,1:T(8,128)(2,1)S(1)}, u32[]{:S(2)}, u32[]{:S(2)}) collective-permute-start(bf16[128,2048]{0,1:T(8,128)(2,1)S(1)} %slice.44), channel_id=1, source_target_pairs={{0,4},{4,8},{8,12},{12,16},{16,20},{20,24},{24,28},{1,5},{5,9},{9,... | collective-permute-start | bytes 1572872 | tf_op jit(solution)/shard_map/ppermute | solution.py:121
  136.1 4.7 %maximum_maximum_fusion = bf16[3,384,2048]{1,2,0:T(8,128)(2,1)} fusion(bf16[1,192,2048]{1,2,0:T(8,128)(2,1)S(1)} %bitcast.44, bf16[1,192,2048]{1,2,0:T(8,128)(2,1)S(1)} %bitcast.51, bf16[1,192,2048]{1,2,0:T(8,128)(2,1)S(1)} %bitcast.49), kind=kLoop, calls=%fused_computation.11 | loop fusion | flops 28311552 | bytes 7077888 | tf_op jit(solution)/shard_map/concatenate | solution.py:45
  140.8 9.2 %copy.52 = bf16[128,64,384,1]{2,1,3,0:T(8,128)(2,1)} copy(bf16[128,64,384,1]{0,2,1,3:T(8,128)(2,1)} %bitcast.43) | data formatting | bytes 12582912 | tf_op jit(solution)/shard_map/optimization_barrier | solution.py:113
  150.1 6.9 %fusion.27 = f32[3,64,128,16]{1,3,0,2:T(8,128)S(1)} fusion(bf16[128,64,384,1]{2,1,3,0:T(8,128)(2,1)} %copy.52, bf16[3,384,128,16]{1,3,2,0:T(8,128)(2,1)} %bitcast.47), kind=kOutput, calls=%fused_computation.38 | convolution fusion | flops 301989888 | bytes 12582912 | tf_op jit(solution)/shard_map/gij,kjgc->kigc/dot_general | solution.py:46
  157.0 3.8 %copy.40 = f32[3,64,128,16]{1,0,3,2:T(4,128)} copy(f32[3,64,128,16]{1,3,0,2:T(8,128)S(1)} %fusion.27) | data formatting | bytes 3145728 | tf_op jit(solution)/shard_map/gij,kjgc->kigc/transpose | solution.py:46
  160.8 5.8 %reshape.31 = f32[192,2048]{0,1:T(8,128)} reshape(f32[3,64,128,16]{1,0,3,2:T(4,128)} %copy.40) | data formatting | bytes 3145728 | tf_op jit(solution)/shard_map/reshape | solution.py:47
  166.6 50.9 %reduce-scatter.2.cloned.1.call-done = f32[192,2048]{1,0:T(8,128)} async-done(((f32[1536,2048]{1,0:T(8,128)}), f32[192,2048]{1,0:T(8,128)}) %reduce-scatter.2.cloned.1.call-update) | async-done | bytes 1572880 | tf_op jit(solution)/shard_map/reduce_scatter | solution.py:116
  225.0 5.0 %reshape.32 = bf16[3,64,128,16]{1,0,3,2:T(4,128)(2,1)} reshape(bf16[192,2048]{0,1:T(8,128)(2,1)} %copy.42) | data formatting | bytes 1572864 | tf_op jit(solution)/shard_map/reshape | solution.py:129
  230.0 6.4 %convolution_bitcast_fusion = f32[128,64,192]{2,1,0:T(8,128)} fusion(bf16[1,192,128,16]{1,3,0,2:T(8,128)(2,1)S(1)} %bitcast.45, bf16[1,192,128,16]{1,3,0,2:T(8,128)(2,1)} %bitcast.52, bf16[1,192,128,16]{1,3,0,2:T(8,128)(2,1)S(1)} %bitcast.50, bf16[3,64,128,16]{1,0,3,2:T(4,128)(2,1)} %reshape.32), kind=kOutput, calls=%fused_computation.19 | convolution fusion | flops 153354240 | bytes 9437184 | tf_op jit(solution)/shard_map/kigc,kjgc->gij/dot_general | solution.py:131
  236.4 8.6 %copy.44 = f32[128,64,192]{0,2,1:T(8,128)} copy(f32[128,64,192]{2,1,0:T(8,128)} %convolution_bitcast_fusion) | data formatting | bytes 12582912 | tf_op jit(solution)/shard_map/kigc,kjgc->gij/dot_general | solution.py:131
  246.8 4.9 %fusion.34 = f32[128,128]{1,0:T(8,128)S(1)} fusion(s32[128]{0:T(128)S(1)} %iota_add_fusion, s32[64]{0:T(128)S(1)} %iota_add_fusion.1, f32[128,64,192]{0,2,1:T(8,128)} %copy.44), kind=kOutput, calls=%fused_computation.47 | convolution fusion | flops 408944640 | bytes 6357760 | tf_op jit(solution)/shard_map/gij,ijs->gs/dot_general | solution.py:139
  258.8 9.0 %copy.54 = bf16[128,64,384,1]{2,1,3,0:T(8,128)(2,1)} copy(bf16[128,64,384,1]{0,2,1,3:T(8,128)(2,1)} %bitcast.42) | data formatting | bytes 12582912 | tf_op jit(solution)/shard_map/optimization_barrier | solution.py:113
  268.2 4.0 %collective-permute-done.11 = f32[128,128]{1,0:T(8,128)S(1)} collective-permute-done((f32[128,128]{1,0:T(8,128)S(1)}, f32[128,128]{1,0:T(8,128)S(1)}, u32[]{:S(2)}, u32[]{:S(2)}) %collective-permute-start.11) | collective-permute-done | bytes 65568 | tf_op jit(solution)/shard_map/ppermute | solution.py:71
  273.7 4.5 %maximum_maximum_fusion.1 = bf16[3,384,2048]{2,1,0:T(8,128)(2,1)} fusion(bf16[1,192,2048]{2,1,0:T(8,128)(2,1)S(1)} %get-tuple-element.49, bf16[1,192,2048]{2,1,0:T(8,128)(2,1)S(1)} %get-tuple-element.48, bf16[1,192,2048]{2,1,0:T(8,128)(2,1)S(1)} %bitcast.48), kind=kLoop, calls=%fused_computation.12 | loop fusion | flops 28311552 | bytes 7077888 | tf_op jit(solution)/shard_map/concatenate | solution.py:45
  278.2 6.7 %copy.46 = bf16[3,384,2048]{1,2,0:T(8,128)(2,1)} copy(bf16[3,384,2048]{2,1,0:T(8,128)(2,1)} %maximum_maximum_fusion.1) | data formatting | bytes 9437184 | tf_op jit(solution)/shard_map/concatenate | solution.py:45
  287.4 6.5 %fusion.30 = f32[3,64,128,16]{1,3,0,2:T(8,128)S(1)} fusion(bf16[128,64,384,1]{2,1,3,0:T(8,128)(2,1)} %copy.54, bf16[3,384,128,16]{1,3,2,0:T(8,128)(2,1)} %bitcast.46), kind=kOutput, calls=%fused_computation.39 | convolution fusion | flops 301989888 | bytes 12582912 | tf_op jit(solution)/shard_map/gij,kjgc->kigc/dot_general | solution.py:46
  297.7 6.0 %reshape.34 = f32[192,2048]{0,1:T(8,128)} reshape(f32[3,64,128,16]{1,0,3,2:T(4,128)} %copy.49) | data formatting | bytes 3145728 | tf_op jit(solution)/shard_map/reshape | solution.py:47
  (80 shorter events, 60.8 us)
Async XLA Ops:
  7.2 68.6 %all-gather.2.cloned.1.call-start = ((), (), s32[]{:S(2)}) async-start(), calls=%async_computation.1 | async-start | bytes 3932160 | tf_op jit(solution)/shard_map/all_gather | solution.py:110
  7.9 209.6 %reduce-scatter.2.cloned.1.call-start = ((), (), s32[]{:S(2)}) async-start(), calls=%async_computation.2 | async-start | bytes 14155776 | tf_op jit(solution)/shard_map/reduce_scatter | solution.py:116
  75.8 1.9 copy-start.6
  79.1 12.2 %collective-permute-start = (bf16[192,1024]{1,0:T(8,128)(2,1)}, bf16[192,1024]{1,0:T(8,128)(2,1)}, u32[]{:S(2)}, u32[]{:S(2)}) collective-permute-start(bf16[192,1024]{1,0:T(8,128)(2,1)} %get-tuple-element.40), channel_id=1, source_target_pairs={{0,4},{4,8},{8,12},{12,16},{16,20},{20,24},{24,28},{28,0},{1,5},{5... | collective-permute-start | bytes 1179656 | tf_op jit(solution)/shard_map/ppermute | solution.py:60
  79.1 14.6 %collective-permute-start.1 = (bf16[192,1024]{1,0:T(8,128)(2,1)}, bf16[192,1024]{1,0:T(8,128)(2,1)}, u32[]{:S(2)}, u32[]{:S(2)}) collective-permute-start(bf16[192,1024]{1,0:T(8,128)(2,1)} %get-tuple-element.39), channel_id=1, source_target_pairs={{0,8},{4,12},{8,16},{12,20},{16,24},{20,28},{24,0},{28,4},{1,9},{5... | collective-permute-start | bytes 1179656 | tf_op jit(solution)/shard_map/ppermute | solution.py:60
  80.6 27.9 %collective-permute-start.2 = (bf16[192,1024]{1,0:T(8,128)(2,1)}, bf16[192,1024]{1,0:T(8,128)(2,1)}, u32[]{:S(2)}, u32[]{:S(2)}) collective-permute-start(bf16[192,1024]{1,0:T(8,128)(2,1)} %get-tuple-element.38), channel_id=1, source_target_pairs={{0,12},{4,16},{8,20},{12,24},{16,28},{20,0},{24,4},{28,8},{1,13},{... | collective-permute-start | bytes 1179656 | tf_op jit(solution)/shard_map/ppermute | solution.py:60
  83.0 26.6 %collective-permute-start.3 = (bf16[192,1024]{1,0:T(8,128)(2,1)}, bf16[192,1024]{1,0:T(8,128)(2,1)}, u32[]{:S(2)}, u32[]{:S(2)}) collective-permute-start(bf16[192,1024]{1,0:T(8,128)(2,1)} %get-tuple-element.37), channel_id=1, source_target_pairs={{0,16},{4,20},{8,24},{12,28},{16,0},{20,4},{24,8},{28,12},{1,17},{... | collective-permute-start | bytes 1179656 | tf_op jit(solution)/shard_map/ppermute | solution.py:60
  83.5 32.7 %copy-start.8 = (bf16[2048,1024]{1,0:T(8,128)(2,1)S(1)}, bf16[2048,1024]{1,0:T(8,128)(2,1)}, u32[]{:S(2)}) copy-start(bf16[2048,1024]{1,0:T(8,128)(2,1)} %param.7) | copy-start | bytes 12582916
  83.5 32.5 %collective-permute-start.4 = (bf16[192,1024]{1,0:T(8,128)(2,1)}, bf16[192,1024]{1,0:T(8,128)(2,1)S(1)}, u32[]{:S(2)}, u32[]{:S(2)}) collective-permute-start(bf16[192,1024]{1,0:T(8,128)(2,1)} %get-tuple-element.36), channel_id=1, source_target_pairs={{0,20},{4,24},{8,28},{12,0},{16,4},{20,8},{24,12},{28,16},{1,21},{... | collective-permute-start | bytes 1179656 | tf_op jit(solution)/shard_map/ppermute | solution.py:60
  91.3 24.8 %collective-permute-start.5 = (bf16[192,1024]{1,0:T(8,128)(2,1)}, bf16[192,1024]{1,0:T(8,128)(2,1)S(1)}, u32[]{:S(2)}, u32[]{:S(2)}) collective-permute-start(bf16[192,1024]{1,0:T(8,128)(2,1)} %get-tuple-element.35), channel_id=1, source_target_pairs={{0,24},{4,28},{8,0},{12,4},{16,8},{20,12},{24,16},{28,20},{1,25},{... | collective-permute-start | bytes 1179656 | tf_op jit(solution)/shard_map/ppermute | solution.py:60
  93.7 22.4 %collective-permute-start.6 = (bf16[192,1024]{1,0:T(8,128)(2,1)S(1)}, bf16[192,1024]{1,0:T(8,128)(2,1)S(1)}, u32[]{:S(2)}, u32[]{:S(2)}) collective-permute-start(bf16[192,1024]{1,0:T(8,128)(2,1)S(1)} %get-tuple-element.34), channel_id=1, source_target_pairs={{0,28},{4,0},{8,4},{12,8},{16,12},{20,16},{24,20},{28,24},{1,29},{... | collective-permute-start | bytes 1179656 | tf_op jit(solution)/shard_map/ppermute | solution.py:60
  125.3 1.1 copy-start.7
  127.0 6.1 %copy-start.1 = (bf16[192,2048]{0,1:T(8,128)(2,1)}, bf16[192,2048]{0,1:T(8,128)(2,1)S(1)}, u32[]{:S(2)}) copy-start(bf16[192,2048]{0,1:T(8,128)(2,1)S(1)} %copy.36) | copy-start | bytes 2359300
  128.7 4.4 %copy-start.3 = (bf16[192,2048]{0,1:T(8,128)(2,1)}, bf16[192,2048]{0,1:T(8,128)(2,1)S(1)}, u32[]{:S(2)}) copy-start(bf16[192,2048]{0,1:T(8,128)(2,1)S(1)} %copy.37) | copy-start | bytes 2359300
  129.2 5.3 %collective-permute-start.7 = (bf16[128,2048]{0,1:T(8,128)(2,1)S(1)}, bf16[128,2048]{0,1:T(8,128)(2,1)S(1)}, u32[]{:S(2)}, u32[]{:S(2)}) collective-permute-start(bf16[128,2048]{0,1:T(8,128)(2,1)S(1)} %slice.44), channel_id=1, source_target_pairs={{0,4},{4,8},{8,12},{12,16},{16,20},{20,24},{24,28},{1,5},{5,9},{9,... | collective-permute-start | bytes 1572872 | tf_op jit(solution)/shard_map/ppermute | solution.py:121
  245.0 6.7 %copy-start.5 = (f32[128,64,192]{0,2,1:T(8,128)S(1)}, f32[128,64,192]{0,2,1:T(8,128)}, u32[]{:S(2)}) copy-start(f32[128,64,192]{0,2,1:T(8,128)} %copy.44) | copy-start | bytes 18874372
  245.0 9.1 %collective-permute-start.8 = (bf16[128,2048]{1,0:T(8,128)(2,1)S(1)}, bf16[128,2048]{1,0:T(8,128)(2,1)S(1)}, u32[]{:S(2)}, u32[]{:S(2)}) collective-permute-start(bf16[128,2048]{1,0:T(8,128)(2,1)S(1)} %slice.47), channel_id=1, source_target_pairs={{4,0},{8,4},{12,8},{16,12},{20,16},{24,20},{28,24},{5,1},{9,5},{13... | collective-permute-start | bytes 1572872 | tf_op jit(solution)/shard_map/ppermute | solution.py:128
  254.2 2.5 collective-permute-start.9
  256.7 11.2 %collective-permute-start.10 = (f32[128,128]{1,0:T(8,128)S(1)}, f32[128,128]{1,0:T(8,128)S(1)}, u32[]{:S(2)}, u32[]{:S(2)}) collective-permute-start(f32[128,128]{1,0:T(8,128)S(1)} %add.196), channel_id=1, source_target_pairs={{0,8},{4,12},{8,0},{12,4},{16,24},{20,28},{24,16},{28,20},{1,9},{5... | collective-permute-start | bytes 196616 | tf_op jit(solution)/shard_map/ppermute | solution.py:71
  267.9 4.3 %collective-permute-start.11 = (f32[128,128]{1,0:T(8,128)S(1)}, f32[128,128]{1,0:T(8,128)S(1)}, u32[]{:S(2)}, u32[]{:S(2)}) collective-permute-start(f32[128,128]{1,0:T(8,128)S(1)} %add.197), channel_id=1, source_target_pairs={{0,16},{4,20},{8,24},{12,28},{16,0},{20,4},{24,8},{28,12},{1,17},{... | collective-permute-start | bytes 196616 | tf_op jit(solution)/shard_map/ppermute | solution.py:71
  272.2 12.7 %collective-permute-start.12 = (f32[128,128]{1,0:T(8,128)S(1)}, f32[128,128]{1,0:T(8,128)S(1)}, u32[]{:S(2)}, u32[]{:S(2)}) collective-permute-start(f32[128,128]{1,0:T(8,128)S(1)} %add_multiply_fusion), channel_id=1, source_target_pairs={{0,1},{1,0},{2,3},{3,2},{4,5},{5,4},{6,7},{7,6},{8,9},{9,8},{10,11... | collective-permute-start | bytes 196616 | tf_op jit(solution)/shard_map/ppermute | solution.py:82
  284.9 18.7 %collective-permute-start.13 = (f32[256,128]{1,0:T(8,128)S(1)}, f32[256,128]{1,0:T(8,128)S(1)}, u32[]{:S(2)}, u32[]{:S(2)}) collective-permute-start(f32[256,128]{1,0:T(8,128)S(1)} %maximum_select_fusion.1), channel_id=1, source_target_pairs={{0,2},{1,3},{2,0},{3,1},{4,6},{5,7},{6,4},{7,5},{8,10},{9,11},{10,... | collective-permute-start | bytes 393224 | tf_op jit(solution)/shard_map/ppermute | solution.py:82
  297.6 6.7 %copy-start.2 = (bf16[192,2048]{0,1:T(8,128)(2,1)S(1)}, bf16[192,2048]{0,1:T(8,128)(2,1)}, u32[]{:S(2)}) copy-start(bf16[192,2048]{0,1:T(8,128)(2,1)} %copy-done.1) | copy-start | bytes 2359300
  297.6 6.7 %copy-start.4 = (bf16[192,2048]{0,1:T(8,128)(2,1)S(1)}, bf16[192,2048]{0,1:T(8,128)(2,1)}, u32[]{:S(2)}) copy-start(bf16[192,2048]{0,1:T(8,128)(2,1)} %copy-done.3) | copy-start | bytes 2359300
  (1 other events, 1.0 us)
Sparse Core Ops, SparseCore 0:
  9.6 66.1 all-gather.1
  125.5 91.9 reduce-scatter.1

commit v13 on v10

--- a/solution.py
+++ b/solution.py
@@ -98,7 +98,7 @@
     per_group = chans * mp_count // groups
     local_groups = chans // per_group
     halo = flen
-    block = 64 if rows % 64 == 0 else rows
+    block = 32 if rows % 32 == 0 else rows
     tiles = rows // block
     width = block + halo
 

time: 308 us -> 315 us (1.023)
  waiting for transfers between devices: 134 us -> 122 us
  local copies, waits for them, and re-layouts: 82.6 us -> 90.1 us
  starting transfers between devices: 26.4 us -> 32.5 us
  matrix products: 36.8 us -> 41.8 us
    reduce_scatter x1, waiting for transfers between devices: 53.1 us -> 33.8 us  [body(): lax.psum_scatter(partial, 'ctx', scatter_dimension=0, tiled=True)]
    optimization_barrier x4, local copies, waits for them, and re-layouts: 28.5 us -> 13.8 us  [body(): lax.optimization_barrier((cot_rows, mats_causal, mats_anti))]
    dot_general x4, matrix products: 9.89 us -> 21.7 us  [filter_apply(): jnp.einsum('gij,kjgc->kigc', m, w4, preferred_element_type=jnp.float32)]
    unnamed x38 -> x40, local copies, waits for them, and re-layouts: 9.3 us -> 19.8 us
    add x2, local copies, waits for them, and re-layouts: 7.46 us -> 15.4 us  [filter_apply(): total = part if total is None else total + part]
    ppermute x3, starting transfers between devices: 3.84 us -> 9.97 us  [butterfly_sum(): x = x + lax.ppermute(x, axis, [(k, k ^ step) for k in range(count)])]
    dot_general x2, matrix products: 7.33 us -> 1.99 us  [body(): jnp.einsum('gij,ijs->gs', piece.astype(jnp.bfloat16), pick, preferred_ele...]
    dot_general x1, local copies, waits for them, and re-layouts: 8.58 us -> 3.61 us  [body(): jnp.einsum('kigc,kjgc->gij', gc4, wp4, preferred_element_type=jnp.float32)]
  transfers between devices with their start and end apart: 16 -> 16, of which waited for: 7 -> 9; matrix products, arithmetic and copies ran while one was open for 28% -> 33% of each run, Pallas kernels for 0% -> 0%
where the time goes in v13:
time: 315 us; the launch traced here: 314 us
  waiting for transfers between devices  122 us (39%)
  local copies, waits for them, and re-layouts  90.1 us (29%)
  matrix products  41.8 us (13%)
  starting transfers between devices  32.5 us (10%)
  between operations  14.6 us (5%)
  other arithmetic  13.6 us (4%)
    all_gather x1, waiting for transfers between devices, body(): cot_rows = lax.all_gather(cotangent, 'mp', axis=1, tiled=True)  62.1 us
    reduce_scatter x1, waiting for transfers between devices, body(): lax.psum_scatter(partial, 'ctx', scatter_dimension=0, tiled=True)  33.8 us
    dot_general x4, matrix products, filter_apply(): jnp.einsum('gij,kjgc->kigc', m, w4, preferred_element_type=jnp.float32)  21.7 us
    ppermute x7, waiting for transfers between devices, exchange_columns(): lax.ppermute(chunk, 'ctx', [(k, (k + shift) % count) for k in range(count)])  19.9 us
    unnamed x40, local copies, waits for them, and re-layouts  19.8 us
    add x2, local copies, waits for them, and re-layouts, filter_apply(): total = part if total is None else total + part  15.4 us
    optimization_barrier x4, local copies, waits for them, and re-layouts, body(): lax.optimization_barrier((cot_rows, mats_causal, mats_anti))  13.8 us
    reshape x2, local copies, waits for them, and re-layouts, filter_apply(): return total.reshape(tiles * block, chans)  13.1 us
  transfers between devices with their start and end apart: 16, of which 9 were waited for; matrix products, arithmetic and copies ran while one was open for 33% of the time, Pallas kernels for 0%

profile of v13, /device:TPU:0, one launch (start us, length us, event | category | flops | bytes accessed | tf_op | source)
XLA Modules:
  0.0 314.4 jit_solution(15251292723391733093)
XLA Ops:
  13.6 62.1 %all-gather.2.cloned.1.call-done = bf16[192,8192]{1,0:T(8,128)(2,1)} async-done(((bf16[192,2048]{1,0:T(8,128)(2,1)}), bf16[192,8192]{1,0:T(8,128)(2,1)}) %all-gather.2.cloned.1.call-update) | async-done | bytes 3145744 | tf_op jit(solution)/shard_map/all_gather | solution.py:114
  83.6 7.7 %collective-permute-done = bf16[192,1024]{1,0:T(8,128)(2,1)} collective-permute-done((bf16[192,1024]{1,0:T(8,128)(2,1)}, bf16[192,1024]{1,0:T(8,128)(2,1)}, u32[]{:S(2)}, u32[]{:S(2)}) %collective-permute-start) | collective-permute-done | bytes 393248 | tf_op jit(solution)/shard_map/ppermute | solution.py:64
  93.9 6.9 %collective-permute-start.6 = (bf16[192,1024]{1,0:T(8,128)(2,1)S(1)}, bf16[192,1024]{1,0:T(8,128)(2,1)S(1)}, u32[]{:S(2)}, u32[]{:S(2)}) collective-permute-start(bf16[192,1024]{1,0:T(8,128)(2,1)S(1)} %get-tuple-element.34), channel_id=1, source_target_pairs={{0,28},{4,0},{8,4},{12,8},{16,12},{20,16},{24,20},{28,24},{1,29},{... | collective-permute-start | bytes 1179656 | tf_op jit(solution)/shard_map/ppermute | solution.py:64
  101.7 6.8 %collective-permute-done.2 = bf16[192,1024]{1,0:T(8,128)(2,1)} collective-permute-done((bf16[192,1024]{1,0:T(8,128)(2,1)}, bf16[192,1024]{1,0:T(8,128)(2,1)}, u32[]{:S(2)}, u32[]{:S(2)}) %collective-permute-start.2) | collective-permute-done | bytes 393248 | tf_op jit(solution)/shard_map/ppermute | solution.py:64
  110.6 5.4 %collective-permute-done.4 = bf16[192,1024]{1,0:T(8,128)(2,1)S(1)} collective-permute-done((bf16[192,1024]{1,0:T(8,128)(2,1)}, bf16[192,1024]{1,0:T(8,128)(2,1)S(1)}, u32[]{:S(2)}, u32[]{:S(2)}) %collective-permute-start.4) | collective-permute-done | bytes 393248 | tf_op jit(solution)/shard_map/ppermute | solution.py:64
  116.2 9.2 %fusion.41 = f32[1536,2048]{1,0:T(8,128)} fusion(bf16[1536,1024]{1,0:T(8,128)(2,1)S(1)} %constant_dynamic-update-slice_fusion.12, bf16[2048,1024]{1,0:T(8,128)(2,1)S(1)} %copy-done.10), kind=kOutput, calls=%fused_computation.94 | convolution fusion | flops 6442450944 | bytes 19922944 | tf_op jit(solution)/shard_map/dot_general | solution.py:8
  130.0 4.5 %collective-permute-start.7 = (bf16[128,2048]{0,1:T(8,128)(2,1)}, bf16[128,2048]{0,1:T(8,128)(2,1)}, u32[]{:S(2)}, u32[]{:S(2)}) collective-permute-start(bf16[128,2048]{0,1:T(8,128)(2,1)} %slice.76), channel_id=1, source_target_pairs={{0,4},{4,8},{8,12},{12,16},{16,20},{20,24},{24,28},{1,5},{5,9},{9,... | collective-permute-start | bytes 1572872 | tf_op jit(solution)/shard_map/ppermute | solution.py:123
  136.3 3.9 %pad_maximum_fusion = (bf16[160,2048]{0,1:T(8,128)(2,1)S(1)}, bf16[160,2048]{0,1:T(8,128)(2,1)S(1)}, bf16[160,2048]{0,1:T(8,128)(2,1)S(1)}, bf16[160,2048]{0,1:T...) fusion(bf16[192,2048]{0,1:T(8,128)(2,1)S(1)} %fusion.11, ...), kind=kLoop, calls=%fused_computation.49 | loop fusion | flops 5242880 | bytes 7602176 | tf_op jit(solution)/shard_map/concatenate | solution.py:124
  147.1 3.3 %copy.84 = bf16[128,32,160,1]{2,1,3,0:T(8,128)(2,1)S(1)} copy(bf16[128,32,160,1]{0,2,1,3:T(8,128)(2,1)} %bitcast.67) | data formatting | bytes 2621440 | tf_op jit(solution)/shard_map/optimization_barrier | solution.py:115
  153.4 5.0 %fusion.42 = f32[128,6,16,32]{3,2,1,0:T(8,128)S(1)} fusion(bf16[6,160,128,16]{1,3,0,2:T(8,128)(2,1)} %constant_dynamic-update-slice_fusion, bf16[128,32,160,1]{2,1,3,0:T(8,128)(2,1)S(1)} %copy.84), kind=kOutput, calls=%fused_computation.95 | convolution fusion | flops 125829120 | bytes 6815744 | tf_op jit(solution)/shard_map/gij,kjgc->kigc/dot_general | solution.py:48
  158.4 5.2 %add_bitcast_fusion.1 = f32[6,32,128,16]{1,3,0,2:T(8,128)S(1)} fusion(f32[128,6,16,32]{3,2,1,0:T(8,128)S(1)} %fusion.42, bf16[6,160,128,16]{1,3,0,2:T(8,128)(2,1)} %constant_dynamic-update-slice_fusion, bf16[128,32,160,1]{2,1,3,0:T(8,128)(2,1)} %copy.85), kind=kOutput, calls=%fused_computation.1 | convolution fusion | flops 126222336 | bytes 8388608 | tf_op jit(solution)/shard_map/gij,kjgc->kigc/dot_general | solution.py:48
  163.6 6.3 %copy.61 = f32[6,32,128,16]{1,0,3,2:T(8,128)} copy(f32[6,32,128,16]{1,3,0,2:T(8,128)S(1)} %add_bitcast_fusion.1) | data formatting | bytes 3145728 | tf_op jit(solution)/shard_map/add | solution.py:49
  169.8 6.0 %reshape.44 = f32[192,2048]{0,1:T(8,128)S(1)} reshape(f32[6,32,128,16]{1,0,3,2:T(8,128)} %copy.61) | data formatting | bytes 3145728 | tf_op jit(solution)/shard_map/reshape | solution.py:51
  175.9 4.6 %copy.87 = bf16[128,32,160,1]{2,1,3,0:T(8,128)(2,1)} copy(bf16[128,32,160,1]{0,2,1,3:T(8,128)(2,1)} %bitcast.65) | data formatting | bytes 2621440 | tf_op jit(solution)/shard_map/optimization_barrier | solution.py:115
  183.4 33.8 %reduce-scatter.2.cloned.1.call-done = f32[192,2048]{1,0:T(8,128)} async-done(((f32[1536,2048]{1,0:T(8,128)}), f32[192,2048]{1,0:T(8,128)}) %reduce-scatter.2.cloned.1.call-update) | async-done | bytes 1572880 | tf_op jit(solution)/shard_map/reduce_scatter | solution.py:118
  219.0 3.2 %multiply_convert_fusion = (bf16[192,2048]{1,0:T(8,128)(2,1)S(1)}, bf16[192,2048]{1,0:T(8,128)(2,1)}) fusion(f32[192,2048]{1,0:T(8,128)} %reduce-scatter.2.cloned.1.call-done, bf16[192,2048]{1,0:T(8,128)(2,1)S(1)} %copy-done.9, f32[192,2048]{1,0:T(8,128)} %copy.62), kind=kLoop, calls=%fused_computation.31 | loop fusion | flops 1966080 | bytes 5505024 | tf_op jit(solution)/shard_map/convert_element_type | solution.py:129
  223.5 3.4 %reshape.45 = bf16[6,32,128,16]{1,0,3,2:T(8,128)(2,1)} reshape(bf16[192,2048]{0,1:T(8,128)(2,1)S(1)} %copy.63) | data formatting | bytes 1572864 | tf_op jit(solution)/shard_map/reshape | solution.py:131
  226.9 7.2 %fusion.7 = f32[128,32,160]{2,1,0:T(8,128)} fusion(bf16[6,160,128,16]{1,3,0,2:T(8,128)(2,1)} %constant_dynamic-update-slice_fusion, bf16[6,32,128,16]{1,0,3,2:T(8,128)(2,1)} %reshape.45), kind=kOutput, calls=%fused_computation.19 | convolution fusion | flops 125829120 | bytes 7340032 | tf_op jit(solution)/shard_map/kigc,kjgc->gij/dot_general | solution.py:133
  234.1 3.6 %copy.65 = f32[128,32,160]{0,2,1:T(8,128)S(1)} copy(f32[128,32,160]{2,1,0:T(8,128)} %fusion.7) | data formatting | bytes 5242880 | tf_op jit(solution)/shard_map/kigc,kjgc->gij/dot_general | solution.py:133
  241.8 6.5 %collective-permute-start.9 = (f32[128,128]{1,0:T(8,128)S(1)}, f32[128,128]{1,0:T(8,128)S(1)}, u32[]{:S(2)}, u32[]{:S(2)}) collective-permute-start(f32[128,128]{1,0:T(8,128)S(1)} %fusion.27), channel_id=1, source_target_pairs={{0,4},{4,0},{8,12},{12,8},{16,20},{20,16},{24,28},{28,24},{1,5},{5... | collective-permute-start | bytes 196616 | tf_op jit(solution)/shard_map/ppermute | solution.py:75
  270.3 5.5 %fusion.43 = f32[128,6,16,32]{3,2,1,0:T(8,128)S(1)} fusion(bf16[6,160,128,16]{1,3,0,2:T(8,128)(2,1)} %constant_dynamic-update-slice_fusion.6, bf16[128,32,160,1]{2,1,3,0:T(8,128)(2,1)} %copy.87), kind=kOutput, calls=%fused_computation.96 | convolution fusion | flops 125829120 | bytes 6815744 | tf_op jit(solution)/shard_map/gij,kjgc->kigc/dot_general | solution.py:48
  278.3 6.1 %add_bitcast_fusion = f32[6,32,128,16]{1,3,0,2:T(8,128)} fusion(f32[128,6,16,32]{3,2,1,0:T(8,128)S(1)} %fusion.43, bf16[6,160,128,16]{1,3,0,2:T(8,128)(2,1)S(1)} %bitcast.63, bf16[128,32,160,1]{2,1,3,0:T(8,128)(2,1)} %copy.88), kind=kOutput, calls=%fused_computation | convolution fusion | flops 126222336 | bytes 8388608 | tf_op jit(solution)/shard_map/gij,kjgc->kigc/dot_general | solution.py:48
  284.3 9.1 %copy.81 = f32[6,32,128,16]{1,0,3,2:T(8,128)} copy(f32[6,32,128,16]{1,3,0,2:T(8,128)} %add_bitcast_fusion) | data formatting | bytes 3145728 | tf_op jit(solution)/shard_map/add | solution.py:49
  293.4 7.0 %reshape.46 = f32[192,2048]{0,1:T(8,128)} reshape(f32[6,32,128,16]{1,0,3,2:T(8,128)} %copy.81) | data formatting | bytes 3145728 | tf_op jit(solution)/shard_map/reshape | solution.py:51
  (106 shorter events, 77.7 us)
Async XLA Ops:
  7.2 68.6 %all-gather.2.cloned.1.call-start = ((), (), s32[]{:S(2)}) async-start(), calls=%async_computation.1 | async-start | bytes 3932160 | tf_op jit(solution)/shard_map/all_gather | solution.py:114
  7.9 209.4 %reduce-scatter.2.cloned.1.call-start = ((), (), s32[]{:S(2)}) async-start(), calls=%async_computation.2 | async-start | bytes 14155776 | tf_op jit(solution)/shard_map/reduce_scatter | solution.py:118
  79.1 12.2 %collective-permute-start = (bf16[192,1024]{1,0:T(8,128)(2,1)}, bf16[192,1024]{1,0:T(8,128)(2,1)}, u32[]{:S(2)}, u32[]{:S(2)}) collective-permute-start(bf16[192,1024]{1,0:T(8,128)(2,1)} %get-tuple-element.40), channel_id=1, source_target_pairs={{0,4},{4,8},{8,12},{12,16},{16,20},{20,24},{24,28},{28,0},{1,5},{5... | collective-permute-start | bytes 1179656 | tf_op jit(solution)/shard_map/ppermute | solution.py:64
  79.1 14.7 %collective-permute-start.1 = (bf16[192,1024]{1,0:T(8,128)(2,1)}, bf16[192,1024]{1,0:T(8,128)(2,1)}, u32[]{:S(2)}, u32[]{:S(2)}) collective-permute-start(bf16[192,1024]{1,0:T(8,128)(2,1)} %get-tuple-element.39), channel_id=1, source_target_pairs={{0,8},{4,12},{8,16},{12,20},{16,24},{20,28},{24,0},{28,4},{1,9},{5... | collective-permute-start | bytes 1179656 | tf_op jit(solution)/shard_map/ppermute | solution.py:64
  80.6 27.9 %collective-permute-start.2 = (bf16[192,1024]{1,0:T(8,128)(2,1)}, bf16[192,1024]{1,0:T(8,128)(2,1)}, u32[]{:S(2)}, u32[]{:S(2)}) collective-permute-start(bf16[192,1024]{1,0:T(8,128)(2,1)} %get-tuple-element.38), channel_id=1, source_target_pairs={{0,12},{4,16},{8,20},{12,24},{16,28},{20,0},{24,4},{28,8},{1,13},{... | collective-permute-start | bytes 1179656 | tf_op jit(solution)/shard_map/ppermute | solution.py:64
  83.0 26.6 %collective-permute-start.3 = (bf16[192,1024]{1,0:T(8,128)(2,1)}, bf16[192,1024]{1,0:T(8,128)(2,1)}, u32[]{:S(2)}, u32[]{:S(2)}) collective-permute-start(bf16[192,1024]{1,0:T(8,128)(2,1)} %get-tuple-element.37), channel_id=1, source_target_pairs={{0,16},{4,20},{8,24},{12,28},{16,0},{20,4},{24,8},{28,12},{1,17},{... | collective-permute-start | bytes 1179656 | tf_op jit(solution)/shard_map/ppermute | solution.py:64
  83.5 32.5 %collective-permute-start.4 = (bf16[192,1024]{1,0:T(8,128)(2,1)}, bf16[192,1024]{1,0:T(8,128)(2,1)S(1)}, u32[]{:S(2)}, u32[]{:S(2)}) collective-permute-start(bf16[192,1024]{1,0:T(8,128)(2,1)} %get-tuple-element.36), channel_id=1, source_target_pairs={{0,20},{4,24},{8,28},{12,0},{16,4},{20,8},{24,12},{28,16},{1,21},{... | collective-permute-start | bytes 1179656 | tf_op jit(solution)/shard_map/ppermute | solution.py:64
  91.3 24.8 %collective-permute-start.5 = (bf16[192,1024]{1,0:T(8,128)(2,1)}, bf16[192,1024]{1,0:T(8,128)(2,1)S(1)}, u32[]{:S(2)}, u32[]{:S(2)}) collective-permute-start(bf16[192,1024]{1,0:T(8,128)(2,1)} %get-tuple-element.35), channel_id=1, source_target_pairs={{0,24},{4,28},{8,0},{12,4},{16,8},{20,12},{24,16},{28,20},{1,25},{... | collective-permute-start | bytes 1179656 | tf_op jit(solution)/shard_map/ppermute | solution.py:64
  92.7 23.5 %copy-start.10 = (bf16[2048,1024]{1,0:T(8,128)(2,1)S(1)}, bf16[2048,1024]{1,0:T(8,128)(2,1)}, u32[]{:S(2)}) copy-start(bf16[2048,1024]{1,0:T(8,128)(2,1)} %param.7) | copy-start | bytes 12582916
  93.9 22.2 %collective-permute-start.6 = (bf16[192,1024]{1,0:T(8,128)(2,1)S(1)}, bf16[192,1024]{1,0:T(8,128)(2,1)S(1)}, u32[]{:S(2)}, u32[]{:S(2)}) collective-permute-start(bf16[192,1024]{1,0:T(8,128)(2,1)S(1)} %get-tuple-element.34), channel_id=1, source_target_pairs={{0,28},{4,0},{8,4},{12,8},{16,12},{20,16},{24,20},{28,24},{1,29},{... | collective-permute-start | bytes 1179656 | tf_op jit(solution)/shard_map/ppermute | solution.py:64
  128.7 11.5 %copy-start.2 = (bf16[192,2048]{0,1:T(8,128)(2,1)}, bf16[192,2048]{0,1:T(8,128)(2,1)S(1)}, u32[]{:S(2)}) copy-start(bf16[192,2048]{0,1:T(8,128)(2,1)S(1)} %copy.57) | copy-start | bytes 2359300
  130.0 6.3 %collective-permute-start.7 = (bf16[128,2048]{0,1:T(8,128)(2,1)}, bf16[128,2048]{0,1:T(8,128)(2,1)}, u32[]{:S(2)}, u32[]{:S(2)}) collective-permute-start(bf16[128,2048]{0,1:T(8,128)(2,1)} %slice.76), channel_id=1, source_target_pairs={{0,4},{4,8},{8,12},{12,16},{16,20},{20,24},{24,28},{1,5},{5,9},{9,... | collective-permute-start | bytes 1572872 | tf_op jit(solution)/shard_map/ppermute | solution.py:123
  183.4 35.5 %copy-start.9 = (bf16[192,2048]{1,0:T(8,128)(2,1)S(1)}, bf16[192,2048]{1,0:T(8,128)(2,1)}, u32[]{:S(2)}) copy-start(bf16[192,2048]{1,0:T(8,128)(2,1)} %param.8) | copy-start | bytes 2359300
  237.7 4.0 %collective-permute-start.8 = (bf16[128,2048]{1,0:T(8,128)(2,1)}, bf16[128,2048]{1,0:T(8,128)(2,1)S(1)}, u32[]{:S(2)}, u32[]{:S(2)}) collective-permute-start(bf16[128,2048]{1,0:T(8,128)(2,1)} %slice.85), channel_id=1, source_target_pairs={{4,0},{8,4},{12,8},{16,12},{20,16},{24,20},{28,24},{5,1},{9,5},{13... | collective-permute-start | bytes 1572872 | tf_op jit(solution)/shard_map/ppermute | solution.py:130
  241.8 18.1 %collective-permute-start.9 = (f32[128,128]{1,0:T(8,128)S(1)}, f32[128,128]{1,0:T(8,128)S(1)}, u32[]{:S(2)}, u32[]{:S(2)}) collective-permute-start(f32[128,128]{1,0:T(8,128)S(1)} %fusion.27), channel_id=1, source_target_pairs={{0,4},{4,0},{8,12},{12,8},{16,20},{20,16},{24,28},{28,24},{1,5},{5... | collective-permute-start | bytes 196616 | tf_op jit(solution)/shard_map/ppermute | solution.py:75
  257.3 6.0 %copy-start.7 = (bf16[160,2048]{1,0:T(8,128)(2,1)S(1)}, bf16[160,2048]{1,0:T(8,128)(2,1)}, u32[]{:S(2)}) copy-start(bf16[160,2048]{1,0:T(8,128)(2,1)} %get-tuple-element.54) | copy-start | bytes 1966084
  259.9 4.5 %collective-permute-start.10 = (f32[128,128]{1,0:T(8,128)S(1)}, f32[128,128]{1,0:T(8,128)S(1)}, u32[]{:S(2)}, u32[]{:S(2)}) collective-permute-start(f32[128,128]{1,0:T(8,128)S(1)} %add.210), channel_id=1, source_target_pairs={{0,8},{4,12},{8,0},{12,4},{16,24},{20,28},{24,16},{28,20},{1,9},{5... | collective-permute-start | bytes 196616 | tf_op jit(solution)/shard_map/ppermute | solution.py:75
  264.4 4.3 %collective-permute-start.11 = (f32[128,128]{1,0:T(8,128)S(1)}, f32[128,128]{1,0:T(8,128)S(1)}, u32[]{:S(2)}, u32[]{:S(2)}) collective-permute-start(f32[128,128]{1,0:T(8,128)S(1)} %add.211), channel_id=1, source_target_pairs={{0,16},{4,20},{8,24},{12,28},{16,0},{20,4},{24,8},{28,12},{1,17},{... | collective-permute-start | bytes 196616 | tf_op jit(solution)/shard_map/ppermute | solution.py:75
  268.7 9.6 %slice-start = ((s8[6291456]{0:T(1024)(128)(4,1)}), s8[4194304]{0:T(1024)(128)(4,1)S(1)}, s32[]{:S(2)}) async-start(s8[6291456]{0:T(1024)(128)(4,1)} %bitcast.62), calls=%async_computation.3 | async-start | bytes 8388608
  268.7 9.5 %slice-start.1 = ((s8[6291456]{0:T(1024)(128)(4,1)}), s8[2097152]{0:T(1024)(128)(4,1)S(1)}, s32[]{:S(2)}) async-start(s8[6291456]{0:T(1024)(128)(4,1)} %bitcast.62), calls=%async_computation.4 | async-start | bytes 4194304
  268.8 7.0 %collective-permute-start.12 = (f32[128,128]{1,0:T(8,128)S(1)}, f32[128,128]{1,0:T(8,128)S(1)}, u32[]{:S(2)}, u32[]{:S(2)}) collective-permute-start(f32[128,128]{1,0:T(8,128)S(1)} %add_multiply_fusion), channel_id=1, source_target_pairs={{0,1},{1,0},{2,3},{3,2},{4,5},{5,4},{6,7},{7,6},{8,9},{9,8},{10,11... | collective-permute-start | bytes 196616 | tf_op jit(solution)/shard_map/ppermute | solution.py:86
  275.8 24.7 %collective-permute-start.13 = (f32[256,128]{1,0:T(8,128)S(1)}, f32[256,128]{1,0:T(8,128)S(1)}, u32[]{:S(2)}, u32[]{:S(2)}) collective-permute-start(f32[256,128]{1,0:T(8,128)S(1)} %maximum_select_fusion.1), channel_id=1, source_target_pairs={{0,2},{1,3},{2,0},{3,1},{4,6},{5,7},{6,4},{7,5},{8,10},{9,11},{10,... | collective-permute-start | bytes 393224 | tf_op jit(solution)/shard_map/ppermute | solution.py:86
  293.4 7.8 %copy-start.1 = (bf16[192,2048]{0,1:T(8,128)(2,1)S(1)}, bf16[192,2048]{0,1:T(8,128)(2,1)}, u32[]{:S(2)}) copy-start(bf16[192,2048]{0,1:T(8,128)(2,1)} %copy-done) | copy-start | bytes 2359300
  293.4 7.8 %copy-start.3 = (bf16[192,2048]{0,1:T(8,128)(2,1)S(1)}, bf16[192,2048]{0,1:T(8,128)(2,1)}, u32[]{:S(2)}) copy-start(bf16[192,2048]{0,1:T(8,128)(2,1)} %copy-done.2) | copy-start | bytes 2359300
  (5 other events, 15.1 us)
Sparse Core Ops, SparseCore 0:
  9.6 66.1 all-gather.1
  125.5 91.7 reduce-scatter.1

commit v14 on v12

--- a/solution.py
+++ b/solution.py
@@ -42,9 +42,10 @@
 
 def filter_apply(mat, wins, groups, per_group):
     tiles, width, chans = wins.shape
-    w4 = jnp.concatenate([wins, wins], 1).reshape(tiles, 2 * width, groups, per_group)
-    total = jnp.einsum("gij,kjgc->kigc", mat, w4, preferred_element_type=jnp.float32)
-    return total.reshape(tiles * mat.shape[1], chans)
+    w4 = wins.reshape(tiles, width, groups, per_group)
+    both = jnp.einsum("gij,kjgc->kigc", mat, w4, preferred_element_type=jnp.float32)
+    block = mat.shape[1] // 2
+    return (both[:, :block] + both[:, block:]).reshape(tiles * block, chans)
 
 
 def exchange_columns(x, count):
@@ -108,8 +109,8 @@
     mats_anti = toeplitz_mats(taps, block, width, halo, False, zero)
 
     cot_rows = lax.all_gather(cotangent, "mp", axis=1, tiled=True)
-    mats_causal = jnp.concatenate(mats_causal, 2)
-    mats_anti = jnp.concatenate(mats_anti, 2)
+    mats_causal = jnp.concatenate(mats_causal, 1)
+    mats_anti = jnp.concatenate(mats_anti, 1)
     cot_rows, mats_causal, mats_anti = lax.optimization_barrier((cot_rows, mats_causal, mats_anti))
     cot_cols = exchange_columns(cot_rows, ctx_count)
     partial = contract(cot_cols, out_weight)

time: 319 us -> 312 us (0.978)
  other arithmetic: 23.5 us -> 20.1 us
    concatenate x3 -> x2, other arithmetic: 14.4 us -> 6.45 us  [the longest x1 5.13 us: body(): mats_causal = jnp.concatenate(mats_causal, 1)]
    transpose x2 -> x0, local copies, waits for them, and re-layouts: 7.54 us -> none  [filter_apply(): jnp.einsum('gij,kjgc->kigc', mat, w4, preferred_element_type=jnp.float32)]
    add x0 -> x2, local copies, waits for them, and re-layouts: none -> 7.52 us  [filter_apply(): return (both[:, :block] + both[:, block:]).reshape(tiles * block, chans)]
    concatenate x1 -> x0, local copies, waits for them, and re-layouts: 6.67 us -> none  [filter_apply(): jnp.concatenate([wins, wins], 1)]
    slice x0 -> x2, local copies, waits for them, and re-layouts: none -> 4.48 us  [windows(): return jnp.stack([x[k * block:k * block + width] for k in range(tiles)])]
    ppermute x3, waiting for transfers between devices: 4.88 us -> 0.91 us  [butterfly_sum(): x = x + lax.ppermute(x, axis, [(k, k ^ step) for k in range(count)])]
  transfers between devices with their start and end apart: 16 -> 16, of which waited for: 8 -> 7; matrix products, arithmetic and copies ran while one was open for 30% -> 28% of each run, Pallas kernels for 0% -> 0%
where the time goes in v14:
time: 312 us; the launch traced here: 311 us
  waiting for transfers between devices  130 us (42%)
  local copies, waits for them, and re-layouts  81 us (26%)
  matrix products  38.2 us (12%)
  starting transfers between devices  26.8 us (9%)
  other arithmetic  20.1 us (6%)
  between operations  14.4 us (5%)
    all_gather x1, waiting for transfers between devices, body(): cot_rows = lax.all_gather(cotangent, 'mp', axis=1, tiled=True)  54.3 us
    reduce_scatter x1, waiting for transfers between devices, body(): lax.psum_scatter(partial, 'ctx', scatter_dimension=0, tiled=True)  53.2 us
    optimization_barrier x2, local copies, waits for them, and re-layouts, body(): lax.optimization_barrier((cot_rows, mats_causal, mats_anti))  20.1 us
    ppermute x7, waiting for transfers between devices, exchange_columns(): lax.ppermute(chunk, 'ctx', [(k, (k + shift) % count) for k in range(count)])  19.9 us
    ppermute x7, starting transfers between devices, exchange_columns(): lax.ppermute(chunk, 'ctx', [(k, (k + shift) % count) for k in range(count)])  12.8 us
    reshape x2, local copies, waits for them, and re-layouts, filter_apply(): return (both[:, :block] + both[:, block:]).reshape(tiles * block, chans)  11.8 us
    dot_general x2, matrix products, filter_apply(): jnp.einsum('gij,kjgc->kigc', mat, w4, preferred_element_type=jnp.float32)  11.3 us
    unnamed x22, local copies, waits for them, and re-layouts  9.58 us
  transfers between devices with their start and end apart: 16, of which 7 were waited for; matrix products, arithmetic and copies ran while one was open for 28% of the time, Pallas kernels for 0%

profile of v14, /device:TPU:0, one launch (start us, length us, event | category | flops | bytes accessed | tf_op | source)
XLA Modules:
  0.0 310.9 jit_solution(8773252865321703373)
XLA Ops:
  16.3 5.1 %pad_maximum_fusion = (bf16[128,128,192]{0,2,1:T(8,128)(2,1)}, bf16[128,128,192]{0,2,1:T(8,128)(2,1)}) fusion(bf16[128,64,192]{0,2,1:T(8,128)(2,1)S(1)} %get-tuple-element.33, bf16[128,64,192]{0,2,1:T(8,128)(2,1)S(1)} %get-tuple-element.32, bf16[128,64,192]{0,2,1:T(8,128)(2,1)S(1)} %get-tuple-element.31, bf16[128,64,192]{0,2,1:T(8,128)(2,1)S(1)} %get-tuple-element.30), kind=kLoop, calls=%fused_computation.3 | loop fusion | flops 6291456 | bytes 25165824 | tf_op jit(solution)/shard_map/concatenate | solution.py:112
  21.4 54.3 %all-gather.2.cloned.1.call-done = bf16[192,8192]{1,0:T(8,128)(2,1)} async-done(((bf16[192,2048]{1,0:T(8,128)(2,1)}), bf16[192,8192]{1,0:T(8,128)(2,1)}) %all-gather.2.cloned.1.call-update) | async-done | bytes 3145744 | tf_op jit(solution)/shard_map/all_gather | solution.py:111
  83.6 7.7 %collective-permute-done = bf16[192,1024]{1,0:T(8,128)(2,1)} collective-permute-done((bf16[192,1024]{1,0:T(8,128)(2,1)}, bf16[192,1024]{1,0:T(8,128)(2,1)}, u32[]{:S(2)}, u32[]{:S(2)}) %collective-permute-start) | collective-permute-done | bytes 393248 | tf_op jit(solution)/shard_map/ppermute | solution.py:61
  93.7 7.0 %collective-permute-start.6 = (bf16[192,1024]{1,0:T(8,128)(2,1)S(1)}, bf16[192,1024]{1,0:T(8,128)(2,1)S(1)}, u32[]{:S(2)}, u32[]{:S(2)}) collective-permute-start(bf16[192,1024]{1,0:T(8,128)(2,1)S(1)} %get-tuple-element.34), channel_id=1, source_target_pairs={{0,28},{4,0},{8,4},{12,8},{16,12},{20,16},{24,20},{28,24},{1,29},{... | collective-permute-start | bytes 1179656 | tf_op jit(solution)/shard_map/ppermute | solution.py:61
  101.8 6.8 %collective-permute-done.2 = bf16[192,1024]{1,0:T(8,128)(2,1)} collective-permute-done((bf16[192,1024]{1,0:T(8,128)(2,1)}, bf16[192,1024]{1,0:T(8,128)(2,1)}, u32[]{:S(2)}, u32[]{:S(2)}) %collective-permute-start.2) | collective-permute-done | bytes 393248 | tf_op jit(solution)/shard_map/ppermute | solution.py:61
  110.6 5.5 %collective-permute-done.4 = bf16[192,1024]{1,0:T(8,128)(2,1)S(1)} collective-permute-done((bf16[192,1024]{1,0:T(8,128)(2,1)}, bf16[192,1024]{1,0:T(8,128)(2,1)S(1)}, u32[]{:S(2)}, u32[]{:S(2)}) %collective-permute-start.4) | collective-permute-done | bytes 393248 | tf_op jit(solution)/shard_map/ppermute | solution.py:61
  116.2 9.1 %fusion.45 = f32[1536,2048]{1,0:T(8,128)} fusion(bf16[1536,1024]{1,0:T(8,128)(2,1)S(1)} %constant_dynamic-update-slice_fusion, bf16[2048,1024]{1,0:T(8,128)(2,1)S(1)} %copy-done.8), kind=kOutput, calls=%fused_computation.83 | convolution fusion | flops 6442450944 | bytes 19922944 | tf_op jit(solution)/shard_map/dot_general | solution.py:8
  130.0 4.2 %collective-permute-start.7 = (bf16[128,2048]{0,1:T(8,128)(2,1)S(1)}, bf16[128,2048]{0,1:T(8,128)(2,1)S(1)}, u32[]{:S(2)}, u32[]{:S(2)}) collective-permute-start(bf16[128,2048]{0,1:T(8,128)(2,1)S(1)} %slice.60), channel_id=1, source_target_pairs={{0,4},{4,8},{8,12},{12,16},{16,20},{20,24},{24,28},{1,5},{5,9},{9,... | collective-permute-start | bytes 1572872 | tf_op jit(solution)/shard_map/ppermute | solution.py:122
  137.5 10.3 %copy.60 = bf16[128,128,192,1]{1,2,3,0:T(8,128)(2,1)} copy(bf16[128,128,192,1]{0,2,1,3:T(8,128)(2,1)} %bitcast.42) | data formatting | bytes 12582912 | tf_op jit(solution)/shard_map/optimization_barrier | solution.py:114
  147.9 5.7 %convolution_bitcast_fusion.1 = f32[3,128,128,16]{1,3,0,2:T(8,128)S(1)} fusion(bf16[128,128,192,1]{1,2,3,0:T(8,128)(2,1)} %copy.60, bf16[1,192,128,16]{1,3,0,2:T(8,128)(2,1)S(1)} %bitcast.43, bf16[1,192,128,16]{1,3,0,2:T(8,128)(2,1)} %bitcast.47, bf16[1,192,128,16]{1,3,0,2:T(8,128)(2,1)} %bitcast.45), kind=kOutput, calls=%fused_computation.37 | convolution fusion | flops 304349184 | bytes 11796480 | tf_op jit(solution)/shard_map/gij,kjgc->kigc/dot_general | solution.py:46
  154.4 3.8 %copy.44 = f32[3,64,128,16]{1,0,3,2:T(4,128)} copy(f32[3,64,128,16]{1,3,0,2:T(8,128)S(1)} %slice_add_fusion.1) | data formatting | bytes 3145728 | tf_op jit(solution)/shard_map/add | solution.py:48
  158.2 5.9 %reshape.32 = f32[192,2048]{0,1:T(8,128)} reshape(f32[3,64,128,16]{1,0,3,2:T(4,128)} %copy.44) | data formatting | bytes 3145728 | tf_op jit(solution)/shard_map/reshape | solution.py:48
  164.1 53.2 %reduce-scatter.2.cloned.1.call-done = f32[192,2048]{1,0:T(8,128)} async-done(((f32[1536,2048]{1,0:T(8,128)}), f32[192,2048]{1,0:T(8,128)}) %reduce-scatter.2.cloned.1.call-update) | async-done | bytes 1572880 | tf_op jit(solution)/shard_map/reduce_scatter | solution.py:117
  217.3 2.8 copy.45
  220.0 3.4 %multiply_convert_fusion = (bf16[192,2048]{1,0:T(8,128)(2,1)S(1)}, bf16[192,2048]{1,0:T(8,128)(2,1)}) fusion(f32[192,2048]{1,0:T(8,128)} %reduce-scatter.2.cloned.1.call-done, bf16[192,2048]{1,0:T(8,128)(2,1)} %param.8, f32[192,2048]{1,0:T(8,128)} %copy.45), kind=kLoop, calls=%fused_computation.41 | loop fusion | flops 1966080 | bytes 5505024 | tf_op jit(solution)/shard_map/convert_element_type | solution.py:128
  224.8 5.0 %reshape.33 = bf16[3,64,128,16]{1,0,3,2:T(4,128)(2,1)} reshape(bf16[192,2048]{0,1:T(8,128)(2,1)} %copy.46) | data formatting | bytes 1572864 | tf_op jit(solution)/shard_map/reshape | solution.py:130
  229.7 6.7 %convolution_bitcast_fusion = f32[128,64,192]{2,1,0:T(8,128)} fusion(bf16[3,64,128,16]{1,0,3,2:T(4,128)(2,1)} %reshape.33, bf16[1,192,128,16]{1,3,0,2:T(8,128)(2,1)S(1)} %bitcast.44, bf16[1,192,128,16]{1,3,0,2:T(8,128)(2,1)} %bitcast.48, bf16[1,192,128,16]{1,3,0,2:T(8,128)(2,1)} %bitcast.46), kind=kOutput, calls=%fused_computation.13 | convolution fusion | flops 153354240 | bytes 9437184 | tf_op jit(solution)/shard_map/kigc,kjgc->gij/dot_general | solution.py:132
  236.5 8.6 %copy.48 = f32[128,64,192]{0,2,1:T(8,128)} copy(f32[128,64,192]{2,1,0:T(8,128)} %convolution_bitcast_fusion) | data formatting | bytes 12582912 | tf_op jit(solution)/shard_map/kigc,kjgc->gij/dot_general | solution.py:132
  246.9 4.9 %fusion.28 = f32[128,128]{1,0:T(8,128)S(1)} fusion(s32[128]{0:T(128)S(1)} %iota_add_fusion, s32[64]{0:T(128)S(1)} %iota_add_fusion.1, f32[128,64,192]{0,2,1:T(8,128)} %copy.48), kind=kOutput, calls=%fused_computation.45 | convolution fusion | flops 408944640 | bytes 6357760 | tf_op jit(solution)/shard_map/gij,ijs->gs/dot_general | solution.py:140
  259.7 9.8 %copy.62 = bf16[128,128,192,1]{1,2,3,0:T(8,128)(2,1)} copy(bf16[128,128,192,1]{0,2,1,3:T(8,128)(2,1)} %bitcast.41) | data formatting | bytes 12582912 | tf_op jit(solution)/shard_map/optimization_barrier | solution.py:114
  276.9 5.7 %fusion.24 = f32[3,128,128,16]{1,3,0,2:T(8,128)S(1)} fusion(bf16[128,128,192,1]{1,2,3,0:T(8,128)(2,1)} %copy.62, bf16[1,192,128,16]{1,3,0,2:T(8,128)(2,1)} %bitcast.51, bf16[1,192,128,16]{1,3,0,2:T(8,128)(2,1)} %bitcast.50, bf16[1,192,128,16]{1,3,0,2:T(8,128)(2,1)S(1)} %bitcast.49), kind=kOutput, calls=%fused_computation.36 | convolution fusion | flops 304349184 | bytes 11796480 | tf_op jit(solution)/shard_map/gij,kjgc->kigc/dot_general | solution.py:46
  286.0 3.7 %copy.57 = f32[3,64,128,16]{1,0,3,2:T(4,128)} copy(f32[3,64,128,16]{1,3,0,2:T(8,128)S(1)} %slice_add_fusion) | data formatting | bytes 3145728 | tf_op jit(solution)/shard_map/add | solution.py:48
  289.7 5.9 %reshape.34 = f32[192,2048]{0,1:T(8,128)} reshape(f32[3,64,128,16]{1,0,3,2:T(4,128)} %copy.57) | data formatting | bytes 3145728 | tf_op jit(solution)/shard_map/reshape | solution.py:48
  296.4 3.3 %fusion.21 = (bf16[192,2048]{0,1:T(8,128)(2,1)}, bf16[192,2048]{0,1:T(8,128)(2,1)}) fusion(f32[192,2048]{0,1:T(8,128)} %reshape.34, bf16[192,2048]{0,1:T(8,128)(2,1)S(1)} %copy.41, bf16[192,2048]{0,1:T(8,128)(2,1)S(1)} %copy-done), kind=kLoop, calls=%fused_computation.33 | loop fusion | flops 2359296 | bytes 4718592 | tf_op jit(solution)/shard_map/convert_element_type | solution.py:154
  (81 shorter events, 58.1 us)
Async XLA Ops:
  7.2 68.6 %all-gather.2.cloned.1.call-start = ((), (), s32[]{:S(2)}) async-start(), calls=%async_computation.1 | async-start | bytes 3932160 | tf_op jit(solution)/shard_map/all_gather | solution.py:111
  7.9 209.4 %reduce-scatter.2.cloned.1.call-start = ((), (), s32[]{:S(2)}) async-start(), calls=%async_computation.2 | async-start | bytes 14155776 | tf_op jit(solution)/shard_map/reduce_scatter | solution.py:117
  75.8 1.9 copy-start.3
  79.1 12.2 %collective-permute-start = (bf16[192,1024]{1,0:T(8,128)(2,1)}, bf16[192,1024]{1,0:T(8,128)(2,1)}, u32[]{:S(2)}, u32[]{:S(2)}) collective-permute-start(bf16[192,1024]{1,0:T(8,128)(2,1)} %get-tuple-element.40), channel_id=1, source_target_pairs={{0,4},{4,8},{8,12},{12,16},{16,20},{20,24},{24,28},{28,0},{1,5},{5... | collective-permute-start | bytes 1179656 | tf_op jit(solution)/shard_map/ppermute | solution.py:61
  79.1 14.6 %collective-permute-start.1 = (bf16[192,1024]{1,0:T(8,128)(2,1)}, bf16[192,1024]{1,0:T(8,128)(2,1)}, u32[]{:S(2)}, u32[]{:S(2)}) collective-permute-start(bf16[192,1024]{1,0:T(8,128)(2,1)} %get-tuple-element.39), channel_id=1, source_target_pairs={{0,8},{4,12},{8,16},{12,20},{16,24},{20,28},{24,0},{28,4},{1,9},{5... | collective-permute-start | bytes 1179656 | tf_op jit(solution)/shard_map/ppermute | solution.py:61
  80.6 27.9 %collective-permute-start.2 = (bf16[192,1024]{1,0:T(8,128)(2,1)}, bf16[192,1024]{1,0:T(8,128)(2,1)}, u32[]{:S(2)}, u32[]{:S(2)}) collective-permute-start(bf16[192,1024]{1,0:T(8,128)(2,1)} %get-tuple-element.38), channel_id=1, source_target_pairs={{0,12},{4,16},{8,20},{12,24},{16,28},{20,0},{24,4},{28,8},{1,13},{... | collective-permute-start | bytes 1179656 | tf_op jit(solution)/shard_map/ppermute | solution.py:61
  83.0 26.6 %collective-permute-start.3 = (bf16[192,1024]{1,0:T(8,128)(2,1)}, bf16[192,1024]{1,0:T(8,128)(2,1)}, u32[]{:S(2)}, u32[]{:S(2)}) collective-permute-start(bf16[192,1024]{1,0:T(8,128)(2,1)} %get-tuple-element.37), channel_id=1, source_target_pairs={{0,16},{4,20},{8,24},{12,28},{16,0},{20,4},{24,8},{28,12},{1,17},{... | collective-permute-start | bytes 1179656 | tf_op jit(solution)/shard_map/ppermute | solution.py:61
  83.5 32.7 %copy-start.8 = (bf16[2048,1024]{1,0:T(8,128)(2,1)S(1)}, bf16[2048,1024]{1,0:T(8,128)(2,1)}, u32[]{:S(2)}) copy-start(bf16[2048,1024]{1,0:T(8,128)(2,1)} %param.7) | copy-start | bytes 12582916
  83.5 32.5 %collective-permute-start.4 = (bf16[192,1024]{1,0:T(8,128)(2,1)}, bf16[192,1024]{1,0:T(8,128)(2,1)S(1)}, u32[]{:S(2)}, u32[]{:S(2)}) collective-permute-start(bf16[192,1024]{1,0:T(8,128)(2,1)} %get-tuple-element.36), channel_id=1, source_target_pairs={{0,20},{4,24},{8,28},{12,0},{16,4},{20,8},{24,12},{28,16},{1,21},{... | collective-permute-start | bytes 1179656 | tf_op jit(solution)/shard_map/ppermute | solution.py:61
  91.3 24.8 %collective-permute-start.5 = (bf16[192,1024]{1,0:T(8,128)(2,1)}, bf16[192,1024]{1,0:T(8,128)(2,1)S(1)}, u32[]{:S(2)}, u32[]{:S(2)}) collective-permute-start(bf16[192,1024]{1,0:T(8,128)(2,1)} %get-tuple-element.35), channel_id=1, source_target_pairs={{0,24},{4,28},{8,0},{12,4},{16,8},{20,12},{24,16},{28,20},{1,25},{... | collective-permute-start | bytes 1179656 | tf_op jit(solution)/shard_map/ppermute | solution.py:61
  93.7 22.4 %collective-permute-start.6 = (bf16[192,1024]{1,0:T(8,128)(2,1)S(1)}, bf16[192,1024]{1,0:T(8,128)(2,1)S(1)}, u32[]{:S(2)}, u32[]{:S(2)}) collective-permute-start(bf16[192,1024]{1,0:T(8,128)(2,1)S(1)} %get-tuple-element.34), channel_id=1, source_target_pairs={{0,28},{4,0},{8,4},{12,8},{16,12},{20,16},{24,20},{28,24},{1,29},{... | collective-permute-start | bytes 1179656 | tf_op jit(solution)/shard_map/ppermute | solution.py:61
  125.3 1.1 copy-start.4
  125.3 1.6 copy-start.5
  130.0 5.5 %collective-permute-start.7 = (bf16[128,2048]{0,1:T(8,128)(2,1)S(1)}, bf16[128,2048]{0,1:T(8,128)(2,1)S(1)}, u32[]{:S(2)}, u32[]{:S(2)}) collective-permute-start(bf16[128,2048]{0,1:T(8,128)(2,1)S(1)} %slice.60), channel_id=1, source_target_pairs={{0,4},{4,8},{8,12},{12,16},{16,20},{20,24},{24,28},{1,5},{5,9},{9,... | collective-permute-start | bytes 1572872 | tf_op jit(solution)/shard_map/ppermute | solution.py:122
  245.1 6.7 %copy-start.1 = (f32[128,64,192]{0,2,1:T(8,128)S(1)}, f32[128,64,192]{0,2,1:T(8,128)}, u32[]{:S(2)}) copy-start(f32[128,64,192]{0,2,1:T(8,128)} %copy.48) | copy-start | bytes 18874372
  245.1 9.1 %collective-permute-start.8 = (bf16[128,2048]{1,0:T(8,128)(2,1)S(1)}, bf16[128,2048]{1,0:T(8,128)(2,1)S(1)}, u32[]{:S(2)}, u32[]{:S(2)}) collective-permute-start(bf16[128,2048]{1,0:T(8,128)(2,1)S(1)} %slice.65), channel_id=1, source_target_pairs={{4,0},{8,4},{12,8},{16,12},{20,16},{24,20},{28,24},{5,1},{9,5},{13... | collective-permute-start | bytes 1572872 | tf_op jit(solution)/shard_map/ppermute | solution.py:129
  255.0 2.5 collective-permute-start.9
  257.5 11.9 %collective-permute-start.10 = (f32[128,128]{1,0:T(8,128)S(1)}, f32[128,128]{1,0:T(8,128)S(1)}, u32[]{:S(2)}, u32[]{:S(2)}) collective-permute-start(f32[128,128]{1,0:T(8,128)S(1)} %add.203), channel_id=1, source_target_pairs={{0,8},{4,12},{8,0},{12,4},{16,24},{20,28},{24,16},{28,20},{1,9},{5... | collective-permute-start | bytes 196616 | tf_op jit(solution)/shard_map/ppermute | solution.py:72
  259.7 9.9 %copy-start.7 = (bf16[128,2048]{1,0:T(8,128)(2,1)S(1)}, bf16[128,2048]{1,0:T(8,128)(2,1)}, u32[]{:S(2)}) copy-start(bf16[128,2048]{1,0:T(8,128)(2,1)} %copy-done.6) | copy-start | bytes 1572868
  269.4 7.5 %copy-start.2 = (bf16[192,2048]{0,1:T(8,128)(2,1)S(1)}, bf16[192,2048]{0,1:T(8,128)(2,1)}, u32[]{:S(2)}) copy-start(bf16[192,2048]{0,1:T(8,128)(2,1)} %copy.46) | copy-start | bytes 2359300
  269.4 5.9 %collective-permute-start.11 = (f32[128,128]{1,0:T(8,128)S(1)}, f32[128,128]{1,0:T(8,128)S(1)}, u32[]{:S(2)}, u32[]{:S(2)}) collective-permute-start(f32[128,128]{1,0:T(8,128)S(1)} %add.204), channel_id=1, source_target_pairs={{0,16},{4,20},{8,24},{12,28},{16,0},{20,4},{24,8},{28,12},{1,17},{... | collective-permute-start | bytes 196616 | tf_op jit(solution)/shard_map/ppermute | solution.py:72
  275.4 7.2 %collective-permute-start.12 = (f32[128,128]{1,0:T(8,128)S(1)}, f32[128,128]{1,0:T(8,128)S(1)}, u32[]{:S(2)}, u32[]{:S(2)}) collective-permute-start(f32[128,128]{1,0:T(8,128)S(1)} %add_multiply_fusion), channel_id=1, source_target_pairs={{0,1},{1,0},{2,3},{3,2},{4,5},{5,4},{6,7},{7,6},{8,9},{9,8},{10,11... | collective-permute-start | bytes 196616 | tf_op jit(solution)/shard_map/ppermute | solution.py:83
  282.6 13.0 %collective-permute-start.13 = (f32[256,128]{1,0:T(8,128)S(1)}, f32[256,128]{1,0:T(8,128)S(1)}, u32[]{:S(2)}, u32[]{:S(2)}) collective-permute-start(f32[256,128]{1,0:T(8,128)S(1)} %maximum_select_fusion.1), channel_id=1, source_target_pairs={{0,2},{1,3},{2,0},{3,1},{4,6},{5,7},{6,4},{7,5},{8,10},{9,11},{10,... | collective-permute-start | bytes 393224 | tf_op jit(solution)/shard_map/ppermute | solution.py:83
  289.7 6.6 %copy-start = (bf16[192,2048]{0,1:T(8,128)(2,1)S(1)}, bf16[192,2048]{0,1:T(8,128)(2,1)}, u32[]{:S(2)}) copy-start(bf16[192,2048]{0,1:T(8,128)(2,1)} %copy.42) | copy-start | bytes 2359300
  (1 other events, 0.8 us)
Sparse Core Ops, SparseCore 0:
  9.6 66.1 all-gather.1
  125.5 91.7 reduce-scatter.1

commit v15 on v10

--- a/solution.py
+++ b/solution.py
@@ -147,7 +147,6 @@
     trailing = jnp.concatenate([grad_conv, next_head], 0)
     win_grad = windows(trailing, tiles, block, width)
     grad_product = filter_apply(mats_anti, win_grad, local_groups, per_group)
-    grad_filters, grad_product = lax.optimization_barrier((grad_filters, grad_product))
 
 
     grad_query = (grad_mixed * mixed).astype(jnp.bfloat16)

time: 308 us -> 308 us (level)
  transfers between devices with their start and end apart: 16 -> 16, of which waited for: 7 -> 7; matrix products, arithmetic and copies ran while one was open for 28% -> 30% of each run, Pallas kernels for 0% -> 0%
where the time goes in v15:
time: 308 us; the launch traced here: 307 us
  waiting for transfers between devices  134 us (44%)
  local copies, waits for them, and re-layouts  82.6 us (27%)
  matrix products  36.8 us (12%)
  starting transfers between devices  26.4 us (9%)
  between operations  14.5 us (5%)
  other arithmetic  12.7 us (4%)
    all_gather x1, waiting for transfers between devices, body(): cot_rows = lax.all_gather(cotangent, 'mp', axis=1, tiled=True)  57.9 us
    reduce_scatter x1, waiting for transfers between devices, body(): lax.psum_scatter(partial, 'ctx', scatter_dimension=0, tiled=True)  53.1 us
    optimization_barrier x4, local copies, waits for them, and re-layouts, body(): lax.optimization_barrier((cot_rows, mats_causal, mats_anti))  28.5 us
    ppermute x7, waiting for transfers between devices, exchange_columns(): lax.ppermute(chunk, 'ctx', [(k, (k + shift) % count) for k in range(count)])  19.9 us
    ppermute x7, starting transfers between devices, exchange_columns(): lax.ppermute(chunk, 'ctx', [(k, (k + shift) % count) for k in range(count)])  12.8 us
    reshape x2, local copies, waits for them, and re-layouts, filter_apply(): return total.reshape(tiles * block, chans)  10.8 us
    dot_general x4, matrix products, filter_apply(): jnp.einsum('gij,kjgc->kigc', m, w4, preferred_element_type=jnp.float32)  9.89 us
    unnamed x38, local copies, waits for them, and re-layouts  9.3 us
  transfers between devices with their start and end apart: 16, of which 7 were waited for; matrix products, arithmetic and copies ran while one was open for 30% of the time, Pallas kernels for 0%

profile of v15, /device:TPU:0, one launch (start us, length us, event | category | flops | bytes accessed | tf_op | source)
XLA Modules:
  0.0 306.8 jit_solution(11120602797380386514)
XLA Ops:
  12.6 5.3 %fusion.35 = (bf16[128,64,192]{0,2,1:T(8,128)(2,1)}, bf16[128,64,192]{0,2,1:T(8,128)(2,1)}, bf16[128,64,192]{0,2,1:T(8,128)(2,1)}, bf16[128,64,192]{0,2,1:T(8,128)(2,1)}) fusion(bf16[256,64,192]{0,2,1:T(8,128)(2,1)S(1)} %fusion.5, bf16[256,64,192]{0,2,1:T(8,128)(2,1)S(1)} %fusion.6), kind=kLoop, calls=%fused_computation.73 | loop fusion | bytes 25165824 | tf_op jit(solution)/shard_map/slice | solution.py:30
  17.9 57.9 %all-gather.2.cloned.1.call-done = bf16[192,8192]{1,0:T(8,128)(2,1)} async-done(((bf16[192,2048]{1,0:T(8,128)(2,1)}), bf16[192,8192]{1,0:T(8,128)(2,1)}) %all-gather.2.cloned.1.call-update) | async-done | bytes 3145744 | tf_op jit(solution)/shard_map/all_gather | solution.py:114
  83.5 7.7 %collective-permute-done = bf16[192,1024]{1,0:T(8,128)(2,1)} collective-permute-done((bf16[192,1024]{1,0:T(8,128)(2,1)}, bf16[192,1024]{1,0:T(8,128)(2,1)}, u32[]{:S(2)}, u32[]{:S(2)}) %collective-permute-start) | collective-permute-done | bytes 393248 | tf_op jit(solution)/shard_map/ppermute | solution.py:64
  93.7 7.0 %collective-permute-start.6 = (bf16[192,1024]{1,0:T(8,128)(2,1)S(1)}, bf16[192,1024]{1,0:T(8,128)(2,1)S(1)}, u32[]{:S(2)}, u32[]{:S(2)}) collective-permute-start(bf16[192,1024]{1,0:T(8,128)(2,1)S(1)} %get-tuple-element.34), channel_id=1, source_target_pairs={{0,28},{4,0},{8,4},{12,8},{16,12},{20,16},{24,20},{28,24},{1,29},{... | collective-permute-start | bytes 1179656 | tf_op jit(solution)/shard_map/ppermute | solution.py:64
  101.7 6.8 %collective-permute-done.2 = bf16[192,1024]{1,0:T(8,128)(2,1)} collective-permute-done((bf16[192,1024]{1,0:T(8,128)(2,1)}, bf16[192,1024]{1,0:T(8,128)(2,1)}, u32[]{:S(2)}, u32[]{:S(2)}) %collective-permute-start.2) | collective-permute-done | bytes 393248 | tf_op jit(solution)/shard_map/ppermute | solution.py:64
  110.5 5.4 %collective-permute-done.4 = bf16[192,1024]{1,0:T(8,128)(2,1)S(1)} collective-permute-done((bf16[192,1024]{1,0:T(8,128)(2,1)}, bf16[192,1024]{1,0:T(8,128)(2,1)S(1)}, u32[]{:S(2)}, u32[]{:S(2)}) %collective-permute-start.4) | collective-permute-done | bytes 393248 | tf_op jit(solution)/shard_map/ppermute | solution.py:64
  116.2 9.2 %fusion.37 = f32[1536,2048]{1,0:T(8,128)} fusion(bf16[1536,1024]{1,0:T(8,128)(2,1)S(1)} %constant_dynamic-update-slice_fusion, bf16[2048,1024]{1,0:T(8,128)(2,1)S(1)} %copy-done.16), kind=kOutput, calls=%fused_computation.75 | convolution fusion | flops 6442450944 | bytes 19922944 | tf_op jit(solution)/shard_map/dot_general | solution.py:8
  129.2 3.9 %collective-permute-start.7 = (bf16[128,2048]{0,1:T(8,128)(2,1)S(1)}, bf16[128,2048]{0,1:T(8,128)(2,1)S(1)}, u32[]{:S(2)}, u32[]{:S(2)}) collective-permute-start(bf16[128,2048]{0,1:T(8,128)(2,1)S(1)} %slice.44), channel_id=1, source_target_pairs={{0,4},{4,8},{8,12},{12,16},{16,20},{20,24},{24,28},{1,5},{5,9},{9,... | collective-permute-start | bytes 1572872 | tf_op jit(solution)/shard_map/ppermute | solution.py:123
  136.6 7.2 %copy.67 = bf16[128,64,192,1]{2,1,3,0:T(8,128)(2,1)} copy(bf16[128,64,192,1]{0,2,1,3:T(8,128)(2,1)} %bitcast.51) | data formatting | bytes 6291456 | tf_op jit(solution)/shard_map/optimization_barrier | solution.py:115
  143.8 6.9 %copy.66 = bf16[128,64,192,1]{2,1,3,0:T(8,128)(2,1)} copy(bf16[128,64,192,1]{0,2,1,3:T(8,128)(2,1)} %bitcast.50) | data formatting | bytes 6291456 | tf_op jit(solution)/shard_map/optimization_barrier | solution.py:115
  150.7 3.5 %fusion.34 = f32[128,3,16,64]{3,2,1,0:T(8,128)S(1)} fusion(bf16[128,64,192,1]{2,1,3,0:T(8,128)(2,1)} %copy.67, bf16[1,192,128,16]{1,3,0,2:T(8,128)(2,1)S(1)} %bitcast.45, bf16[1,192,128,16]{1,3,0,2:T(8,128)(2,1)S(1)} %bitcast.58, bf16[1,192,128,16]{1,3,0,2:T(8,128)(2,1)S(1)} %bitcast.55), kind=kOutput, calls=%fused_computation.72 | convolution fusion | flops 153354240 | bytes 7077888 | tf_op jit(solution)/shard_map/gij,kjgc->kigc/dot_general | solution.py:48
  155.9 3.7 %copy.49 = f32[3,64,128,16]{1,0,3,2:T(4,128)} copy(f32[3,64,128,16]{1,3,0,2:T(8,128)S(1)} %add_bitcast_fusion.1) | data formatting | bytes 3145728 | tf_op jit(solution)/shard_map/add | solution.py:49
  159.6 4.8 %reshape.32 = f32[192,2048]{0,1:T(8,128)S(1)} reshape(f32[3,64,128,16]{1,0,3,2:T(4,128)} %copy.49) | data formatting | bytes 3145728 | tf_op jit(solution)/shard_map/reshape | solution.py:51
  164.4 53.1 %reduce-scatter.2.cloned.1.call-done = f32[192,2048]{1,0:T(8,128)} async-done(((f32[1536,2048]{1,0:T(8,128)}), f32[192,2048]{1,0:T(8,128)}) %reduce-scatter.2.cloned.1.call-update) | async-done | bytes 1572880 | tf_op jit(solution)/shard_map/reduce_scatter | solution.py:118
  219.2 3.4 %multiply_convert_fusion = (bf16[192,2048]{1,0:T(8,128)(2,1)S(1)}, bf16[192,2048]{1,0:T(8,128)(2,1)}) fusion(f32[192,2048]{1,0:T(8,128)} %reduce-scatter.2.cloned.1.call-done, bf16[192,2048]{1,0:T(8,128)(2,1)} %param.8, f32[192,2048]{1,0:T(8,128)} %copy.50), kind=kLoop, calls=%fused_computation.32 | loop fusion | flops 1966080 | bytes 5505024 | tf_op jit(solution)/shard_map/convert_element_type | solution.py:129
  225.5 6.8 %convolution_bitcast_fusion = f32[128,64,192]{2,1,0:T(8,128)} fusion(bf16[3,64,128,16]{1,0,3,2:T(4,128)(2,1)} %reshape.33, bf16[1,192,128,16]{1,3,0,2:T(8,128)(2,1)S(1)} %bitcast.47, bf16[1,192,128,16]{1,3,0,2:T(8,128)(2,1)} %bitcast.57, bf16[1,192,128,16]{1,3,0,2:T(8,128)(2,1)} %bitcast.54), kind=kOutput, calls=%fused_computation.11 | convolution fusion | flops 153354240 | bytes 9437184 | tf_op jit(solution)/shard_map/kigc,kjgc->gij/dot_general | solution.py:133
  232.2 8.6 %copy.54 = f32[128,64,192]{0,2,1:T(8,128)} copy(f32[128,64,192]{2,1,0:T(8,128)} %convolution_bitcast_fusion) | data formatting | bytes 12582912 | tf_op jit(solution)/shard_map/kigc,kjgc->gij/dot_general | solution.py:133
  242.6 4.9 %fusion.20 = f32[128,128]{1,0:T(8,128)S(1)} fusion(s32[128]{0:T(128)S(1)} %iota_add_fusion, s32[64]{0:T(128)S(1)} %iota_add_fusion.1, f32[128,64,192]{0,2,1:T(8,128)} %copy.54), kind=kOutput, calls=%fused_computation.37 | convolution fusion | flops 408944640 | bytes 6357760 | tf_op jit(solution)/shard_map/gij,ijs->gs/dot_general | solution.py:141
  252.3 6.9 %copy.69 = bf16[128,64,192,1]{2,1,3,0:T(8,128)(2,1)} copy(bf16[128,64,192,1]{0,2,1,3:T(8,128)(2,1)} %bitcast.49) | data formatting | bytes 6291456 | tf_op jit(solution)/shard_map/optimization_barrier | solution.py:115
  259.2 7.6 %copy.70 = bf16[128,64,192,1]{2,1,3,0:T(8,128)(2,1)} copy(bf16[128,64,192,1]{0,2,1,3:T(8,128)(2,1)S(1)} %bitcast.48) | data formatting | bytes 6291456 | tf_op jit(solution)/shard_map/optimization_barrier | solution.py:115
  273.4 3.5 %fusion.19 = f32[128,3,16,64]{3,2,1,0:T(8,128)S(1)} fusion(bf16[128,64,192,1]{2,1,3,0:T(8,128)(2,1)} %copy.69, bf16[1,192,128,16]{1,3,0,2:T(8,128)(2,1)S(1)} %bitcast.60, bf16[1,192,128,16]{1,3,0,2:T(8,128)(2,1)S(1)} %bitcast.62, bf16[1,192,128,16]{1,3,0,2:T(8,128)(2,1)S(1)} %bitcast.52), kind=kOutput, calls=%fused_computation.36 | convolution fusion | flops 153354240 | bytes 7077888 | tf_op jit(solution)/shard_map/gij,kjgc->kigc/dot_general | solution.py:48
  280.6 3.7 %copy.63 = f32[3,64,128,16]{1,0,3,2:T(4,128)} copy(f32[3,64,128,16]{1,3,0,2:T(8,128)S(1)} %add_bitcast_fusion) | data formatting | bytes 3145728 | tf_op jit(solution)/shard_map/add | solution.py:49
  284.4 6.0 %reshape.34 = f32[192,2048]{0,1:T(8,128)} reshape(f32[3,64,128,16]{1,0,3,2:T(4,128)} %copy.63) | data formatting | bytes 3145728 | tf_op jit(solution)/shard_map/reshape | solution.py:51
  292.9 3.0 fusion.15
  (97 shorter events, 55.5 us)
Async XLA Ops:
  7.2 68.6 %all-gather.2.cloned.1.call-start = ((), (), s32[]{:S(2)}) async-start(), calls=%async_computation.1 | async-start | bytes 3932160 | tf_op jit(solution)/shard_map/all_gather | solution.py:114
  7.9 209.6 %reduce-scatter.2.cloned.1.call-start = ((), (), s32[]{:S(2)}) async-start(), calls=%async_computation.2 | async-start | bytes 14155776 | tf_op jit(solution)/shard_map/reduce_scatter | solution.py:118
  79.1 12.2 %collective-permute-start = (bf16[192,1024]{1,0:T(8,128)(2,1)}, bf16[192,1024]{1,0:T(8,128)(2,1)}, u32[]{:S(2)}, u32[]{:S(2)}) collective-permute-start(bf16[192,1024]{1,0:T(8,128)(2,1)} %get-tuple-element.40), channel_id=1, source_target_pairs={{0,4},{4,8},{8,12},{12,16},{16,20},{20,24},{24,28},{28,0},{1,5},{5... | collective-permute-start | bytes 1179656 | tf_op jit(solution)/shard_map/ppermute | solution.py:64
  79.1 14.6 %collective-permute-start.1 = (bf16[192,1024]{1,0:T(8,128)(2,1)}, bf16[192,1024]{1,0:T(8,128)(2,1)}, u32[]{:S(2)}, u32[]{:S(2)}) collective-permute-start(bf16[192,1024]{1,0:T(8,128)(2,1)} %get-tuple-element.39), channel_id=1, source_target_pairs={{0,8},{4,12},{8,16},{12,20},{16,24},{20,28},{24,0},{28,4},{1,9},{5... | collective-permute-start | bytes 1179656 | tf_op jit(solution)/shard_map/ppermute | solution.py:64
  80.6 27.9 %collective-permute-start.2 = (bf16[192,1024]{1,0:T(8,128)(2,1)}, bf16[192,1024]{1,0:T(8,128)(2,1)}, u32[]{:S(2)}, u32[]{:S(2)}) collective-permute-start(bf16[192,1024]{1,0:T(8,128)(2,1)} %get-tuple-element.38), channel_id=1, source_target_pairs={{0,12},{4,16},{8,20},{12,24},{16,28},{20,0},{24,4},{28,8},{1,13},{... | collective-permute-start | bytes 1179656 | tf_op jit(solution)/shard_map/ppermute | solution.py:64
  82.9 26.6 %collective-permute-start.3 = (bf16[192,1024]{1,0:T(8,128)(2,1)}, bf16[192,1024]{1,0:T(8,128)(2,1)}, u32[]{:S(2)}, u32[]{:S(2)}) collective-permute-start(bf16[192,1024]{1,0:T(8,128)(2,1)} %get-tuple-element.37), channel_id=1, source_target_pairs={{0,16},{4,20},{8,24},{12,28},{16,0},{20,4},{24,8},{28,12},{1,17},{... | collective-permute-start | bytes 1179656 | tf_op jit(solution)/shard_map/ppermute | solution.py:64
  83.5 32.7 %copy-start.16 = (bf16[2048,1024]{1,0:T(8,128)(2,1)S(1)}, bf16[2048,1024]{1,0:T(8,128)(2,1)}, u32[]{:S(2)}) copy-start(bf16[2048,1024]{1,0:T(8,128)(2,1)} %param.7) | copy-start | bytes 12582916
  83.5 32.5 %collective-permute-start.4 = (bf16[192,1024]{1,0:T(8,128)(2,1)}, bf16[192,1024]{1,0:T(8,128)(2,1)S(1)}, u32[]{:S(2)}, u32[]{:S(2)}) collective-permute-start(bf16[192,1024]{1,0:T(8,128)(2,1)} %get-tuple-element.36), channel_id=1, source_target_pairs={{0,20},{4,24},{8,28},{12,0},{16,4},{20,8},{24,12},{28,16},{1,21},{... | collective-permute-start | bytes 1179656 | tf_op jit(solution)/shard_map/ppermute | solution.py:64
  91.3 24.8 %collective-permute-start.5 = (bf16[192,1024]{1,0:T(8,128)(2,1)}, bf16[192,1024]{1,0:T(8,128)(2,1)S(1)}, u32[]{:S(2)}, u32[]{:S(2)}) collective-permute-start(bf16[192,1024]{1,0:T(8,128)(2,1)} %get-tuple-element.35), channel_id=1, source_target_pairs={{0,24},{4,28},{8,0},{12,4},{16,8},{20,12},{24,16},{28,20},{1,25},{... | collective-permute-start | bytes 1179656 | tf_op jit(solution)/shard_map/ppermute | solution.py:64
  93.7 22.4 %collective-permute-start.6 = (bf16[192,1024]{1,0:T(8,128)(2,1)S(1)}, bf16[192,1024]{1,0:T(8,128)(2,1)S(1)}, u32[]{:S(2)}, u32[]{:S(2)}) collective-permute-start(bf16[192,1024]{1,0:T(8,128)(2,1)S(1)} %get-tuple-element.34), channel_id=1, source_target_pairs={{0,28},{4,0},{8,4},{12,8},{16,12},{20,16},{24,20},{28,24},{1,29},{... | collective-permute-start | bytes 1179656 | tf_op jit(solution)/shard_map/ppermute | solution.py:64
  127.0 9.6 %copy-start.4 = (bf16[192,2048]{0,1:T(8,128)(2,1)}, bf16[192,2048]{0,1:T(8,128)(2,1)S(1)}, u32[]{:S(2)}) copy-start(bf16[192,2048]{0,1:T(8,128)(2,1)S(1)} %copy.46) | copy-start | bytes 2359300
  128.7 7.9 %copy-start.6 = (bf16[192,2048]{0,1:T(8,128)(2,1)}, bf16[192,2048]{0,1:T(8,128)(2,1)S(1)}, u32[]{:S(2)}) copy-start(bf16[192,2048]{0,1:T(8,128)(2,1)S(1)} %copy.45) | copy-start | bytes 2359300
  129.2 5.3 %collective-permute-start.7 = (bf16[128,2048]{0,1:T(8,128)(2,1)S(1)}, bf16[128,2048]{0,1:T(8,128)(2,1)S(1)}, u32[]{:S(2)}, u32[]{:S(2)}) collective-permute-start(bf16[128,2048]{0,1:T(8,128)(2,1)S(1)} %slice.44), channel_id=1, source_target_pairs={{0,4},{4,8},{8,12},{12,16},{16,20},{20,24},{24,28},{1,5},{5,9},{9,... | collective-permute-start | bytes 1572872 | tf_op jit(solution)/shard_map/ppermute | solution.py:123
  143.8 6.9 %copy-start.11 = (bf16[192,2048]{0,1:T(8,128)(2,1)S(1)}, bf16[192,2048]{0,1:T(8,128)(2,1)}, u32[]{:S(2)}) copy-start(bf16[192,2048]{0,1:T(8,128)(2,1)} %get-tuple-element.47) | copy-start | bytes 2359300
  222.6 9.6 %copy-start.3 = (bf16[192,2048]{1,0:T(8,128)(2,1)}, bf16[192,2048]{1,0:T(8,128)(2,1)S(1)}, u32[]{:S(2)}) copy-start(bf16[192,2048]{1,0:T(8,128)(2,1)S(1)} %get-tuple-element.44) | copy-start | bytes 2359300
  223.1 9.1 %copy-start.8 = (bf16[192,2048]{0,1:T(8,128)(2,1)}, bf16[192,2048]{0,1:T(8,128)(2,1)S(1)}, u32[]{:S(2)}) copy-start(bf16[192,2048]{0,1:T(8,128)(2,1)S(1)} %copy.51) | copy-start | bytes 2359300
  240.8 9.1 %collective-permute-start.8 = (bf16[128,2048]{1,0:T(8,128)(2,1)S(1)}, bf16[128,2048]{1,0:T(8,128)(2,1)S(1)}, u32[]{:S(2)}, u32[]{:S(2)}) collective-permute-start(bf16[128,2048]{1,0:T(8,128)(2,1)S(1)} %slice.47), channel_id=1, source_target_pairs={{4,0},{8,4},{12,8},{16,12},{20,16},{24,20},{28,24},{5,1},{9,5},{13... | collective-permute-start | bytes 1572872 | tf_op jit(solution)/shard_map/ppermute | solution.py:130
  250.8 16.1 %collective-permute-start.9 = (f32[128,128]{1,0:T(8,128)S(1)}, f32[128,128]{1,0:T(8,128)S(1)}, u32[]{:S(2)}, u32[]{:S(2)}) collective-permute-start(f32[128,128]{1,0:T(8,128)S(1)} %fusion.24), channel_id=1, source_target_pairs={{0,4},{4,0},{8,12},{12,8},{16,20},{20,16},{24,28},{28,24},{1,5},{5... | collective-permute-start | bytes 196616 | tf_op jit(solution)/shard_map/ppermute | solution.py:75
  266.8 6.5 %collective-permute-start.10 = (f32[128,128]{1,0:T(8,128)S(1)}, f32[128,128]{1,0:T(8,128)S(1)}, u32[]{:S(2)}, u32[]{:S(2)}) collective-permute-start(f32[128,128]{1,0:T(8,128)S(1)} %add.212), channel_id=1, source_target_pairs={{0,8},{4,12},{8,0},{12,4},{16,24},{20,28},{24,16},{28,20},{1,9},{5... | collective-permute-start | bytes 196616 | tf_op jit(solution)/shard_map/ppermute | solution.py:75
  273.3 4.3 %collective-permute-start.11 = (f32[128,128]{1,0:T(8,128)S(1)}, f32[128,128]{1,0:T(8,128)S(1)}, u32[]{:S(2)}, u32[]{:S(2)}) collective-permute-start(f32[128,128]{1,0:T(8,128)S(1)} %add.213), channel_id=1, source_target_pairs={{0,16},{4,20},{8,24},{12,28},{16,0},{20,4},{24,8},{28,12},{1,17},{... | collective-permute-start | bytes 196616 | tf_op jit(solution)/shard_map/ppermute | solution.py:75
  277.7 12.7 %collective-permute-start.12 = (f32[128,128]{1,0:T(8,128)S(1)}, f32[128,128]{1,0:T(8,128)S(1)}, u32[]{:S(2)}, u32[]{:S(2)}) collective-permute-start(f32[128,128]{1,0:T(8,128)S(1)} %add_multiply_fusion), channel_id=1, source_target_pairs={{0,1},{1,0},{2,3},{3,2},{4,5},{5,4},{6,7},{7,6},{8,9},{9,8},{10,11... | collective-permute-start | bytes 196616 | tf_op jit(solution)/shard_map/ppermute | solution.py:86
  284.4 8.5 %copy-start.5 = (bf16[192,2048]{0,1:T(8,128)(2,1)S(1)}, bf16[192,2048]{0,1:T(8,128)(2,1)}, u32[]{:S(2)}) copy-start(bf16[192,2048]{0,1:T(8,128)(2,1)} %copy-done.4) | copy-start | bytes 2359300
  284.4 8.5 %copy-start.7 = (bf16[192,2048]{0,1:T(8,128)(2,1)S(1)}, bf16[192,2048]{0,1:T(8,128)(2,1)}, u32[]{:S(2)}) copy-start(bf16[192,2048]{0,1:T(8,128)(2,1)} %copy-done.6) | copy-start | bytes 2359300
  290.4 8.9 %collective-permute-start.13 = (f32[256,128]{1,0:T(8,128)S(1)}, f32[256,128]{1,0:T(8,128)S(1)}, u32[]{:S(2)}, u32[]{:S(2)}) collective-permute-start(f32[256,128]{1,0:T(8,128)S(1)} %maximum_select_fusion.1), channel_id=1, source_target_pairs={{0,2},{1,3},{2,0},{3,1},{4,6},{5,7},{6,4},{7,5},{8,10},{9,11},{10,... | collective-permute-start | bytes 393224 | tf_op jit(solution)/shard_map/ppermute | solution.py:86
  (9 other events, 40.4 us)
Sparse Core Ops, SparseCore 0:
  9.6 66.1 all-gather.1
  125.5 92.0 reduce-scatter.1

commit v16 on v15

--- a/solution.py
+++ b/solution.py
@@ -141,7 +141,6 @@
         term = jnp.einsum("gij,ijs->gs", piece.astype(jnp.bfloat16), pick, preferred_element_type=jnp.float32)
         diag = term if diag is None else diag + term
     scale = (rows * ctx_count * per_group) ** (-0.5)
-    diag, next_head = lax.optimization_barrier((diag, next_head))
     local_filters = butterfly_sum(diag, "ctx", ctx_count) * scale
     grad_filters = butterfly_gather(local_filters, "mp", mp_count)
     trailing = jnp.concatenate([grad_conv, next_head], 0)

time: 308 us -> 314 us (1.019)
  waiting for transfers between devices: 134 us -> 141 us
    ppermute x3, waiting for transfers between devices: 0.68 us -> 5.03 us  [butterfly_sum(): x = x + lax.ppermute(x, axis, [(k, k ^ step) for k in range(count)])]
    unnamed x38 -> x36, local copies, waits for them, and re-layouts: 9.3 us -> 8.59 us
  transfers between devices with their start and end apart: 16 -> 16, of which waited for: 7 -> 10; matrix products, arithmetic and copies ran while one was open for 30% -> 20% of each run, Pallas kernels for 0% -> 0%
where the time goes in v16:
time: 314 us; the launch traced here: 313 us
  waiting for transfers between devices  141 us (45%)
  local copies, waits for them, and re-layouts  83 us (26%)
  matrix products  36.9 us (12%)
  starting transfers between devices  24.9 us (8%)
  between operations  14.5 us (5%)
  other arithmetic  12.8 us (4%)
    all_gather x1, waiting for transfers between devices, body(): cot_rows = lax.all_gather(cotangent, 'mp', axis=1, tiled=True)  57.9 us
    reduce_scatter x1, waiting for transfers between devices, body(): lax.psum_scatter(partial, 'ctx', scatter_dimension=0, tiled=True)  52.9 us
    optimization_barrier x4, local copies, waits for them, and re-layouts, body(): lax.optimization_barrier((cot_rows, mats_causal, mats_anti))  28.7 us
    ppermute x7, waiting for transfers between devices, exchange_columns(): lax.ppermute(chunk, 'ctx', [(k, (k + shift) % count) for k in range(count)])  19.9 us
    ppermute x7, starting transfers between devices, exchange_columns(): lax.ppermute(chunk, 'ctx', [(k, (k + shift) % count) for k in range(count)])  12.8 us
    reshape x2, local copies, waits for them, and re-layouts, filter_apply(): return total.reshape(tiles * block, chans)  10.8 us
    dot_general x4, matrix products, filter_apply(): jnp.einsum('gij,kjgc->kigc', m, w4, preferred_element_type=jnp.float32)  9.91 us
    dot_general x1, matrix products, contract(): lax.dot_general(left, right, (((1,), (1,)), ((), ())), preferred_element_...  9.16 us
  transfers between devices with their start and end apart: 16, of which 10 were waited for; matrix products, arithmetic and copies ran while one was open for 20% of the time, Pallas kernels for 0%

profile of v16, /device:TPU:0, one launch (start us, length us, event | category | flops | bytes accessed | tf_op | source)
XLA Modules:
  0.0 312.8 jit_solution(6226833361021639188)
XLA Ops:
  12.6 5.3 %fusion.35 = (bf16[128,64,192]{0,2,1:T(8,128)(2,1)}, bf16[128,64,192]{0,2,1:T(8,128)(2,1)}, bf16[128,64,192]{0,2,1:T(8,128)(2,1)}, bf16[128,64,192]{0,2,1:T(8,128)(2,1)}) fusion(bf16[256,64,192]{0,2,1:T(8,128)(2,1)S(1)} %fusion.5, bf16[256,64,192]{0,2,1:T(8,128)(2,1)S(1)} %fusion.6), kind=kLoop, calls=%fused_computation.73 | loop fusion | bytes 25165824 | tf_op jit(solution)/shard_map/slice | solution.py:30
  17.9 57.9 %all-gather.2.cloned.1.call-done = bf16[192,8192]{1,0:T(8,128)(2,1)} async-done(((bf16[192,2048]{1,0:T(8,128)(2,1)}), bf16[192,8192]{1,0:T(8,128)(2,1)}) %all-gather.2.cloned.1.call-update) | async-done | bytes 3145744 | tf_op jit(solution)/shard_map/all_gather | solution.py:114
  83.6 7.7 %collective-permute-done = bf16[192,1024]{1,0:T(8,128)(2,1)} collective-permute-done((bf16[192,1024]{1,0:T(8,128)(2,1)}, bf16[192,1024]{1,0:T(8,128)(2,1)}, u32[]{:S(2)}, u32[]{:S(2)}) %collective-permute-start) | collective-permute-done | bytes 393248 | tf_op jit(solution)/shard_map/ppermute | solution.py:64
  93.7 7.0 %collective-permute-start.6 = (bf16[192,1024]{1,0:T(8,128)(2,1)S(1)}, bf16[192,1024]{1,0:T(8,128)(2,1)S(1)}, u32[]{:S(2)}, u32[]{:S(2)}) collective-permute-start(bf16[192,1024]{1,0:T(8,128)(2,1)S(1)} %get-tuple-element.30), channel_id=1, source_target_pairs={{0,28},{4,0},{8,4},{12,8},{16,12},{20,16},{24,20},{28,24},{1,29},{... | collective-permute-start | bytes 1179656 | tf_op jit(solution)/shard_map/ppermute | solution.py:64
  101.7 6.8 %collective-permute-done.2 = bf16[192,1024]{1,0:T(8,128)(2,1)} collective-permute-done((bf16[192,1024]{1,0:T(8,128)(2,1)}, bf16[192,1024]{1,0:T(8,128)(2,1)}, u32[]{:S(2)}, u32[]{:S(2)}) %collective-permute-start.2) | collective-permute-done | bytes 393248 | tf_op jit(solution)/shard_map/ppermute | solution.py:64
  110.6 5.4 %collective-permute-done.4 = bf16[192,1024]{1,0:T(8,128)(2,1)S(1)} collective-permute-done((bf16[192,1024]{1,0:T(8,128)(2,1)}, bf16[192,1024]{1,0:T(8,128)(2,1)S(1)}, u32[]{:S(2)}, u32[]{:S(2)}) %collective-permute-start.4) | collective-permute-done | bytes 393248 | tf_op jit(solution)/shard_map/ppermute | solution.py:64
  116.2 9.2 %fusion.37 = f32[1536,2048]{1,0:T(8,128)} fusion(bf16[1536,1024]{1,0:T(8,128)(2,1)S(1)} %constant_dynamic-update-slice_fusion, bf16[2048,1024]{1,0:T(8,128)(2,1)S(1)} %copy-done.15), kind=kOutput, calls=%fused_computation.75 | convolution fusion | flops 6442450944 | bytes 19922944 | tf_op jit(solution)/shard_map/dot_general | solution.py:8
  129.2 3.9 %collective-permute-start.7 = (bf16[128,2048]{0,1:T(8,128)(2,1)S(1)}, bf16[128,2048]{0,1:T(8,128)(2,1)S(1)}, u32[]{:S(2)}, u32[]{:S(2)}) collective-permute-start(bf16[128,2048]{0,1:T(8,128)(2,1)S(1)} %slice.44), channel_id=1, source_target_pairs={{0,4},{4,8},{8,12},{12,16},{16,20},{20,24},{24,28},{1,5},{5,9},{9,... | collective-permute-start | bytes 1572872 | tf_op jit(solution)/shard_map/ppermute | solution.py:123
  136.6 7.2 %copy.67 = bf16[128,64,192,1]{2,1,3,0:T(8,128)(2,1)} copy(bf16[128,64,192,1]{0,2,1,3:T(8,128)(2,1)} %bitcast.51) | data formatting | bytes 6291456 | tf_op jit(solution)/shard_map/optimization_barrier | solution.py:115
  143.8 7.0 %copy.66 = bf16[128,64,192,1]{2,1,3,0:T(8,128)(2,1)} copy(bf16[128,64,192,1]{0,2,1,3:T(8,128)(2,1)} %bitcast.50) | data formatting | bytes 6291456 | tf_op jit(solution)/shard_map/optimization_barrier | solution.py:115
  150.8 3.5 %fusion.34 = f32[128,3,16,64]{3,2,1,0:T(8,128)S(1)} fusion(bf16[128,64,192,1]{2,1,3,0:T(8,128)(2,1)} %copy.67, bf16[1,192,128,16]{1,3,0,2:T(8,128)(2,1)S(1)} %bitcast.45, bf16[1,192,128,16]{1,3,0,2:T(8,128)(2,1)S(1)} %bitcast.58, bf16[1,192,128,16]{1,3,0,2:T(8,128)(2,1)S(1)} %bitcast.55), kind=kOutput, calls=%fused_computation.72 | convolution fusion | flops 153354240 | bytes 7077888 | tf_op jit(solution)/shard_map/gij,kjgc->kigc/dot_general | solution.py:48
  156.0 3.7 %copy.49 = f32[3,64,128,16]{1,0,3,2:T(4,128)} copy(f32[3,64,128,16]{1,3,0,2:T(8,128)S(1)} %add_bitcast_fusion.1) | data formatting | bytes 3145728 | tf_op jit(solution)/shard_map/add | solution.py:49
  159.8 4.9 %reshape.32 = f32[192,2048]{0,1:T(8,128)S(1)} reshape(f32[3,64,128,16]{1,0,3,2:T(4,128)} %copy.49) | data formatting | bytes 3145728 | tf_op jit(solution)/shard_map/reshape | solution.py:51
  164.6 52.9 %reduce-scatter.2.cloned.1.call-done = f32[192,2048]{1,0:T(8,128)} async-done(((f32[1536,2048]{1,0:T(8,128)}), f32[192,2048]{1,0:T(8,128)}) %reduce-scatter.2.cloned.1.call-update) | async-done | bytes 1572880 | tf_op jit(solution)/shard_map/reduce_scatter | solution.py:118
  219.3 3.4 %multiply_convert_fusion = (bf16[192,2048]{1,0:T(8,128)(2,1)S(1)}, bf16[192,2048]{1,0:T(8,128)(2,1)}) fusion(f32[192,2048]{1,0:T(8,128)} %reduce-scatter.2.cloned.1.call-done, bf16[192,2048]{1,0:T(8,128)(2,1)} %param.8, f32[192,2048]{1,0:T(8,128)} %copy.50), kind=kLoop, calls=%fused_computation.32 | loop fusion | flops 1966080 | bytes 5505024 | tf_op jit(solution)/shard_map/convert_element_type | solution.py:129
  225.5 6.8 %convolution_bitcast_fusion = f32[128,64,192]{2,1,0:T(8,128)} fusion(bf16[3,64,128,16]{1,0,3,2:T(4,128)(2,1)} %reshape.34, bf16[1,192,128,16]{1,3,0,2:T(8,128)(2,1)S(1)} %bitcast.47, bf16[1,192,128,16]{1,3,0,2:T(8,128)(2,1)} %bitcast.57, bf16[1,192,128,16]{1,3,0,2:T(8,128)(2,1)} %bitcast.54), kind=kOutput, calls=%fused_computation.11 | convolution fusion | flops 153354240 | bytes 9437184 | tf_op jit(solution)/shard_map/kigc,kjgc->gij/dot_general | solution.py:133
  232.2 8.6 %copy.62 = f32[128,64,192]{0,2,1:T(8,128)} copy(f32[128,64,192]{2,1,0:T(8,128)} %convolution_bitcast_fusion) | data formatting | bytes 12582912 | tf_op jit(solution)/shard_map/kigc,kjgc->gij/dot_general | solution.py:133
  240.8 5.0 %fusion.20 = f32[128,128]{1,0:T(8,128)S(1)} fusion(s32[128]{0:T(128)S(1)} %iota_add_fusion, s32[64]{0:T(128)S(1)} %iota_add_fusion.1, f32[128,64,192]{0,2,1:T(8,128)} %copy.62), kind=kOutput, calls=%fused_computation.37 | convolution fusion | flops 408944640 | bytes 6357760 | tf_op jit(solution)/shard_map/gij,ijs->gs/dot_general | solution.py:141
  251.0 3.0 collective-permute-done.10
  265.2 6.9 %copy.68 = bf16[128,64,192,1]{2,1,3,0:T(8,128)(2,1)} copy(bf16[128,64,192,1]{0,2,1,3:T(8,128)(2,1)} %bitcast.49) | data formatting | bytes 6291456 | tf_op jit(solution)/shard_map/optimization_barrier | solution.py:115
  272.1 7.6 %copy.69 = bf16[128,64,192,1]{2,1,3,0:T(8,128)(2,1)} copy(bf16[128,64,192,1]{0,2,1,3:T(8,128)(2,1)S(1)} %bitcast.48) | data formatting | bytes 6291456 | tf_op jit(solution)/shard_map/optimization_barrier | solution.py:115
  284.9 3.5 %fusion.19 = f32[128,3,16,64]{3,2,1,0:T(8,128)S(1)} fusion(bf16[128,64,192,1]{2,1,3,0:T(8,128)(2,1)} %copy.68, bf16[1,192,128,16]{1,3,0,2:T(8,128)(2,1)S(1)} %bitcast.60, bf16[1,192,128,16]{1,3,0,2:T(8,128)(2,1)S(1)} %bitcast.62, bf16[1,192,128,16]{1,3,0,2:T(8,128)(2,1)S(1)} %bitcast.52), kind=kOutput, calls=%fused_computation.36 | convolution fusion | flops 153354240 | bytes 7077888 | tf_op jit(solution)/shard_map/gij,kjgc->kigc/dot_general | solution.py:48
  289.9 3.8 %copy.59 = f32[3,64,128,16]{1,0,3,2:T(4,128)} copy(f32[3,64,128,16]{1,3,0,2:T(8,128)S(1)} %add_bitcast_fusion) | data formatting | bytes 3145728 | tf_op jit(solution)/shard_map/add | solution.py:49
  293.7 6.0 %reshape.33 = f32[192,2048]{0,1:T(8,128)} reshape(f32[3,64,128,16]{1,0,3,2:T(4,128)} %copy.59) | data formatting | bytes 3145728 | tf_op jit(solution)/shard_map/reshape | solution.py:51
  (95 shorter events, 61.5 us)
Async XLA Ops:
  7.2 68.6 %all-gather.2.cloned.1.call-start = ((), (), s32[]{:S(2)}) async-start(), calls=%async_computation.1 | async-start | bytes 3932160 | tf_op jit(solution)/shard_map/all_gather | solution.py:114
  7.9 209.6 %reduce-scatter.2.cloned.1.call-start = ((), (), s32[]{:S(2)}) async-start(), calls=%async_computation.2 | async-start | bytes 14155776 | tf_op jit(solution)/shard_map/reduce_scatter | solution.py:118
  79.1 12.2 %collective-permute-start = (bf16[192,1024]{1,0:T(8,128)(2,1)}, bf16[192,1024]{1,0:T(8,128)(2,1)}, u32[]{:S(2)}, u32[]{:S(2)}) collective-permute-start(bf16[192,1024]{1,0:T(8,128)(2,1)} %get-tuple-element.36), channel_id=1, source_target_pairs={{0,4},{4,8},{8,12},{12,16},{16,20},{20,24},{24,28},{28,0},{1,5},{5... | collective-permute-start | bytes 1179656 | tf_op jit(solution)/shard_map/ppermute | solution.py:64
  79.1 14.6 %collective-permute-start.1 = (bf16[192,1024]{1,0:T(8,128)(2,1)}, bf16[192,1024]{1,0:T(8,128)(2,1)}, u32[]{:S(2)}, u32[]{:S(2)}) collective-permute-start(bf16[192,1024]{1,0:T(8,128)(2,1)} %get-tuple-element.35), channel_id=1, source_target_pairs={{0,8},{4,12},{8,16},{12,20},{16,24},{20,28},{24,0},{28,4},{1,9},{5... | collective-permute-start | bytes 1179656 | tf_op jit(solution)/shard_map/ppermute | solution.py:64
  80.6 27.9 %collective-permute-start.2 = (bf16[192,1024]{1,0:T(8,128)(2,1)}, bf16[192,1024]{1,0:T(8,128)(2,1)}, u32[]{:S(2)}, u32[]{:S(2)}) collective-permute-start(bf16[192,1024]{1,0:T(8,128)(2,1)} %get-tuple-element.34), channel_id=1, source_target_pairs={{0,12},{4,16},{8,20},{12,24},{16,28},{20,0},{24,4},{28,8},{1,13},{... | collective-permute-start | bytes 1179656 | tf_op jit(solution)/shard_map/ppermute | solution.py:64
  83.0 26.6 %collective-permute-start.3 = (bf16[192,1024]{1,0:T(8,128)(2,1)}, bf16[192,1024]{1,0:T(8,128)(2,1)}, u32[]{:S(2)}, u32[]{:S(2)}) collective-permute-start(bf16[192,1024]{1,0:T(8,128)(2,1)} %get-tuple-element.33), channel_id=1, source_target_pairs={{0,16},{4,20},{8,24},{12,28},{16,0},{20,4},{24,8},{28,12},{1,17},{... | collective-permute-start | bytes 1179656 | tf_op jit(solution)/shard_map/ppermute | solution.py:64
  83.5 32.7 %copy-start.15 = (bf16[2048,1024]{1,0:T(8,128)(2,1)S(1)}, bf16[2048,1024]{1,0:T(8,128)(2,1)}, u32[]{:S(2)}) copy-start(bf16[2048,1024]{1,0:T(8,128)(2,1)} %param.7) | copy-start | bytes 12582916
  83.5 32.5 %collective-permute-start.4 = (bf16[192,1024]{1,0:T(8,128)(2,1)}, bf16[192,1024]{1,0:T(8,128)(2,1)S(1)}, u32[]{:S(2)}, u32[]{:S(2)}) collective-permute-start(bf16[192,1024]{1,0:T(8,128)(2,1)} %get-tuple-element.32), channel_id=1, source_target_pairs={{0,20},{4,24},{8,28},{12,0},{16,4},{20,8},{24,12},{28,16},{1,21},{... | collective-permute-start | bytes 1179656 | tf_op jit(solution)/shard_map/ppermute | solution.py:64
  91.3 24.8 %collective-permute-start.5 = (bf16[192,1024]{1,0:T(8,128)(2,1)}, bf16[192,1024]{1,0:T(8,128)(2,1)S(1)}, u32[]{:S(2)}, u32[]{:S(2)}) collective-permute-start(bf16[192,1024]{1,0:T(8,128)(2,1)} %get-tuple-element.31), channel_id=1, source_target_pairs={{0,24},{4,28},{8,0},{12,4},{16,8},{20,12},{24,16},{28,20},{1,25},{... | collective-permute-start | bytes 1179656 | tf_op jit(solution)/shard_map/ppermute | solution.py:64
  93.7 22.4 %collective-permute-start.6 = (bf16[192,1024]{1,0:T(8,128)(2,1)S(1)}, bf16[192,1024]{1,0:T(8,128)(2,1)S(1)}, u32[]{:S(2)}, u32[]{:S(2)}) collective-permute-start(bf16[192,1024]{1,0:T(8,128)(2,1)S(1)} %get-tuple-element.30), channel_id=1, source_target_pairs={{0,28},{4,0},{8,4},{12,8},{16,12},{20,16},{24,20},{28,24},{1,29},{... | collective-permute-start | bytes 1179656 | tf_op jit(solution)/shard_map/ppermute | solution.py:64
  127.0 9.6 %copy-start.4 = (bf16[192,2048]{0,1:T(8,128)(2,1)}, bf16[192,2048]{0,1:T(8,128)(2,1)S(1)}, u32[]{:S(2)}) copy-start(bf16[192,2048]{0,1:T(8,128)(2,1)S(1)} %copy.46) | copy-start | bytes 2359300
  128.7 7.9 %copy-start.6 = (bf16[192,2048]{0,1:T(8,128)(2,1)}, bf16[192,2048]{0,1:T(8,128)(2,1)S(1)}, u32[]{:S(2)}) copy-start(bf16[192,2048]{0,1:T(8,128)(2,1)S(1)} %copy.45) | copy-start | bytes 2359300
  129.2 5.3 %collective-permute-start.7 = (bf16[128,2048]{0,1:T(8,128)(2,1)S(1)}, bf16[128,2048]{0,1:T(8,128)(2,1)S(1)}, u32[]{:S(2)}, u32[]{:S(2)}) collective-permute-start(bf16[128,2048]{0,1:T(8,128)(2,1)S(1)} %slice.44), channel_id=1, source_target_pairs={{0,4},{4,8},{8,12},{12,16},{16,20},{20,24},{24,28},{1,5},{5,9},{9,... | collective-permute-start | bytes 1572872 | tf_op jit(solution)/shard_map/ppermute | solution.py:123
  143.8 7.0 %copy-start.10 = (bf16[192,2048]{0,1:T(8,128)(2,1)S(1)}, bf16[192,2048]{0,1:T(8,128)(2,1)}, u32[]{:S(2)}) copy-start(bf16[192,2048]{0,1:T(8,128)(2,1)} %get-tuple-element.42) | copy-start | bytes 2359300
  143.8 7.0 %copy-start.11 = (bf16[192,2048]{0,1:T(8,128)(2,1)S(1)}, bf16[192,2048]{0,1:T(8,128)(2,1)}, u32[]{:S(2)}) copy-start(bf16[192,2048]{0,1:T(8,128)(2,1)} %get-tuple-element.43) | copy-start | bytes 2359300
  222.7 32.7 %copy-start.3 = (bf16[192,2048]{1,0:T(8,128)(2,1)}, bf16[192,2048]{1,0:T(8,128)(2,1)S(1)}, u32[]{:S(2)}) copy-start(bf16[192,2048]{1,0:T(8,128)(2,1)S(1)} %get-tuple-element.40) | copy-start | bytes 2359300
  223.2 9.1 %copy-start.8 = (bf16[192,2048]{0,1:T(8,128)(2,1)}, bf16[192,2048]{0,1:T(8,128)(2,1)S(1)}, u32[]{:S(2)}) copy-start(bf16[192,2048]{0,1:T(8,128)(2,1)S(1)} %copy.51) | copy-start | bytes 2359300
  248.3 1.3 collective-permute-start.9
  249.6 4.3 %collective-permute-start.10 = (f32[128,128]{1,0:T(8,128)S(1)}, f32[128,128]{1,0:T(8,128)S(1)}, u32[]{:S(2)}, u32[]{:S(2)}) collective-permute-start(f32[128,128]{1,0:T(8,128)S(1)} %add.212), channel_id=1, source_target_pairs={{0,8},{4,12},{8,0},{12,4},{16,24},{20,28},{24,16},{28,20},{1,9},{5... | collective-permute-start | bytes 196616 | tf_op jit(solution)/shard_map/ppermute | solution.py:75
  254.0 4.3 %collective-permute-start.11 = (f32[128,128]{1,0:T(8,128)S(1)}, f32[128,128]{1,0:T(8,128)S(1)}, u32[]{:S(2)}, u32[]{:S(2)}) collective-permute-start(f32[128,128]{1,0:T(8,128)S(1)} %add.213), channel_id=1, source_target_pairs={{0,16},{4,20},{8,24},{12,28},{16,0},{20,4},{24,8},{28,12},{1,17},{... | collective-permute-start | bytes 196616 | tf_op jit(solution)/shard_map/ppermute | solution.py:75
  256.2 24.3 %collective-permute-start.8 = (bf16[128,2048]{1,0:T(8,128)(2,1)}, bf16[128,2048]{1,0:T(8,128)(2,1)}, u32[]{:S(2)}, u32[]{:S(2)}) collective-permute-start(bf16[128,2048]{1,0:T(8,128)(2,1)} %slice.47), channel_id=1, source_target_pairs={{4,0},{8,4},{12,8},{16,12},{20,16},{24,20},{28,24},{5,1},{9,5},{13... | collective-permute-start | bytes 1572872 | tf_op jit(solution)/shard_map/ppermute | solution.py:130
  258.3 4.4 %collective-permute-start.12 = (f32[128,128]{1,0:T(8,128)S(1)}, f32[128,128]{1,0:T(8,128)S(1)}, u32[]{:S(2)}, u32[]{:S(2)}) collective-permute-start(f32[128,128]{1,0:T(8,128)S(1)} %add_multiply_fusion), channel_id=1, source_target_pairs={{0,1},{1,0},{2,3},{3,2},{4,5},{5,4},{6,7},{7,6},{8,9},{9,8},{10,11... | collective-permute-start | bytes 196616 | tf_op jit(solution)/shard_map/ppermute | solution.py:86
  262.7 17.1 %collective-permute-start.13 = (f32[256,128]{1,0:T(8,128)S(1)}, f32[256,128]{1,0:T(8,128)S(1)}, u32[]{:S(2)}, u32[]{:S(2)}) collective-permute-start(f32[256,128]{1,0:T(8,128)S(1)} %maximum_select_fusion.1), channel_id=1, source_target_pairs={{0,2},{1,3},{2,0},{3,1},{4,6},{5,7},{6,4},{7,5},{8,10},{9,11},{10,... | collective-permute-start | bytes 393224 | tf_op jit(solution)/shard_map/ppermute | solution.py:86
  265.2 6.9 %copy-start.2 = (bf16[128,64,192]{0,2,1:T(8,128)(2,1)S(1)}, bf16[128,64,192]{0,2,1:T(8,128)(2,1)}, u32[]{:S(2)}) copy-start(bf16[128,64,192]{0,2,1:T(8,128)(2,1)} %get-tuple-element.17) | copy-start | bytes 9437188
  (8 other events, 31.8 us)
Sparse Core Ops, SparseCore 0:
  9.6 66.1 all-gather.1
  125.5 92.0 reduce-scatter.1
